TPU v7x, 32 devices: a whole 2x2x4 slice. The times are simulated.
32 devices in a mesh: gx: 4 (over x, core), gy: 4 (over z), gz: 2 (over y).
Axes of the slice: x: 2, y: 2, z: 4, core: 2. Of those that a mesh axis runs over, the one named last changes fastest.
Arguments:
- adjoint: float32 [5, 128, 64, 256], P(None, 'gx', 'gy', 'gz'), may hold values from -6 to 6
- stencil_weights: float32 [3, 2, 3, 5, 128, 64, 256], P(None, None, None, None, 'gx', 'gy', 'gz'), as said below
- flux_plus: float32 [3, 5, 5], replicated, may hold values from -1.5 to 1.5
- flux_minus: float32 [3, 5, 5], replicated, may hold values from -1.5 to 1.5
- wall_row: int32 [512], P(('gx', 'gy', 'gz')), may hold values from 0 to 511
- wall_panel: int32 [512, 128], P(('gx', 'gy', 'gz')), may hold values from 0 to 1023
- wall_coef: float32 [5, 512, 128], P(None, ('gx', 'gy', 'gz')), may hold values from -1.2 to 1.2
- wall_count: int32 [32], P(('gx', 'gy', 'gz')), may hold values from 1 to 16, 256 in all
- panel_owner: int32 [1024], replicated, may hold values from 0 to 31, as said below
Outputs:
- section_adjoint: float32 [5, 128, 64, 256], P(None, 'gx', 'gy', 'gz')
- panel_sens: float32 [1024], P(('gx', 'gy', 'gz'))
Inputs may be any that keep to these rules, and one draw needn't show every extreme that they name: `stencil_weights`: Positive; the three candidate weights of one direction, side, field and cell sum to one up to rounding. `panel_owner`: each device index owns exactly 32 panels.
All inputs are finite; a program needn't handle non-finite values. No bound on the sum of `wall_count` on one device may be relied on, other than what follows from the above.
Results may differ from a plain program's by a relative error of at most 0.00012.
Values sent between devices are 32-bit elements; how exact they have to be, the bound alone decides.
No kernel may reach another device: no remote copies, remote signals or barrier semaphores. Data moves between devices by JAX's collectives and lax.ppermute only.
A program may use at most 128 MiB of HBM per device.

v0:
```python
import jax
import jax.numpy as jnp
from jax import lax
from jax.experimental import pallas as pl
from jax.experimental.pallas import tpu as pltpu
from jax.sharding import PartitionSpec as P

AXES = ("gx", "gy", "gz")
STEP = 0.4
SECTION = 0.25
XC = 4
F32 = jnp.float32
HI = lax.Precision.HIGHEST
VMEM = pl.BlockSpec(memory_space=pltpu.VMEM)
SMEM = pl.BlockSpec(memory_space=pltpu.SMEM)


def shift_from(x, axis, by):
    n = lax.axis_size(axis)
    return lax.ppermute(x, axis, [(i, (i + by) % n) for i in range(n)])


def iotas(ny, nz):
    return (
        lax.broadcasted_iota(jnp.int32, (ny, nz), 0),
        lax.broadcasted_iota(jnp.int32, (ny, nz), 1),
    )


def fronts_kernel(adj_ref, xf_ref, yf_ref, zf_ref):
    nf, nx, ny, nz = adj_ref.shape
    row, lane = iotas(ny, nz)
    for f in range(nf):
        xf_ref[f] = adj_ref[f, 0]
        zacc = jnp.zeros((ny, nz), F32)
        for x in range(nx):
            s = adj_ref[f, x]
            yf_ref[f, pl.ds(x, 1), :] = s[0:1, :]
            zacc = zacc + pltpu.roll(jnp.where(lane == 0, s, 0.0), x, 1)
        zf_ref[f] = zacc


def offset_terms(plus, minus, w):
    p0, p1, p2 = plus * w(0, 0), plus * w(0, 1), plus * w(0, 2)
    m0, m1, m2 = minus * w(1, 0), minus * w(1, 1), minus * w(1, 2)
    a = p1 + m2
    b = p2 + m1
    return [
        p0 * (1.0 / 3.0),
        p0 * (-7.0 / 6.0) + a * (-1.0 / 6.0),
        p0 * (11.0 / 6.0) + a * (5.0 / 6.0) + b * (1.0 / 3.0),
        a * (1.0 / 3.0) + b * (5.0 / 6.0) + m0 * (11.0 / 6.0),
        b * (-1.0 / 6.0) + m0 * (-7.0 / 6.0),
        m0 * (1.0 / 3.0),
    ]


def split_wrap(terms, idx, n, axis):
    inner = terms[2]
    wrap = None
    for o in (0, 1, 3, 4, 5):
        s = o - 2
        r = pltpu.roll(terms[o], s % n, axis)
        valid = (idx >= s) if s > 0 else (idx < n + s)
        inner = inner + jnp.where(valid, r, 0.0)
        piece = jnp.where(valid, 0.0, r)
        wrap = piece if wrap is None else wrap + piece
    return inner, wrap


def stencil_kernel(fp_ref, fm_ref, adj_ref, xf_ref, yf_ref, zf_ref, w_ref,
                   sec_ref, xl_ref, xr_ref, yl_ref, yr_ref, zl_ref, zr_ref, acc_ref):
    nf, nx, ny, nz = adj_ref.shape
    i = pl.program_id(0)
    row, lane = iotas(ny, nz)

    @pl.when(i == 0)
    def _():
        acc_ref[...] = jnp.zeros_like(acc_ref)
        zl_ref[...] = jnp.zeros_like(zl_ref)
        zr_ref[...] = jnp.zeros_like(zr_ref)

    def flux(d, diff):
        plus, minus = [], []
        for f in range(nf):
            p = m = None
            for g in range(nf):
                k = (d * nf + g) * nf + f
                tp = diff[g] * fp_ref[k]
                tm = diff[g] * fm_ref[k]
                p = tp if p is None else p + tp
                m = tm if m is None else m + tm
            plus.append(p)
            minus.append(m)
        return plus, minus

    yr_parts = {}
    yl_parts = {}
    for xl in range(XC):
        x = i * XC + xl
        a = [adj_ref[f, x] for f in range(nf)]
        last = x == nx - 1
        nxt = jnp.minimum(x + 1, nx - 1)
        an_x = [jnp.where(last, xf_ref[f], adj_ref[f, nxt]) for f in range(nf)]
        an_y = [
            jnp.where(row == ny - 1, yf_ref[f, pl.ds(x, 1), :], pltpu.roll(a[f], ny - 1, 0))
            for f in range(nf)
        ]
        zshift = nz - 1 - x
        an_z = [
            jnp.where(lane == nz - 1, pltpu.roll(zf_ref[f], zshift, 1), pltpu.roll(a[f], nz - 1, 1))
            for f in range(nf)
        ]
        fx = flux(0, [an_x[g] - a[g] for g in range(nf)])
        fy = flux(1, [an_y[g] - a[g] for g in range(nf)])
        fz = flux(2, [an_z[g] - a[g] for g in range(nf)])
        for f in range(nf):
            sx = offset_terms(fx[0][f], fx[1][f], lambda s, k: w_ref[0, s, k, f, xl])
            sy = offset_terms(fy[0][f], fy[1][f], lambda s, k: w_ref[1, s, k, f, xl])
            sz = offset_terms(fz[0][f], fz[1][f], lambda s, k: w_ref[2, s, k, f, xl])
            iy, wy = split_wrap(sy, row, ny, 0)
            iz, wz = split_wrap(sz, lane, nz, 1)
            for o in range(6):
                val = sx[o] if o != 2 else sx[2] + iy + iz
                acc_ref[f, x + o] = acc_ref[f, x + o] + val
            rear = pltpu.roll(jnp.where(row < 3, wy, 0.0), 4 * (xl % 2), 0)[0:8]
            lead = pltpu.roll(jnp.where(row >= ny - 2, wy, 0.0), 2 + 2 * (xl % 4), 0)[0:8]
            kr = (f, xl // 2)
            kl = (f, xl // 4)
            yr_parts[kr] = rear if kr not in yr_parts else yr_parts[kr] + rear
            yl_parts[kl] = lead if kl not in yl_parts else yl_parts[kl] + lead
            zr_ref[f] = zr_ref[f] + pltpu.roll(jnp.where(lane < 3, wz, 0.0), 4 * x, 1)
            zl_ref[f] = zl_ref[f] + pltpu.roll(jnp.where(lane >= nz - 2, wz, 0.0), 2 + 4 * x, 1)
    for (f, t), v in yr_parts.items():
        yr_ref[f, t] = v
    for (f, t), v in yl_parts.items():
        yl_ref[f, t] = v

    @pl.when(i == pl.num_programs(0) - 1)
    def _():
        def body(x, c):
            for f in range(nf):
                sec_ref[f, x] = SECTION * (adj_ref[f, x] + acc_ref[f, x + 2])
            return c

        lax.fori_loop(0, nx, body, 0)
        for f in range(nf):
            xl_ref[f] = acc_ref[f, 0:2]
            xr_ref[f] = acc_ref[f, nx + 2:nx + 5]


def fix_kernel(row_ref, cnt_ref, sec_ref, axl_ref, axr_ref, ayl_ref, ayr_ref, azl_ref, azr_ref,
               coef_ref, out_ref, wt_ref):
    nf, nx, ny, nz = sec_ref.shape
    row, lane = iotas(ny, nz)
    pad = jnp.zeros((ny - 8, nz), F32)
    for x in range(nx):
        for f in range(nf):
            ty = jnp.concatenate([ayr_ref[f, x // 2], pad], 0)
            add = jnp.where(row < 3, pltpu.roll(ty, (ny - 4 * (x % 2)) % ny, 0), 0.0)
            ty = jnp.concatenate([ayl_ref[f, x // 4], pad], 0)
            add = add + jnp.where(row >= ny - 2, pltpu.roll(ty, (ny - 2 - 2 * (x % 4)) % ny, 0), 0.0)
            add = add + jnp.where(lane < 3, pltpu.roll(azr_ref[f], (nz - 4 * x) % nz, 1), 0.0)
            add = add + jnp.where(lane >= nz - 2, pltpu.roll(azl_ref[f], (nz - 2 - 4 * x) % nz, 1), 0.0)
            if x < 3:
                add = add + axr_ref[f, x]
            if x >= nx - 2:
                add = add + axl_ref[f, x - (nx - 2)]
            out_ref[f, x] = sec_ref[f, x] + SECTION * add
    live_n = cnt_ref[0]
    for r in range(wt_ref.shape[0]):
        idx = row_ref[r]
        lx = idx // ny
        ly = idx % ny
        val = None
        for f in range(nf):
            v = out_ref[f, lx, pl.ds(ly, 1), :] * coef_ref[f, pl.ds(r, 1), :]
            val = v if val is None else val + v
        wt_ref[pl.ds(r, 1), :] = val * jnp.where(r < live_n, 1.0, 0.0).astype(F32)


def on_device(ndev, adjoint, stencil_weights, flux_plus, flux_minus, wall_row, wall_panel, wall_coef,
              wall_count, panel_owner):
    nf, nx, ny, nz = adjoint.shape
    assert nx % XC == 0 and XC % 4 == 0 and ny == 16 and nx * 4 <= nz
    xf, yf, zf = pl.pallas_call(
        fronts_kernel,
        out_shape=(
            jax.ShapeDtypeStruct((nf, ny, nz), F32),
            jax.ShapeDtypeStruct((nf, nx, nz), F32),
            jax.ShapeDtypeStruct((nf, ny, nz), F32),
        ),
        in_specs=[VMEM],
        out_specs=(VMEM, VMEM, VMEM),
    )(adjoint)
    xf = shift_from(xf, "gx", -1)
    yf = shift_from(yf, "gy", -1)
    zf = shift_from(zf, "gz", -1)
    fp = (STEP * flux_plus).reshape(-1)
    fm = (STEP * flux_minus).reshape(-1)
    const4 = lambda i: (0, 0, 0, 0)
    const3 = lambda i: (0, 0, 0)
    sec, xl, xr, yl, yr, zl, zr = pl.pallas_call(
        stencil_kernel,
        grid=(nx // XC,),
        out_shape=(
            jax.ShapeDtypeStruct((nf, nx, ny, nz), F32),
            jax.ShapeDtypeStruct((nf, 2, ny, nz), F32),
            jax.ShapeDtypeStruct((nf, 3, ny, nz), F32),
            jax.ShapeDtypeStruct((nf, nx // 4, 8, nz), F32),
            jax.ShapeDtypeStruct((nf, nx // 2, 8, nz), F32),
            jax.ShapeDtypeStruct((nf, ny, nz), F32),
            jax.ShapeDtypeStruct((nf, ny, nz), F32),
        ),
        in_specs=[
            SMEM,
            SMEM,
            pl.BlockSpec((nf, nx, ny, nz), const4),
            pl.BlockSpec((nf, ny, nz), const3),
            pl.BlockSpec((nf, nx, nz), const3),
            pl.BlockSpec((nf, ny, nz), const3),
            pl.BlockSpec((3, 2, 3, nf, XC, ny, nz), lambda i: (0, 0, 0, 0, i, 0, 0)),
        ],
        out_specs=(
            pl.BlockSpec((nf, nx, ny, nz), const4),
            pl.BlockSpec((nf, 2, ny, nz), const4),
            pl.BlockSpec((nf, 3, ny, nz), const4),
            pl.BlockSpec((nf, XC // 4, 8, nz), lambda i: (0, i, 0, 0)),
            pl.BlockSpec((nf, XC // 2, 8, nz), lambda i: (0, i, 0, 0)),
            pl.BlockSpec((nf, ny, nz), const3),
            pl.BlockSpec((nf, ny, nz), const3),
        ),
        scratch_shapes=[pltpu.VMEM((nf, nx + 5, ny, nz), F32)],
        compiler_params=pltpu.CompilerParams(dimension_semantics=("arbitrary",)),
    )(fp, fm, adjoint, xf, yf, zf, stencil_weights)
    axl = shift_from(xl, "gx", -1)
    axr = shift_from(xr, "gx", 1)
    ayl = shift_from(yl, "gy", -1)
    ayr = shift_from(yr, "gy", 1)
    azl = shift_from(zl, "gz", -1)
    azr = shift_from(zr, "gz", 1)
    nr = wall_row.shape[0]
    section, wt = pl.pallas_call(
        fix_kernel,
        out_shape=(
            jax.ShapeDtypeStruct((nf, nx, ny, nz), F32),
            jax.ShapeDtypeStruct((nr, nz), F32),
        ),
        in_specs=[SMEM, SMEM] + [VMEM] * 8,
        out_specs=(VMEM, VMEM),
        input_output_aliases={2: 0},
    )(wall_row, wall_count, sec, axl, axr, ayl, ayr, azl, azr, wall_coef)

    npan = panel_owner.shape[0]
    per = npan // ndev
    nb = 32
    na = npan // nb
    pa = wall_panel // nb
    pb = wall_panel % nb
    oh_a = (pa[..., None] == jnp.arange(na, dtype=jnp.int32)).astype(F32) * wt[..., None]
    oh_b = (pb[..., None] == jnp.arange(nb, dtype=jnp.int32)).astype(F32)
    tp = jnp.einsum("rza,rzb->ab", oh_a, oh_b, precision=HI).reshape(npan)
    own_oh = (panel_owner[:, None] == jnp.arange(ndev, dtype=jnp.int32)).astype(F32)
    rank = jnp.sum(jnp.cumsum(own_oh, axis=0) * own_oh, axis=1) - 1.0
    rank_oh = (rank[:, None] == jnp.arange(per, dtype=F32)).astype(F32)
    t = jnp.einsum("po,pk->ok", own_oh * tp[:, None], rank_oh, precision=HI)
    got = lax.all_to_all(t, AXES, 0, 0, tiled=True)
    return section, jnp.sum(got, axis=0)


def solution(mesh):
    ndev = mesh.size
    placed = (
        P(None, "gx", "gy", "gz"),
        P(None, None, None, None, "gx", "gy", "gz"),
        P(),
        P(),
        P(AXES),
        P(AXES, None),
        P(None, AXES, None),
        P(AXES),
        P(),
    )
    return jax.shard_map(
        lambda *args: on_device(ndev, *args),
        mesh=mesh,
        in_specs=placed,
        out_specs=(P(None, "gx", "gy", "gz"), P(AXES)),
        check_vma=False,
    )
```

profile of v0, /device:TPU:0, one launch (start us, length us, event | category | flops | bytes accessed | tf_op | source)
XLA Modules:
  0.0 69.8 jit_solution(5632891865237810817)
XLA Ops:
  0.6 0.0 copy-start.10
  0.6 0.0 copy-start.12
  0.7 0.0 copy-start.9
  0.7 0.0 copy-start.11
  0.7 2.3 %shard_map.104 = (f32[5,16,128]{2,1,0:T(8,128)}, f32[5,32,128]{2,1,0:T(8,128)}, f32[5,16,128]{2,1,0:T(8,128)}) custom-call(f32[5,32,16,128]{3,2,1,0:T(8,128)} %adj_ref.3), custom_call_target="tpu_custom_call" | custom-call | tf_op jit(solution)/shard_map/pallas_call | solution.py:186
  3.0 5.0 %collective-permute-start.1 = (f32[5,32,128]{2,1,0:T(8,128)}, f32[5,32,128]{2,1,0:T(8,128)S(1)}, u32[]{:S(2)}, u32[]{:S(2)}) collective-permute-start(f32[5,32,128]{2,1,0:T(8,128)} %get-tuple-element.15), channel_id=1, source_target_pairs={{0,6},{2,0},{4,2},{6,4},{1,7},{3,1},{5,3},{7,5},{8,14},{10,8},{12,... | collective-permute-start | bytes 245768 | tf_op jit(solution)/shard_map/ppermute | solution.py:20
  8.1 0.7 collective-permute-start
  8.7 1.5 %collective-permute-start.2 = (f32[5,16,128]{2,1,0:T(8,128)}, f32[5,16,128]{2,1,0:T(8,128)S(1)}, u32[]{:S(2)}, u32[]{:S(2)}) collective-permute-start(f32[5,16,128]{2,1,0:T(8,128)} %get-tuple-element.16), channel_id=1, source_target_pairs={{0,1},{1,0},{2,3},{3,2},{4,5},{5,4},{6,7},{7,6},{8,9},{9,8},{10,11... | collective-permute-start | bytes 122888 | tf_op jit(solution)/shard_map/ppermute | solution.py:20
  10.2 0.0 copy-done.10
  10.2 0.0 copy-done.12
  10.3 0.0 copy-done.9
  10.3 9.0 %reduce-window.6 = f32[32,8,128]{2,1,0:T(8,128)S(1)} reduce-window(f32[32,8,128]{2,1,0:T(8,128)S(1)} %fusion.10, f32[]{:T(128)} %constant.38.clone.1), window={size=1x1x128 pad=0_0x0_0x127_0}, to_apply=%region_0.1 | reduce-window | flops 4161536 | bytes 262148 | tf_op jit(solution)/shard_map/reduce-window
  19.3 0.1 slice.8
  19.4 0.1 copy.20
  19.6 0.1 copy.21
  19.7 0.1 broadcast_add_fusion
  19.8 0.0 copy-done.11
  19.8 0.6 reshape.35.fp_ref
  20.4 0.6 reshape.36.fm_ref
  21.0 0.0 collective-permute-done.xf_ref
  21.0 0.0 copy-start.5
  21.0 0.0 collective-permute-done.2.zf_ref
  21.0 0.0 copy-start.6
  21.1 0.0 collective-permute-done.1.yf_ref
  21.1 0.6 copy-done.5
  21.6 0.0 copy-done.6
  21.7 0.0 copy-start.3
  21.7 0.6 copy-done.3
  22.3 17.7 %shard_map.105 = (f32[5,32,16,128]{3,2,1,0:T(8,128)}, f32[5,2,16,128]{3,2,1,0:T(8,128)}, f32[5,3,16,128]{3,2,1,0:T(8,128)}, f32[5,8,8,128]{3,2,1,0:T(8,128)}, f3...) custom-call(f32[75]{0:T(128)} %reshape.35.fp_ref, f32[75]{0:T(128)} %reshape.36.fm_ref, ...), custom_call_target="tpu_custom_call" | custom-call | tf_op jit(solution)/shard_map/pallas_call | solution.py:203
  40.0 0.1 collective-permute-start.6
  40.1 0.6 collective-permute-start.7
  40.7 3.8 %collective-permute-start.5 = (f32[5,8,8,128]{3,2,1,0:T(8,128)}, f32[5,8,8,128]{3,2,1,0:T(8,128)S(1)}, u32[]{:S(2)}, u32[]{:S(2)}) collective-permute-start(f32[5,8,8,128]{3,2,1,0:T(8,128)} %get-tuple-element.20), channel_id=1, source_target_pairs={{0,6},{2,0},{4,2},{6,4},{1,7},{3,1},{5,3},{7,5},{8,14},{10,8},{12,... | collective-permute-start | bytes 491528 | tf_op jit(solution)/shard_map/ppermute | solution.py:20
  44.5 0.0 collective-permute-start.4
  44.5 1.7 %collective-permute-start.3 = (f32[5,2,16,128]{3,2,1,0:T(8,128)}, f32[5,2,16,128]{3,2,1,0:T(8,128)S(1)}, u32[]{:S(2)}, u32[]{:S(2)}) collective-permute-start(f32[5,2,16,128]{3,2,1,0:T(8,128)} %get-tuple-element.18), channel_id=1, source_target_pairs={{0,24},{8,0},{16,8},{24,16},{1,25},{9,1},{17,9},{25,17},{2,26},{10... | collective-permute-start | bytes 245768 | tf_op jit(solution)/shard_map/ppermute | solution.py:20
  46.2 0.0 collective-permute-done.7.azl_ref
  46.2 0.0 copy-start.7
  46.2 1.5 %collective-permute-start.8 = (f32[5,16,128]{2,1,0:T(8,128)}, f32[5,16,128]{2,1,0:T(8,128)S(1)}, u32[]{:S(2)}, u32[]{:S(2)}) collective-permute-start(f32[5,16,128]{2,1,0:T(8,128)} %get-tuple-element.23), channel_id=1, source_target_pairs={{0,1},{1,0},{2,3},{3,2},{4,5},{5,4},{6,7},{7,6},{8,9},{9,8},{10,11... | collective-permute-start | bytes 122888 | tf_op jit(solution)/shard_map/ppermute | solution.py:20
  48.4 2.0 %collective-permute-done.8.azr_ref = f32[5,16,128]{2,1,0:T(8,128)S(1)} collective-permute-done((f32[5,16,128]{2,1,0:T(8,128)}, f32[5,16,128]{2,1,0:T(8,128)S(1)}, u32[]{:S(2)}, u32[]{:S(2)}) %collective-permute-start.8) | collective-permute-done | bytes 40992 | tf_op jit(solution)/shard_map/ppermute | solution.py:20
  50.5 0.0 copy-start.8
  50.5 0.0 collective-permute-done.3.axl_ref
  50.5 0.0 copy-start.4
  50.5 0.0 collective-permute-done.4.axr_ref
  50.5 0.0 copy-start.2
  50.5 2.9 %collective-permute-done.5.ayl_ref = f32[5,8,8,128]{3,2,1,0:T(8,128)S(1)} collective-permute-done((f32[5,8,8,128]{3,2,1,0:T(8,128)}, f32[5,8,8,128]{3,2,1,0:T(8,128)S(1)}, u32[]{:S(2)}, u32[]{:S(2)}) %collective-permute-start.5) | collective-permute-done | bytes 163872 | tf_op jit(solution)/shard_map/ppermute | solution.py:20
  53.4 0.0 copy-start.1
  53.4 0.0 collective-permute-done.6.ayr_ref
  53.4 0.0 copy-start
  53.4 0.0 copy-done.7
  53.4 0.0 copy-done.8
  53.4 0.0 copy-done.4
  53.4 0.0 copy-done.2
  53.4 0.6 copy-done.1
  54.0 0.1 copy-done
  54.1 3.4 %shard_map.106 = (f32[5,32,16,128]{3,2,1,0:T(8,128)}, f32[16,128]{1,0:T(8,128)}) custom-call(s32[16]{0:T(128)} %row_ref.1, s32[1]{0:T(128)S(6)} %copy.26.cnt_ref, f32[5,32,16,128]{3,2,1,0:T(8,128)} %get-tuple-element.17.sec_ref, f32[5,2,16,128]{3,2,1,0:T(8,128)} %copy-done.4, f32[5,3,16,128]{3,2,1,0:T(8,128)} %copy-done.2, ...), custom_call_target="tpu_custom_call", output_to_operand_aliasing={{0}: (2, {})} | custom-call | tf_op jit(solution)/shard_map/pallas_call | solution.py:243
  57.5 1.0 %convolution_bitcast_fusion = f32[32,32]{1,0:T(8,128)S(1)} fusion(s32[16,128]{1,0:T(8,128)S(1)} %get-tuple-element.27, f32[16,128]{1,0:T(8,128)} %get-tuple-element.25, s32[16,128]{1,0:T(8,128)S(1)} %get-tuple-element.26), kind=kOutput, calls=%fused_computation | convolution fusion | flops 25362432 | bytes 28672 | tf_op jit(solution)/shard_map/rza,rzb->ab/dot_general | solution.py:262
  58.5 0.1 mul.31
  58.6 0.4 fusion
  59.0 10.2 %all_to_all.9 = f32[32,1,32]{2,1,0:T(1,128)S(1)} all-to-all(f32[32,1,32]{2,1,0:T(1,128)S(1)} %bitcast.23), channel_id=1, replica_groups=mesh['gx'=4,'gy'=4,'gz'=2] {'gx','gy','gz'}, dimensions={0} | all-to-all | bytes 8192 | tf_op jit(solution)/shard_map/all_to_all | solution.py:267
  69.2 0.6 reduce_sum.19
  (10 shorter events, 0.1 us)
Async XLA Ops:
  0.6 9.6 %copy-start.10 = (f32[3,5,5]{2,0,1:T(4,128)S(1)}, f32[3,5,5]{2,0,1:T(4,128)}, u32[]{:S(2)}) copy-start(f32[3,5,5]{2,0,1:T(4,128)} %param.11) | copy-start | bytes 904
  0.6 9.6 %copy-start.12 = (s32[16,128]{1,0:T(8,128)S(1)}, s32[16,128]{1,0:T(8,128)}, u32[]{:S(2)}) copy-start(s32[16,128]{1,0:T(8,128)} %param.14) | copy-start | bytes 24580
  0.7 9.6 %copy-start.9 = (s32[1024]{0:T(1024)S(1)}, s32[1024]{0:T(1024)}, u32[]{:S(2)}) copy-start(s32[1024]{0:T(1024)} %param.17) | copy-start | bytes 12292
  0.7 19.1 %copy-start.11 = (f32[3,5,5]{2,0,1:T(4,128)S(1)}, f32[3,5,5]{2,0,1:T(4,128)}, u32[]{:S(2)}) copy-start(f32[3,5,5]{2,0,1:T(4,128)} %param.12) | copy-start | bytes 904
  3.0 18.0 %collective-permute-start.1 = (f32[5,32,128]{2,1,0:T(8,128)}, f32[5,32,128]{2,1,0:T(8,128)S(1)}, u32[]{:S(2)}, u32[]{:S(2)}) collective-permute-start(f32[5,32,128]{2,1,0:T(8,128)} %get-tuple-element.15), channel_id=1, source_target_pairs={{0,6},{2,0},{4,2},{6,4},{1,7},{3,1},{5,3},{7,5},{8,14},{10,8},{12,... | collective-permute-start | bytes 245768 | tf_op jit(solution)/shard_map/ppermute | solution.py:20
  8.1 13.0 %collective-permute-start = (f32[5,16,128]{2,1,0:T(8,128)}, f32[5,16,128]{2,1,0:T(8,128)S(1)}, u32[]{:S(2)}, u32[]{:S(2)}) collective-permute-start(f32[5,16,128]{2,1,0:T(8,128)} %get-tuple-element.14), channel_id=1, source_target_pairs={{0,24},{8,0},{16,8},{24,16},{1,25},{9,1},{17,9},{25,17},{2,26},{10... | collective-permute-start | bytes 122888 | tf_op jit(solution)/shard_map/ppermute | solution.py:20
  8.7 12.3 %collective-permute-start.2 = (f32[5,16,128]{2,1,0:T(8,128)}, f32[5,16,128]{2,1,0:T(8,128)S(1)}, u32[]{:S(2)}, u32[]{:S(2)}) collective-permute-start(f32[5,16,128]{2,1,0:T(8,128)} %get-tuple-element.16), channel_id=1, source_target_pairs={{0,1},{1,0},{2,3},{3,2},{4,5},{5,4},{6,7},{7,6},{8,9},{9,8},{10,11... | collective-permute-start | bytes 122888 | tf_op jit(solution)/shard_map/ppermute | solution.py:20
  21.0 0.6 copy-start.5
  21.0 0.6 copy-start.6
  21.7 0.6 copy-start.3
  40.0 13.4 %collective-permute-start.6 = (f32[5,16,8,128]{3,2,1,0:T(8,128)}, f32[5,16,8,128]{3,2,1,0:T(8,128)S(1)}, u32[]{:S(2)}, u32[]{:S(2)}) collective-permute-start(f32[5,16,8,128]{3,2,1,0:T(8,128)} %get-tuple-element.21), channel_id=1, source_target_pairs={{0,2},{2,4},{4,6},{6,0},{1,3},{3,5},{5,7},{7,1},{8,10},{10,12},{12... | collective-permute-start | bytes 983048 | tf_op jit(solution)/shard_map/ppermute | solution.py:20
  40.1 6.2 %collective-permute-start.7 = (f32[5,16,128]{2,1,0:T(8,128)}, f32[5,16,128]{2,1,0:T(8,128)S(1)}, u32[]{:S(2)}, u32[]{:S(2)}) collective-permute-start(f32[5,16,128]{2,1,0:T(8,128)} %get-tuple-element.22), channel_id=1, source_target_pairs={{0,1},{1,0},{2,3},{3,2},{4,5},{5,4},{6,7},{7,6},{8,9},{9,8},{10,11... | collective-permute-start | bytes 122888 | tf_op jit(solution)/shard_map/ppermute | solution.py:20
  40.7 12.7 %collective-permute-start.5 = (f32[5,8,8,128]{3,2,1,0:T(8,128)}, f32[5,8,8,128]{3,2,1,0:T(8,128)S(1)}, u32[]{:S(2)}, u32[]{:S(2)}) collective-permute-start(f32[5,8,8,128]{3,2,1,0:T(8,128)} %get-tuple-element.20), channel_id=1, source_target_pairs={{0,6},{2,0},{4,2},{6,4},{1,7},{3,1},{5,3},{7,5},{8,14},{10,8},{12,... | collective-permute-start | bytes 491528 | tf_op jit(solution)/shard_map/ppermute | solution.py:20
  44.5 6.0 %collective-permute-start.4 = (f32[5,3,16,128]{3,2,1,0:T(8,128)}, f32[5,3,16,128]{3,2,1,0:T(8,128)S(1)}, u32[]{:S(2)}, u32[]{:S(2)}) collective-permute-start(f32[5,3,16,128]{3,2,1,0:T(8,128)} %get-tuple-element.19), channel_id=1, source_target_pairs={{0,8},{8,16},{16,24},{24,0},{1,9},{9,17},{17,25},{25,1},{2,10},{10... | collective-permute-start | bytes 368648 | tf_op jit(solution)/shard_map/ppermute | solution.py:20
  44.5 6.0 %collective-permute-start.3 = (f32[5,2,16,128]{3,2,1,0:T(8,128)}, f32[5,2,16,128]{3,2,1,0:T(8,128)S(1)}, u32[]{:S(2)}, u32[]{:S(2)}) collective-permute-start(f32[5,2,16,128]{3,2,1,0:T(8,128)} %get-tuple-element.18), channel_id=1, source_target_pairs={{0,24},{8,0},{16,8},{24,16},{1,25},{9,1},{17,9},{25,17},{2,26},{10... | collective-permute-start | bytes 245768 | tf_op jit(solution)/shard_map/ppermute | solution.py:20
  46.2 7.2 %copy-start.7 = (f32[5,16,128]{2,1,0:T(8,128)}, f32[5,16,128]{2,1,0:T(8,128)S(1)}, u32[]{:S(2)}) copy-start(f32[5,16,128]{2,1,0:T(8,128)S(1)} %collective-permute-done.7.azl_ref) | copy-start | bytes 122884
  46.2 4.2 %collective-permute-start.8 = (f32[5,16,128]{2,1,0:T(8,128)}, f32[5,16,128]{2,1,0:T(8,128)S(1)}, u32[]{:S(2)}, u32[]{:S(2)}) collective-permute-start(f32[5,16,128]{2,1,0:T(8,128)} %get-tuple-element.23), channel_id=1, source_target_pairs={{0,1},{1,0},{2,3},{3,2},{4,5},{5,4},{6,7},{7,6},{8,9},{9,8},{10,11... | collective-permute-start | bytes 122888 | tf_op jit(solution)/shard_map/ppermute | solution.py:20
  50.5 2.9 %copy-start.8 = (f32[5,16,128]{2,1,0:T(8,128)}, f32[5,16,128]{2,1,0:T(8,128)S(1)}, u32[]{:S(2)}) copy-start(f32[5,16,128]{2,1,0:T(8,128)S(1)} %collective-permute-done.8.azr_ref) | copy-start | bytes 122884
  50.5 2.9 %copy-start.4 = (f32[5,2,16,128]{3,2,1,0:T(8,128)}, f32[5,2,16,128]{3,2,1,0:T(8,128)S(1)}, u32[]{:S(2)}) copy-start(f32[5,2,16,128]{3,2,1,0:T(8,128)S(1)} %collective-permute-done.3.axl_ref) | copy-start | bytes 245764
  50.5 2.9 %copy-start.2 = (f32[5,3,16,128]{3,2,1,0:T(8,128)}, f32[5,3,16,128]{3,2,1,0:T(8,128)S(1)}, u32[]{:S(2)}) copy-start(f32[5,3,16,128]{3,2,1,0:T(8,128)S(1)} %collective-permute-done.4.axr_ref) | copy-start | bytes 368644
  53.4 0.7 copy-start.1
  53.4 0.8 %copy-start = (f32[5,16,8,128]{3,2,1,0:T(8,128)}, f32[5,16,8,128]{3,2,1,0:T(8,128)S(1)}, u32[]{:S(2)}) copy-start(f32[5,16,8,128]{3,2,1,0:T(8,128)S(1)} %collective-permute-done.6.ayr_ref) | copy-start | bytes 983044
where the time goes:
time: 70.3 us; the launch traced here: 69.8 us
  Pallas kernels  23.4 us (33%)
  starting transfers between devices  14.9 us (21%)
  blocking collectives  10.2 us (15%)
  other arithmetic  9.78 us (14%)
  waiting for transfers between devices  4.96 us (7%)
  local copies, waits for them, and re-layouts  3.59 us (5%)
  between operations  1.49 us (2%)
  matrix products  1.38 us (2%)
    pallas_call x1, Pallas kernels, on_device(): pl.pallas_call(stencil_kernel, grid=(nx // XC,), out_shape=(jax.ShapeDtyp...  17.7 us
    ppermute x9, starting transfers between devices, shift_from(): return lax.ppermute(x, axis, [(i, (i + by) % n) for i in range(n)])  14.9 us
    all_to_all x1, blocking collectives, on_device(): got = lax.all_to_all(t, AXES, 0, 0, tiled=True)  10.2 us
    another operation x3, other arithmetic  9.15 us
    ppermute x9, waiting for transfers between devices, shift_from(): return lax.ppermute(x, axis, [(i, (i + by) % n) for i in range(n)])  4.96 us
    pallas_call x1, Pallas kernels, on_device(): pl.pallas_call(fix_kernel, out_shape=(jax.ShapeDtypeStruct((nf, nx, ny, n...  3.35 us
    pallas_call x1, Pallas kernels, on_device(): pl.pallas_call(fronts_kernel, out_shape=(jax.ShapeDtypeStruct((nf, ny, nz...  2.35 us
    unnamed x26, local copies, waits for them, and re-layouts  2 us
  transfers between devices with their start and end apart: 9, of which 2 were waited for; matrix products, arithmetic and copies ran while one was open for 15% of the time, Pallas kernels for 0%

commit v1 on v0

--- a/solution.py
+++ b/solution.py
@@ -85,9 +85,8 @@
         for f in range(nf):
             p = m = None
             for g in range(nf):
-                k = (d * nf + g) * nf + f
-                tp = diff[g] * fp_ref[k]
-                tm = diff[g] * fm_ref[k]
+                tp = diff[g] * (STEP * fp_ref[d, g, f])
+                tm = diff[g] * (STEP * fm_ref[d, g, f])
                 p = tp if p is None else p + tp
                 m = tm if m is None else m + tm
             plus.append(p)
@@ -196,8 +195,6 @@
     xf = shift_from(xf, "gx", -1)
     yf = shift_from(yf, "gy", -1)
     zf = shift_from(zf, "gz", -1)
-    fp = (STEP * flux_plus).reshape(-1)
-    fm = (STEP * flux_minus).reshape(-1)
     const4 = lambda i: (0, 0, 0, 0)
     const3 = lambda i: (0, 0, 0)
     sec, xl, xr, yl, yr, zl, zr = pl.pallas_call(
@@ -232,13 +229,16 @@
         ),
         scratch_shapes=[pltpu.VMEM((nf, nx + 5, ny, nz), F32)],
         compiler_params=pltpu.CompilerParams(dimension_semantics=("arbitrary",)),
-    )(fp, fm, adjoint, xf, yf, zf, stencil_weights)
+    )(flux_plus, flux_minus, adjoint, xf, yf, zf, stencil_weights)
     axl = shift_from(xl, "gx", -1)
     axr = shift_from(xr, "gx", 1)
     ayl = shift_from(yl, "gy", -1)
     ayr = shift_from(yr, "gy", 1)
-    azl = shift_from(zl, "gz", -1)
-    azr = shift_from(zr, "gz", 1)
+    if lax.axis_size("gz") == 2:
+        azl, azr = shift_from(jnp.stack([zl, zr]), "gz", 1)
+    else:
+        azl = shift_from(zl, "gz", -1)
+        azr = shift_from(zr, "gz", 1)
     nr = wall_row.shape[0]
     section, wt = pl.pallas_call(
         fix_kernel,
@@ -261,7 +261,12 @@
     oh_b = (pb[..., None] == jnp.arange(nb, dtype=jnp.int32)).astype(F32)
     tp = jnp.einsum("rza,rzb->ab", oh_a, oh_b, precision=HI).reshape(npan)
     own_oh = (panel_owner[:, None] == jnp.arange(ndev, dtype=jnp.int32)).astype(F32)
-    rank = jnp.sum(jnp.cumsum(own_oh, axis=0) * own_oh, axis=1) - 1.0
+    oh3 = own_oh.reshape(na, nb, ndev)
+    below_b = (jnp.arange(nb)[None, :] < jnp.arange(nb)[:, None]).astype(F32)
+    below_a = (jnp.arange(na)[None, :] < jnp.arange(na)[:, None]).astype(F32)
+    inner = jnp.einsum("bc,acd->abd", below_b, oh3, precision=HI)
+    before = jnp.einsum("ac,cd->ad", below_a, jnp.sum(oh3, axis=1), precision=HI)
+    rank = jnp.sum((inner + before[:, None, :]) * oh3, axis=2).reshape(npan)
     rank_oh = (rank[:, None] == jnp.arange(per, dtype=F32)).astype(F32)
     t = jnp.einsum("po,pk->ok", own_oh * tp[:, None], rank_oh, precision=HI)
     got = lax.all_to_all(t, AXES, 0, 0, tiled=True)

time: 70.3 us -> 64.3 us (0.915)
  other arithmetic: 9.78 us -> 1.59 us
  matrix products: 1.38 us -> 2.42 us
  waiting for transfers between devices: 4.96 us -> 5.92 us
    another operation x3 -> x1, other arithmetic: 9.15 us -> 0.81 us  [on_device(): azl, azr = shift_from(jnp.stack([zl, zr]), 'gz', 1)]
    unnamed x26 -> x24, local copies, waits for them, and re-layouts: 2 us -> 3.23 us
    reshape x2 -> x0, local copies, waits for them, and re-layouts: 1.22 us -> none  [the longest x1 0.63 us: on_device(): fm = (STEP * flux_minus).reshape(-1)]
    ppermute x9 -> x8, waiting for transfers between devices: 4.96 us -> 5.92 us  [shift_from(): return lax.ppermute(x, axis, [(i, (i + by) % n) for i in range(n)])]
    ppermute x9 -> x8, starting transfers between devices: 14.9 us -> 14.3 us  [shift_from(): return lax.ppermute(x, axis, [(i, (i + by) % n) for i in range(n)])]
  transfers between devices with their start and end apart: 9 -> 8, of which waited for: 2 -> 4; matrix products, arithmetic and copies ran while one was open for 15% -> 4% of each run, Pallas kernels for 0% -> 0%
where the time goes in v1:
time: 64.3 us; the launch traced here: 63.8 us
  Pallas kernels  23.3 us (36%)
  starting transfers between devices  14.3 us (22%)
  blocking collectives  10.8 us (17%)
  waiting for transfers between devices  5.92 us (9%)
  local copies, waits for them, and re-layouts  4.07 us (6%)
  matrix products  2.42 us (4%)
  other arithmetic  1.59 us (2%)
  between operations  1.41 us (2%)
    pallas_call x1, Pallas kernels, on_device(): pl.pallas_call(stencil_kernel, grid=(nx // XC,), out_shape=(jax.ShapeDtyp...  17.6 us
    ppermute x8, starting transfers between devices, shift_from(): return lax.ppermute(x, axis, [(i, (i + by) % n) for i in range(n)])  14.3 us
    all_to_all x1, blocking collectives, on_device(): got = lax.all_to_all(t, AXES, 0, 0, tiled=True)  10.8 us
    ppermute x8, waiting for transfers between devices, shift_from(): return lax.ppermute(x, axis, [(i, (i + by) % n) for i in range(n)])  5.92 us
    pallas_call x1, Pallas kernels, on_device(): pl.pallas_call(fix_kernel, out_shape=(jax.ShapeDtypeStruct((nf, nx, ny, n...  3.35 us
    unnamed x24, local copies, waits for them, and re-layouts  3.23 us
    pallas_call x1, Pallas kernels, on_device(): pl.pallas_call(fronts_kernel, out_shape=(jax.ShapeDtypeStruct((nf, ny, nz...  2.35 us
  transfers between devices with their start and end apart: 8, of which 4 were waited for; matrix products, arithmetic and copies ran while one was open for 4% of the time, Pallas kernels for 0%

profile of v1, /device:TPU:0, one launch (start us, length us, event | category | flops | bytes accessed | tf_op | source)
XLA Modules:
  0.0 63.8 jit_solution(17755939642625306526)
XLA Ops:
  0.6 0.0 copy-start.10
  0.6 0.0 copy-start.9
  0.7 0.0 copy-start.7
  0.7 0.0 copy-start.8
  0.7 2.4 %shard_map.104 = (f32[5,16,128]{2,1,0:T(8,128)}, f32[5,32,128]{2,1,0:T(8,128)}, f32[5,16,128]{2,1,0:T(8,128)}) custom-call(f32[5,32,16,128]{3,2,1,0:T(8,128)} %adj_ref.3), custom_call_target="tpu_custom_call" | custom-call | tf_op jit(solution)/shard_map/pallas_call | solution.py:185
  3.0 5.0 %collective-permute-start.1 = (f32[5,32,128]{2,1,0:T(8,128)}, f32[5,32,128]{2,1,0:T(8,128)S(1)}, u32[]{:S(2)}, u32[]{:S(2)}) collective-permute-start(f32[5,32,128]{2,1,0:T(8,128)} %get-tuple-element.15), channel_id=1, source_target_pairs={{0,6},{2,0},{4,2},{6,4},{1,7},{3,1},{5,3},{7,5},{8,14},{10,8},{12,... | collective-permute-start | bytes 245768 | tf_op jit(solution)/shard_map/ppermute | solution.py:20
  8.1 0.7 %collective-permute-start = (f32[5,16,128]{2,1,0:T(8,128)}, f32[5,16,128]{2,1,0:T(8,128)S(1)}, u32[]{:S(2)}, u32[]{:S(2)}) collective-permute-start(f32[5,16,128]{2,1,0:T(8,128)} %get-tuple-element.14), channel_id=1, source_target_pairs={{0,24},{8,0},{16,8},{24,16},{1,25},{9,1},{17,9},{25,17},{2,26},{10... | collective-permute-start | bytes 122888 | tf_op jit(solution)/shard_map/ppermute | solution.py:20
  8.7 1.5 %collective-permute-start.2 = (f32[5,16,128]{2,1,0:T(8,128)}, f32[5,16,128]{2,1,0:T(8,128)S(1)}, u32[]{:S(2)}, u32[]{:S(2)}) collective-permute-start(f32[5,16,128]{2,1,0:T(8,128)} %get-tuple-element.16), channel_id=1, source_target_pairs={{0,1},{1,0},{2,3},{3,2},{4,5},{5,4},{6,7},{7,6},{8,9},{9,8},{10,11... | collective-permute-start | bytes 122888 | tf_op jit(solution)/shard_map/ppermute | solution.py:20
  10.2 0.0 copy-done.10
  10.2 0.1 eq.75
  10.3 0.2 convert_reduce_fusion
  10.5 0.1 fusion.15
  10.7 0.0 copy-done.9
  10.7 0.0 copy-done.7
  10.7 0.6 copy.14.fp_ref
  11.3 0.0 copy-done.8
  11.3 0.6 copy.15.fm_ref
  12.6 0.0 collective-permute-done.xf_ref
  12.6 0.0 copy-start.5
  12.6 0.4 collective-permute-done.2.zf_ref
  12.9 0.0 copy-start.6
  12.9 0.0 collective-permute-done.1.yf_ref
  12.9 0.3 copy-done.5
  13.2 0.3 copy-done.6
  13.5 0.0 copy-start.3
  13.5 0.6 %copy-done.3 = f32[5,32,128]{2,1,0:T(8,128)} copy-done((f32[5,32,128]{2,1,0:T(8,128)}, f32[5,32,128]{2,1,0:T(8,128)S(1)}, u32[]{:S(2)}) %copy-start.3) | copy-done | bytes 81944
  14.2 17.6 %shard_map.105 = (f32[5,32,16,128]{3,2,1,0:T(8,128)}, f32[5,2,16,128]{3,2,1,0:T(8,128)}, f32[5,3,16,128]{3,2,1,0:T(8,128)}, f32[5,8,8,128]{3,2,1,0:T(8,128)}, f3...) custom-call(f32[3,5,5]{2,1,0:T(8,128)} %copy.14.fp_ref, f32[3,5,5]{2,1,0:T(8,128)} %copy.15.fm_ref, ...), custom_call_target="tpu_custom_call" | custom-call | tf_op jit(solution)/shard_map/pallas_call | solution.py:200
  31.8 0.8 %pad_maximum_fusion = f32[2,5,16,128]{3,2,1,0:T(8,128)S(1)} fusion(f32[1,5,16,128]{3,2,1,0:T(8,128)} %bitcast.22, f32[1,5,16,128]{3,2,1,0:T(8,128)} %bitcast.21), kind=kLoop, calls=%fused_computation.23 | loop fusion | flops 20480 | bytes 163840 | tf_op jit(solution)/shard_map/stack | solution.py:238
  32.6 1.5 %collective-permute-start.7 = (f32[2,5,16,128]{3,2,1,0:T(8,128)S(1)}, f32[2,5,16,128]{3,2,1,0:T(8,128)S(1)}, u32[]{:S(2)}, u32[]{:S(2)}) collective-permute-start(f32[2,5,16,128]{3,2,1,0:T(8,128)S(1)} %pad_maximum_fusion), channel_id=1, source_target_pairs={{0,1},{1,0},{2,3},{3,2},{4,5},{5,4},{6,7},{7,6},{8,9},{9,8},{10,11... | collective-permute-start | bytes 245768 | tf_op jit(solution)/shard_map/ppermute | solution.py:20
  34.1 0.0 collective-permute-start.6
  34.1 0.3 fusion.2
  34.4 0.1 eq.79
  34.5 3.8 %collective-permute-start.5 = (f32[5,8,8,128]{3,2,1,0:T(8,128)}, f32[5,8,8,128]{3,2,1,0:T(8,128)S(1)}, u32[]{:S(2)}, u32[]{:S(2)}) collective-permute-start(f32[5,8,8,128]{3,2,1,0:T(8,128)} %get-tuple-element.20), channel_id=1, source_target_pairs={{0,6},{2,0},{4,2},{6,4},{1,7},{3,1},{5,3},{7,5},{8,14},{10,8},{12,... | collective-permute-start | bytes 491528 | tf_op jit(solution)/shard_map/ppermute | solution.py:20
  38.3 0.0 collective-permute-start.4
  38.3 1.7 %collective-permute-start.3 = (f32[5,2,16,128]{3,2,1,0:T(8,128)}, f32[5,2,16,128]{3,2,1,0:T(8,128)S(1)}, u32[]{:S(2)}, u32[]{:S(2)}) collective-permute-start(f32[5,2,16,128]{3,2,1,0:T(8,128)} %get-tuple-element.18), channel_id=1, source_target_pairs={{0,24},{8,0},{16,8},{24,16},{1,25},{9,1},{17,9},{25,17},{2,26},{10... | collective-permute-start | bytes 245768 | tf_op jit(solution)/shard_map/ppermute | solution.py:20
  40.0 0.0 collective-permute-done.7
  40.0 0.6 slice_bitcast_fusion
  40.7 1.7 %collective-permute-done.3.axl_ref = f32[5,2,16,128]{3,2,1,0:T(8,128)S(1)} collective-permute-done((f32[5,2,16,128]{3,2,1,0:T(8,128)}, f32[5,2,16,128]{3,2,1,0:T(8,128)S(1)}, u32[]{:S(2)}, u32[]{:S(2)}) %collective-permute-start.3) | collective-permute-done | bytes 81952 | tf_op jit(solution)/shard_map/ppermute | solution.py:20
  42.4 0.0 copy-start.4
  42.4 0.6 collective-permute-done.4.axr_ref
  43.0 0.0 copy-start.2
  43.0 3.3 %collective-permute-done.5.ayl_ref = f32[5,8,8,128]{3,2,1,0:T(8,128)S(1)} collective-permute-done((f32[5,8,8,128]{3,2,1,0:T(8,128)}, f32[5,8,8,128]{3,2,1,0:T(8,128)S(1)}, u32[]{:S(2)}, u32[]{:S(2)}) %collective-permute-start.5) | collective-permute-done | bytes 163872 | tf_op jit(solution)/shard_map/ppermute | solution.py:20
  46.2 0.0 copy-start.1
  46.2 0.0 collective-permute-done.6.ayr_ref
  46.2 0.0 copy-start
  46.2 0.0 copy-done.4
  46.2 0.0 copy-done.2
  46.2 0.6 copy-done.1
  46.9 0.1 copy-done
  47.0 3.4 %shard_map.106 = (f32[5,32,16,128]{3,2,1,0:T(8,128)}, f32[16,128]{1,0:T(8,128)}) custom-call(s32[16]{0:T(128)} %row_ref.1, s32[1]{0:T(128)S(6)} %copy.18.cnt_ref, f32[5,32,16,128]{3,2,1,0:T(8,128)} %get-tuple-element.17.sec_ref, f32[5,2,16,128]{3,2,1,0:T(8,128)} %copy-done.4, f32[5,3,16,128]{3,2,1,0:T(8,128)} %copy-done.2, ...), custom_call_target="tpu_custom_call", output_to_operand_aliasing={{0}: (2, {})} | custom-call | tf_op jit(solution)/shard_map/pallas_call | solution.py:243
  50.3 1.0 %convolution_bitcast_fusion = f32[32,32]{1,0:T(8,128)S(1)} fusion(s32[16,128]{1,0:T(8,128)S(1)} %get-tuple-element.29, f32[16,128]{1,0:T(8,128)} %get-tuple-element.25, s32[16,128]{1,0:T(8,128)S(1)} %get-tuple-element.28), kind=kOutput, calls=%fused_computation.4 | convolution fusion | flops 25362432 | bytes 28672 | tf_op jit(solution)/shard_map/rza,rzb->ab/dot_general | solution.py:262
  51.3 0.1 mul.23
  51.4 1.0 %fusion.3 = f32[32,32]{1,0:T(8,128)S(1)} fusion(f32[1024]{0:T(1024)S(1)} %eq.79, f32[1024]{0:T(1024)S(1)} %mul.23, s32[1024]{0:T(1024)S(1)} %copy-done.10), kind=kOutput, calls=%fused_computation.8 | convolution fusion | flops 12681216 | bytes 16384 | tf_op jit(solution)/shard_map/po,pk->ok/dot_general | solution.py:271
  52.4 10.8 %all_to_all.9 = f32[32,1,32]{2,1,0:T(1,128)S(1)} all-to-all(f32[32,1,32]{2,1,0:T(1,128)S(1)} %bitcast.23), channel_id=1, replica_groups=mesh['gx'=4,'gy'=4,'gz'=2] {'gx','gy','gz'}, dimensions={0} | all-to-all | bytes 8192 | tf_op jit(solution)/shard_map/all_to_all | solution.py:272
  63.2 0.6 reduce_sum.29
  (1 shorter events, 0.0 us)
Async XLA Ops:
  0.6 9.6 %copy-start.10 = (s32[1024]{0:T(1024)S(1)}, s32[1024]{0:T(1024)}, u32[]{:S(2)}) copy-start(s32[1024]{0:T(1024)} %param.17) | copy-start | bytes 12292
  0.6 10.0 %copy-start.9 = (s32[16,128]{1,0:T(8,128)S(1)}, s32[16,128]{1,0:T(8,128)}, u32[]{:S(2)}) copy-start(s32[16,128]{1,0:T(8,128)} %param.14) | copy-start | bytes 24580
  0.7 10.0 %copy-start.7 = (f32[3,5,5]{2,0,1:T(4,128)S(1)}, f32[3,5,5]{2,0,1:T(4,128)}, u32[]{:S(2)}) copy-start(f32[3,5,5]{2,0,1:T(4,128)} %param.11) | copy-start | bytes 904
  0.7 10.7 %copy-start.8 = (f32[3,5,5]{2,0,1:T(4,128)S(1)}, f32[3,5,5]{2,0,1:T(4,128)}, u32[]{:S(2)}) copy-start(f32[3,5,5]{2,0,1:T(4,128)} %param.12) | copy-start | bytes 904
  3.0 9.9 %collective-permute-start.1 = (f32[5,32,128]{2,1,0:T(8,128)}, f32[5,32,128]{2,1,0:T(8,128)S(1)}, u32[]{:S(2)}, u32[]{:S(2)}) collective-permute-start(f32[5,32,128]{2,1,0:T(8,128)} %get-tuple-element.15), channel_id=1, source_target_pairs={{0,6},{2,0},{4,2},{6,4},{1,7},{3,1},{5,3},{7,5},{8,14},{10,8},{12,... | collective-permute-start | bytes 245768 | tf_op jit(solution)/shard_map/ppermute | solution.py:20
  8.1 4.5 %collective-permute-start = (f32[5,16,128]{2,1,0:T(8,128)}, f32[5,16,128]{2,1,0:T(8,128)S(1)}, u32[]{:S(2)}, u32[]{:S(2)}) collective-permute-start(f32[5,16,128]{2,1,0:T(8,128)} %get-tuple-element.14), channel_id=1, source_target_pairs={{0,24},{8,0},{16,8},{24,16},{1,25},{9,1},{17,9},{25,17},{2,26},{10... | collective-permute-start | bytes 122888 | tf_op jit(solution)/shard_map/ppermute | solution.py:20
  8.7 4.2 %collective-permute-start.2 = (f32[5,16,128]{2,1,0:T(8,128)}, f32[5,16,128]{2,1,0:T(8,128)S(1)}, u32[]{:S(2)}, u32[]{:S(2)}) collective-permute-start(f32[5,16,128]{2,1,0:T(8,128)} %get-tuple-element.16), channel_id=1, source_target_pairs={{0,1},{1,0},{2,3},{3,2},{4,5},{5,4},{6,7},{7,6},{8,9},{9,8},{10,11... | collective-permute-start | bytes 122888 | tf_op jit(solution)/shard_map/ppermute | solution.py:20
  12.6 0.6 copy-start.5
  12.9 0.6 copy-start.6
  13.5 0.6 %copy-start.3 = (f32[5,32,128]{2,1,0:T(8,128)}, f32[5,32,128]{2,1,0:T(8,128)S(1)}, u32[]{:S(2)}) copy-start(f32[5,32,128]{2,1,0:T(8,128)S(1)} %collective-permute-done.1.yf_ref) | copy-start | bytes 245764
  32.6 7.4 %collective-permute-start.7 = (f32[2,5,16,128]{3,2,1,0:T(8,128)S(1)}, f32[2,5,16,128]{3,2,1,0:T(8,128)S(1)}, u32[]{:S(2)}, u32[]{:S(2)}) collective-permute-start(f32[2,5,16,128]{3,2,1,0:T(8,128)S(1)} %pad_maximum_fusion), channel_id=1, source_target_pairs={{0,1},{1,0},{2,3},{3,2},{4,5},{5,4},{6,7},{7,6},{8,9},{9,8},{10,11... | collective-permute-start | bytes 245768 | tf_op jit(solution)/shard_map/ppermute | solution.py:20
  34.1 12.1 %collective-permute-start.6 = (f32[5,16,8,128]{3,2,1,0:T(8,128)}, f32[5,16,8,128]{3,2,1,0:T(8,128)S(1)}, u32[]{:S(2)}, u32[]{:S(2)}) collective-permute-start(f32[5,16,8,128]{3,2,1,0:T(8,128)} %get-tuple-element.21), channel_id=1, source_target_pairs={{0,2},{2,4},{4,6},{6,0},{1,3},{3,5},{5,7},{7,1},{8,10},{10,12},{12... | collective-permute-start | bytes 983048 | tf_op jit(solution)/shard_map/ppermute | solution.py:20
  34.5 11.8 %collective-permute-start.5 = (f32[5,8,8,128]{3,2,1,0:T(8,128)}, f32[5,8,8,128]{3,2,1,0:T(8,128)S(1)}, u32[]{:S(2)}, u32[]{:S(2)}) collective-permute-start(f32[5,8,8,128]{3,2,1,0:T(8,128)} %get-tuple-element.20), channel_id=1, source_target_pairs={{0,6},{2,0},{4,2},{6,4},{1,7},{3,1},{5,3},{7,5},{8,14},{10,8},{12,... | collective-permute-start | bytes 491528 | tf_op jit(solution)/shard_map/ppermute | solution.py:20
  38.3 4.7 %collective-permute-start.4 = (f32[5,3,16,128]{3,2,1,0:T(8,128)}, f32[5,3,16,128]{3,2,1,0:T(8,128)S(1)}, u32[]{:S(2)}, u32[]{:S(2)}) collective-permute-start(f32[5,3,16,128]{3,2,1,0:T(8,128)} %get-tuple-element.19), channel_id=1, source_target_pairs={{0,8},{8,16},{16,24},{24,0},{1,9},{9,17},{17,25},{25,1},{2,10},{10... | collective-permute-start | bytes 368648 | tf_op jit(solution)/shard_map/ppermute | solution.py:20
  38.3 4.1 %collective-permute-start.3 = (f32[5,2,16,128]{3,2,1,0:T(8,128)}, f32[5,2,16,128]{3,2,1,0:T(8,128)S(1)}, u32[]{:S(2)}, u32[]{:S(2)}) collective-permute-start(f32[5,2,16,128]{3,2,1,0:T(8,128)} %get-tuple-element.18), channel_id=1, source_target_pairs={{0,24},{8,0},{16,8},{24,16},{1,25},{9,1},{17,9},{25,17},{2,26},{10... | collective-permute-start | bytes 245768 | tf_op jit(solution)/shard_map/ppermute | solution.py:20
  42.4 3.8 %copy-start.4 = (f32[5,2,16,128]{3,2,1,0:T(8,128)}, f32[5,2,16,128]{3,2,1,0:T(8,128)S(1)}, u32[]{:S(2)}) copy-start(f32[5,2,16,128]{3,2,1,0:T(8,128)S(1)} %collective-permute-done.3.axl_ref) | copy-start | bytes 245764
  43.0 3.3 %copy-start.2 = (f32[5,3,16,128]{3,2,1,0:T(8,128)}, f32[5,3,16,128]{3,2,1,0:T(8,128)S(1)}, u32[]{:S(2)}) copy-start(f32[5,3,16,128]{3,2,1,0:T(8,128)S(1)} %collective-permute-done.4.axr_ref) | copy-start | bytes 368644
  46.2 0.7 %copy-start.1 = (f32[5,8,8,128]{3,2,1,0:T(8,128)}, f32[5,8,8,128]{3,2,1,0:T(8,128)S(1)}, u32[]{:S(2)}) copy-start(f32[5,8,8,128]{3,2,1,0:T(8,128)S(1)} %collective-permute-done.5.ayl_ref) | copy-start | bytes 491524
  46.2 0.8 %copy-start = (f32[5,16,8,128]{3,2,1,0:T(8,128)}, f32[5,16,8,128]{3,2,1,0:T(8,128)S(1)}, u32[]{:S(2)}) copy-start(f32[5,16,8,128]{3,2,1,0:T(8,128)S(1)} %collective-permute-done.6.ayr_ref) | copy-start | bytes 983044

commit v2 on v1

--- a/solution.py
+++ b/solution.py
@@ -55,17 +55,28 @@
     ]
 
 
-def split_wrap(terms, idx, n, axis):
-    inner = terms[2]
-    wrap = None
-    for o in (0, 1, 3, 4, 5):
-        s = o - 2
-        r = pltpu.roll(terms[o], s % n, axis)
-        valid = (idx >= s) if s > 0 else (idx < n + s)
-        inner = inner + jnp.where(valid, r, 0.0)
-        piece = jnp.where(valid, 0.0, r)
-        wrap = piece if wrap is None else wrap + piece
-    return inner, wrap
+def rolled_sum(terms, n, axis):
+    r = {o: pltpu.roll(terms[o], (o - 2) % n, axis) for o in (0, 1, 3, 4, 5)}
+    tot = terms[2] + r[0] + r[1] + r[3] + r[4] + r[5]
+    return r, tot
+
+
+def split_rows(terms, row8, ny):
+    r, tot = rolled_sum(terms, ny, 0)
+    h = ny - 8
+    wr = (jnp.where(row8 < 1, r[3][0:8], 0.0) + jnp.where(row8 < 2, r[4][0:8], 0.0)
+          + jnp.where(row8 < 3, r[5][0:8], 0.0))
+    wl = jnp.where(row8 >= 6, r[0][h:ny], 0.0) + jnp.where(row8 >= 7, r[1][h:ny], 0.0)
+    inner = jnp.concatenate([tot[0:8] - wr, tot[8:h], tot[h:ny] - wl], 0) if h > 8 else \
+        jnp.concatenate([tot[0:8] - wr, tot[h:ny] - wl], 0)
+    return inner, wr, wl
+
+
+def split_lanes(terms, lane, nz):
+    r, tot = rolled_sum(terms, nz, 1)
+    wr = jnp.where(lane < 1, r[3], 0.0) + jnp.where(lane < 2, r[4], 0.0) + jnp.where(lane < 3, r[5], 0.0)
+    wl = jnp.where(lane >= nz - 2, r[0], 0.0) + jnp.where(lane >= nz - 1, r[1], 0.0)
+    return tot - wr - wl, wr, wl
 
 
 def stencil_kernel(fp_ref, fm_ref, adj_ref, xf_ref, yf_ref, zf_ref, w_ref,
@@ -73,6 +84,7 @@
     nf, nx, ny, nz = adj_ref.shape
     i = pl.program_id(0)
     row, lane = iotas(ny, nz)
+    row8 = lax.broadcasted_iota(jnp.int32, (8, nz), 0)
 
     @pl.when(i == 0)
     def _():
@@ -117,19 +129,19 @@
             sx = offset_terms(fx[0][f], fx[1][f], lambda s, k: w_ref[0, s, k, f, xl])
             sy = offset_terms(fy[0][f], fy[1][f], lambda s, k: w_ref[1, s, k, f, xl])
             sz = offset_terms(fz[0][f], fz[1][f], lambda s, k: w_ref[2, s, k, f, xl])
-            iy, wy = split_wrap(sy, row, ny, 0)
-            iz, wz = split_wrap(sz, lane, nz, 1)
+            iy, wyr, wyl = split_rows(sy, row8, ny)
+            iz, wzr, wzl = split_lanes(sz, lane, nz)
             for o in range(6):
                 val = sx[o] if o != 2 else sx[2] + iy + iz
                 acc_ref[f, x + o] = acc_ref[f, x + o] + val
-            rear = pltpu.roll(jnp.where(row < 3, wy, 0.0), 4 * (xl % 2), 0)[0:8]
-            lead = pltpu.roll(jnp.where(row >= ny - 2, wy, 0.0), 2 + 2 * (xl % 4), 0)[0:8]
+            rear = pltpu.roll(wyr, 4 * (xl % 2), 0)
+            lead = pltpu.roll(wyl, (2 + 2 * (xl % 4)) % 8, 0)
             kr = (f, xl // 2)
             kl = (f, xl // 4)
             yr_parts[kr] = rear if kr not in yr_parts else yr_parts[kr] + rear
             yl_parts[kl] = lead if kl not in yl_parts else yl_parts[kl] + lead
-            zr_ref[f] = zr_ref[f] + pltpu.roll(jnp.where(lane < 3, wz, 0.0), 4 * x, 1)
-            zl_ref[f] = zl_ref[f] + pltpu.roll(jnp.where(lane >= nz - 2, wz, 0.0), 2 + 4 * x, 1)
+            zr_ref[f] = zr_ref[f] + pltpu.roll(wzr, 4 * x, 1)
+            zl_ref[f] = zl_ref[f] + pltpu.roll(wzl, 2 + 4 * x, 1)
     for (f, t), v in yr_parts.items():
         yr_ref[f, t] = v
     for (f, t), v in yl_parts.items():

time: 64.3 us -> 64.2 us (level)
  no operation moved by 1% of the time
where the time goes in v2:
time: 64.2 us; the launch traced here: 63.6 us
  Pallas kernels  23.1 us (36%)
  starting transfers between devices  14.3 us (22%)
  blocking collectives  10.8 us (17%)
  waiting for transfers between devices  5.92 us (9%)
  local copies, waits for them, and re-layouts  4.07 us (6%)
  matrix products  2.41 us (4%)
  other arithmetic  1.59 us (2%)
  between operations  1.41 us (2%)
    pallas_call x1, Pallas kernels, on_device(): pl.pallas_call(stencil_kernel, grid=(nx // XC,), out_shape=(jax.ShapeDtyp...  17.4 us
    ppermute x8, starting transfers between devices, shift_from(): return lax.ppermute(x, axis, [(i, (i + by) % n) for i in range(n)])  14.3 us
    all_to_all x1, blocking collectives, on_device(): got = lax.all_to_all(t, AXES, 0, 0, tiled=True)  10.8 us
    ppermute x8, waiting for transfers between devices, shift_from(): return lax.ppermute(x, axis, [(i, (i + by) % n) for i in range(n)])  5.92 us
    pallas_call x1, Pallas kernels, on_device(): pl.pallas_call(fix_kernel, out_shape=(jax.ShapeDtypeStruct((nf, nx, ny, n...  3.35 us
    unnamed x24, local copies, waits for them, and re-layouts  3.23 us
    pallas_call x1, Pallas kernels, on_device(): pl.pallas_call(fronts_kernel, out_shape=(jax.ShapeDtypeStruct((nf, ny, nz...  2.35 us
  transfers between devices with their start and end apart: 8, of which 4 were waited for; matrix products, arithmetic and copies ran while one was open for 4% of the time, Pallas kernels for 0%

profile of v2, /device:TPU:0, one launch (start us, length us, event | category | flops | bytes accessed | tf_op | source)
XLA Modules:
  0.0 63.6 jit_solution(12887409571322915374)
XLA Ops:
  0.6 0.0 copy-start.10
  0.6 0.0 copy-start.9
  0.7 0.0 copy-start.7
  0.7 0.0 copy-start.8
  0.7 2.4 %shard_map.104 = (f32[5,16,128]{2,1,0:T(8,128)}, f32[5,32,128]{2,1,0:T(8,128)}, f32[5,16,128]{2,1,0:T(8,128)}) custom-call(f32[5,32,16,128]{3,2,1,0:T(8,128)} %adj_ref.3), custom_call_target="tpu_custom_call" | custom-call | tf_op jit(solution)/shard_map/pallas_call | solution.py:197
  3.0 5.0 %collective-permute-start.1 = (f32[5,32,128]{2,1,0:T(8,128)}, f32[5,32,128]{2,1,0:T(8,128)S(1)}, u32[]{:S(2)}, u32[]{:S(2)}) collective-permute-start(f32[5,32,128]{2,1,0:T(8,128)} %get-tuple-element.15), channel_id=1, source_target_pairs={{0,6},{2,0},{4,2},{6,4},{1,7},{3,1},{5,3},{7,5},{8,14},{10,8},{12,... | collective-permute-start | bytes 245768 | tf_op jit(solution)/shard_map/ppermute | solution.py:20
  8.1 0.7 %collective-permute-start = (f32[5,16,128]{2,1,0:T(8,128)}, f32[5,16,128]{2,1,0:T(8,128)S(1)}, u32[]{:S(2)}, u32[]{:S(2)}) collective-permute-start(f32[5,16,128]{2,1,0:T(8,128)} %get-tuple-element.14), channel_id=1, source_target_pairs={{0,24},{8,0},{16,8},{24,16},{1,25},{9,1},{17,9},{25,17},{2,26},{10... | collective-permute-start | bytes 122888 | tf_op jit(solution)/shard_map/ppermute | solution.py:20
  8.7 1.5 %collective-permute-start.2 = (f32[5,16,128]{2,1,0:T(8,128)}, f32[5,16,128]{2,1,0:T(8,128)S(1)}, u32[]{:S(2)}, u32[]{:S(2)}) collective-permute-start(f32[5,16,128]{2,1,0:T(8,128)} %get-tuple-element.16), channel_id=1, source_target_pairs={{0,1},{1,0},{2,3},{3,2},{4,5},{5,4},{6,7},{7,6},{8,9},{9,8},{10,11... | collective-permute-start | bytes 122888 | tf_op jit(solution)/shard_map/ppermute | solution.py:20
  10.2 0.0 copy-done.10
  10.2 0.1 eq.75
  10.3 0.2 convert_reduce_fusion
  10.5 0.1 fusion.15
  10.7 0.0 copy-done.9
  10.7 0.0 copy-done.7
  10.7 0.6 copy.14.fp_ref
  11.3 0.0 copy-done.8
  11.3 0.6 copy.15.fm_ref
  12.6 0.0 collective-permute-done.xf_ref
  12.6 0.0 copy-start.5
  12.6 0.4 collective-permute-done.2.zf_ref
  12.9 0.0 copy-start.6
  12.9 0.0 collective-permute-done.1.yf_ref
  12.9 0.3 copy-done.5
  13.2 0.3 copy-done.6
  13.5 0.0 copy-start.3
  13.5 0.6 %copy-done.3 = f32[5,32,128]{2,1,0:T(8,128)} copy-done((f32[5,32,128]{2,1,0:T(8,128)}, f32[5,32,128]{2,1,0:T(8,128)S(1)}, u32[]{:S(2)}) %copy-start.3) | copy-done | bytes 81944
  14.2 17.4 %shard_map.105 = (f32[5,32,16,128]{3,2,1,0:T(8,128)}, f32[5,2,16,128]{3,2,1,0:T(8,128)}, f32[5,3,16,128]{3,2,1,0:T(8,128)}, f32[5,8,8,128]{3,2,1,0:T(8,128)}, f3...) custom-call(f32[3,5,5]{2,1,0:T(8,128)} %copy.14.fp_ref, f32[3,5,5]{2,1,0:T(8,128)} %copy.15.fm_ref, ...), custom_call_target="tpu_custom_call" | custom-call | tf_op jit(solution)/shard_map/pallas_call | solution.py:212
  31.6 0.8 %pad_maximum_fusion = f32[2,5,16,128]{3,2,1,0:T(8,128)S(1)} fusion(f32[1,5,16,128]{3,2,1,0:T(8,128)} %bitcast.22, f32[1,5,16,128]{3,2,1,0:T(8,128)} %bitcast.21), kind=kLoop, calls=%fused_computation.23 | loop fusion | flops 20480 | bytes 163840 | tf_op jit(solution)/shard_map/stack | solution.py:250
  32.4 1.5 %collective-permute-start.7 = (f32[2,5,16,128]{3,2,1,0:T(8,128)S(1)}, f32[2,5,16,128]{3,2,1,0:T(8,128)S(1)}, u32[]{:S(2)}, u32[]{:S(2)}) collective-permute-start(f32[2,5,16,128]{3,2,1,0:T(8,128)S(1)} %pad_maximum_fusion), channel_id=1, source_target_pairs={{0,1},{1,0},{2,3},{3,2},{4,5},{5,4},{6,7},{7,6},{8,9},{9,8},{10,11... | collective-permute-start | bytes 245768 | tf_op jit(solution)/shard_map/ppermute | solution.py:20
  34.0 0.0 collective-permute-start.6
  34.0 0.3 fusion.2
  34.2 0.1 eq.79
  34.3 3.8 %collective-permute-start.5 = (f32[5,8,8,128]{3,2,1,0:T(8,128)}, f32[5,8,8,128]{3,2,1,0:T(8,128)S(1)}, u32[]{:S(2)}, u32[]{:S(2)}) collective-permute-start(f32[5,8,8,128]{3,2,1,0:T(8,128)} %get-tuple-element.20), channel_id=1, source_target_pairs={{0,6},{2,0},{4,2},{6,4},{1,7},{3,1},{5,3},{7,5},{8,14},{10,8},{12,... | collective-permute-start | bytes 491528 | tf_op jit(solution)/shard_map/ppermute | solution.py:20
  38.1 0.0 collective-permute-start.4
  38.1 1.7 %collective-permute-start.3 = (f32[5,2,16,128]{3,2,1,0:T(8,128)}, f32[5,2,16,128]{3,2,1,0:T(8,128)S(1)}, u32[]{:S(2)}, u32[]{:S(2)}) collective-permute-start(f32[5,2,16,128]{3,2,1,0:T(8,128)} %get-tuple-element.18), channel_id=1, source_target_pairs={{0,24},{8,0},{16,8},{24,16},{1,25},{9,1},{17,9},{25,17},{2,26},{10... | collective-permute-start | bytes 245768 | tf_op jit(solution)/shard_map/ppermute | solution.py:20
  39.9 0.0 collective-permute-done.7
  39.9 0.6 slice_bitcast_fusion
  40.5 1.7 %collective-permute-done.3.axl_ref = f32[5,2,16,128]{3,2,1,0:T(8,128)S(1)} collective-permute-done((f32[5,2,16,128]{3,2,1,0:T(8,128)}, f32[5,2,16,128]{3,2,1,0:T(8,128)S(1)}, u32[]{:S(2)}, u32[]{:S(2)}) %collective-permute-start.3) | collective-permute-done | bytes 81952 | tf_op jit(solution)/shard_map/ppermute | solution.py:20
  42.3 0.0 copy-start.4
  42.3 0.6 collective-permute-done.4.axr_ref
  42.8 0.0 copy-start.2
  42.8 3.3 %collective-permute-done.5.ayl_ref = f32[5,8,8,128]{3,2,1,0:T(8,128)S(1)} collective-permute-done((f32[5,8,8,128]{3,2,1,0:T(8,128)}, f32[5,8,8,128]{3,2,1,0:T(8,128)S(1)}, u32[]{:S(2)}, u32[]{:S(2)}) %collective-permute-start.5) | collective-permute-done | bytes 163872 | tf_op jit(solution)/shard_map/ppermute | solution.py:20
  46.1 0.0 copy-start.1
  46.1 0.0 collective-permute-done.6.ayr_ref
  46.1 0.0 copy-start
  46.1 0.0 copy-done.4
  46.1 0.0 copy-done.2
  46.1 0.6 copy-done.1
  46.7 0.1 copy-done
  46.8 3.4 %shard_map.106 = (f32[5,32,16,128]{3,2,1,0:T(8,128)}, f32[16,128]{1,0:T(8,128)}) custom-call(s32[16]{0:T(128)} %row_ref.1, s32[1]{0:T(128)S(6)} %copy.18.cnt_ref, f32[5,32,16,128]{3,2,1,0:T(8,128)} %get-tuple-element.17.sec_ref, f32[5,2,16,128]{3,2,1,0:T(8,128)} %copy-done.4, f32[5,3,16,128]{3,2,1,0:T(8,128)} %copy-done.2, ...), custom_call_target="tpu_custom_call", output_to_operand_aliasing={{0}: (2, {})} | custom-call | tf_op jit(solution)/shard_map/pallas_call | solution.py:255
  50.2 1.0 %convolution_bitcast_fusion = f32[32,32]{1,0:T(8,128)S(1)} fusion(s32[16,128]{1,0:T(8,128)S(1)} %get-tuple-element.29, f32[16,128]{1,0:T(8,128)} %get-tuple-element.25, s32[16,128]{1,0:T(8,128)S(1)} %get-tuple-element.28), kind=kOutput, calls=%fused_computation.4 | convolution fusion | flops 25362432 | bytes 28672 | tf_op jit(solution)/shard_map/rza,rzb->ab/dot_general | solution.py:274
  51.2 0.1 mul.23
  51.3 1.0 %fusion.3 = f32[32,32]{1,0:T(8,128)S(1)} fusion(f32[1024]{0:T(1024)S(1)} %eq.79, f32[1024]{0:T(1024)S(1)} %mul.23, s32[1024]{0:T(1024)S(1)} %copy-done.10), kind=kOutput, calls=%fused_computation.8 | convolution fusion | flops 12681216 | bytes 16384 | tf_op jit(solution)/shard_map/po,pk->ok/dot_general | solution.py:283
  52.3 10.8 %all_to_all.9 = f32[32,1,32]{2,1,0:T(1,128)S(1)} all-to-all(f32[32,1,32]{2,1,0:T(1,128)S(1)} %bitcast.23), channel_id=1, replica_groups=mesh['gx'=4,'gy'=4,'gz'=2] {'gx','gy','gz'}, dimensions={0} | all-to-all | bytes 8192 | tf_op jit(solution)/shard_map/all_to_all | solution.py:284
  63.1 0.6 reduce_sum.29
  (1 shorter events, 0.0 us)
Async XLA Ops:
  0.6 9.6 %copy-start.10 = (s32[1024]{0:T(1024)S(1)}, s32[1024]{0:T(1024)}, u32[]{:S(2)}) copy-start(s32[1024]{0:T(1024)} %param.17) | copy-start | bytes 12292
  0.6 10.0 %copy-start.9 = (s32[16,128]{1,0:T(8,128)S(1)}, s32[16,128]{1,0:T(8,128)}, u32[]{:S(2)}) copy-start(s32[16,128]{1,0:T(8,128)} %param.14) | copy-start | bytes 24580
  0.7 10.0 %copy-start.7 = (f32[3,5,5]{2,0,1:T(4,128)S(1)}, f32[3,5,5]{2,0,1:T(4,128)}, u32[]{:S(2)}) copy-start(f32[3,5,5]{2,0,1:T(4,128)} %param.11) | copy-start | bytes 904
  0.7 10.7 %copy-start.8 = (f32[3,5,5]{2,0,1:T(4,128)S(1)}, f32[3,5,5]{2,0,1:T(4,128)}, u32[]{:S(2)}) copy-start(f32[3,5,5]{2,0,1:T(4,128)} %param.12) | copy-start | bytes 904
  3.0 9.9 %collective-permute-start.1 = (f32[5,32,128]{2,1,0:T(8,128)}, f32[5,32,128]{2,1,0:T(8,128)S(1)}, u32[]{:S(2)}, u32[]{:S(2)}) collective-permute-start(f32[5,32,128]{2,1,0:T(8,128)} %get-tuple-element.15), channel_id=1, source_target_pairs={{0,6},{2,0},{4,2},{6,4},{1,7},{3,1},{5,3},{7,5},{8,14},{10,8},{12,... | collective-permute-start | bytes 245768 | tf_op jit(solution)/shard_map/ppermute | solution.py:20
  8.1 4.5 %collective-permute-start = (f32[5,16,128]{2,1,0:T(8,128)}, f32[5,16,128]{2,1,0:T(8,128)S(1)}, u32[]{:S(2)}, u32[]{:S(2)}) collective-permute-start(f32[5,16,128]{2,1,0:T(8,128)} %get-tuple-element.14), channel_id=1, source_target_pairs={{0,24},{8,0},{16,8},{24,16},{1,25},{9,1},{17,9},{25,17},{2,26},{10... | collective-permute-start | bytes 122888 | tf_op jit(solution)/shard_map/ppermute | solution.py:20
  8.7 4.2 %collective-permute-start.2 = (f32[5,16,128]{2,1,0:T(8,128)}, f32[5,16,128]{2,1,0:T(8,128)S(1)}, u32[]{:S(2)}, u32[]{:S(2)}) collective-permute-start(f32[5,16,128]{2,1,0:T(8,128)} %get-tuple-element.16), channel_id=1, source_target_pairs={{0,1},{1,0},{2,3},{3,2},{4,5},{5,4},{6,7},{7,6},{8,9},{9,8},{10,11... | collective-permute-start | bytes 122888 | tf_op jit(solution)/shard_map/ppermute | solution.py:20
  12.6 0.6 copy-start.5
  12.9 0.6 copy-start.6
  13.5 0.6 %copy-start.3 = (f32[5,32,128]{2,1,0:T(8,128)}, f32[5,32,128]{2,1,0:T(8,128)S(1)}, u32[]{:S(2)}) copy-start(f32[5,32,128]{2,1,0:T(8,128)S(1)} %collective-permute-done.1.yf_ref) | copy-start | bytes 245764
  32.4 7.4 %collective-permute-start.7 = (f32[2,5,16,128]{3,2,1,0:T(8,128)S(1)}, f32[2,5,16,128]{3,2,1,0:T(8,128)S(1)}, u32[]{:S(2)}, u32[]{:S(2)}) collective-permute-start(f32[2,5,16,128]{3,2,1,0:T(8,128)S(1)} %pad_maximum_fusion), channel_id=1, source_target_pairs={{0,1},{1,0},{2,3},{3,2},{4,5},{5,4},{6,7},{7,6},{8,9},{9,8},{10,11... | collective-permute-start | bytes 245768 | tf_op jit(solution)/shard_map/ppermute | solution.py:20
  34.0 12.1 %collective-permute-start.6 = (f32[5,16,8,128]{3,2,1,0:T(8,128)}, f32[5,16,8,128]{3,2,1,0:T(8,128)S(1)}, u32[]{:S(2)}, u32[]{:S(2)}) collective-permute-start(f32[5,16,8,128]{3,2,1,0:T(8,128)} %get-tuple-element.21), channel_id=1, source_target_pairs={{0,2},{2,4},{4,6},{6,0},{1,3},{3,5},{5,7},{7,1},{8,10},{10,12},{12... | collective-permute-start | bytes 983048 | tf_op jit(solution)/shard_map/ppermute | solution.py:20
  34.3 11.8 %collective-permute-start.5 = (f32[5,8,8,128]{3,2,1,0:T(8,128)}, f32[5,8,8,128]{3,2,1,0:T(8,128)S(1)}, u32[]{:S(2)}, u32[]{:S(2)}) collective-permute-start(f32[5,8,8,128]{3,2,1,0:T(8,128)} %get-tuple-element.20), channel_id=1, source_target_pairs={{0,6},{2,0},{4,2},{6,4},{1,7},{3,1},{5,3},{7,5},{8,14},{10,8},{12,... | collective-permute-start | bytes 491528 | tf_op jit(solution)/shard_map/ppermute | solution.py:20
  38.1 4.7 %collective-permute-start.4 = (f32[5,3,16,128]{3,2,1,0:T(8,128)}, f32[5,3,16,128]{3,2,1,0:T(8,128)S(1)}, u32[]{:S(2)}, u32[]{:S(2)}) collective-permute-start(f32[5,3,16,128]{3,2,1,0:T(8,128)} %get-tuple-element.19), channel_id=1, source_target_pairs={{0,8},{8,16},{16,24},{24,0},{1,9},{9,17},{17,25},{25,1},{2,10},{10... | collective-permute-start | bytes 368648 | tf_op jit(solution)/shard_map/ppermute | solution.py:20
  38.1 4.1 %collective-permute-start.3 = (f32[5,2,16,128]{3,2,1,0:T(8,128)}, f32[5,2,16,128]{3,2,1,0:T(8,128)S(1)}, u32[]{:S(2)}, u32[]{:S(2)}) collective-permute-start(f32[5,2,16,128]{3,2,1,0:T(8,128)} %get-tuple-element.18), channel_id=1, source_target_pairs={{0,24},{8,0},{16,8},{24,16},{1,25},{9,1},{17,9},{25,17},{2,26},{10... | collective-permute-start | bytes 245768 | tf_op jit(solution)/shard_map/ppermute | solution.py:20
  42.3 3.8 %copy-start.4 = (f32[5,2,16,128]{3,2,1,0:T(8,128)}, f32[5,2,16,128]{3,2,1,0:T(8,128)S(1)}, u32[]{:S(2)}) copy-start(f32[5,2,16,128]{3,2,1,0:T(8,128)S(1)} %collective-permute-done.3.axl_ref) | copy-start | bytes 245764
  42.8 3.3 %copy-start.2 = (f32[5,3,16,128]{3,2,1,0:T(8,128)}, f32[5,3,16,128]{3,2,1,0:T(8,128)S(1)}, u32[]{:S(2)}) copy-start(f32[5,3,16,128]{3,2,1,0:T(8,128)S(1)} %collective-permute-done.4.axr_ref) | copy-start | bytes 368644
  46.1 0.7 %copy-start.1 = (f32[5,8,8,128]{3,2,1,0:T(8,128)}, f32[5,8,8,128]{3,2,1,0:T(8,128)S(1)}, u32[]{:S(2)}) copy-start(f32[5,8,8,128]{3,2,1,0:T(8,128)S(1)} %collective-permute-done.5.ayl_ref) | copy-start | bytes 491524
  46.1 0.8 %copy-start = (f32[5,16,8,128]{3,2,1,0:T(8,128)}, f32[5,16,8,128]{3,2,1,0:T(8,128)S(1)}, u32[]{:S(2)}) copy-start(f32[5,16,8,128]{3,2,1,0:T(8,128)S(1)} %collective-permute-done.6.ayr_ref) | copy-start | bytes 983044

commit v3 on v2

--- a/solution.py
+++ b/solution.py
@@ -109,37 +109,39 @@
     yl_parts = {}
     for xl in range(XC):
         x = i * XC + xl
-        a = [adj_ref[f, x] for f in range(nf)]
         last = x == nx - 1
         nxt = jnp.minimum(x + 1, nx - 1)
-        an_x = [jnp.where(last, xf_ref[f], adj_ref[f, nxt]) for f in range(nf)]
-        an_y = [
-            jnp.where(row == ny - 1, yf_ref[f, pl.ds(x, 1), :], pltpu.roll(a[f], ny - 1, 0))
-            for f in range(nf)
-        ]
-        zshift = nz - 1 - x
-        an_z = [
-            jnp.where(lane == nz - 1, pltpu.roll(zf_ref[f], zshift, 1), pltpu.roll(a[f], nz - 1, 1))
-            for f in range(nf)
-        ]
-        fx = flux(0, [an_x[g] - a[g] for g in range(nf)])
-        fy = flux(1, [an_y[g] - a[g] for g in range(nf)])
-        fz = flux(2, [an_z[g] - a[g] for g in range(nf)])
-        for f in range(nf):
-            sx = offset_terms(fx[0][f], fx[1][f], lambda s, k: w_ref[0, s, k, f, xl])
-            sy = offset_terms(fy[0][f], fy[1][f], lambda s, k: w_ref[1, s, k, f, xl])
-            sz = offset_terms(fz[0][f], fz[1][f], lambda s, k: w_ref[2, s, k, f, xl])
+        a = [adj_ref[f, x] for f in range(nf)]
+        plus, minus = flux(0, [jnp.where(last, xf_ref[g], adj_ref[g, nxt]) - a[g] for g in range(nf)])
+        for f in range(nf):
+            sx = offset_terms(plus[f], minus[f], lambda s, k: w_ref[0, s, k, f, xl])
+            for o in range(6):
+                acc_ref[f, x + o] = acc_ref[f, x + o] + sx[o]
+        a = [adj_ref[f, x] for f in range(nf)]
+        plus, minus = flux(1, [
+            jnp.where(row == ny - 1, yf_ref[g, pl.ds(x, 1), :], pltpu.roll(a[g], ny - 1, 0)) - a[g]
+            for g in range(nf)
+        ])
+        for f in range(nf):
+            sy = offset_terms(plus[f], minus[f], lambda s, k: w_ref[1, s, k, f, xl])
             iy, wyr, wyl = split_rows(sy, row8, ny)
-            iz, wzr, wzl = split_lanes(sz, lane, nz)
-            for o in range(6):
-                val = sx[o] if o != 2 else sx[2] + iy + iz
-                acc_ref[f, x + o] = acc_ref[f, x + o] + val
+            acc_ref[f, x + 2] = acc_ref[f, x + 2] + iy
             rear = pltpu.roll(wyr, 4 * (xl % 2), 0)
             lead = pltpu.roll(wyl, (2 + 2 * (xl % 4)) % 8, 0)
             kr = (f, xl // 2)
             kl = (f, xl // 4)
             yr_parts[kr] = rear if kr not in yr_parts else yr_parts[kr] + rear
             yl_parts[kl] = lead if kl not in yl_parts else yl_parts[kl] + lead
+        a = [adj_ref[f, x] for f in range(nf)]
+        zshift = nz - 1 - x
+        plus, minus = flux(2, [
+            jnp.where(lane == nz - 1, pltpu.roll(zf_ref[g], zshift, 1), pltpu.roll(a[g], nz - 1, 1)) - a[g]
+            for g in range(nf)
+        ])
+        for f in range(nf):
+            sz = offset_terms(plus[f], minus[f], lambda s, k: w_ref[2, s, k, f, xl])
+            iz, wzr, wzl = split_lanes(sz, lane, nz)
+            acc_ref[f, x + 2] = acc_ref[f, x + 2] + iz
             zr_ref[f] = zr_ref[f] + pltpu.roll(wzr, 4 * x, 1)
             zl_ref[f] = zl_ref[f] + pltpu.roll(wzl, 2 + 4 * x, 1)
     for (f, t), v in yr_parts.items():

time: 64.2 us -> 64.4 us (level)
  no operation moved by 1% of the time
where the time goes in v3:
time: 64.4 us; the launch traced here: 63.8 us
  Pallas kernels  23.3 us (36%)
  starting transfers between devices  14.3 us (22%)
  blocking collectives  10.8 us (17%)
  waiting for transfers between devices  5.92 us (9%)
  local copies, waits for them, and re-layouts  4.07 us (6%)
  matrix products  2.42 us (4%)
  other arithmetic  1.59 us (2%)
  between operations  1.41 us (2%)
    pallas_call x1, Pallas kernels, on_device(): pl.pallas_call(stencil_kernel, grid=(nx // XC,), out_shape=(jax.ShapeDtyp...  17.6 us
    ppermute x8, starting transfers between devices, shift_from(): return lax.ppermute(x, axis, [(i, (i + by) % n) for i in range(n)])  14.3 us
    all_to_all x1, blocking collectives, on_device(): got = lax.all_to_all(t, AXES, 0, 0, tiled=True)  10.8 us
    ppermute x8, waiting for transfers between devices, shift_from(): return lax.ppermute(x, axis, [(i, (i + by) % n) for i in range(n)])  5.92 us
    pallas_call x1, Pallas kernels, on_device(): pl.pallas_call(fix_kernel, out_shape=(jax.ShapeDtypeStruct((nf, nx, ny, n...  3.35 us
    unnamed x24, local copies, waits for them, and re-layouts  3.23 us
    pallas_call x1, Pallas kernels, on_device(): pl.pallas_call(fronts_kernel, out_shape=(jax.ShapeDtypeStruct((nf, ny, nz...  2.35 us
  transfers between devices with their start and end apart: 8, of which 4 were waited for; matrix products, arithmetic and copies ran while one was open for 4% of the time, Pallas kernels for 0%

profile of v3, /device:TPU:0, one launch (start us, length us, event | category | flops | bytes accessed | tf_op | source)
XLA Modules:
  0.0 63.8 jit_solution(14480328039752302064)
XLA Ops:
  0.6 0.0 copy-start.10
  0.6 0.0 copy-start.9
  0.7 0.0 copy-start.7
  0.7 0.0 copy-start.8
  0.7 2.4 %shard_map.104 = (f32[5,16,128]{2,1,0:T(8,128)}, f32[5,32,128]{2,1,0:T(8,128)}, f32[5,16,128]{2,1,0:T(8,128)}) custom-call(f32[5,32,16,128]{3,2,1,0:T(8,128)} %adj_ref.3), custom_call_target="tpu_custom_call" | custom-call | tf_op jit(solution)/shard_map/pallas_call | solution.py:199
  3.0 5.0 %collective-permute-start.1 = (f32[5,32,128]{2,1,0:T(8,128)}, f32[5,32,128]{2,1,0:T(8,128)S(1)}, u32[]{:S(2)}, u32[]{:S(2)}) collective-permute-start(f32[5,32,128]{2,1,0:T(8,128)} %get-tuple-element.15), channel_id=1, source_target_pairs={{0,6},{2,0},{4,2},{6,4},{1,7},{3,1},{5,3},{7,5},{8,14},{10,8},{12,... | collective-permute-start | bytes 245768 | tf_op jit(solution)/shard_map/ppermute | solution.py:20
  8.1 0.7 %collective-permute-start = (f32[5,16,128]{2,1,0:T(8,128)}, f32[5,16,128]{2,1,0:T(8,128)S(1)}, u32[]{:S(2)}, u32[]{:S(2)}) collective-permute-start(f32[5,16,128]{2,1,0:T(8,128)} %get-tuple-element.14), channel_id=1, source_target_pairs={{0,24},{8,0},{16,8},{24,16},{1,25},{9,1},{17,9},{25,17},{2,26},{10... | collective-permute-start | bytes 122888 | tf_op jit(solution)/shard_map/ppermute | solution.py:20
  8.7 1.5 %collective-permute-start.2 = (f32[5,16,128]{2,1,0:T(8,128)}, f32[5,16,128]{2,1,0:T(8,128)S(1)}, u32[]{:S(2)}, u32[]{:S(2)}) collective-permute-start(f32[5,16,128]{2,1,0:T(8,128)} %get-tuple-element.16), channel_id=1, source_target_pairs={{0,1},{1,0},{2,3},{3,2},{4,5},{5,4},{6,7},{7,6},{8,9},{9,8},{10,11... | collective-permute-start | bytes 122888 | tf_op jit(solution)/shard_map/ppermute | solution.py:20
  10.2 0.0 copy-done.10
  10.2 0.1 eq.75
  10.3 0.2 convert_reduce_fusion
  10.5 0.1 fusion.15
  10.7 0.0 copy-done.9
  10.7 0.0 copy-done.7
  10.7 0.6 copy.14.fp_ref
  11.3 0.0 copy-done.8
  11.3 0.6 copy.15.fm_ref
  12.6 0.0 collective-permute-done.xf_ref
  12.6 0.0 copy-start.5
  12.6 0.4 collective-permute-done.2.zf_ref
  12.9 0.0 copy-start.6
  12.9 0.0 collective-permute-done.1.yf_ref
  12.9 0.3 copy-done.5
  13.2 0.3 copy-done.6
  13.5 0.0 copy-start.3
  13.5 0.6 %copy-done.3 = f32[5,32,128]{2,1,0:T(8,128)} copy-done((f32[5,32,128]{2,1,0:T(8,128)}, f32[5,32,128]{2,1,0:T(8,128)S(1)}, u32[]{:S(2)}) %copy-start.3) | copy-done | bytes 81944
  14.2 17.6 %shard_map.105 = (f32[5,32,16,128]{3,2,1,0:T(8,128)}, f32[5,2,16,128]{3,2,1,0:T(8,128)}, f32[5,3,16,128]{3,2,1,0:T(8,128)}, f32[5,8,8,128]{3,2,1,0:T(8,128)}, f3...) custom-call(f32[3,5,5]{2,1,0:T(8,128)} %copy.14.fp_ref, f32[3,5,5]{2,1,0:T(8,128)} %copy.15.fm_ref, ...), custom_call_target="tpu_custom_call" | custom-call | tf_op jit(solution)/shard_map/pallas_call | solution.py:214
  31.8 0.8 %pad_maximum_fusion = f32[2,5,16,128]{3,2,1,0:T(8,128)S(1)} fusion(f32[1,5,16,128]{3,2,1,0:T(8,128)} %bitcast.22, f32[1,5,16,128]{3,2,1,0:T(8,128)} %bitcast.21), kind=kLoop, calls=%fused_computation.23 | loop fusion | flops 20480 | bytes 163840 | tf_op jit(solution)/shard_map/stack | solution.py:252
  32.6 1.5 %collective-permute-start.7 = (f32[2,5,16,128]{3,2,1,0:T(8,128)S(1)}, f32[2,5,16,128]{3,2,1,0:T(8,128)S(1)}, u32[]{:S(2)}, u32[]{:S(2)}) collective-permute-start(f32[2,5,16,128]{3,2,1,0:T(8,128)S(1)} %pad_maximum_fusion), channel_id=1, source_target_pairs={{0,1},{1,0},{2,3},{3,2},{4,5},{5,4},{6,7},{7,6},{8,9},{9,8},{10,11... | collective-permute-start | bytes 245768 | tf_op jit(solution)/shard_map/ppermute | solution.py:20
  34.1 0.0 collective-permute-start.6
  34.1 0.3 fusion.2
  34.4 0.1 eq.79
  34.5 3.8 %collective-permute-start.5 = (f32[5,8,8,128]{3,2,1,0:T(8,128)}, f32[5,8,8,128]{3,2,1,0:T(8,128)S(1)}, u32[]{:S(2)}, u32[]{:S(2)}) collective-permute-start(f32[5,8,8,128]{3,2,1,0:T(8,128)} %get-tuple-element.20), channel_id=1, source_target_pairs={{0,6},{2,0},{4,2},{6,4},{1,7},{3,1},{5,3},{7,5},{8,14},{10,8},{12,... | collective-permute-start | bytes 491528 | tf_op jit(solution)/shard_map/ppermute | solution.py:20
  38.3 0.0 collective-permute-start.4
  38.3 1.7 %collective-permute-start.3 = (f32[5,2,16,128]{3,2,1,0:T(8,128)}, f32[5,2,16,128]{3,2,1,0:T(8,128)S(1)}, u32[]{:S(2)}, u32[]{:S(2)}) collective-permute-start(f32[5,2,16,128]{3,2,1,0:T(8,128)} %get-tuple-element.18), channel_id=1, source_target_pairs={{0,24},{8,0},{16,8},{24,16},{1,25},{9,1},{17,9},{25,17},{2,26},{10... | collective-permute-start | bytes 245768 | tf_op jit(solution)/shard_map/ppermute | solution.py:20
  40.1 0.0 collective-permute-done.7
  40.1 0.6 slice_bitcast_fusion
  40.7 1.7 %collective-permute-done.3.axl_ref = f32[5,2,16,128]{3,2,1,0:T(8,128)S(1)} collective-permute-done((f32[5,2,16,128]{3,2,1,0:T(8,128)}, f32[5,2,16,128]{3,2,1,0:T(8,128)S(1)}, u32[]{:S(2)}, u32[]{:S(2)}) %collective-permute-start.3) | collective-permute-done | bytes 81952 | tf_op jit(solution)/shard_map/ppermute | solution.py:20
  42.4 0.0 copy-start.4
  42.4 0.6 collective-permute-done.4.axr_ref
  43.0 0.0 copy-start.2
  43.0 3.3 %collective-permute-done.5.ayl_ref = f32[5,8,8,128]{3,2,1,0:T(8,128)S(1)} collective-permute-done((f32[5,8,8,128]{3,2,1,0:T(8,128)}, f32[5,8,8,128]{3,2,1,0:T(8,128)S(1)}, u32[]{:S(2)}, u32[]{:S(2)}) %collective-permute-start.5) | collective-permute-done | bytes 163872 | tf_op jit(solution)/shard_map/ppermute | solution.py:20
  46.3 0.0 copy-start.1
  46.3 0.0 collective-permute-done.6.ayr_ref
  46.3 0.0 copy-start
  46.3 0.0 copy-done.4
  46.3 0.0 copy-done.2
  46.3 0.6 copy-done.1
  46.9 0.1 copy-done
  47.0 3.4 %shard_map.106 = (f32[5,32,16,128]{3,2,1,0:T(8,128)}, f32[16,128]{1,0:T(8,128)}) custom-call(s32[16]{0:T(128)} %row_ref.1, s32[1]{0:T(128)S(6)} %copy.18.cnt_ref, f32[5,32,16,128]{3,2,1,0:T(8,128)} %get-tuple-element.17.sec_ref, f32[5,2,16,128]{3,2,1,0:T(8,128)} %copy-done.4, f32[5,3,16,128]{3,2,1,0:T(8,128)} %copy-done.2, ...), custom_call_target="tpu_custom_call", output_to_operand_aliasing={{0}: (2, {})} | custom-call | tf_op jit(solution)/shard_map/pallas_call | solution.py:257
  50.4 1.0 %convolution_bitcast_fusion = f32[32,32]{1,0:T(8,128)S(1)} fusion(s32[16,128]{1,0:T(8,128)S(1)} %get-tuple-element.29, f32[16,128]{1,0:T(8,128)} %get-tuple-element.25, s32[16,128]{1,0:T(8,128)S(1)} %get-tuple-element.28), kind=kOutput, calls=%fused_computation.4 | convolution fusion | flops 25362432 | bytes 28672 | tf_op jit(solution)/shard_map/rza,rzb->ab/dot_general | solution.py:276
  51.4 0.1 mul.23
  51.5 1.0 %fusion.3 = f32[32,32]{1,0:T(8,128)S(1)} fusion(f32[1024]{0:T(1024)S(1)} %eq.79, f32[1024]{0:T(1024)S(1)} %mul.23, s32[1024]{0:T(1024)S(1)} %copy-done.10), kind=kOutput, calls=%fused_computation.8 | convolution fusion | flops 12681216 | bytes 16384 | tf_op jit(solution)/shard_map/po,pk->ok/dot_general | solution.py:285
  52.5 10.8 %all_to_all.9 = f32[32,1,32]{2,1,0:T(1,128)S(1)} all-to-all(f32[32,1,32]{2,1,0:T(1,128)S(1)} %bitcast.23), channel_id=1, replica_groups=mesh['gx'=4,'gy'=4,'gz'=2] {'gx','gy','gz'}, dimensions={0} | all-to-all | bytes 8192 | tf_op jit(solution)/shard_map/all_to_all | solution.py:286
  63.2 0.6 reduce_sum.29
  (1 shorter events, 0.0 us)
Async XLA Ops:
  0.6 9.6 %copy-start.10 = (s32[1024]{0:T(1024)S(1)}, s32[1024]{0:T(1024)}, u32[]{:S(2)}) copy-start(s32[1024]{0:T(1024)} %param.17) | copy-start | bytes 12292
  0.6 10.0 %copy-start.9 = (s32[16,128]{1,0:T(8,128)S(1)}, s32[16,128]{1,0:T(8,128)}, u32[]{:S(2)}) copy-start(s32[16,128]{1,0:T(8,128)} %param.14) | copy-start | bytes 24580
  0.7 10.0 %copy-start.7 = (f32[3,5,5]{2,0,1:T(4,128)S(1)}, f32[3,5,5]{2,0,1:T(4,128)}, u32[]{:S(2)}) copy-start(f32[3,5,5]{2,0,1:T(4,128)} %param.11) | copy-start | bytes 904
  0.7 10.7 %copy-start.8 = (f32[3,5,5]{2,0,1:T(4,128)S(1)}, f32[3,5,5]{2,0,1:T(4,128)}, u32[]{:S(2)}) copy-start(f32[3,5,5]{2,0,1:T(4,128)} %param.12) | copy-start | bytes 904
  3.0 9.9 %collective-permute-start.1 = (f32[5,32,128]{2,1,0:T(8,128)}, f32[5,32,128]{2,1,0:T(8,128)S(1)}, u32[]{:S(2)}, u32[]{:S(2)}) collective-permute-start(f32[5,32,128]{2,1,0:T(8,128)} %get-tuple-element.15), channel_id=1, source_target_pairs={{0,6},{2,0},{4,2},{6,4},{1,7},{3,1},{5,3},{7,5},{8,14},{10,8},{12,... | collective-permute-start | bytes 245768 | tf_op jit(solution)/shard_map/ppermute | solution.py:20
  8.1 4.5 %collective-permute-start = (f32[5,16,128]{2,1,0:T(8,128)}, f32[5,16,128]{2,1,0:T(8,128)S(1)}, u32[]{:S(2)}, u32[]{:S(2)}) collective-permute-start(f32[5,16,128]{2,1,0:T(8,128)} %get-tuple-element.14), channel_id=1, source_target_pairs={{0,24},{8,0},{16,8},{24,16},{1,25},{9,1},{17,9},{25,17},{2,26},{10... | collective-permute-start | bytes 122888 | tf_op jit(solution)/shard_map/ppermute | solution.py:20
  8.7 4.2 %collective-permute-start.2 = (f32[5,16,128]{2,1,0:T(8,128)}, f32[5,16,128]{2,1,0:T(8,128)S(1)}, u32[]{:S(2)}, u32[]{:S(2)}) collective-permute-start(f32[5,16,128]{2,1,0:T(8,128)} %get-tuple-element.16), channel_id=1, source_target_pairs={{0,1},{1,0},{2,3},{3,2},{4,5},{5,4},{6,7},{7,6},{8,9},{9,8},{10,11... | collective-permute-start | bytes 122888 | tf_op jit(solution)/shard_map/ppermute | solution.py:20
  12.6 0.6 copy-start.5
  12.9 0.6 copy-start.6
  13.5 0.6 %copy-start.3 = (f32[5,32,128]{2,1,0:T(8,128)}, f32[5,32,128]{2,1,0:T(8,128)S(1)}, u32[]{:S(2)}) copy-start(f32[5,32,128]{2,1,0:T(8,128)S(1)} %collective-permute-done.1.yf_ref) | copy-start | bytes 245764
  32.6 7.4 %collective-permute-start.7 = (f32[2,5,16,128]{3,2,1,0:T(8,128)S(1)}, f32[2,5,16,128]{3,2,1,0:T(8,128)S(1)}, u32[]{:S(2)}, u32[]{:S(2)}) collective-permute-start(f32[2,5,16,128]{3,2,1,0:T(8,128)S(1)} %pad_maximum_fusion), channel_id=1, source_target_pairs={{0,1},{1,0},{2,3},{3,2},{4,5},{5,4},{6,7},{7,6},{8,9},{9,8},{10,11... | collective-permute-start | bytes 245768 | tf_op jit(solution)/shard_map/ppermute | solution.py:20
  34.1 12.1 %collective-permute-start.6 = (f32[5,16,8,128]{3,2,1,0:T(8,128)}, f32[5,16,8,128]{3,2,1,0:T(8,128)S(1)}, u32[]{:S(2)}, u32[]{:S(2)}) collective-permute-start(f32[5,16,8,128]{3,2,1,0:T(8,128)} %get-tuple-element.21), channel_id=1, source_target_pairs={{0,2},{2,4},{4,6},{6,0},{1,3},{3,5},{5,7},{7,1},{8,10},{10,12},{12... | collective-permute-start | bytes 983048 | tf_op jit(solution)/shard_map/ppermute | solution.py:20
  34.5 11.8 %collective-permute-start.5 = (f32[5,8,8,128]{3,2,1,0:T(8,128)}, f32[5,8,8,128]{3,2,1,0:T(8,128)S(1)}, u32[]{:S(2)}, u32[]{:S(2)}) collective-permute-start(f32[5,8,8,128]{3,2,1,0:T(8,128)} %get-tuple-element.20), channel_id=1, source_target_pairs={{0,6},{2,0},{4,2},{6,4},{1,7},{3,1},{5,3},{7,5},{8,14},{10,8},{12,... | collective-permute-start | bytes 491528 | tf_op jit(solution)/shard_map/ppermute | solution.py:20
  38.3 4.7 %collective-permute-start.4 = (f32[5,3,16,128]{3,2,1,0:T(8,128)}, f32[5,3,16,128]{3,2,1,0:T(8,128)S(1)}, u32[]{:S(2)}, u32[]{:S(2)}) collective-permute-start(f32[5,3,16,128]{3,2,1,0:T(8,128)} %get-tuple-element.19), channel_id=1, source_target_pairs={{0,8},{8,16},{16,24},{24,0},{1,9},{9,17},{17,25},{25,1},{2,10},{10... | collective-permute-start | bytes 368648 | tf_op jit(solution)/shard_map/ppermute | solution.py:20
  38.3 4.1 %collective-permute-start.3 = (f32[5,2,16,128]{3,2,1,0:T(8,128)}, f32[5,2,16,128]{3,2,1,0:T(8,128)S(1)}, u32[]{:S(2)}, u32[]{:S(2)}) collective-permute-start(f32[5,2,16,128]{3,2,1,0:T(8,128)} %get-tuple-element.18), channel_id=1, source_target_pairs={{0,24},{8,0},{16,8},{24,16},{1,25},{9,1},{17,9},{25,17},{2,26},{10... | collective-permute-start | bytes 245768 | tf_op jit(solution)/shard_map/ppermute | solution.py:20
  42.4 3.8 %copy-start.4 = (f32[5,2,16,128]{3,2,1,0:T(8,128)}, f32[5,2,16,128]{3,2,1,0:T(8,128)S(1)}, u32[]{:S(2)}) copy-start(f32[5,2,16,128]{3,2,1,0:T(8,128)S(1)} %collective-permute-done.3.axl_ref) | copy-start | bytes 245764
  43.0 3.3 %copy-start.2 = (f32[5,3,16,128]{3,2,1,0:T(8,128)}, f32[5,3,16,128]{3,2,1,0:T(8,128)S(1)}, u32[]{:S(2)}) copy-start(f32[5,3,16,128]{3,2,1,0:T(8,128)S(1)} %collective-permute-done.4.axr_ref) | copy-start | bytes 368644
  46.3 0.7 %copy-start.1 = (f32[5,8,8,128]{3,2,1,0:T(8,128)}, f32[5,8,8,128]{3,2,1,0:T(8,128)S(1)}, u32[]{:S(2)}) copy-start(f32[5,8,8,128]{3,2,1,0:T(8,128)S(1)} %collective-permute-done.5.ayl_ref) | copy-start | bytes 491524
  46.3 0.8 %copy-start = (f32[5,16,8,128]{3,2,1,0:T(8,128)}, f32[5,16,8,128]{3,2,1,0:T(8,128)S(1)}, u32[]{:S(2)}) copy-start(f32[5,16,8,128]{3,2,1,0:T(8,128)S(1)} %collective-permute-done.6.ayr_ref) | copy-start | bytes 983044

commit v4 on v3

--- a/solution.py
+++ b/solution.py
@@ -80,7 +80,7 @@
 
 
 def stencil_kernel(fp_ref, fm_ref, adj_ref, xf_ref, yf_ref, zf_ref, w_ref,
-                   sec_ref, xl_ref, xr_ref, yl_ref, yr_ref, zl_ref, zr_ref, acc_ref):
+                   sec_ref, xl_ref, xr_ref, yl_ref, yr_ref, zz_ref, acc_ref):
     nf, nx, ny, nz = adj_ref.shape
     i = pl.program_id(0)
     row, lane = iotas(ny, nz)
@@ -89,8 +89,7 @@
     @pl.when(i == 0)
     def _():
         acc_ref[...] = jnp.zeros_like(acc_ref)
-        zl_ref[...] = jnp.zeros_like(zl_ref)
-        zr_ref[...] = jnp.zeros_like(zr_ref)
+        zz_ref[...] = jnp.zeros_like(zz_ref)
 
     def flux(d, diff):
         plus, minus = [], []
@@ -142,8 +141,8 @@
             sz = offset_terms(plus[f], minus[f], lambda s, k: w_ref[2, s, k, f, xl])
             iz, wzr, wzl = split_lanes(sz, lane, nz)
             acc_ref[f, x + 2] = acc_ref[f, x + 2] + iz
-            zr_ref[f] = zr_ref[f] + pltpu.roll(wzr, 4 * x, 1)
-            zl_ref[f] = zl_ref[f] + pltpu.roll(wzl, 2 + 4 * x, 1)
+            zz_ref[0, f] = zz_ref[0, f] + pltpu.roll(wzl, 2 + 4 * x, 1)
+            zz_ref[1, f] = zz_ref[1, f] + pltpu.roll(wzr, 4 * x, 1)
     for (f, t), v in yr_parts.items():
         yr_ref[f, t] = v
     for (f, t), v in yl_parts.items():
@@ -162,7 +161,7 @@
             xr_ref[f] = acc_ref[f, nx + 2:nx + 5]
 
 
-def fix_kernel(row_ref, cnt_ref, sec_ref, axl_ref, axr_ref, ayl_ref, ayr_ref, azl_ref, azr_ref,
+def fix_kernel(row_ref, cnt_ref, sec_ref, axl_ref, axr_ref, ayl_ref, ayr_ref, az_ref,
                coef_ref, out_ref, wt_ref):
     nf, nx, ny, nz = sec_ref.shape
     row, lane = iotas(ny, nz)
@@ -173,8 +172,8 @@
             add = jnp.where(row < 3, pltpu.roll(ty, (ny - 4 * (x % 2)) % ny, 0), 0.0)
             ty = jnp.concatenate([ayl_ref[f, x // 4], pad], 0)
             add = add + jnp.where(row >= ny - 2, pltpu.roll(ty, (ny - 2 - 2 * (x % 4)) % ny, 0), 0.0)
-            add = add + jnp.where(lane < 3, pltpu.roll(azr_ref[f], (nz - 4 * x) % nz, 1), 0.0)
-            add = add + jnp.where(lane >= nz - 2, pltpu.roll(azl_ref[f], (nz - 2 - 4 * x) % nz, 1), 0.0)
+            add = add + jnp.where(lane < 3, pltpu.roll(az_ref[1, f], (nz - 4 * x) % nz, 1), 0.0)
+            add = add + jnp.where(lane >= nz - 2, pltpu.roll(az_ref[0, f], (nz - 2 - 4 * x) % nz, 1), 0.0)
             if x < 3:
                 add = add + axr_ref[f, x]
             if x >= nx - 2:
@@ -211,7 +210,7 @@
     zf = shift_from(zf, "gz", -1)
     const4 = lambda i: (0, 0, 0, 0)
     const3 = lambda i: (0, 0, 0)
-    sec, xl, xr, yl, yr, zl, zr = pl.pallas_call(
+    sec, xl, xr, yl, yr, zz = pl.pallas_call(
         stencil_kernel,
         grid=(nx // XC,),
         out_shape=(
@@ -220,8 +219,7 @@
             jax.ShapeDtypeStruct((nf, 3, ny, nz), F32),
             jax.ShapeDtypeStruct((nf, nx // 4, 8, nz), F32),
             jax.ShapeDtypeStruct((nf, nx // 2, 8, nz), F32),
-            jax.ShapeDtypeStruct((nf, ny, nz), F32),
-            jax.ShapeDtypeStruct((nf, ny, nz), F32),
+            jax.ShapeDtypeStruct((2, nf, ny, nz), F32),
         ),
         in_specs=[
             SMEM,
@@ -238,8 +236,7 @@
             pl.BlockSpec((nf, 3, ny, nz), const4),
             pl.BlockSpec((nf, XC // 4, 8, nz), lambda i: (0, i, 0, 0)),
             pl.BlockSpec((nf, XC // 2, 8, nz), lambda i: (0, i, 0, 0)),
-            pl.BlockSpec((nf, ny, nz), const3),
-            pl.BlockSpec((nf, ny, nz), const3),
+            pl.BlockSpec((2, nf, ny, nz), const4),
         ),
         scratch_shapes=[pltpu.VMEM((nf, nx + 5, ny, nz), F32)],
         compiler_params=pltpu.CompilerParams(dimension_semantics=("arbitrary",)),
@@ -249,10 +246,9 @@
     ayl = shift_from(yl, "gy", -1)
     ayr = shift_from(yr, "gy", 1)
     if lax.axis_size("gz") == 2:
-        azl, azr = shift_from(jnp.stack([zl, zr]), "gz", 1)
+        az = shift_from(zz, "gz", 1)
     else:
-        azl = shift_from(zl, "gz", -1)
-        azr = shift_from(zr, "gz", 1)
+        az = jnp.stack([shift_from(zz[0], "gz", -1), shift_from(zz[1], "gz", 1)])
     nr = wall_row.shape[0]
     section, wt = pl.pallas_call(
         fix_kernel,
@@ -260,10 +256,10 @@
             jax.ShapeDtypeStruct((nf, nx, ny, nz), F32),
             jax.ShapeDtypeStruct((nr, nz), F32),
         ),
-        in_specs=[SMEM, SMEM] + [VMEM] * 8,
+        in_specs=[SMEM, SMEM] + [VMEM] * 7,
         out_specs=(VMEM, VMEM),
         input_output_aliases={2: 0},
-    )(wall_row, wall_count, sec, axl, axr, ayl, ayr, azl, azr, wall_coef)
+    )(wall_row, wall_count, sec, axl, axr, ayl, ayr, az, wall_coef)
 
     npan = panel_owner.shape[0]
     per = npan // ndev

time: 64.4 us -> 62.7 us (0.974)
  waiting for transfers between devices: 5.92 us -> 5.07 us
  other arithmetic: 1.59 us -> 0.79 us
  blocking collectives: 10.8 us -> 11.5 us
  local copies, waits for them, and re-layouts: 4.07 us -> 3.41 us
    ppermute x8, waiting for transfers between devices: 5.92 us -> 5.07 us  [shift_from(): return lax.ppermute(x, axis, [(i, (i + by) % n) for i in range(n)])]
    another operation x1 -> x0, other arithmetic: 0.81 us -> none  [on_device(): azl, azr = shift_from(jnp.stack([zl, zr]), 'gz', 1)]
    all_to_all x1, blocking collectives: 10.8 us -> 11.5 us  [on_device(): got = lax.all_to_all(t, AXES, 0, 0, tiled=True)]
    unnamed x24 -> x26, local copies, waits for them, and re-layouts: 3.23 us -> 3.2 us
  transfers between devices with their start and end apart: 8 -> 8, of which waited for: 4 -> 5; matrix products, arithmetic and copies ran while one was open for 4% -> 3% of each run, Pallas kernels for 0% -> 0%
where the time goes in v4:
time: 62.7 us; the launch traced here: 62.2 us
  Pallas kernels  23.2 us (37%)
  starting transfers between devices  14.4 us (23%)
  blocking collectives  11.5 us (18%)
  waiting for transfers between devices  5.07 us (8%)
  local copies, waits for them, and re-layouts  3.41 us (5%)
  matrix products  2.42 us (4%)
  between operations  1.39 us (2%)
  other arithmetic  0.79 us (1%)
    pallas_call x1, Pallas kernels, on_device(): pl.pallas_call(stencil_kernel, grid=(nx // XC,), out_shape=(jax.ShapeDtyp...  17.5 us
    ppermute x8, starting transfers between devices, shift_from(): return lax.ppermute(x, axis, [(i, (i + by) % n) for i in range(n)])  14.4 us
    all_to_all x1, blocking collectives, on_device(): got = lax.all_to_all(t, AXES, 0, 0, tiled=True)  11.5 us
    ppermute x8, waiting for transfers between devices, shift_from(): return lax.ppermute(x, axis, [(i, (i + by) % n) for i in range(n)])  5.07 us
    pallas_call x1, Pallas kernels, on_device(): pl.pallas_call(fix_kernel, out_shape=(jax.ShapeDtypeStruct((nf, nx, ny, n...  3.37 us
    unnamed x26, local copies, waits for them, and re-layouts  3.2 us
    pallas_call x1, Pallas kernels, on_device(): pl.pallas_call(fronts_kernel, out_shape=(jax.ShapeDtypeStruct((nf, ny, nz...  2.35 us
  transfers between devices with their start and end apart: 8, of which 5 were waited for; matrix products, arithmetic and copies ran while one was open for 3% of the time, Pallas kernels for 0%

profile of v4, /device:TPU:0, one launch (start us, length us, event | category | flops | bytes accessed | tf_op | source)
XLA Modules:
  0.0 62.2 jit_solution(15053714333284496711)
XLA Ops:
  0.6 0.0 copy-start.11
  0.6 0.0 copy-start.8
  0.7 0.0 copy-start.9
  0.7 2.3 %shard_map.104 = (f32[5,16,128]{2,1,0:T(8,128)}, f32[5,32,128]{2,1,0:T(8,128)}, f32[5,16,128]{2,1,0:T(8,128)}) custom-call(f32[5,32,16,128]{3,2,1,0:T(8,128)} %adj_ref.3), custom_call_target="tpu_custom_call" | custom-call | tf_op jit(solution)/shard_map/pallas_call | solution.py:198
  3.0 5.0 %collective-permute-start.1 = (f32[5,32,128]{2,1,0:T(8,128)}, f32[5,32,128]{2,1,0:T(8,128)S(1)}, u32[]{:S(2)}, u32[]{:S(2)}) collective-permute-start(f32[5,32,128]{2,1,0:T(8,128)} %get-tuple-element.14), channel_id=1, source_target_pairs={{0,6},{2,0},{4,2},{6,4},{1,7},{3,1},{5,3},{7,5},{8,14},{10,8},{12,... | collective-permute-start | bytes 245768 | tf_op jit(solution)/shard_map/ppermute | solution.py:20
  8.1 0.7 %collective-permute-start = (f32[5,16,128]{2,1,0:T(8,128)}, f32[5,16,128]{2,1,0:T(8,128)S(1)}, u32[]{:S(2)}, u32[]{:S(2)}) collective-permute-start(f32[5,16,128]{2,1,0:T(8,128)} %get-tuple-element.13), channel_id=1, source_target_pairs={{0,24},{8,0},{16,8},{24,16},{1,25},{9,1},{17,9},{25,17},{2,26},{10... | collective-permute-start | bytes 122888 | tf_op jit(solution)/shard_map/ppermute | solution.py:20
  8.7 1.5 %collective-permute-start.2 = (f32[5,16,128]{2,1,0:T(8,128)}, f32[5,16,128]{2,1,0:T(8,128)S(1)}, u32[]{:S(2)}, u32[]{:S(2)}) collective-permute-start(f32[5,16,128]{2,1,0:T(8,128)} %get-tuple-element.15), channel_id=1, source_target_pairs={{0,1},{1,0},{2,3},{3,2},{4,5},{5,4},{6,7},{7,6},{8,9},{9,8},{10,11... | collective-permute-start | bytes 122888 | tf_op jit(solution)/shard_map/ppermute | solution.py:20
  10.2 0.0 copy-done.11
  10.2 0.1 eq.75
  10.3 0.2 convert_reduce_fusion
  10.5 0.1 fusion.15
  10.6 0.0 copy-done.8
  10.7 0.6 copy.14.fp_ref
  11.3 0.0 copy-done.9
  11.3 0.6 copy.15.fm_ref
  11.9 0.0 copy-start.10
  11.9 0.0 collective-permute-done.xf_ref
  11.9 0.0 copy-start.6
  11.9 1.0 %collective-permute-done.2.zf_ref = f32[5,16,128]{2,1,0:T(8,128)S(1)} collective-permute-done((f32[5,16,128]{2,1,0:T(8,128)}, f32[5,16,128]{2,1,0:T(8,128)S(1)}, u32[]{:S(2)}, u32[]{:S(2)}) %collective-permute-start.2) | collective-permute-done | bytes 40992 | tf_op jit(solution)/shard_map/ppermute | solution.py:20
  12.9 0.0 copy-start.7
  12.9 0.0 collective-permute-done.1.yf_ref
  12.9 0.0 copy-done.6
  12.9 0.6 copy-done.7
  13.5 0.0 copy-start.3
  13.5 0.6 %copy-done.3 = f32[5,32,128]{2,1,0:T(8,128)} copy-done((f32[5,32,128]{2,1,0:T(8,128)}, f32[5,32,128]{2,1,0:T(8,128)S(1)}, u32[]{:S(2)}) %copy-start.3) | copy-done | bytes 81944
  14.2 17.5 %shard_map.105 = (f32[5,32,16,128]{3,2,1,0:T(8,128)}, f32[5,2,16,128]{3,2,1,0:T(8,128)}, f32[5,3,16,128]{3,2,1,0:T(8,128)}, f32[5,8,8,128]{3,2,1,0:T(8,128)}, f3...) custom-call(f32[3,5,5]{2,1,0:T(8,128)} %copy.14.fp_ref, f32[3,5,5]{2,1,0:T(8,128)} %copy.15.fm_ref, ...), custom_call_target="tpu_custom_call" | custom-call | tf_op jit(solution)/shard_map/pallas_call | solution.py:213
  31.7 0.1 collective-permute-start.6
  31.8 3.8 %collective-permute-start.5 = (f32[5,8,8,128]{3,2,1,0:T(8,128)}, f32[5,8,8,128]{3,2,1,0:T(8,128)S(1)}, u32[]{:S(2)}, u32[]{:S(2)}) collective-permute-start(f32[5,8,8,128]{3,2,1,0:T(8,128)} %get-tuple-element.19), channel_id=1, source_target_pairs={{0,6},{2,0},{4,2},{6,4},{1,7},{3,1},{5,3},{7,5},{8,14},{10,8},{12,... | collective-permute-start | bytes 491528 | tf_op jit(solution)/shard_map/ppermute | solution.py:20
  35.6 0.0 copy-done.10
  36.3 0.1 collective-permute-start.4
  36.3 1.7 %collective-permute-start.3 = (f32[5,2,16,128]{3,2,1,0:T(8,128)}, f32[5,2,16,128]{3,2,1,0:T(8,128)S(1)}, u32[]{:S(2)}, u32[]{:S(2)}) collective-permute-start(f32[5,2,16,128]{3,2,1,0:T(8,128)} %get-tuple-element.17), channel_id=1, source_target_pairs={{0,24},{8,0},{16,8},{24,16},{1,25},{9,1},{17,9},{25,17},{2,26},{10... | collective-permute-start | bytes 245768 | tf_op jit(solution)/shard_map/ppermute | solution.py:20
  38.1 1.5 %collective-permute-start.7 = (f32[2,5,16,128]{3,2,1,0:T(8,128)}, f32[2,5,16,128]{3,2,1,0:T(8,128)S(1)}, u32[]{:S(2)}, u32[]{:S(2)}) collective-permute-start(f32[2,5,16,128]{3,2,1,0:T(8,128)} %get-tuple-element.21), channel_id=1, source_target_pairs={{0,1},{1,0},{2,3},{3,2},{4,5},{5,4},{6,7},{7,6},{8,9},{9,8},{10,11... | collective-permute-start | bytes 245768 | tf_op jit(solution)/shard_map/ppermute | solution.py:20
  39.6 0.3 fusion.2
  39.9 0.1 eq.79
  39.9 0.5 collective-permute-done.3.axl_ref
  40.4 0.0 copy-start.4
  40.4 2.3 %collective-permute-done.7.az_ref = f32[2,5,16,128]{3,2,1,0:T(8,128)S(1)} collective-permute-done((f32[2,5,16,128]{3,2,1,0:T(8,128)}, f32[2,5,16,128]{3,2,1,0:T(8,128)S(1)}, u32[]{:S(2)}, u32[]{:S(2)}) %collective-permute-start.7) | collective-permute-done | bytes 81952 | tf_op jit(solution)/shard_map/ppermute | solution.py:20
  42.7 0.0 copy-start.5
  42.7 0.0 collective-permute-done.4.axr_ref
  42.7 0.0 copy-start.2
  42.7 1.0 %collective-permute-done.5.ayl_ref = f32[5,8,8,128]{3,2,1,0:T(8,128)S(1)} collective-permute-done((f32[5,8,8,128]{3,2,1,0:T(8,128)}, f32[5,8,8,128]{3,2,1,0:T(8,128)S(1)}, u32[]{:S(2)}, u32[]{:S(2)}) %collective-permute-start.5) | collective-permute-done | bytes 163872 | tf_op jit(solution)/shard_map/ppermute | solution.py:20
  43.7 0.0 copy-start.1
  43.7 0.3 collective-permute-done.6.ayr_ref
  44.0 0.0 copy-start
  44.0 0.0 copy-done.4
  44.0 0.0 copy-done.5
  44.0 0.0 copy-done.2
  44.0 0.4 copy-done.1
  44.3 0.3 copy-done
  44.7 3.4 %shard_map.106 = (f32[5,32,16,128]{3,2,1,0:T(8,128)}, f32[16,128]{1,0:T(8,128)}) custom-call(s32[16]{0:T(128)} %row_ref.1, s32[1]{0:T(128)S(6)} %copy.18.cnt_ref, f32[5,32,16,128]{3,2,1,0:T(8,128)} %get-tuple-element.16.sec_ref, f32[5,2,16,128]{3,2,1,0:T(8,128)} %copy-done.4, f32[5,3,16,128]{3,2,1,0:T(8,128)} %copy-done.2, ...), custom_call_target="tpu_custom_call", output_to_operand_aliasing={{0}: (2, {})} | custom-call | tf_op jit(solution)/shard_map/pallas_call | solution.py:253
  48.0 1.0 %convolution_bitcast_fusion = f32[32,32]{1,0:T(8,128)S(1)} fusion(s32[16,128]{1,0:T(8,128)S(1)} %get-tuple-element.25, f32[16,128]{1,0:T(8,128)} %get-tuple-element.23, s32[16,128]{1,0:T(8,128)S(1)} %get-tuple-element.24), kind=kOutput, calls=%fused_computation.4 | convolution fusion | flops 25362432 | bytes 28672 | tf_op jit(solution)/shard_map/rza,rzb->ab/dot_general | solution.py:272
  49.0 0.1 mul.23
  49.1 1.0 %fusion.3 = f32[32,32]{1,0:T(8,128)S(1)} fusion(f32[1024]{0:T(1024)S(1)} %eq.79, f32[1024]{0:T(1024)S(1)} %mul.23, s32[1024]{0:T(1024)S(1)} %copy-done.11), kind=kOutput, calls=%fused_computation.8 | convolution fusion | flops 12681216 | bytes 16384 | tf_op jit(solution)/shard_map/po,pk->ok/dot_general | solution.py:281
  50.1 11.5 %all_to_all.9 = f32[32,1,32]{2,1,0:T(1,128)S(1)} all-to-all(f32[32,1,32]{2,1,0:T(1,128)S(1)} %bitcast.15), channel_id=1, replica_groups=mesh['gx'=4,'gy'=4,'gz'=2] {'gx','gy','gz'}, dimensions={0} | all-to-all | bytes 8192 | tf_op jit(solution)/shard_map/all_to_all | solution.py:282
  61.6 0.6 reduce_sum.29
  (1 shorter events, 0.0 us)
Async XLA Ops:
  0.6 9.6 %copy-start.11 = (s32[1024]{0:T(1024)S(1)}, s32[1024]{0:T(1024)}, u32[]{:S(2)}) copy-start(s32[1024]{0:T(1024)} %param.17) | copy-start | bytes 12292
  0.6 10.0 %copy-start.8 = (f32[3,5,5]{2,0,1:T(4,128)S(1)}, f32[3,5,5]{2,0,1:T(4,128)}, u32[]{:S(2)}) copy-start(f32[3,5,5]{2,0,1:T(4,128)} %param.11) | copy-start | bytes 904
  0.7 10.6 %copy-start.9 = (f32[3,5,5]{2,0,1:T(4,128)S(1)}, f32[3,5,5]{2,0,1:T(4,128)}, u32[]{:S(2)}) copy-start(f32[3,5,5]{2,0,1:T(4,128)} %param.12) | copy-start | bytes 904
  3.0 9.9 %collective-permute-start.1 = (f32[5,32,128]{2,1,0:T(8,128)}, f32[5,32,128]{2,1,0:T(8,128)S(1)}, u32[]{:S(2)}, u32[]{:S(2)}) collective-permute-start(f32[5,32,128]{2,1,0:T(8,128)} %get-tuple-element.14), channel_id=1, source_target_pairs={{0,6},{2,0},{4,2},{6,4},{1,7},{3,1},{5,3},{7,5},{8,14},{10,8},{12,... | collective-permute-start | bytes 245768 | tf_op jit(solution)/shard_map/ppermute | solution.py:20
  8.1 3.8 %collective-permute-start = (f32[5,16,128]{2,1,0:T(8,128)}, f32[5,16,128]{2,1,0:T(8,128)S(1)}, u32[]{:S(2)}, u32[]{:S(2)}) collective-permute-start(f32[5,16,128]{2,1,0:T(8,128)} %get-tuple-element.13), channel_id=1, source_target_pairs={{0,24},{8,0},{16,8},{24,16},{1,25},{9,1},{17,9},{25,17},{2,26},{10... | collective-permute-start | bytes 122888 | tf_op jit(solution)/shard_map/ppermute | solution.py:20
  8.7 4.2 %collective-permute-start.2 = (f32[5,16,128]{2,1,0:T(8,128)}, f32[5,16,128]{2,1,0:T(8,128)S(1)}, u32[]{:S(2)}, u32[]{:S(2)}) collective-permute-start(f32[5,16,128]{2,1,0:T(8,128)} %get-tuple-element.15), channel_id=1, source_target_pairs={{0,1},{1,0},{2,3},{3,2},{4,5},{5,4},{6,7},{7,6},{8,9},{9,8},{10,11... | collective-permute-start | bytes 122888 | tf_op jit(solution)/shard_map/ppermute | solution.py:20
  11.9 23.7 %copy-start.10 = (s32[16,128]{1,0:T(8,128)S(1)}, s32[16,128]{1,0:T(8,128)}, u32[]{:S(2)}) copy-start(s32[16,128]{1,0:T(8,128)} %param.14) | copy-start | bytes 24580
  11.9 1.1 %copy-start.6 = (f32[5,16,128]{2,1,0:T(8,128)}, f32[5,16,128]{2,1,0:T(8,128)S(1)}, u32[]{:S(2)}) copy-start(f32[5,16,128]{2,1,0:T(8,128)S(1)} %collective-permute-done.xf_ref) | copy-start | bytes 122884
  12.9 0.6 copy-start.7
  13.5 0.6 %copy-start.3 = (f32[5,32,128]{2,1,0:T(8,128)}, f32[5,32,128]{2,1,0:T(8,128)S(1)}, u32[]{:S(2)}) copy-start(f32[5,32,128]{2,1,0:T(8,128)S(1)} %collective-permute-done.1.yf_ref) | copy-start | bytes 245764
  31.7 12.2 %collective-permute-start.6 = (f32[5,16,8,128]{3,2,1,0:T(8,128)}, f32[5,16,8,128]{3,2,1,0:T(8,128)S(1)}, u32[]{:S(2)}, u32[]{:S(2)}) collective-permute-start(f32[5,16,8,128]{3,2,1,0:T(8,128)} %get-tuple-element.20), channel_id=1, source_target_pairs={{0,2},{2,4},{4,6},{6,0},{1,3},{3,5},{5,7},{7,1},{8,10},{10,12},{12... | collective-permute-start | bytes 983048 | tf_op jit(solution)/shard_map/ppermute | solution.py:20
  31.8 11.9 %collective-permute-start.5 = (f32[5,8,8,128]{3,2,1,0:T(8,128)}, f32[5,8,8,128]{3,2,1,0:T(8,128)S(1)}, u32[]{:S(2)}, u32[]{:S(2)}) collective-permute-start(f32[5,8,8,128]{3,2,1,0:T(8,128)} %get-tuple-element.19), channel_id=1, source_target_pairs={{0,6},{2,0},{4,2},{6,4},{1,7},{3,1},{5,3},{7,5},{8,14},{10,8},{12,... | collective-permute-start | bytes 491528 | tf_op jit(solution)/shard_map/ppermute | solution.py:20
  36.3 6.5 %collective-permute-start.4 = (f32[5,3,16,128]{3,2,1,0:T(8,128)}, f32[5,3,16,128]{3,2,1,0:T(8,128)S(1)}, u32[]{:S(2)}, u32[]{:S(2)}) collective-permute-start(f32[5,3,16,128]{3,2,1,0:T(8,128)} %get-tuple-element.18), channel_id=1, source_target_pairs={{0,8},{8,16},{16,24},{24,0},{1,9},{9,17},{17,25},{25,1},{2,10},{10... | collective-permute-start | bytes 368648 | tf_op jit(solution)/shard_map/ppermute | solution.py:20
  36.3 4.1 %collective-permute-start.3 = (f32[5,2,16,128]{3,2,1,0:T(8,128)}, f32[5,2,16,128]{3,2,1,0:T(8,128)S(1)}, u32[]{:S(2)}, u32[]{:S(2)}) collective-permute-start(f32[5,2,16,128]{3,2,1,0:T(8,128)} %get-tuple-element.17), channel_id=1, source_target_pairs={{0,24},{8,0},{16,8},{24,16},{1,25},{9,1},{17,9},{25,17},{2,26},{10... | collective-permute-start | bytes 245768 | tf_op jit(solution)/shard_map/ppermute | solution.py:20
  38.1 4.7 %collective-permute-start.7 = (f32[2,5,16,128]{3,2,1,0:T(8,128)}, f32[2,5,16,128]{3,2,1,0:T(8,128)S(1)}, u32[]{:S(2)}, u32[]{:S(2)}) collective-permute-start(f32[2,5,16,128]{3,2,1,0:T(8,128)} %get-tuple-element.21), channel_id=1, source_target_pairs={{0,1},{1,0},{2,3},{3,2},{4,5},{5,4},{6,7},{7,6},{8,9},{9,8},{10,11... | collective-permute-start | bytes 245768 | tf_op jit(solution)/shard_map/ppermute | solution.py:20
  40.4 3.5 %copy-start.4 = (f32[5,2,16,128]{3,2,1,0:T(8,128)}, f32[5,2,16,128]{3,2,1,0:T(8,128)S(1)}, u32[]{:S(2)}) copy-start(f32[5,2,16,128]{3,2,1,0:T(8,128)S(1)} %collective-permute-done.3.axl_ref) | copy-start | bytes 245764
  42.7 1.3 %copy-start.5 = (f32[2,5,16,128]{3,2,1,0:T(8,128)}, f32[2,5,16,128]{3,2,1,0:T(8,128)S(1)}, u32[]{:S(2)}) copy-start(f32[2,5,16,128]{3,2,1,0:T(8,128)S(1)} %collective-permute-done.7.az_ref) | copy-start | bytes 245764
  42.7 1.3 %copy-start.2 = (f32[5,3,16,128]{3,2,1,0:T(8,128)}, f32[5,3,16,128]{3,2,1,0:T(8,128)S(1)}, u32[]{:S(2)}) copy-start(f32[5,3,16,128]{3,2,1,0:T(8,128)S(1)} %collective-permute-done.4.axr_ref) | copy-start | bytes 368644
  43.7 0.7 %copy-start.1 = (f32[5,8,8,128]{3,2,1,0:T(8,128)}, f32[5,8,8,128]{3,2,1,0:T(8,128)S(1)}, u32[]{:S(2)}) copy-start(f32[5,8,8,128]{3,2,1,0:T(8,128)S(1)} %collective-permute-done.5.ayl_ref) | copy-start | bytes 491524
  44.0 0.7 %copy-start = (f32[5,16,8,128]{3,2,1,0:T(8,128)}, f32[5,16,8,128]{3,2,1,0:T(8,128)S(1)}, u32[]{:S(2)}) copy-start(f32[5,16,8,128]{3,2,1,0:T(8,128)S(1)} %collective-permute-done.6.ayr_ref) | copy-start | bytes 983044

commit v5 on v4

--- a/solution.py
+++ b/solution.py
@@ -265,20 +265,25 @@
     per = npan // ndev
     nb = 32
     na = npan // nb
-    pa = wall_panel // nb
-    pb = wall_panel % nb
-    oh_a = (pa[..., None] == jnp.arange(na, dtype=jnp.int32)).astype(F32) * wt[..., None]
-    oh_b = (pb[..., None] == jnp.arange(nb, dtype=jnp.int32)).astype(F32)
-    tp = jnp.einsum("rza,rzb->ab", oh_a, oh_b, precision=HI).reshape(npan)
     own_oh = (panel_owner[:, None] == jnp.arange(ndev, dtype=jnp.int32)).astype(F32)
     oh3 = own_oh.reshape(na, nb, ndev)
     below_b = (jnp.arange(nb)[None, :] < jnp.arange(nb)[:, None]).astype(F32)
     below_a = (jnp.arange(na)[None, :] < jnp.arange(na)[:, None]).astype(F32)
     inner = jnp.einsum("bc,acd->abd", below_b, oh3, precision=HI)
     before = jnp.einsum("ac,cd->ad", below_a, jnp.sum(oh3, axis=1), precision=HI)
-    rank = jnp.sum((inner + before[:, None, :]) * oh3, axis=2).reshape(npan)
-    rank_oh = (rank[:, None] == jnp.arange(per, dtype=F32)).astype(F32)
-    t = jnp.einsum("po,pk->ok", own_oh * tp[:, None], rank_oh, precision=HI)
+    rank = jnp.sum((inner + before[:, None, :]) * oh3, axis=2)
+    oh_a = (wall_panel[..., None] // nb == jnp.arange(na, dtype=jnp.int32)).astype(F32)
+    oh_b = (wall_panel[..., None] % nb == jnp.arange(nb, dtype=jnp.int32)).astype(F32)
+
+    def lookup(table):
+        picked = jnp.einsum("rza,ab->rzb", oh_a, table, precision=HI) * oh_b
+        return jnp.round(jnp.sum(picked, axis=2)).astype(jnp.int32)
+
+    cell_own = lookup(panel_owner.reshape(na, nb).astype(F32))
+    cell_rank = lookup(rank)
+    oh_o = (cell_own[..., None] == jnp.arange(ndev, dtype=jnp.int32)).astype(F32)
+    oh_k = (cell_rank[..., None] == jnp.arange(per, dtype=jnp.int32)).astype(F32)
+    t = jnp.einsum("rzo,rzk->ok", oh_o * wt[..., None], oh_k, precision=HI)
     got = lax.all_to_all(t, AXES, 0, 0, tiled=True)
     return section, jnp.sum(got, axis=0)
 

time: 62.7 us -> 61.6 us (0.982)
  blocking collectives: 11.5 us -> 10.7 us
    all_to_all x1, blocking collectives: 11.5 us -> 10.7 us  [on_device(): got = lax.all_to_all(t, AXES, 0, 0, tiled=True)]
    dot_general x2 -> x3, matrix products: 2.02 us -> 1.66 us  [the longest x1 0.99 us: on_device(): t = jnp.einsum('rzo,rzk->ok', oh_o * wt[..., None], oh_k, precision=HI)]
  transfers between devices with their start and end apart: 8 -> 8, of which waited for: 5 -> 4; matrix products, arithmetic and copies ran while one was open for 3% -> 4% of each run, Pallas kernels for 0% -> 0%
where the time goes in v5:
time: 61.6 us; the launch traced here: 61.1 us
  Pallas kernels  23.2 us (38%)
  starting transfers between devices  14.4 us (23%)
  blocking collectives  10.7 us (17%)
  waiting for transfers between devices  5.2 us (8%)
  local copies, waits for them, and re-layouts  3.31 us (5%)
  matrix products  2.08 us (3%)
  between operations  1.43 us (2%)
  other arithmetic  0.79 us (1%)
    pallas_call x1, Pallas kernels, on_device(): pl.pallas_call(stencil_kernel, grid=(nx // XC,), out_shape=(jax.ShapeDtyp...  17.5 us
    ppermute x8, starting transfers between devices, shift_from(): return lax.ppermute(x, axis, [(i, (i + by) % n) for i in range(n)])  14.4 us
    all_to_all x1, blocking collectives, on_device(): got = lax.all_to_all(t, AXES, 0, 0, tiled=True)  10.7 us
    ppermute x8, waiting for transfers between devices, shift_from(): return lax.ppermute(x, axis, [(i, (i + by) % n) for i in range(n)])  5.2 us
    pallas_call x1, Pallas kernels, on_device(): pl.pallas_call(fix_kernel, out_shape=(jax.ShapeDtypeStruct((nf, nx, ny, n...  3.37 us
    unnamed x26, local copies, waits for them, and re-layouts  3.24 us
    pallas_call x1, Pallas kernels, on_device(): pl.pallas_call(fronts_kernel, out_shape=(jax.ShapeDtypeStruct((nf, ny, nz...  2.35 us
  transfers between devices with their start and end apart: 8, of which 4 were waited for; matrix products, arithmetic and copies ran while one was open for 4% of the time, Pallas kernels for 0%

profile of v5, /device:TPU:0, one launch (start us, length us, event | category | flops | bytes accessed | tf_op | source)
XLA Modules:
  0.0 61.1 jit_solution(506864570969638722)
XLA Ops:
  0.6 0.0 copy-start.11
  0.6 0.0 copy-start.10
  0.7 0.0 copy-start.8
  0.7 0.0 copy-start.9
  0.7 2.4 %shard_map.104 = (f32[5,16,128]{2,1,0:T(8,128)}, f32[5,32,128]{2,1,0:T(8,128)}, f32[5,16,128]{2,1,0:T(8,128)}) custom-call(f32[5,32,16,128]{3,2,1,0:T(8,128)} %adj_ref.3), custom_call_target="tpu_custom_call" | custom-call | tf_op jit(solution)/shard_map/pallas_call | solution.py:198
  3.0 5.0 %collective-permute-start.1 = (f32[5,32,128]{2,1,0:T(8,128)}, f32[5,32,128]{2,1,0:T(8,128)S(1)}, u32[]{:S(2)}, u32[]{:S(2)}) collective-permute-start(f32[5,32,128]{2,1,0:T(8,128)} %get-tuple-element.14), channel_id=1, source_target_pairs={{0,6},{2,0},{4,2},{6,4},{1,7},{3,1},{5,3},{7,5},{8,14},{10,8},{12,... | collective-permute-start | bytes 245768 | tf_op jit(solution)/shard_map/ppermute | solution.py:20
  8.1 0.7 %collective-permute-start = (f32[5,16,128]{2,1,0:T(8,128)}, f32[5,16,128]{2,1,0:T(8,128)S(1)}, u32[]{:S(2)}, u32[]{:S(2)}) collective-permute-start(f32[5,16,128]{2,1,0:T(8,128)} %get-tuple-element.13), channel_id=1, source_target_pairs={{0,24},{8,0},{16,8},{24,16},{1,25},{9,1},{17,9},{25,17},{2,26},{10... | collective-permute-start | bytes 122888 | tf_op jit(solution)/shard_map/ppermute | solution.py:20
  8.7 1.5 %collective-permute-start.2 = (f32[5,16,128]{2,1,0:T(8,128)}, f32[5,16,128]{2,1,0:T(8,128)S(1)}, u32[]{:S(2)}, u32[]{:S(2)}) collective-permute-start(f32[5,16,128]{2,1,0:T(8,128)} %get-tuple-element.15), channel_id=1, source_target_pairs={{0,1},{1,0},{2,3},{3,2},{4,5},{5,4},{6,7},{7,6},{8,9},{9,8},{10,11... | collective-permute-start | bytes 122888 | tf_op jit(solution)/shard_map/ppermute | solution.py:20
  10.2 0.0 copy-done.11
  10.2 0.1 reshape.62
  10.3 0.2 convert_reduce_fusion
  10.5 0.1 fusion.16
  10.7 0.3 fusion.2
  11.0 0.0 copy-done.10
  11.0 0.3 fusion.3
  11.3 0.0 copy-done.8
  11.3 0.6 copy.24.fp_ref
  11.9 0.0 copy-done.9
  11.9 0.6 copy.25.fm_ref
  12.5 0.0 collective-permute-done.xf_ref
  12.5 0.0 copy-start.6
  12.5 0.4 collective-permute-done.2.zf_ref
  12.9 0.0 copy-start.7
  12.9 0.0 collective-permute-done.1.yf_ref
  12.9 0.2 copy-done.6
  13.2 0.4 copy-done.7
  13.5 0.0 copy-start.3
  13.5 0.6 %copy-done.3 = f32[5,32,128]{2,1,0:T(8,128)} copy-done((f32[5,32,128]{2,1,0:T(8,128)}, f32[5,32,128]{2,1,0:T(8,128)S(1)}, u32[]{:S(2)}) %copy-start.3) | copy-done | bytes 81944
  14.2 17.5 %shard_map.105 = (f32[5,32,16,128]{3,2,1,0:T(8,128)}, f32[5,2,16,128]{3,2,1,0:T(8,128)}, f32[5,3,16,128]{3,2,1,0:T(8,128)}, f32[5,8,8,128]{3,2,1,0:T(8,128)}, f3...) custom-call(f32[3,5,5]{2,1,0:T(8,128)} %copy.24.fp_ref, f32[3,5,5]{2,1,0:T(8,128)} %copy.25.fm_ref, ...), custom_call_target="tpu_custom_call" | custom-call | tf_op jit(solution)/shard_map/pallas_call | solution.py:213
  31.7 0.1 collective-permute-start.6
  31.8 0.3 fusion.4
  32.1 3.9 %collective-permute-start.5 = (f32[5,8,8,128]{3,2,1,0:T(8,128)}, f32[5,8,8,128]{3,2,1,0:T(8,128)S(1)}, u32[]{:S(2)}, u32[]{:S(2)}) collective-permute-start(f32[5,8,8,128]{3,2,1,0:T(8,128)} %get-tuple-element.19), channel_id=1, source_target_pairs={{0,6},{2,0},{4,2},{6,4},{1,7},{3,1},{5,3},{7,5},{8,14},{10,8},{12,... | collective-permute-start | bytes 491528 | tf_op jit(solution)/shard_map/ppermute | solution.py:20
  36.0 0.0 collective-permute-start.4
  36.0 1.7 %collective-permute-start.3 = (f32[5,2,16,128]{3,2,1,0:T(8,128)}, f32[5,2,16,128]{3,2,1,0:T(8,128)S(1)}, u32[]{:S(2)}, u32[]{:S(2)}) collective-permute-start(f32[5,2,16,128]{3,2,1,0:T(8,128)} %get-tuple-element.17), channel_id=1, source_target_pairs={{0,24},{8,0},{16,8},{24,16},{1,25},{9,1},{17,9},{25,17},{2,26},{10... | collective-permute-start | bytes 245768 | tf_op jit(solution)/shard_map/ppermute | solution.py:20
  37.7 1.5 %collective-permute-start.7 = (f32[2,5,16,128]{3,2,1,0:T(8,128)}, f32[2,5,16,128]{3,2,1,0:T(8,128)S(1)}, u32[]{:S(2)}, u32[]{:S(2)}) collective-permute-start(f32[2,5,16,128]{3,2,1,0:T(8,128)} %get-tuple-element.21), channel_id=1, source_target_pairs={{0,1},{1,0},{2,3},{3,2},{4,5},{5,4},{6,7},{7,6},{8,9},{9,8},{10,11... | collective-permute-start | bytes 245768 | tf_op jit(solution)/shard_map/ppermute | solution.py:20
  39.9 0.2 collective-permute-done.3.axl_ref
  40.1 0.0 copy-start.4
  40.1 2.3 %collective-permute-done.7.az_ref = f32[2,5,16,128]{3,2,1,0:T(8,128)S(1)} collective-permute-done((f32[2,5,16,128]{3,2,1,0:T(8,128)}, f32[2,5,16,128]{3,2,1,0:T(8,128)S(1)}, u32[]{:S(2)}, u32[]{:S(2)}) %collective-permute-start.7) | collective-permute-done | bytes 81952 | tf_op jit(solution)/shard_map/ppermute | solution.py:20
  42.4 0.0 copy-start.5
  42.4 0.0 collective-permute-done.4.axr_ref
  42.4 0.0 copy-start.2
  42.4 2.3 %collective-permute-done.5.ayl_ref = f32[5,8,8,128]{3,2,1,0:T(8,128)S(1)} collective-permute-done((f32[5,8,8,128]{3,2,1,0:T(8,128)}, f32[5,8,8,128]{3,2,1,0:T(8,128)S(1)}, u32[]{:S(2)}, u32[]{:S(2)}) %collective-permute-start.5) | collective-permute-done | bytes 163872 | tf_op jit(solution)/shard_map/ppermute | solution.py:20
  44.7 0.0 copy-start.1
  44.7 0.0 collective-permute-done.6.ayr_ref
  44.7 0.0 copy-start
  44.7 0.0 copy-done.4
  44.7 0.0 copy-done.5
  44.8 0.0 copy-done.2
  44.8 0.6 %copy-done.1 = f32[5,8,8,128]{3,2,1,0:T(8,128)} copy-done((f32[5,8,8,128]{3,2,1,0:T(8,128)}, f32[5,8,8,128]{3,2,1,0:T(8,128)S(1)}, u32[]{:S(2)}) %copy-start.1) | copy-done | bytes 163864
  45.4 0.1 copy-done
  45.5 3.4 %shard_map.106 = (f32[5,32,16,128]{3,2,1,0:T(8,128)}, f32[16,128]{1,0:T(8,128)}) custom-call(s32[16]{0:T(128)} %row_ref.1, s32[1]{0:T(128)S(6)} %copy.38.cnt_ref, f32[5,32,16,128]{3,2,1,0:T(8,128)} %get-tuple-element.16.sec_ref, f32[5,2,16,128]{3,2,1,0:T(8,128)} %copy-done.4, f32[5,3,16,128]{3,2,1,0:T(8,128)} %copy-done.2, ...), custom_call_target="tpu_custom_call", output_to_operand_aliasing={{0}: (2, {})} | custom-call | tf_op jit(solution)/shard_map/pallas_call | solution.py:253
  48.9 1.0 %fusion.6 = f32[32,32,1]{1,0,2:T(8,128)S(1)} fusion(s32[16,128]{1,0:T(8,128)S(1)} %get-tuple-element.26, f32[16,128]{1,0:T(8,128)} %get-tuple-element.23, s32[16,128]{1,0:T(8,128)S(1)} %get-tuple-element.27), kind=kOutput, calls=%fused_computation.12 | convolution fusion | flops 25362432 | bytes 28672 | tf_op jit(solution)/shard_map/rzo,rzk->ok/dot_general | solution.py:286
  49.9 10.7 %all_to_all.9 = f32[32,1,32]{2,1,0:T(1,128)S(1)} all-to-all(f32[32,1,32]{2,1,0:T(1,128)S(1)} %bitcast.20), channel_id=1, replica_groups=mesh['gx'=4,'gy'=4,'gz'=2] {'gx','gy','gz'}, dimensions={0} | all-to-all | bytes 8192 | tf_op jit(solution)/shard_map/all_to_all | solution.py:287
  60.6 0.6 reduce_sum.49
  (2 shorter events, 0.0 us)
Async XLA Ops:
  0.6 9.6 %copy-start.11 = (s32[1024]{0:T(1024)S(1)}, s32[1024]{0:T(1024)}, u32[]{:S(2)}) copy-start(s32[1024]{0:T(1024)} %param.17) | copy-start | bytes 12292
  0.6 10.3 %copy-start.10 = (s32[16,128]{1,0:T(8,128)S(1)}, s32[16,128]{1,0:T(8,128)}, u32[]{:S(2)}) copy-start(s32[16,128]{1,0:T(8,128)} %param.14) | copy-start | bytes 24580
  0.7 10.7 %copy-start.8 = (f32[3,5,5]{2,0,1:T(4,128)S(1)}, f32[3,5,5]{2,0,1:T(4,128)}, u32[]{:S(2)}) copy-start(f32[3,5,5]{2,0,1:T(4,128)} %param.11) | copy-start | bytes 904
  0.7 11.3 %copy-start.9 = (f32[3,5,5]{2,0,1:T(4,128)S(1)}, f32[3,5,5]{2,0,1:T(4,128)}, u32[]{:S(2)}) copy-start(f32[3,5,5]{2,0,1:T(4,128)} %param.12) | copy-start | bytes 904
  3.0 9.9 %collective-permute-start.1 = (f32[5,32,128]{2,1,0:T(8,128)}, f32[5,32,128]{2,1,0:T(8,128)S(1)}, u32[]{:S(2)}, u32[]{:S(2)}) collective-permute-start(f32[5,32,128]{2,1,0:T(8,128)} %get-tuple-element.14), channel_id=1, source_target_pairs={{0,6},{2,0},{4,2},{6,4},{1,7},{3,1},{5,3},{7,5},{8,14},{10,8},{12,... | collective-permute-start | bytes 245768 | tf_op jit(solution)/shard_map/ppermute | solution.py:20
  8.1 4.5 %collective-permute-start = (f32[5,16,128]{2,1,0:T(8,128)}, f32[5,16,128]{2,1,0:T(8,128)S(1)}, u32[]{:S(2)}, u32[]{:S(2)}) collective-permute-start(f32[5,16,128]{2,1,0:T(8,128)} %get-tuple-element.13), channel_id=1, source_target_pairs={{0,24},{8,0},{16,8},{24,16},{1,25},{9,1},{17,9},{25,17},{2,26},{10... | collective-permute-start | bytes 122888 | tf_op jit(solution)/shard_map/ppermute | solution.py:20
  8.7 4.2 %collective-permute-start.2 = (f32[5,16,128]{2,1,0:T(8,128)}, f32[5,16,128]{2,1,0:T(8,128)S(1)}, u32[]{:S(2)}, u32[]{:S(2)}) collective-permute-start(f32[5,16,128]{2,1,0:T(8,128)} %get-tuple-element.15), channel_id=1, source_target_pairs={{0,1},{1,0},{2,3},{3,2},{4,5},{5,4},{6,7},{7,6},{8,9},{9,8},{10,11... | collective-permute-start | bytes 122888 | tf_op jit(solution)/shard_map/ppermute | solution.py:20
  12.5 0.6 %copy-start.6 = (f32[5,16,128]{2,1,0:T(8,128)}, f32[5,16,128]{2,1,0:T(8,128)S(1)}, u32[]{:S(2)}) copy-start(f32[5,16,128]{2,1,0:T(8,128)S(1)} %collective-permute-done.xf_ref) | copy-start | bytes 122884
  12.9 0.6 copy-start.7
  13.5 0.7 %copy-start.3 = (f32[5,32,128]{2,1,0:T(8,128)}, f32[5,32,128]{2,1,0:T(8,128)S(1)}, u32[]{:S(2)}) copy-start(f32[5,32,128]{2,1,0:T(8,128)S(1)} %collective-permute-done.1.yf_ref) | copy-start | bytes 245764
  31.7 13.0 %collective-permute-start.6 = (f32[5,16,8,128]{3,2,1,0:T(8,128)}, f32[5,16,8,128]{3,2,1,0:T(8,128)S(1)}, u32[]{:S(2)}, u32[]{:S(2)}) collective-permute-start(f32[5,16,8,128]{3,2,1,0:T(8,128)} %get-tuple-element.20), channel_id=1, source_target_pairs={{0,2},{2,4},{4,6},{6,0},{1,3},{3,5},{5,7},{7,1},{8,10},{10,12},{12... | collective-permute-start | bytes 983048 | tf_op jit(solution)/shard_map/ppermute | solution.py:20
  32.1 12.6 %collective-permute-start.5 = (f32[5,8,8,128]{3,2,1,0:T(8,128)}, f32[5,8,8,128]{3,2,1,0:T(8,128)S(1)}, u32[]{:S(2)}, u32[]{:S(2)}) collective-permute-start(f32[5,8,8,128]{3,2,1,0:T(8,128)} %get-tuple-element.19), channel_id=1, source_target_pairs={{0,6},{2,0},{4,2},{6,4},{1,7},{3,1},{5,3},{7,5},{8,14},{10,8},{12,... | collective-permute-start | bytes 491528 | tf_op jit(solution)/shard_map/ppermute | solution.py:20
  36.0 6.4 %collective-permute-start.4 = (f32[5,3,16,128]{3,2,1,0:T(8,128)}, f32[5,3,16,128]{3,2,1,0:T(8,128)S(1)}, u32[]{:S(2)}, u32[]{:S(2)}) collective-permute-start(f32[5,3,16,128]{3,2,1,0:T(8,128)} %get-tuple-element.18), channel_id=1, source_target_pairs={{0,8},{8,16},{16,24},{24,0},{1,9},{9,17},{17,25},{25,1},{2,10},{10... | collective-permute-start | bytes 368648 | tf_op jit(solution)/shard_map/ppermute | solution.py:20
  36.0 4.1 %collective-permute-start.3 = (f32[5,2,16,128]{3,2,1,0:T(8,128)}, f32[5,2,16,128]{3,2,1,0:T(8,128)S(1)}, u32[]{:S(2)}, u32[]{:S(2)}) collective-permute-start(f32[5,2,16,128]{3,2,1,0:T(8,128)} %get-tuple-element.17), channel_id=1, source_target_pairs={{0,24},{8,0},{16,8},{24,16},{1,25},{9,1},{17,9},{25,17},{2,26},{10... | collective-permute-start | bytes 245768 | tf_op jit(solution)/shard_map/ppermute | solution.py:20
  37.7 4.7 %collective-permute-start.7 = (f32[2,5,16,128]{3,2,1,0:T(8,128)}, f32[2,5,16,128]{3,2,1,0:T(8,128)S(1)}, u32[]{:S(2)}, u32[]{:S(2)}) collective-permute-start(f32[2,5,16,128]{3,2,1,0:T(8,128)} %get-tuple-element.21), channel_id=1, source_target_pairs={{0,1},{1,0},{2,3},{3,2},{4,5},{5,4},{6,7},{7,6},{8,9},{9,8},{10,11... | collective-permute-start | bytes 245768 | tf_op jit(solution)/shard_map/ppermute | solution.py:20
  40.1 4.6 %copy-start.4 = (f32[5,2,16,128]{3,2,1,0:T(8,128)}, f32[5,2,16,128]{3,2,1,0:T(8,128)S(1)}, u32[]{:S(2)}) copy-start(f32[5,2,16,128]{3,2,1,0:T(8,128)S(1)} %collective-permute-done.3.axl_ref) | copy-start | bytes 245764
  42.4 2.4 %copy-start.5 = (f32[2,5,16,128]{3,2,1,0:T(8,128)}, f32[2,5,16,128]{3,2,1,0:T(8,128)S(1)}, u32[]{:S(2)}) copy-start(f32[2,5,16,128]{3,2,1,0:T(8,128)S(1)} %collective-permute-done.7.az_ref) | copy-start | bytes 245764
  42.4 2.4 %copy-start.2 = (f32[5,3,16,128]{3,2,1,0:T(8,128)}, f32[5,3,16,128]{3,2,1,0:T(8,128)S(1)}, u32[]{:S(2)}) copy-start(f32[5,3,16,128]{3,2,1,0:T(8,128)S(1)} %collective-permute-done.4.axr_ref) | copy-start | bytes 368644
  44.7 0.7 %copy-start.1 = (f32[5,8,8,128]{3,2,1,0:T(8,128)}, f32[5,8,8,128]{3,2,1,0:T(8,128)S(1)}, u32[]{:S(2)}) copy-start(f32[5,8,8,128]{3,2,1,0:T(8,128)S(1)} %collective-permute-done.5.ayl_ref) | copy-start | bytes 491524
  44.7 0.8 %copy-start = (f32[5,16,8,128]{3,2,1,0:T(8,128)}, f32[5,16,8,128]{3,2,1,0:T(8,128)S(1)}, u32[]{:S(2)}) copy-start(f32[5,16,8,128]{3,2,1,0:T(8,128)S(1)} %collective-permute-done.6.ayr_ref) | copy-start | bytes 983044

commit v6 on v5

--- a/solution.py
+++ b/solution.py
@@ -13,6 +13,7 @@
 HI = lax.Precision.HIGHEST
 VMEM = pl.BlockSpec(memory_space=pltpu.VMEM)
 SMEM = pl.BlockSpec(memory_space=pltpu.SMEM)
+ANY = pl.BlockSpec(memory_space=pl.ANY)
 
 
 def shift_from(x, axis, by):
@@ -27,7 +28,8 @@
     )
 
 
-def fronts_kernel(adj_ref, xf_ref, yf_ref, zf_ref):
+def fronts_kernel(adj_ref, ysl_ref, xf_ref, zf_ref):
+    del ysl_ref
     nf, nx, ny, nz = adj_ref.shape
     row, lane = iotas(ny, nz)
     for f in range(nf):
@@ -35,7 +37,6 @@
         zacc = jnp.zeros((ny, nz), F32)
         for x in range(nx):
             s = adj_ref[f, x]
-            yf_ref[f, pl.ds(x, 1), :] = s[0:1, :]
             zacc = zacc + pltpu.roll(jnp.where(lane == 0, s, 0.0), x, 1)
         zf_ref[f] = zacc
 
@@ -195,18 +196,18 @@
               wall_count, panel_owner):
     nf, nx, ny, nz = adjoint.shape
     assert nx % XC == 0 and XC % 4 == 0 and ny == 16 and nx * 4 <= nz
-    xf, yf, zf = pl.pallas_call(
+    ysl = adjoint[:, :, 0, :]
+    yf = shift_from(ysl, "gy", -1)
+    xf, zf = pl.pallas_call(
         fronts_kernel,
         out_shape=(
             jax.ShapeDtypeStruct((nf, ny, nz), F32),
-            jax.ShapeDtypeStruct((nf, nx, nz), F32),
             jax.ShapeDtypeStruct((nf, ny, nz), F32),
         ),
-        in_specs=[VMEM],
-        out_specs=(VMEM, VMEM, VMEM),
-    )(adjoint)
+        in_specs=[VMEM, ANY],
+        out_specs=(VMEM, VMEM),
+    )(adjoint, ysl)
     xf = shift_from(xf, "gx", -1)
-    yf = shift_from(yf, "gy", -1)
     zf = shift_from(zf, "gz", -1)
     const4 = lambda i: (0, 0, 0, 0)
     const3 = lambda i: (0, 0, 0)

time: 61.6 us -> 62.8 us (1.019)
  local copies, waits for them, and re-layouts: 3.31 us -> 4.44 us
    slice x0 -> x1, local copies, waits for them, and re-layouts: none -> 1.14 us  [on_device(): ysl = adjoint[:, :, 0, :]]
    unnamed x26 -> x28, local copies, waits for them, and re-layouts: 3.24 us -> 3.23 us
  transfers between devices with their start and end apart: 8 -> 8, of which waited for: 4 -> 4; matrix products, arithmetic and copies ran while one was open for 4% -> 4% of each run, Pallas kernels for 0% -> 4%
where the time goes in v6:
time: 62.8 us; the launch traced here: 62.3 us
  Pallas kernels  23.2 us (37%)
  starting transfers between devices  14.5 us (23%)
  blocking collectives  10.7 us (17%)
  waiting for transfers between devices  5.21 us (8%)
  local copies, waits for them, and re-layouts  4.44 us (7%)
  matrix products  2.07 us (3%)
  between operations  1.44 us (2%)
  other arithmetic  0.79 us (1%)
    pallas_call x1, Pallas kernels, on_device(): pl.pallas_call(stencil_kernel, grid=(nx // XC,), out_shape=(jax.ShapeDtyp...  17.5 us
    ppermute x8, starting transfers between devices, shift_from(): return lax.ppermute(x, axis, [(i, (i + by) % n) for i in range(n)])  14.5 us
    all_to_all x1, blocking collectives, on_device(): got = lax.all_to_all(t, AXES, 0, 0, tiled=True)  10.7 us
    ppermute x8, waiting for transfers between devices, shift_from(): return lax.ppermute(x, axis, [(i, (i + by) % n) for i in range(n)])  5.21 us
    pallas_call x1, Pallas kernels, on_device(): pl.pallas_call(fix_kernel, out_shape=(jax.ShapeDtypeStruct((nf, nx, ny, n...  3.37 us
    unnamed x28, local copies, waits for them, and re-layouts  3.23 us
    pallas_call x1, Pallas kernels, on_device(): pl.pallas_call(fronts_kernel, out_shape=(jax.ShapeDtypeStruct((nf, ny, nz...  2.33 us
  transfers between devices with their start and end apart: 8, of which 4 were waited for; matrix products, arithmetic and copies ran while one was open for 4% of the time, Pallas kernels for 4%

profile of v6, /device:TPU:0, one launch (start us, length us, event | category | flops | bytes accessed | tf_op | source)
XLA Modules:
  0.0 62.3 jit_solution(15253305761336221168)
XLA Ops:
  0.6 0.0 copy-start.12
  0.6 0.0 copy-start.11
  0.6 1.1 %slice.3 = f32[5,32,1,128]{3,2,1,0:T(1,128)S(1)} slice(f32[5,32,16,128]{3,2,1,0:T(8,128)} %adj_ref.3), slice={[0:5], [0:32], [0:1], [0:128]} | slice | bytes 163840 | tf_op jit(solution)/shard_map/slice | solution.py:199
  1.8 0.0 copy-start
  1.8 0.0 copy-start.9
  1.8 0.0 copy-start.10
  1.8 5.1 %collective-permute-start.1 = (f32[5,32,128]{2,1,0:T(8,128)S(1)}, f32[5,32,128]{2,1,0:T(8,128)S(1)}, u32[]{:S(2)}, u32[]{:S(2)}) collective-permute-start(f32[5,32,128]{2,1,0:T(8,128)S(1)} %bitcast.23), channel_id=1, source_target_pairs={{0,6},{2,0},{4,2},{6,4},{1,7},{3,1},{5,3},{7,5},{8,14},{10,8},{12,... | collective-permute-start | bytes 245768 | tf_op jit(solution)/shard_map/ppermute | solution.py:21
  6.9 0.0 copy-done
  6.9 2.3 %shard_map.104 = (f32[5,16,128]{2,1,0:T(8,128)}, f32[5,16,128]{2,1,0:T(8,128)}) custom-call(f32[5,32,16,128]{3,2,1,0:T(8,128)} %adj_ref.3, f32[5,32,128]{2,1,0:T(8,128)} %bitcast.24), custom_call_target="tpu_custom_call" | custom-call | tf_op jit(solution)/shard_map/pallas_call | solution.py:201
  9.3 0.7 %collective-permute-start = (f32[5,16,128]{2,1,0:T(8,128)}, f32[5,16,128]{2,1,0:T(8,128)S(1)}, u32[]{:S(2)}, u32[]{:S(2)}) collective-permute-start(f32[5,16,128]{2,1,0:T(8,128)} %get-tuple-element.12), channel_id=1, source_target_pairs={{0,24},{8,0},{16,8},{24,16},{1,25},{9,1},{17,9},{25,17},{2,26},{10... | collective-permute-start | bytes 122888 | tf_op jit(solution)/shard_map/ppermute | solution.py:21
  9.9 1.5 %collective-permute-start.2 = (f32[5,16,128]{2,1,0:T(8,128)}, f32[5,16,128]{2,1,0:T(8,128)S(1)}, u32[]{:S(2)}, u32[]{:S(2)}) collective-permute-start(f32[5,16,128]{2,1,0:T(8,128)} %get-tuple-element.13), channel_id=1, source_target_pairs={{0,1},{1,0},{2,3},{3,2},{4,5},{5,4},{6,7},{7,6},{8,9},{9,8},{10,11... | collective-permute-start | bytes 122888 | tf_op jit(solution)/shard_map/ppermute | solution.py:21
  11.4 0.0 copy-done.12
  11.4 0.1 reshape.62
  11.5 0.2 convert_reduce_fusion
  11.7 0.1 fusion.16
  11.9 0.3 fusion.2
  12.2 0.0 copy-done.11
  12.2 0.3 fusion.3
  12.5 0.0 copy-done.9
  12.5 0.6 copy.28.fp_ref
  13.1 0.0 copy-done.10
  13.1 0.6 copy.29.fm_ref
  13.7 0.0 collective-permute-done.xf_ref
  13.7 0.0 copy-start.7
  13.7 0.4 collective-permute-done.2.zf_ref
  14.1 0.0 copy-start.8
  14.1 0.0 collective-permute-done.1.yf_ref
  14.1 0.2 copy-done.7
  14.3 0.4 copy-done.8
  14.7 0.0 copy-start.4
  14.7 0.6 %copy-done.4 = f32[5,32,128]{2,1,0:T(8,128)} copy-done((f32[5,32,128]{2,1,0:T(8,128)}, f32[5,32,128]{2,1,0:T(8,128)S(1)}, u32[]{:S(2)}) %copy-start.4) | copy-done | bytes 81944
  15.4 17.5 %shard_map.105 = (f32[5,32,16,128]{3,2,1,0:T(8,128)}, f32[5,2,16,128]{3,2,1,0:T(8,128)}, f32[5,3,16,128]{3,2,1,0:T(8,128)}, f32[5,8,8,128]{3,2,1,0:T(8,128)}, f3...) custom-call(f32[3,5,5]{2,1,0:T(8,128)} %copy.28.fp_ref, f32[3,5,5]{2,1,0:T(8,128)} %copy.29.fm_ref, ...), custom_call_target="tpu_custom_call" | custom-call | tf_op jit(solution)/shard_map/pallas_call | solution.py:214
  32.9 0.1 collective-permute-start.6
  33.0 0.3 fusion.4
  33.3 3.9 %collective-permute-start.5 = (f32[5,8,8,128]{3,2,1,0:T(8,128)}, f32[5,8,8,128]{3,2,1,0:T(8,128)S(1)}, u32[]{:S(2)}, u32[]{:S(2)}) collective-permute-start(f32[5,8,8,128]{3,2,1,0:T(8,128)} %get-tuple-element.17), channel_id=1, source_target_pairs={{0,6},{2,0},{4,2},{6,4},{1,7},{3,1},{5,3},{7,5},{8,14},{10,8},{12,... | collective-permute-start | bytes 491528 | tf_op jit(solution)/shard_map/ppermute | solution.py:21
  37.2 0.0 collective-permute-start.4
  37.2 1.7 %collective-permute-start.3 = (f32[5,2,16,128]{3,2,1,0:T(8,128)}, f32[5,2,16,128]{3,2,1,0:T(8,128)S(1)}, u32[]{:S(2)}, u32[]{:S(2)}) collective-permute-start(f32[5,2,16,128]{3,2,1,0:T(8,128)} %get-tuple-element.15), channel_id=1, source_target_pairs={{0,24},{8,0},{16,8},{24,16},{1,25},{9,1},{17,9},{25,17},{2,26},{10... | collective-permute-start | bytes 245768 | tf_op jit(solution)/shard_map/ppermute | solution.py:21
  38.9 1.5 %collective-permute-start.7 = (f32[2,5,16,128]{3,2,1,0:T(8,128)}, f32[2,5,16,128]{3,2,1,0:T(8,128)S(1)}, u32[]{:S(2)}, u32[]{:S(2)}) collective-permute-start(f32[2,5,16,128]{3,2,1,0:T(8,128)} %get-tuple-element.19), channel_id=1, source_target_pairs={{0,1},{1,0},{2,3},{3,2},{4,5},{5,4},{6,7},{7,6},{8,9},{9,8},{10,11... | collective-permute-start | bytes 245768 | tf_op jit(solution)/shard_map/ppermute | solution.py:21
  41.1 0.2 collective-permute-done.3.axl_ref
  41.3 0.0 copy-start.5
  41.3 2.3 %collective-permute-done.7.az_ref = f32[2,5,16,128]{3,2,1,0:T(8,128)S(1)} collective-permute-done((f32[2,5,16,128]{3,2,1,0:T(8,128)}, f32[2,5,16,128]{3,2,1,0:T(8,128)S(1)}, u32[]{:S(2)}, u32[]{:S(2)}) %collective-permute-start.7) | collective-permute-done | bytes 81952 | tf_op jit(solution)/shard_map/ppermute | solution.py:21
  43.6 0.0 copy-start.6
  43.6 0.0 collective-permute-done.4.axr_ref
  43.6 0.0 copy-start.3
  43.6 2.3 %collective-permute-done.5.ayl_ref = f32[5,8,8,128]{3,2,1,0:T(8,128)S(1)} collective-permute-done((f32[5,8,8,128]{3,2,1,0:T(8,128)}, f32[5,8,8,128]{3,2,1,0:T(8,128)S(1)}, u32[]{:S(2)}, u32[]{:S(2)}) %collective-permute-start.5) | collective-permute-done | bytes 163872 | tf_op jit(solution)/shard_map/ppermute | solution.py:21
  45.9 0.0 copy-start.2
  45.9 0.0 collective-permute-done.6.ayr_ref
  45.9 0.0 copy-start.1
  45.9 0.0 copy-done.5
  45.9 0.0 copy-done.6
  45.9 0.0 copy-done.3
  45.9 0.6 %copy-done.2 = f32[5,8,8,128]{3,2,1,0:T(8,128)} copy-done((f32[5,8,8,128]{3,2,1,0:T(8,128)}, f32[5,8,8,128]{3,2,1,0:T(8,128)S(1)}, u32[]{:S(2)}) %copy-start.2) | copy-done | bytes 163864
  46.6 0.1 copy-done.1
  46.7 3.4 %shard_map.106 = (f32[5,32,16,128]{3,2,1,0:T(8,128)}, f32[16,128]{1,0:T(8,128)}) custom-call(s32[16]{0:T(128)} %row_ref.1, s32[1]{0:T(128)S(6)} %copy.43.cnt_ref, f32[5,32,16,128]{3,2,1,0:T(8,128)} %get-tuple-element.14.sec_ref, f32[5,2,16,128]{3,2,1,0:T(8,128)} %copy-done.5, f32[5,3,16,128]{3,2,1,0:T(8,128)} %copy-done.3, ...), custom_call_target="tpu_custom_call", output_to_operand_aliasing={{0}: (2, {})} | custom-call | tf_op jit(solution)/shard_map/pallas_call | solution.py:254
  50.1 1.0 %fusion.6 = f32[32,32,1]{1,0,2:T(8,128)S(1)} fusion(s32[16,128]{1,0:T(8,128)S(1)} %get-tuple-element.24, f32[16,128]{1,0:T(8,128)} %get-tuple-element.21, s32[16,128]{1,0:T(8,128)S(1)} %get-tuple-element.25), kind=kOutput, calls=%fused_computation.12 | convolution fusion | flops 25362432 | bytes 28672 | tf_op jit(solution)/shard_map/rzo,rzk->ok/dot_general | solution.py:287
  51.1 10.7 %all_to_all.9 = f32[32,1,32]{2,1,0:T(1,128)S(1)} all-to-all(f32[32,1,32]{2,1,0:T(1,128)S(1)} %bitcast.25), channel_id=1, replica_groups=mesh['gx'=4,'gy'=4,'gz'=2] {'gx','gy','gz'}, dimensions={0} | all-to-all | bytes 8192 | tf_op jit(solution)/shard_map/all_to_all | solution.py:288
  61.7 0.6 reduce_sum.49
  (2 shorter events, 0.0 us)
Async XLA Ops:
  0.6 10.8 %copy-start.12 = (s32[1024]{0:T(1024)S(1)}, s32[1024]{0:T(1024)}, u32[]{:S(2)}) copy-start(s32[1024]{0:T(1024)} %param.17) | copy-start | bytes 12292
  0.6 11.5 %copy-start.11 = (s32[16,128]{1,0:T(8,128)S(1)}, s32[16,128]{1,0:T(8,128)}, u32[]{:S(2)}) copy-start(s32[16,128]{1,0:T(8,128)} %param.14) | copy-start | bytes 24580
  1.8 5.1 %copy-start = (f32[5,32,1,128]{3,2,1,0:T(1,128)}, f32[5,32,1,128]{3,2,1,0:T(1,128)S(1)}, u32[]{:S(2)}) copy-start(f32[5,32,1,128]{3,2,1,0:T(1,128)S(1)} %slice.3) | copy-start | bytes 245764
  1.8 10.7 %copy-start.9 = (f32[3,5,5]{2,0,1:T(4,128)S(1)}, f32[3,5,5]{2,0,1:T(4,128)}, u32[]{:S(2)}) copy-start(f32[3,5,5]{2,0,1:T(4,128)} %param.11) | copy-start | bytes 904
  1.8 11.3 %copy-start.10 = (f32[3,5,5]{2,0,1:T(4,128)S(1)}, f32[3,5,5]{2,0,1:T(4,128)}, u32[]{:S(2)}) copy-start(f32[3,5,5]{2,0,1:T(4,128)} %param.12) | copy-start | bytes 904
  1.8 12.3 %collective-permute-start.1 = (f32[5,32,128]{2,1,0:T(8,128)S(1)}, f32[5,32,128]{2,1,0:T(8,128)S(1)}, u32[]{:S(2)}, u32[]{:S(2)}) collective-permute-start(f32[5,32,128]{2,1,0:T(8,128)S(1)} %bitcast.23), channel_id=1, source_target_pairs={{0,6},{2,0},{4,2},{6,4},{1,7},{3,1},{5,3},{7,5},{8,14},{10,8},{12,... | collective-permute-start | bytes 245768 | tf_op jit(solution)/shard_map/ppermute | solution.py:21
  9.3 4.5 %collective-permute-start = (f32[5,16,128]{2,1,0:T(8,128)}, f32[5,16,128]{2,1,0:T(8,128)S(1)}, u32[]{:S(2)}, u32[]{:S(2)}) collective-permute-start(f32[5,16,128]{2,1,0:T(8,128)} %get-tuple-element.12), channel_id=1, source_target_pairs={{0,24},{8,0},{16,8},{24,16},{1,25},{9,1},{17,9},{25,17},{2,26},{10... | collective-permute-start | bytes 122888 | tf_op jit(solution)/shard_map/ppermute | solution.py:21
  9.9 4.2 %collective-permute-start.2 = (f32[5,16,128]{2,1,0:T(8,128)}, f32[5,16,128]{2,1,0:T(8,128)S(1)}, u32[]{:S(2)}, u32[]{:S(2)}) collective-permute-start(f32[5,16,128]{2,1,0:T(8,128)} %get-tuple-element.13), channel_id=1, source_target_pairs={{0,1},{1,0},{2,3},{3,2},{4,5},{5,4},{6,7},{7,6},{8,9},{9,8},{10,11... | collective-permute-start | bytes 122888 | tf_op jit(solution)/shard_map/ppermute | solution.py:21
  13.7 0.6 copy-start.7
  14.1 0.6 copy-start.8
  14.7 0.6 %copy-start.4 = (f32[5,32,128]{2,1,0:T(8,128)}, f32[5,32,128]{2,1,0:T(8,128)S(1)}, u32[]{:S(2)}) copy-start(f32[5,32,128]{2,1,0:T(8,128)S(1)} %collective-permute-done.1.yf_ref) | copy-start | bytes 245764
  32.9 13.0 %collective-permute-start.6 = (f32[5,16,8,128]{3,2,1,0:T(8,128)}, f32[5,16,8,128]{3,2,1,0:T(8,128)S(1)}, u32[]{:S(2)}, u32[]{:S(2)}) collective-permute-start(f32[5,16,8,128]{3,2,1,0:T(8,128)} %get-tuple-element.18), channel_id=1, source_target_pairs={{0,2},{2,4},{4,6},{6,0},{1,3},{3,5},{5,7},{7,1},{8,10},{10,12},{12... | collective-permute-start | bytes 983048 | tf_op jit(solution)/shard_map/ppermute | solution.py:21
  33.3 12.6 %collective-permute-start.5 = (f32[5,8,8,128]{3,2,1,0:T(8,128)}, f32[5,8,8,128]{3,2,1,0:T(8,128)S(1)}, u32[]{:S(2)}, u32[]{:S(2)}) collective-permute-start(f32[5,8,8,128]{3,2,1,0:T(8,128)} %get-tuple-element.17), channel_id=1, source_target_pairs={{0,6},{2,0},{4,2},{6,4},{1,7},{3,1},{5,3},{7,5},{8,14},{10,8},{12,... | collective-permute-start | bytes 491528 | tf_op jit(solution)/shard_map/ppermute | solution.py:21
  37.2 6.4 %collective-permute-start.4 = (f32[5,3,16,128]{3,2,1,0:T(8,128)}, f32[5,3,16,128]{3,2,1,0:T(8,128)S(1)}, u32[]{:S(2)}, u32[]{:S(2)}) collective-permute-start(f32[5,3,16,128]{3,2,1,0:T(8,128)} %get-tuple-element.16), channel_id=1, source_target_pairs={{0,8},{8,16},{16,24},{24,0},{1,9},{9,17},{17,25},{25,1},{2,10},{10... | collective-permute-start | bytes 368648 | tf_op jit(solution)/shard_map/ppermute | solution.py:21
  37.2 4.1 %collective-permute-start.3 = (f32[5,2,16,128]{3,2,1,0:T(8,128)}, f32[5,2,16,128]{3,2,1,0:T(8,128)S(1)}, u32[]{:S(2)}, u32[]{:S(2)}) collective-permute-start(f32[5,2,16,128]{3,2,1,0:T(8,128)} %get-tuple-element.15), channel_id=1, source_target_pairs={{0,24},{8,0},{16,8},{24,16},{1,25},{9,1},{17,9},{25,17},{2,26},{10... | collective-permute-start | bytes 245768 | tf_op jit(solution)/shard_map/ppermute | solution.py:21
  38.9 4.7 %collective-permute-start.7 = (f32[2,5,16,128]{3,2,1,0:T(8,128)}, f32[2,5,16,128]{3,2,1,0:T(8,128)S(1)}, u32[]{:S(2)}, u32[]{:S(2)}) collective-permute-start(f32[2,5,16,128]{3,2,1,0:T(8,128)} %get-tuple-element.19), channel_id=1, source_target_pairs={{0,1},{1,0},{2,3},{3,2},{4,5},{5,4},{6,7},{7,6},{8,9},{9,8},{10,11... | collective-permute-start | bytes 245768 | tf_op jit(solution)/shard_map/ppermute | solution.py:21
  41.3 4.6 %copy-start.5 = (f32[5,2,16,128]{3,2,1,0:T(8,128)}, f32[5,2,16,128]{3,2,1,0:T(8,128)S(1)}, u32[]{:S(2)}) copy-start(f32[5,2,16,128]{3,2,1,0:T(8,128)S(1)} %collective-permute-done.3.axl_ref) | copy-start | bytes 245764
  43.6 2.4 %copy-start.6 = (f32[2,5,16,128]{3,2,1,0:T(8,128)}, f32[2,5,16,128]{3,2,1,0:T(8,128)S(1)}, u32[]{:S(2)}) copy-start(f32[2,5,16,128]{3,2,1,0:T(8,128)S(1)} %collective-permute-done.7.az_ref) | copy-start | bytes 245764
  43.6 2.4 %copy-start.3 = (f32[5,3,16,128]{3,2,1,0:T(8,128)}, f32[5,3,16,128]{3,2,1,0:T(8,128)S(1)}, u32[]{:S(2)}) copy-start(f32[5,3,16,128]{3,2,1,0:T(8,128)S(1)} %collective-permute-done.4.axr_ref) | copy-start | bytes 368644
  45.9 0.7 %copy-start.2 = (f32[5,8,8,128]{3,2,1,0:T(8,128)}, f32[5,8,8,128]{3,2,1,0:T(8,128)S(1)}, u32[]{:S(2)}) copy-start(f32[5,8,8,128]{3,2,1,0:T(8,128)S(1)} %collective-permute-done.5.ayl_ref) | copy-start | bytes 491524
  45.9 0.8 %copy-start.1 = (f32[5,16,8,128]{3,2,1,0:T(8,128)}, f32[5,16,8,128]{3,2,1,0:T(8,128)S(1)}, u32[]{:S(2)}) copy-start(f32[5,16,8,128]{3,2,1,0:T(8,128)S(1)} %collective-permute-done.6.ayr_ref) | copy-start | bytes 983044

commit v7 on v5

--- a/solution.py
+++ b/solution.py
@@ -8,7 +8,7 @@
 AXES = ("gx", "gy", "gz")
 STEP = 0.4
 SECTION = 0.25
-XC = 4
+XC = 8
 F32 = jnp.float32
 HI = lax.Precision.HIGHEST
 VMEM = pl.BlockSpec(memory_space=pltpu.VMEM)

time: 61.6 us -> 62.8 us (1.019)
  Pallas kernels: 23.2 us -> 24.7 us
    pallas_call x1, Pallas kernels: 17.5 us -> 19 us  [on_device(): pl.pallas_call(stencil_kernel, grid=(nx // XC,), out_shape=(jax.ShapeDtyp...]
where the time goes in v7:
time: 62.8 us; the launch traced here: 62.6 us
  Pallas kernels  24.7 us (39%)
  starting transfers between devices  14.4 us (23%)
  blocking collectives  10.7 us (17%)
  waiting for transfers between devices  5.2 us (8%)
  local copies, waits for them, and re-layouts  3.31 us (5%)
  matrix products  2.08 us (3%)
  between operations  1.43 us (2%)
  other arithmetic  0.79 us (1%)
    pallas_call x1, Pallas kernels, on_device(): pl.pallas_call(stencil_kernel, grid=(nx // XC,), out_shape=(jax.ShapeDtyp...  19 us
    ppermute x8, starting transfers between devices, shift_from(): return lax.ppermute(x, axis, [(i, (i + by) % n) for i in range(n)])  14.4 us
    all_to_all x1, blocking collectives, on_device(): got = lax.all_to_all(t, AXES, 0, 0, tiled=True)  10.7 us
    ppermute x8, waiting for transfers between devices, shift_from(): return lax.ppermute(x, axis, [(i, (i + by) % n) for i in range(n)])  5.2 us
    pallas_call x1, Pallas kernels, on_device(): pl.pallas_call(fix_kernel, out_shape=(jax.ShapeDtypeStruct((nf, nx, ny, n...  3.37 us
    unnamed x26, local copies, waits for them, and re-layouts  3.24 us
    pallas_call x1, Pallas kernels, on_device(): pl.pallas_call(fronts_kernel, out_shape=(jax.ShapeDtypeStruct((nf, ny, nz...  2.35 us
  transfers between devices with their start and end apart: 8, of which 4 were waited for; matrix products, arithmetic and copies ran while one was open for 4% of the time, Pallas kernels for 0%

profile of v7, /device:TPU:0, one launch (start us, length us, event | category | flops | bytes accessed | tf_op | source)
XLA Modules:
  0.0 62.6 jit_solution(1143165152214580242)
XLA Ops:
  0.6 0.0 copy-start.11
  0.6 0.0 copy-start.10
  0.7 0.0 copy-start.8
  0.7 0.0 copy-start.9
  0.7 2.4 %shard_map.104 = (f32[5,16,128]{2,1,0:T(8,128)}, f32[5,32,128]{2,1,0:T(8,128)}, f32[5,16,128]{2,1,0:T(8,128)}) custom-call(f32[5,32,16,128]{3,2,1,0:T(8,128)} %adj_ref.3), custom_call_target="tpu_custom_call" | custom-call | tf_op jit(solution)/shard_map/pallas_call | solution.py:198
  3.0 5.0 %collective-permute-start.1 = (f32[5,32,128]{2,1,0:T(8,128)}, f32[5,32,128]{2,1,0:T(8,128)S(1)}, u32[]{:S(2)}, u32[]{:S(2)}) collective-permute-start(f32[5,32,128]{2,1,0:T(8,128)} %get-tuple-element.14), channel_id=1, source_target_pairs={{0,6},{2,0},{4,2},{6,4},{1,7},{3,1},{5,3},{7,5},{8,14},{10,8},{12,... | collective-permute-start | bytes 245768 | tf_op jit(solution)/shard_map/ppermute | solution.py:20
  8.1 0.7 %collective-permute-start = (f32[5,16,128]{2,1,0:T(8,128)}, f32[5,16,128]{2,1,0:T(8,128)S(1)}, u32[]{:S(2)}, u32[]{:S(2)}) collective-permute-start(f32[5,16,128]{2,1,0:T(8,128)} %get-tuple-element.13), channel_id=1, source_target_pairs={{0,24},{8,0},{16,8},{24,16},{1,25},{9,1},{17,9},{25,17},{2,26},{10... | collective-permute-start | bytes 122888 | tf_op jit(solution)/shard_map/ppermute | solution.py:20
  8.7 1.5 %collective-permute-start.2 = (f32[5,16,128]{2,1,0:T(8,128)}, f32[5,16,128]{2,1,0:T(8,128)S(1)}, u32[]{:S(2)}, u32[]{:S(2)}) collective-permute-start(f32[5,16,128]{2,1,0:T(8,128)} %get-tuple-element.15), channel_id=1, source_target_pairs={{0,1},{1,0},{2,3},{3,2},{4,5},{5,4},{6,7},{7,6},{8,9},{9,8},{10,11... | collective-permute-start | bytes 122888 | tf_op jit(solution)/shard_map/ppermute | solution.py:20
  10.2 0.0 copy-done.11
  10.2 0.1 reshape.62
  10.3 0.2 convert_reduce_fusion
  10.5 0.1 fusion.16
  10.7 0.3 fusion.2
  11.0 0.0 copy-done.10
  11.0 0.3 fusion.3
  11.3 0.0 copy-done.8
  11.3 0.6 copy.24.fp_ref
  11.9 0.0 copy-done.9
  11.9 0.6 copy.25.fm_ref
  12.5 0.0 collective-permute-done.xf_ref
  12.5 0.0 copy-start.6
  12.5 0.4 collective-permute-done.2.zf_ref
  12.9 0.0 copy-start.7
  12.9 0.0 collective-permute-done.1.yf_ref
  12.9 0.2 copy-done.6
  13.2 0.4 copy-done.7
  13.5 0.0 copy-start.3
  13.5 0.6 %copy-done.3 = f32[5,32,128]{2,1,0:T(8,128)} copy-done((f32[5,32,128]{2,1,0:T(8,128)}, f32[5,32,128]{2,1,0:T(8,128)S(1)}, u32[]{:S(2)}) %copy-start.3) | copy-done | bytes 81944
  14.2 19.0 %shard_map.105 = (f32[5,32,16,128]{3,2,1,0:T(8,128)}, f32[5,2,16,128]{3,2,1,0:T(8,128)}, f32[5,3,16,128]{3,2,1,0:T(8,128)}, f32[5,8,8,128]{3,2,1,0:T(8,128)}, f3...) custom-call(f32[3,5,5]{2,1,0:T(8,128)} %copy.24.fp_ref, f32[3,5,5]{2,1,0:T(8,128)} %copy.25.fm_ref, ...), custom_call_target="tpu_custom_call" | custom-call | tf_op jit(solution)/shard_map/pallas_call | solution.py:213
  33.2 0.1 collective-permute-start.6
  33.2 0.3 fusion.4
  33.6 3.9 %collective-permute-start.5 = (f32[5,8,8,128]{3,2,1,0:T(8,128)}, f32[5,8,8,128]{3,2,1,0:T(8,128)S(1)}, u32[]{:S(2)}, u32[]{:S(2)}) collective-permute-start(f32[5,8,8,128]{3,2,1,0:T(8,128)} %get-tuple-element.19), channel_id=1, source_target_pairs={{0,6},{2,0},{4,2},{6,4},{1,7},{3,1},{5,3},{7,5},{8,14},{10,8},{12,... | collective-permute-start | bytes 491528 | tf_op jit(solution)/shard_map/ppermute | solution.py:20
  37.4 0.0 collective-permute-start.4
  37.4 1.7 %collective-permute-start.3 = (f32[5,2,16,128]{3,2,1,0:T(8,128)}, f32[5,2,16,128]{3,2,1,0:T(8,128)S(1)}, u32[]{:S(2)}, u32[]{:S(2)}) collective-permute-start(f32[5,2,16,128]{3,2,1,0:T(8,128)} %get-tuple-element.17), channel_id=1, source_target_pairs={{0,24},{8,0},{16,8},{24,16},{1,25},{9,1},{17,9},{25,17},{2,26},{10... | collective-permute-start | bytes 245768 | tf_op jit(solution)/shard_map/ppermute | solution.py:20
  39.2 1.5 %collective-permute-start.7 = (f32[2,5,16,128]{3,2,1,0:T(8,128)}, f32[2,5,16,128]{3,2,1,0:T(8,128)S(1)}, u32[]{:S(2)}, u32[]{:S(2)}) collective-permute-start(f32[2,5,16,128]{3,2,1,0:T(8,128)} %get-tuple-element.21), channel_id=1, source_target_pairs={{0,1},{1,0},{2,3},{3,2},{4,5},{5,4},{6,7},{7,6},{8,9},{9,8},{10,11... | collective-permute-start | bytes 245768 | tf_op jit(solution)/shard_map/ppermute | solution.py:20
  41.4 0.2 collective-permute-done.3.axl_ref
  41.6 0.0 copy-start.4
  41.6 2.3 %collective-permute-done.7.az_ref = f32[2,5,16,128]{3,2,1,0:T(8,128)S(1)} collective-permute-done((f32[2,5,16,128]{3,2,1,0:T(8,128)}, f32[2,5,16,128]{3,2,1,0:T(8,128)S(1)}, u32[]{:S(2)}, u32[]{:S(2)}) %collective-permute-start.7) | collective-permute-done | bytes 81952 | tf_op jit(solution)/shard_map/ppermute | solution.py:20
  43.8 0.0 copy-start.5
  43.8 0.0 collective-permute-done.4.axr_ref
  43.8 0.0 copy-start.2
  43.9 2.3 %collective-permute-done.5.ayl_ref = f32[5,8,8,128]{3,2,1,0:T(8,128)S(1)} collective-permute-done((f32[5,8,8,128]{3,2,1,0:T(8,128)}, f32[5,8,8,128]{3,2,1,0:T(8,128)S(1)}, u32[]{:S(2)}, u32[]{:S(2)}) %collective-permute-start.5) | collective-permute-done | bytes 163872 | tf_op jit(solution)/shard_map/ppermute | solution.py:20
  46.2 0.0 copy-start.1
  46.2 0.0 collective-permute-done.6.ayr_ref
  46.2 0.0 copy-start
  46.2 0.0 copy-done.4
  46.2 0.0 copy-done.5
  46.2 0.0 copy-done.2
  46.2 0.6 %copy-done.1 = f32[5,8,8,128]{3,2,1,0:T(8,128)} copy-done((f32[5,8,8,128]{3,2,1,0:T(8,128)}, f32[5,8,8,128]{3,2,1,0:T(8,128)S(1)}, u32[]{:S(2)}) %copy-start.1) | copy-done | bytes 163864
  46.8 0.1 copy-done
  47.0 3.4 %shard_map.106 = (f32[5,32,16,128]{3,2,1,0:T(8,128)}, f32[16,128]{1,0:T(8,128)}) custom-call(s32[16]{0:T(128)} %row_ref.1, s32[1]{0:T(128)S(6)} %copy.38.cnt_ref, f32[5,32,16,128]{3,2,1,0:T(8,128)} %get-tuple-element.16.sec_ref, f32[5,2,16,128]{3,2,1,0:T(8,128)} %copy-done.4, f32[5,3,16,128]{3,2,1,0:T(8,128)} %copy-done.2, ...), custom_call_target="tpu_custom_call", output_to_operand_aliasing={{0}: (2, {})} | custom-call | tf_op jit(solution)/shard_map/pallas_call | solution.py:253
  50.3 1.0 %fusion.6 = f32[32,32,1]{1,0,2:T(8,128)S(1)} fusion(s32[16,128]{1,0:T(8,128)S(1)} %get-tuple-element.26, f32[16,128]{1,0:T(8,128)} %get-tuple-element.23, s32[16,128]{1,0:T(8,128)S(1)} %get-tuple-element.27), kind=kOutput, calls=%fused_computation.12 | convolution fusion | flops 25362432 | bytes 28672 | tf_op jit(solution)/shard_map/rzo,rzk->ok/dot_general | solution.py:286
  51.3 10.7 %all_to_all.9 = f32[32,1,32]{2,1,0:T(1,128)S(1)} all-to-all(f32[32,1,32]{2,1,0:T(1,128)S(1)} %bitcast.20), channel_id=1, replica_groups=mesh['gx'=4,'gy'=4,'gz'=2] {'gx','gy','gz'}, dimensions={0} | all-to-all | bytes 8192 | tf_op jit(solution)/shard_map/all_to_all | solution.py:287
  62.0 0.6 reduce_sum.49
  (2 shorter events, 0.0 us)
Async XLA Ops:
  0.6 9.6 %copy-start.11 = (s32[1024]{0:T(1024)S(1)}, s32[1024]{0:T(1024)}, u32[]{:S(2)}) copy-start(s32[1024]{0:T(1024)} %param.17) | copy-start | bytes 12292
  0.6 10.3 %copy-start.10 = (s32[16,128]{1,0:T(8,128)S(1)}, s32[16,128]{1,0:T(8,128)}, u32[]{:S(2)}) copy-start(s32[16,128]{1,0:T(8,128)} %param.14) | copy-start | bytes 24580
  0.7 10.7 %copy-start.8 = (f32[3,5,5]{2,0,1:T(4,128)S(1)}, f32[3,5,5]{2,0,1:T(4,128)}, u32[]{:S(2)}) copy-start(f32[3,5,5]{2,0,1:T(4,128)} %param.11) | copy-start | bytes 904
  0.7 11.3 %copy-start.9 = (f32[3,5,5]{2,0,1:T(4,128)S(1)}, f32[3,5,5]{2,0,1:T(4,128)}, u32[]{:S(2)}) copy-start(f32[3,5,5]{2,0,1:T(4,128)} %param.12) | copy-start | bytes 904
  3.0 9.9 %collective-permute-start.1 = (f32[5,32,128]{2,1,0:T(8,128)}, f32[5,32,128]{2,1,0:T(8,128)S(1)}, u32[]{:S(2)}, u32[]{:S(2)}) collective-permute-start(f32[5,32,128]{2,1,0:T(8,128)} %get-tuple-element.14), channel_id=1, source_target_pairs={{0,6},{2,0},{4,2},{6,4},{1,7},{3,1},{5,3},{7,5},{8,14},{10,8},{12,... | collective-permute-start | bytes 245768 | tf_op jit(solution)/shard_map/ppermute | solution.py:20
  8.1 4.5 %collective-permute-start = (f32[5,16,128]{2,1,0:T(8,128)}, f32[5,16,128]{2,1,0:T(8,128)S(1)}, u32[]{:S(2)}, u32[]{:S(2)}) collective-permute-start(f32[5,16,128]{2,1,0:T(8,128)} %get-tuple-element.13), channel_id=1, source_target_pairs={{0,24},{8,0},{16,8},{24,16},{1,25},{9,1},{17,9},{25,17},{2,26},{10... | collective-permute-start | bytes 122888 | tf_op jit(solution)/shard_map/ppermute | solution.py:20
  8.7 4.2 %collective-permute-start.2 = (f32[5,16,128]{2,1,0:T(8,128)}, f32[5,16,128]{2,1,0:T(8,128)S(1)}, u32[]{:S(2)}, u32[]{:S(2)}) collective-permute-start(f32[5,16,128]{2,1,0:T(8,128)} %get-tuple-element.15), channel_id=1, source_target_pairs={{0,1},{1,0},{2,3},{3,2},{4,5},{5,4},{6,7},{7,6},{8,9},{9,8},{10,11... | collective-permute-start | bytes 122888 | tf_op jit(solution)/shard_map/ppermute | solution.py:20
  12.5 0.6 copy-start.6
  12.9 0.6 copy-start.7
  13.5 0.7 %copy-start.3 = (f32[5,32,128]{2,1,0:T(8,128)}, f32[5,32,128]{2,1,0:T(8,128)S(1)}, u32[]{:S(2)}) copy-start(f32[5,32,128]{2,1,0:T(8,128)S(1)} %collective-permute-done.1.yf_ref) | copy-start | bytes 245764
  33.2 13.0 %collective-permute-start.6 = (f32[5,16,8,128]{3,2,1,0:T(8,128)}, f32[5,16,8,128]{3,2,1,0:T(8,128)S(1)}, u32[]{:S(2)}, u32[]{:S(2)}) collective-permute-start(f32[5,16,8,128]{3,2,1,0:T(8,128)} %get-tuple-element.20), channel_id=1, source_target_pairs={{0,2},{2,4},{4,6},{6,0},{1,3},{3,5},{5,7},{7,1},{8,10},{10,12},{12... | collective-permute-start | bytes 983048 | tf_op jit(solution)/shard_map/ppermute | solution.py:20
  33.6 12.6 %collective-permute-start.5 = (f32[5,8,8,128]{3,2,1,0:T(8,128)}, f32[5,8,8,128]{3,2,1,0:T(8,128)S(1)}, u32[]{:S(2)}, u32[]{:S(2)}) collective-permute-start(f32[5,8,8,128]{3,2,1,0:T(8,128)} %get-tuple-element.19), channel_id=1, source_target_pairs={{0,6},{2,0},{4,2},{6,4},{1,7},{3,1},{5,3},{7,5},{8,14},{10,8},{12,... | collective-permute-start | bytes 491528 | tf_op jit(solution)/shard_map/ppermute | solution.py:20
  37.4 6.4 %collective-permute-start.4 = (f32[5,3,16,128]{3,2,1,0:T(8,128)}, f32[5,3,16,128]{3,2,1,0:T(8,128)S(1)}, u32[]{:S(2)}, u32[]{:S(2)}) collective-permute-start(f32[5,3,16,128]{3,2,1,0:T(8,128)} %get-tuple-element.18), channel_id=1, source_target_pairs={{0,8},{8,16},{16,24},{24,0},{1,9},{9,17},{17,25},{25,1},{2,10},{10... | collective-permute-start | bytes 368648 | tf_op jit(solution)/shard_map/ppermute | solution.py:20
  37.4 4.1 %collective-permute-start.3 = (f32[5,2,16,128]{3,2,1,0:T(8,128)}, f32[5,2,16,128]{3,2,1,0:T(8,128)S(1)}, u32[]{:S(2)}, u32[]{:S(2)}) collective-permute-start(f32[5,2,16,128]{3,2,1,0:T(8,128)} %get-tuple-element.17), channel_id=1, source_target_pairs={{0,24},{8,0},{16,8},{24,16},{1,25},{9,1},{17,9},{25,17},{2,26},{10... | collective-permute-start | bytes 245768 | tf_op jit(solution)/shard_map/ppermute | solution.py:20
  39.2 4.7 %collective-permute-start.7 = (f32[2,5,16,128]{3,2,1,0:T(8,128)}, f32[2,5,16,128]{3,2,1,0:T(8,128)S(1)}, u32[]{:S(2)}, u32[]{:S(2)}) collective-permute-start(f32[2,5,16,128]{3,2,1,0:T(8,128)} %get-tuple-element.21), channel_id=1, source_target_pairs={{0,1},{1,0},{2,3},{3,2},{4,5},{5,4},{6,7},{7,6},{8,9},{9,8},{10,11... | collective-permute-start | bytes 245768 | tf_op jit(solution)/shard_map/ppermute | solution.py:20
  41.6 4.6 %copy-start.4 = (f32[5,2,16,128]{3,2,1,0:T(8,128)}, f32[5,2,16,128]{3,2,1,0:T(8,128)S(1)}, u32[]{:S(2)}) copy-start(f32[5,2,16,128]{3,2,1,0:T(8,128)S(1)} %collective-permute-done.3.axl_ref) | copy-start | bytes 245764
  43.8 2.3 %copy-start.5 = (f32[2,5,16,128]{3,2,1,0:T(8,128)}, f32[2,5,16,128]{3,2,1,0:T(8,128)S(1)}, u32[]{:S(2)}) copy-start(f32[2,5,16,128]{3,2,1,0:T(8,128)S(1)} %collective-permute-done.7.az_ref) | copy-start | bytes 245764
  43.8 2.4 %copy-start.2 = (f32[5,3,16,128]{3,2,1,0:T(8,128)}, f32[5,3,16,128]{3,2,1,0:T(8,128)S(1)}, u32[]{:S(2)}) copy-start(f32[5,3,16,128]{3,2,1,0:T(8,128)S(1)} %collective-permute-done.4.axr_ref) | copy-start | bytes 368644
  46.2 0.7 %copy-start.1 = (f32[5,8,8,128]{3,2,1,0:T(8,128)}, f32[5,8,8,128]{3,2,1,0:T(8,128)S(1)}, u32[]{:S(2)}) copy-start(f32[5,8,8,128]{3,2,1,0:T(8,128)S(1)} %collective-permute-done.5.ayl_ref) | copy-start | bytes 491524
  46.2 0.8 %copy-start = (f32[5,16,8,128]{3,2,1,0:T(8,128)}, f32[5,16,8,128]{3,2,1,0:T(8,128)S(1)}, u32[]{:S(2)}) copy-start(f32[5,16,8,128]{3,2,1,0:T(8,128)S(1)} %collective-permute-done.6.ayr_ref) | copy-start | bytes 983044

commit v8 on v5

--- a/solution.py
+++ b/solution.py
@@ -163,32 +163,40 @@
 
 def fix_kernel(row_ref, cnt_ref, sec_ref, axl_ref, axr_ref, ayl_ref, ayr_ref, az_ref,
                coef_ref, out_ref, wt_ref):
-    nf, nx, ny, nz = sec_ref.shape
+    nf, _, ny, nz = sec_ref.shape
+    i = pl.program_id(0)
+    last = pl.num_programs(0) - 1
     row, lane = iotas(ny, nz)
     pad = jnp.zeros((ny - 8, nz), F32)
-    for x in range(nx):
-        for f in range(nf):
-            ty = jnp.concatenate([ayr_ref[f, x // 2], pad], 0)
-            add = jnp.where(row < 3, pltpu.roll(ty, (ny - 4 * (x % 2)) % ny, 0), 0.0)
-            ty = jnp.concatenate([ayl_ref[f, x // 4], pad], 0)
-            add = add + jnp.where(row >= ny - 2, pltpu.roll(ty, (ny - 2 - 2 * (x % 4)) % ny, 0), 0.0)
-            add = add + jnp.where(lane < 3, pltpu.roll(az_ref[1, f], (nz - 4 * x) % nz, 1), 0.0)
-            add = add + jnp.where(lane >= nz - 2, pltpu.roll(az_ref[0, f], (nz - 2 - 4 * x) % nz, 1), 0.0)
-            if x < 3:
-                add = add + axr_ref[f, x]
-            if x >= nx - 2:
-                add = add + axl_ref[f, x - (nx - 2)]
-            out_ref[f, x] = sec_ref[f, x] + SECTION * add
+    for xl in range(XC):
+        x = i * XC + xl
+        zr_shift = lax.rem(nz - 4 * x, nz)
+        zl_shift = lax.rem(2 * nz - 2 - 4 * x, nz)
+        for f in range(nf):
+            ty = jnp.concatenate([ayr_ref[f, xl // 2], pad], 0)
+            add = jnp.where(row < 3, pltpu.roll(ty, (ny - 4 * (xl % 2)) % ny, 0), 0.0)
+            ty = jnp.concatenate([ayl_ref[f, xl // 4], pad], 0)
+            add = add + jnp.where(row >= ny - 2, pltpu.roll(ty, (ny - 2 - 2 * (xl % 4)) % ny, 0), 0.0)
+            add = add + jnp.where(lane < 3, pltpu.roll(az_ref[1, f], zr_shift, 1), 0.0)
+            add = add + jnp.where(lane >= nz - 2, pltpu.roll(az_ref[0, f], zl_shift, 1), 0.0)
+            if xl < 3:
+                add = add + jnp.where(i == 0, axr_ref[f, xl], 0.0)
+            if xl >= XC - 2:
+                add = add + jnp.where(i == last, axl_ref[f, xl - (XC - 2)], 0.0)
+            out_ref[f, xl] = sec_ref[f, xl] + SECTION * add
     live_n = cnt_ref[0]
     for r in range(wt_ref.shape[0]):
         idx = row_ref[r]
         lx = idx // ny
         ly = idx % ny
-        val = None
-        for f in range(nf):
-            v = out_ref[f, lx, pl.ds(ly, 1), :] * coef_ref[f, pl.ds(r, 1), :]
-            val = v if val is None else val + v
-        wt_ref[pl.ds(r, 1), :] = val * jnp.where(r < live_n, 1.0, 0.0).astype(F32)
+
+        @pl.when(lx // XC == i)
+        def _():
+            val = None
+            for f in range(nf):
+                v = out_ref[f, lx % XC, pl.ds(ly, 1), :] * coef_ref[f, pl.ds(r, 1), :]
+                val = v if val is None else val + v
+            wt_ref[pl.ds(r, 1), :] = val * jnp.where(r < live_n, 1.0, 0.0).astype(F32)
 
 
 def on_device(ndev, adjoint, stencil_weights, flux_plus, flux_minus, wall_row, wall_panel, wall_coef,
@@ -252,13 +260,28 @@
     nr = wall_row.shape[0]
     section, wt = pl.pallas_call(
         fix_kernel,
+        grid=(nx // XC,),
         out_shape=(
             jax.ShapeDtypeStruct((nf, nx, ny, nz), F32),
             jax.ShapeDtypeStruct((nr, nz), F32),
         ),
-        in_specs=[SMEM, SMEM] + [VMEM] * 7,
-        out_specs=(VMEM, VMEM),
+        in_specs=[
+            SMEM,
+            SMEM,
+            pl.BlockSpec((nf, XC, ny, nz), lambda i: (0, i, 0, 0)),
+            pl.BlockSpec((nf, 2, ny, nz), const4),
+            pl.BlockSpec((nf, 3, ny, nz), const4),
+            pl.BlockSpec((nf, XC // 4, 8, nz), lambda i: (0, i, 0, 0)),
+            pl.BlockSpec((nf, XC // 2, 8, nz), lambda i: (0, i, 0, 0)),
+            pl.BlockSpec((2, nf, ny, nz), const4),
+            pl.BlockSpec((nf, nr, nz), const3),
+        ],
+        out_specs=(
+            pl.BlockSpec((nf, XC, ny, nz), lambda i: (0, i, 0, 0)),
+            pl.BlockSpec((nr, nz), lambda i: (0, 0)),
+        ),
         input_output_aliases={2: 0},
+        compiler_params=pltpu.CompilerParams(dimension_semantics=("arbitrary",)),
     )(wall_row, wall_count, sec, axl, axr, ayl, ayr, az, wall_coef)
 
     npan = panel_owner.shape[0]

time: 61.6 us -> 65.7 us (1.067)
  Pallas kernels: 23.2 us -> 27.2 us
    pallas_call x1, Pallas kernels: 3.37 us -> 7.37 us  [on_device(): pl.pallas_call(fix_kernel, grid=(nx // XC,), out_shape=(jax.ShapeDtypeStr...]
where the time goes in v8:
time: 65.7 us; the launch traced here: 65.1 us
  Pallas kernels  27.2 us (41%)
  starting transfers between devices  14.4 us (22%)
  blocking collectives  10.7 us (16%)
  waiting for transfers between devices  5.2 us (8%)
  local copies, waits for them, and re-layouts  3.31 us (5%)
  matrix products  2.08 us (3%)
  between operations  1.43 us (2%)
  other arithmetic  0.79 us (1%)
    pallas_call x1, Pallas kernels, on_device(): pl.pallas_call(stencil_kernel, grid=(nx // XC,), out_shape=(jax.ShapeDtyp...  17.5 us
    ppermute x8, starting transfers between devices, shift_from(): return lax.ppermute(x, axis, [(i, (i + by) % n) for i in range(n)])  14.4 us
    all_to_all x1, blocking collectives, on_device(): got = lax.all_to_all(t, AXES, 0, 0, tiled=True)  10.7 us
    pallas_call x1, Pallas kernels, on_device(): pl.pallas_call(fix_kernel, grid=(nx // XC,), out_shape=(jax.ShapeDtypeStr...  7.37 us
    ppermute x8, waiting for transfers between devices, shift_from(): return lax.ppermute(x, axis, [(i, (i + by) % n) for i in range(n)])  5.2 us
    unnamed x26, local copies, waits for them, and re-layouts  3.24 us
    pallas_call x1, Pallas kernels, on_device(): pl.pallas_call(fronts_kernel, out_shape=(jax.ShapeDtypeStruct((nf, ny, nz...  2.35 us
  transfers between devices with their start and end apart: 8, of which 4 were waited for; matrix products, arithmetic and copies ran while one was open for 4% of the time, Pallas kernels for 0%

profile of v8, /device:TPU:0, one launch (start us, length us, event | category | flops | bytes accessed | tf_op | source)
XLA Modules:
  0.0 65.1 jit_solution(319031808326572362)
XLA Ops:
  0.6 0.0 copy-start.11
  0.6 0.0 copy-start.10
  0.7 0.0 copy-start.8
  0.7 0.0 copy-start.9
  0.7 2.4 %shard_map.104 = (f32[5,16,128]{2,1,0:T(8,128)}, f32[5,32,128]{2,1,0:T(8,128)}, f32[5,16,128]{2,1,0:T(8,128)}) custom-call(f32[5,32,16,128]{3,2,1,0:T(8,128)} %adj_ref.3), custom_call_target="tpu_custom_call" | custom-call | tf_op jit(solution)/shard_map/pallas_call | solution.py:206
  3.0 5.0 %collective-permute-start.1 = (f32[5,32,128]{2,1,0:T(8,128)}, f32[5,32,128]{2,1,0:T(8,128)S(1)}, u32[]{:S(2)}, u32[]{:S(2)}) collective-permute-start(f32[5,32,128]{2,1,0:T(8,128)} %get-tuple-element.14), channel_id=1, source_target_pairs={{0,6},{2,0},{4,2},{6,4},{1,7},{3,1},{5,3},{7,5},{8,14},{10,8},{12,... | collective-permute-start | bytes 245768 | tf_op jit(solution)/shard_map/ppermute | solution.py:20
  8.1 0.7 collective-permute-start
  8.7 1.5 %collective-permute-start.2 = (f32[5,16,128]{2,1,0:T(8,128)}, f32[5,16,128]{2,1,0:T(8,128)S(1)}, u32[]{:S(2)}, u32[]{:S(2)}) collective-permute-start(f32[5,16,128]{2,1,0:T(8,128)} %get-tuple-element.15), channel_id=1, source_target_pairs={{0,1},{1,0},{2,3},{3,2},{4,5},{5,4},{6,7},{7,6},{8,9},{9,8},{10,11... | collective-permute-start | bytes 122888 | tf_op jit(solution)/shard_map/ppermute | solution.py:20
  10.2 0.0 copy-done.11
  10.2 0.1 reshape.62
  10.3 0.2 convert_reduce_fusion
  10.5 0.1 fusion.16
  10.7 0.3 fusion.2
  11.0 0.0 copy-done.10
  11.0 0.3 fusion.3
  11.3 0.0 copy-done.8
  11.3 0.6 copy.24.fp_ref
  11.9 0.0 copy-done.9
  11.9 0.6 copy.25.fm_ref
  12.5 0.0 collective-permute-done.xf_ref
  12.5 0.0 copy-start.6
  12.5 0.4 collective-permute-done.2.zf_ref
  12.9 0.0 copy-start.7
  12.9 0.0 collective-permute-done.1.yf_ref
  12.9 0.2 copy-done.6
  13.2 0.4 copy-done.7
  13.5 0.0 copy-start.3
  13.5 0.6 copy-done.3
  14.2 17.5 %shard_map.105 = (f32[5,32,16,128]{3,2,1,0:T(8,128)}, f32[5,2,16,128]{3,2,1,0:T(8,128)}, f32[5,3,16,128]{3,2,1,0:T(8,128)}, f32[5,8,8,128]{3,2,1,0:T(8,128)}, f3...) custom-call(f32[3,5,5]{2,1,0:T(8,128)} %copy.24.fp_ref, f32[3,5,5]{2,1,0:T(8,128)} %copy.25.fm_ref, ...), custom_call_target="tpu_custom_call" | custom-call | tf_op jit(solution)/shard_map/pallas_call | solution.py:221
  31.7 0.1 collective-permute-start.6
  31.8 0.3 fusion.4
  32.1 3.9 %collective-permute-start.5 = (f32[5,8,8,128]{3,2,1,0:T(8,128)}, f32[5,8,8,128]{3,2,1,0:T(8,128)S(1)}, u32[]{:S(2)}, u32[]{:S(2)}) collective-permute-start(f32[5,8,8,128]{3,2,1,0:T(8,128)} %get-tuple-element.19), channel_id=1, source_target_pairs={{0,6},{2,0},{4,2},{6,4},{1,7},{3,1},{5,3},{7,5},{8,14},{10,8},{12,... | collective-permute-start | bytes 491528 | tf_op jit(solution)/shard_map/ppermute | solution.py:20
  36.0 0.0 collective-permute-start.4
  36.0 1.7 %collective-permute-start.3 = (f32[5,2,16,128]{3,2,1,0:T(8,128)}, f32[5,2,16,128]{3,2,1,0:T(8,128)S(1)}, u32[]{:S(2)}, u32[]{:S(2)}) collective-permute-start(f32[5,2,16,128]{3,2,1,0:T(8,128)} %get-tuple-element.17), channel_id=1, source_target_pairs={{0,24},{8,0},{16,8},{24,16},{1,25},{9,1},{17,9},{25,17},{2,26},{10... | collective-permute-start | bytes 245768 | tf_op jit(solution)/shard_map/ppermute | solution.py:20
  37.7 1.5 %collective-permute-start.7 = (f32[2,5,16,128]{3,2,1,0:T(8,128)}, f32[2,5,16,128]{3,2,1,0:T(8,128)S(1)}, u32[]{:S(2)}, u32[]{:S(2)}) collective-permute-start(f32[2,5,16,128]{3,2,1,0:T(8,128)} %get-tuple-element.21), channel_id=1, source_target_pairs={{0,1},{1,0},{2,3},{3,2},{4,5},{5,4},{6,7},{7,6},{8,9},{9,8},{10,11... | collective-permute-start | bytes 245768 | tf_op jit(solution)/shard_map/ppermute | solution.py:20
  39.9 0.2 collective-permute-done.3.axl_ref
  40.1 0.0 copy-start.4
  40.1 2.3 %collective-permute-done.7.az_ref = f32[2,5,16,128]{3,2,1,0:T(8,128)S(1)} collective-permute-done((f32[2,5,16,128]{3,2,1,0:T(8,128)}, f32[2,5,16,128]{3,2,1,0:T(8,128)S(1)}, u32[]{:S(2)}, u32[]{:S(2)}) %collective-permute-start.7) | collective-permute-done | bytes 81952 | tf_op jit(solution)/shard_map/ppermute | solution.py:20
  42.4 0.0 copy-start.5
  42.4 0.0 collective-permute-done.4.axr_ref
  42.4 0.0 copy-start.2
  42.4 2.3 %collective-permute-done.5.ayl_ref = f32[5,8,8,128]{3,2,1,0:T(8,128)S(1)} collective-permute-done((f32[5,8,8,128]{3,2,1,0:T(8,128)}, f32[5,8,8,128]{3,2,1,0:T(8,128)S(1)}, u32[]{:S(2)}, u32[]{:S(2)}) %collective-permute-start.5) | collective-permute-done | bytes 163872 | tf_op jit(solution)/shard_map/ppermute | solution.py:20
  44.7 0.0 copy-start.1
  44.7 0.0 collective-permute-done.6.ayr_ref
  44.7 0.0 copy-start
  44.7 0.0 copy-done.4
  44.7 0.0 copy-done.5
  44.8 0.0 copy-done.2
  44.8 0.6 copy-done.1
  45.4 0.1 copy-done
  45.5 7.4 %shard_map.106 = (f32[5,32,16,128]{3,2,1,0:T(8,128)}, f32[16,128]{1,0:T(8,128)}) custom-call(s32[16]{0:T(128)} %row_ref.1, s32[1]{0:T(128)S(6)} %copy.38.cnt_ref, f32[5,32,16,128]{3,2,1,0:T(8,128)} %get-tuple-element.16.sec_ref, f32[5,2,16,128]{3,2,1,0:T(8,128)} %copy-done.4, f32[5,3,16,128]{3,2,1,0:T(8,128)} %copy-done.2, ...), custom_call_target="tpu_custom_call", output_to_operand_aliasing={{0}: (2, {})} | custom-call | tf_op jit(solution)/shard_map/pallas_call | solution.py:261
  52.9 1.0 %fusion.6 = f32[32,32,1]{1,0,2:T(8,128)S(1)} fusion(s32[16,128]{1,0:T(8,128)S(1)} %get-tuple-element.26, f32[16,128]{1,0:T(8,128)} %get-tuple-element.23, s32[16,128]{1,0:T(8,128)S(1)} %get-tuple-element.27), kind=kOutput, calls=%fused_computation.12 | convolution fusion | flops 25362432 | bytes 28672 | tf_op jit(solution)/shard_map/rzo,rzk->ok/dot_general | solution.py:309
  53.9 10.7 %all_to_all.9 = f32[32,1,32]{2,1,0:T(1,128)S(1)} all-to-all(f32[32,1,32]{2,1,0:T(1,128)S(1)} %bitcast.20), channel_id=1, replica_groups=mesh['gx'=4,'gy'=4,'gz'=2] {'gx','gy','gz'}, dimensions={0} | all-to-all | bytes 8192 | tf_op jit(solution)/shard_map/all_to_all | solution.py:310
  64.5 0.6 reduce_sum.49
  (2 shorter events, 0.0 us)
Async XLA Ops:
  0.6 9.6 %copy-start.11 = (s32[1024]{0:T(1024)S(1)}, s32[1024]{0:T(1024)}, u32[]{:S(2)}) copy-start(s32[1024]{0:T(1024)} %param.17) | copy-start | bytes 12292
  0.6 10.3 %copy-start.10 = (s32[16,128]{1,0:T(8,128)S(1)}, s32[16,128]{1,0:T(8,128)}, u32[]{:S(2)}) copy-start(s32[16,128]{1,0:T(8,128)} %param.14) | copy-start | bytes 24580
  0.7 10.7 %copy-start.8 = (f32[3,5,5]{2,0,1:T(4,128)S(1)}, f32[3,5,5]{2,0,1:T(4,128)}, u32[]{:S(2)}) copy-start(f32[3,5,5]{2,0,1:T(4,128)} %param.11) | copy-start | bytes 904
  0.7 11.3 %copy-start.9 = (f32[3,5,5]{2,0,1:T(4,128)S(1)}, f32[3,5,5]{2,0,1:T(4,128)}, u32[]{:S(2)}) copy-start(f32[3,5,5]{2,0,1:T(4,128)} %param.12) | copy-start | bytes 904
  3.0 9.9 %collective-permute-start.1 = (f32[5,32,128]{2,1,0:T(8,128)}, f32[5,32,128]{2,1,0:T(8,128)S(1)}, u32[]{:S(2)}, u32[]{:S(2)}) collective-permute-start(f32[5,32,128]{2,1,0:T(8,128)} %get-tuple-element.14), channel_id=1, source_target_pairs={{0,6},{2,0},{4,2},{6,4},{1,7},{3,1},{5,3},{7,5},{8,14},{10,8},{12,... | collective-permute-start | bytes 245768 | tf_op jit(solution)/shard_map/ppermute | solution.py:20
  8.1 4.5 %collective-permute-start = (f32[5,16,128]{2,1,0:T(8,128)}, f32[5,16,128]{2,1,0:T(8,128)S(1)}, u32[]{:S(2)}, u32[]{:S(2)}) collective-permute-start(f32[5,16,128]{2,1,0:T(8,128)} %get-tuple-element.13), channel_id=1, source_target_pairs={{0,24},{8,0},{16,8},{24,16},{1,25},{9,1},{17,9},{25,17},{2,26},{10... | collective-permute-start | bytes 122888 | tf_op jit(solution)/shard_map/ppermute | solution.py:20
  8.7 4.2 %collective-permute-start.2 = (f32[5,16,128]{2,1,0:T(8,128)}, f32[5,16,128]{2,1,0:T(8,128)S(1)}, u32[]{:S(2)}, u32[]{:S(2)}) collective-permute-start(f32[5,16,128]{2,1,0:T(8,128)} %get-tuple-element.15), channel_id=1, source_target_pairs={{0,1},{1,0},{2,3},{3,2},{4,5},{5,4},{6,7},{7,6},{8,9},{9,8},{10,11... | collective-permute-start | bytes 122888 | tf_op jit(solution)/shard_map/ppermute | solution.py:20
  12.5 0.6 copy-start.6
  12.9 0.6 copy-start.7
  13.5 0.7 copy-start.3
  31.7 13.0 %collective-permute-start.6 = (f32[5,16,8,128]{3,2,1,0:T(8,128)}, f32[5,16,8,128]{3,2,1,0:T(8,128)S(1)}, u32[]{:S(2)}, u32[]{:S(2)}) collective-permute-start(f32[5,16,8,128]{3,2,1,0:T(8,128)} %get-tuple-element.20), channel_id=1, source_target_pairs={{0,2},{2,4},{4,6},{6,0},{1,3},{3,5},{5,7},{7,1},{8,10},{10,12},{12... | collective-permute-start | bytes 983048 | tf_op jit(solution)/shard_map/ppermute | solution.py:20
  32.1 12.6 %collective-permute-start.5 = (f32[5,8,8,128]{3,2,1,0:T(8,128)}, f32[5,8,8,128]{3,2,1,0:T(8,128)S(1)}, u32[]{:S(2)}, u32[]{:S(2)}) collective-permute-start(f32[5,8,8,128]{3,2,1,0:T(8,128)} %get-tuple-element.19), channel_id=1, source_target_pairs={{0,6},{2,0},{4,2},{6,4},{1,7},{3,1},{5,3},{7,5},{8,14},{10,8},{12,... | collective-permute-start | bytes 491528 | tf_op jit(solution)/shard_map/ppermute | solution.py:20
  36.0 6.4 %collective-permute-start.4 = (f32[5,3,16,128]{3,2,1,0:T(8,128)}, f32[5,3,16,128]{3,2,1,0:T(8,128)S(1)}, u32[]{:S(2)}, u32[]{:S(2)}) collective-permute-start(f32[5,3,16,128]{3,2,1,0:T(8,128)} %get-tuple-element.18), channel_id=1, source_target_pairs={{0,8},{8,16},{16,24},{24,0},{1,9},{9,17},{17,25},{25,1},{2,10},{10... | collective-permute-start | bytes 368648 | tf_op jit(solution)/shard_map/ppermute | solution.py:20
  36.0 4.1 %collective-permute-start.3 = (f32[5,2,16,128]{3,2,1,0:T(8,128)}, f32[5,2,16,128]{3,2,1,0:T(8,128)S(1)}, u32[]{:S(2)}, u32[]{:S(2)}) collective-permute-start(f32[5,2,16,128]{3,2,1,0:T(8,128)} %get-tuple-element.17), channel_id=1, source_target_pairs={{0,24},{8,0},{16,8},{24,16},{1,25},{9,1},{17,9},{25,17},{2,26},{10... | collective-permute-start | bytes 245768 | tf_op jit(solution)/shard_map/ppermute | solution.py:20
  37.7 4.7 %collective-permute-start.7 = (f32[2,5,16,128]{3,2,1,0:T(8,128)}, f32[2,5,16,128]{3,2,1,0:T(8,128)S(1)}, u32[]{:S(2)}, u32[]{:S(2)}) collective-permute-start(f32[2,5,16,128]{3,2,1,0:T(8,128)} %get-tuple-element.21), channel_id=1, source_target_pairs={{0,1},{1,0},{2,3},{3,2},{4,5},{5,4},{6,7},{7,6},{8,9},{9,8},{10,11... | collective-permute-start | bytes 245768 | tf_op jit(solution)/shard_map/ppermute | solution.py:20
  40.1 4.6 %copy-start.4 = (f32[5,2,16,128]{3,2,1,0:T(8,128)}, f32[5,2,16,128]{3,2,1,0:T(8,128)S(1)}, u32[]{:S(2)}) copy-start(f32[5,2,16,128]{3,2,1,0:T(8,128)S(1)} %collective-permute-done.3.axl_ref) | copy-start | bytes 245764
  42.4 2.4 %copy-start.5 = (f32[2,5,16,128]{3,2,1,0:T(8,128)}, f32[2,5,16,128]{3,2,1,0:T(8,128)S(1)}, u32[]{:S(2)}) copy-start(f32[2,5,16,128]{3,2,1,0:T(8,128)S(1)} %collective-permute-done.7.az_ref) | copy-start | bytes 245764
  42.4 2.4 %copy-start.2 = (f32[5,3,16,128]{3,2,1,0:T(8,128)}, f32[5,3,16,128]{3,2,1,0:T(8,128)S(1)}, u32[]{:S(2)}) copy-start(f32[5,3,16,128]{3,2,1,0:T(8,128)S(1)} %collective-permute-done.4.axr_ref) | copy-start | bytes 368644
  44.7 0.7 %copy-start.1 = (f32[5,8,8,128]{3,2,1,0:T(8,128)}, f32[5,8,8,128]{3,2,1,0:T(8,128)S(1)}, u32[]{:S(2)}) copy-start(f32[5,8,8,128]{3,2,1,0:T(8,128)S(1)} %collective-permute-done.5.ayl_ref) | copy-start | bytes 491524
  44.7 0.8 %copy-start = (f32[5,16,8,128]{3,2,1,0:T(8,128)}, f32[5,16,8,128]{3,2,1,0:T(8,128)S(1)}, u32[]{:S(2)}) copy-start(f32[5,16,8,128]{3,2,1,0:T(8,128)S(1)} %collective-permute-done.6.ayr_ref) | copy-start | bytes 983044

commit v9 on v5

--- a/solution.py
+++ b/solution.py
@@ -79,9 +79,9 @@
     return tot - wr - wl, wr, wl
 
 
-def stencil_kernel(fp_ref, fm_ref, adj_ref, xf_ref, yf_ref, zf_ref, w_ref,
+def stencil_kernel(fp_ref, fm_ref, adj_ref, adjn_ref, xf_ref, yf_ref, zf_ref, w_ref,
                    sec_ref, xl_ref, xr_ref, yl_ref, yr_ref, zz_ref, acc_ref):
-    nf, nx, ny, nz = adj_ref.shape
+    nf, nx, ny, nz = sec_ref.shape
     i = pl.program_id(0)
     row, lane = iotas(ny, nz)
     row8 = lax.broadcasted_iota(jnp.int32, (8, nz), 0)
@@ -108,15 +108,18 @@
     yl_parts = {}
     for xl in range(XC):
         x = i * XC + xl
-        last = x == nx - 1
-        nxt = jnp.minimum(x + 1, nx - 1)
-        a = [adj_ref[f, x] for f in range(nf)]
-        plus, minus = flux(0, [jnp.where(last, xf_ref[g], adj_ref[g, nxt]) - a[g] for g in range(nf)])
+        a = [adj_ref[f, xl] for f in range(nf)]
+        if xl < XC - 1:
+            an_x = [adj_ref[g, xl + 1] for g in range(nf)]
+        else:
+            last = i == pl.num_programs(0) - 1
+            an_x = [jnp.where(last, xf_ref[g], adjn_ref[g, 0]) for g in range(nf)]
+        plus, minus = flux(0, [an_x[g] - a[g] for g in range(nf)])
         for f in range(nf):
             sx = offset_terms(plus[f], minus[f], lambda s, k: w_ref[0, s, k, f, xl])
             for o in range(6):
                 acc_ref[f, x + o] = acc_ref[f, x + o] + sx[o]
-        a = [adj_ref[f, x] for f in range(nf)]
+        a = [adj_ref[f, xl] for f in range(nf)]
         plus, minus = flux(1, [
             jnp.where(row == ny - 1, yf_ref[g, pl.ds(x, 1), :], pltpu.roll(a[g], ny - 1, 0)) - a[g]
             for g in range(nf)
@@ -124,14 +127,14 @@
         for f in range(nf):
             sy = offset_terms(plus[f], minus[f], lambda s, k: w_ref[1, s, k, f, xl])
             iy, wyr, wyl = split_rows(sy, row8, ny)
-            acc_ref[f, x + 2] = acc_ref[f, x + 2] + iy
+            acc_ref[f, x + 2] = acc_ref[f, x + 2] + (iy + adj_ref[f, xl])
             rear = pltpu.roll(wyr, 4 * (xl % 2), 0)
             lead = pltpu.roll(wyl, (2 + 2 * (xl % 4)) % 8, 0)
             kr = (f, xl // 2)
             kl = (f, xl // 4)
             yr_parts[kr] = rear if kr not in yr_parts else yr_parts[kr] + rear
             yl_parts[kl] = lead if kl not in yl_parts else yl_parts[kl] + lead
-        a = [adj_ref[f, x] for f in range(nf)]
+        a = [adj_ref[f, xl] for f in range(nf)]
         zshift = nz - 1 - x
         plus, minus = flux(2, [
             jnp.where(lane == nz - 1, pltpu.roll(zf_ref[g], zshift, 1), pltpu.roll(a[g], nz - 1, 1)) - a[g]
@@ -152,7 +155,7 @@
     def _():
         def body(x, c):
             for f in range(nf):
-                sec_ref[f, x] = SECTION * (adj_ref[f, x] + acc_ref[f, x + 2])
+                sec_ref[f, x] = SECTION * acc_ref[f, x + 2]
             return c
 
         lax.fori_loop(0, nx, body, 0)
@@ -224,7 +227,8 @@
         in_specs=[
             SMEM,
             SMEM,
-            pl.BlockSpec((nf, nx, ny, nz), const4),
+            pl.BlockSpec((nf, XC, ny, nz), lambda i: (0, i, 0, 0)),
+            pl.BlockSpec((nf, 1, ny, nz), lambda i: (0, jnp.minimum((i + 1) * XC, nx - 1), 0, 0)),
             pl.BlockSpec((nf, ny, nz), const3),
             pl.BlockSpec((nf, nx, nz), const3),
             pl.BlockSpec((nf, ny, nz), const3),
@@ -240,7 +244,7 @@
         ),
         scratch_shapes=[pltpu.VMEM((nf, nx + 5, ny, nz), F32)],
         compiler_params=pltpu.CompilerParams(dimension_semantics=("arbitrary",)),
-    )(flux_plus, flux_minus, adjoint, xf, yf, zf, stencil_weights)
+    )(flux_plus, flux_minus, adjoint, adjoint, xf, yf, zf, stencil_weights)
     axl = shift_from(xl, "gx", -1)
     axr = shift_from(xr, "gx", 1)
     ayl = shift_from(yl, "gy", -1)

time: 61.6 us -> 61.5 us (level)
  no operation moved by 1% of the time
where the time goes in v9:
time: 61.5 us; the launch traced here: 61.1 us
  Pallas kernels  23.2 us (38%)
  starting transfers between devices  14.4 us (23%)
  blocking collectives  10.7 us (17%)
  waiting for transfers between devices  5.21 us (8%)
  local copies, waits for them, and re-layouts  3.31 us (5%)
  matrix products  2.08 us (3%)
  between operations  1.43 us (2%)
  other arithmetic  0.79 us (1%)
    pallas_call x1, Pallas kernels, on_device(): pl.pallas_call(stencil_kernel, grid=(nx // XC,), out_shape=(jax.ShapeDtyp...  17.5 us
    ppermute x8, starting transfers between devices, shift_from(): return lax.ppermute(x, axis, [(i, (i + by) % n) for i in range(n)])  14.4 us
    all_to_all x1, blocking collectives, on_device(): got = lax.all_to_all(t, AXES, 0, 0, tiled=True)  10.7 us
    ppermute x8, waiting for transfers between devices, shift_from(): return lax.ppermute(x, axis, [(i, (i + by) % n) for i in range(n)])  5.21 us
    pallas_call x1, Pallas kernels, on_device(): pl.pallas_call(fix_kernel, out_shape=(jax.ShapeDtypeStruct((nf, nx, ny, n...  3.37 us
    unnamed x26, local copies, waits for them, and re-layouts  3.24 us
    pallas_call x1, Pallas kernels, on_device(): pl.pallas_call(fronts_kernel, out_shape=(jax.ShapeDtypeStruct((nf, ny, nz...  2.35 us
  transfers between devices with their start and end apart: 8, of which 4 were waited for; matrix products, arithmetic and copies ran while one was open for 4% of the time, Pallas kernels for 0%

profile of v9, /device:TPU:0, one launch (start us, length us, event | category | flops | bytes accessed | tf_op | source)
XLA Modules:
  0.0 61.1 jit_solution(7597899735272692151)
XLA Ops:
  0.6 0.0 copy-start.11
  0.6 0.0 copy-start.10
  0.7 0.0 copy-start.8
  0.7 0.0 copy-start.9
  0.7 2.4 %shard_map.104 = (f32[5,16,128]{2,1,0:T(8,128)}, f32[5,32,128]{2,1,0:T(8,128)}, f32[5,16,128]{2,1,0:T(8,128)}) custom-call(f32[5,32,16,128]{3,2,1,0:T(8,128)} %adjn_ref.1), custom_call_target="tpu_custom_call" | custom-call | tf_op jit(solution)/shard_map/pallas_call | solution.py:201
  3.0 5.0 %collective-permute-start.1 = (f32[5,32,128]{2,1,0:T(8,128)}, f32[5,32,128]{2,1,0:T(8,128)S(1)}, u32[]{:S(2)}, u32[]{:S(2)}) collective-permute-start(f32[5,32,128]{2,1,0:T(8,128)} %get-tuple-element.14), channel_id=1, source_target_pairs={{0,6},{2,0},{4,2},{6,4},{1,7},{3,1},{5,3},{7,5},{8,14},{10,8},{12,... | collective-permute-start | bytes 245768 | tf_op jit(solution)/shard_map/ppermute | solution.py:20
  8.1 0.7 %collective-permute-start = (f32[5,16,128]{2,1,0:T(8,128)}, f32[5,16,128]{2,1,0:T(8,128)S(1)}, u32[]{:S(2)}, u32[]{:S(2)}) collective-permute-start(f32[5,16,128]{2,1,0:T(8,128)} %get-tuple-element.13), channel_id=1, source_target_pairs={{0,24},{8,0},{16,8},{24,16},{1,25},{9,1},{17,9},{25,17},{2,26},{10... | collective-permute-start | bytes 122888 | tf_op jit(solution)/shard_map/ppermute | solution.py:20
  8.7 1.5 %collective-permute-start.2 = (f32[5,16,128]{2,1,0:T(8,128)}, f32[5,16,128]{2,1,0:T(8,128)S(1)}, u32[]{:S(2)}, u32[]{:S(2)}) collective-permute-start(f32[5,16,128]{2,1,0:T(8,128)} %get-tuple-element.15), channel_id=1, source_target_pairs={{0,1},{1,0},{2,3},{3,2},{4,5},{5,4},{6,7},{7,6},{8,9},{9,8},{10,11... | collective-permute-start | bytes 122888 | tf_op jit(solution)/shard_map/ppermute | solution.py:20
  10.2 0.0 copy-done.11
  10.2 0.1 reshape.62
  10.3 0.2 convert_reduce_fusion
  10.5 0.1 fusion.16
  10.7 0.3 fusion.2
  11.0 0.0 copy-done.10
  11.0 0.3 fusion.3
  11.3 0.0 copy-done.8
  11.3 0.6 copy.24.fp_ref
  11.9 0.0 copy-done.9
  11.9 0.6 copy.25.fm_ref
  12.5 0.0 collective-permute-done.xf_ref
  12.5 0.0 copy-start.6
  12.5 0.4 collective-permute-done.2.zf_ref
  12.9 0.0 copy-start.7
  12.9 0.0 collective-permute-done.1.yf_ref
  12.9 0.2 copy-done.6
  13.2 0.4 copy-done.7
  13.5 0.0 copy-start.5
  13.5 0.6 %copy-done.5 = f32[5,32,128]{2,1,0:T(8,128)} copy-done((f32[5,32,128]{2,1,0:T(8,128)}, f32[5,32,128]{2,1,0:T(8,128)S(1)}, u32[]{:S(2)}) %copy-start.5) | copy-done | bytes 81944
  14.2 17.5 %shard_map.105 = (f32[5,32,16,128]{3,2,1,0:T(8,128)}, f32[5,2,16,128]{3,2,1,0:T(8,128)}, f32[5,3,16,128]{3,2,1,0:T(8,128)}, f32[5,8,8,128]{3,2,1,0:T(8,128)}, f3...) custom-call(f32[3,5,5]{2,1,0:T(8,128)} %copy.24.fp_ref, f32[3,5,5]{2,1,0:T(8,128)} %copy.25.fm_ref, ...), custom_call_target="tpu_custom_call" | custom-call | tf_op jit(solution)/shard_map/pallas_call | solution.py:216
  31.7 0.1 collective-permute-start.6
  31.8 0.3 fusion.4
  32.1 3.9 %collective-permute-start.5 = (f32[5,8,8,128]{3,2,1,0:T(8,128)}, f32[5,8,8,128]{3,2,1,0:T(8,128)S(1)}, u32[]{:S(2)}, u32[]{:S(2)}) collective-permute-start(f32[5,8,8,128]{3,2,1,0:T(8,128)} %get-tuple-element.19), channel_id=1, source_target_pairs={{0,6},{2,0},{4,2},{6,4},{1,7},{3,1},{5,3},{7,5},{8,14},{10,8},{12,... | collective-permute-start | bytes 491528 | tf_op jit(solution)/shard_map/ppermute | solution.py:20
  36.0 0.0 collective-permute-start.4
  36.0 1.7 %collective-permute-start.3 = (f32[5,2,16,128]{3,2,1,0:T(8,128)}, f32[5,2,16,128]{3,2,1,0:T(8,128)S(1)}, u32[]{:S(2)}, u32[]{:S(2)}) collective-permute-start(f32[5,2,16,128]{3,2,1,0:T(8,128)} %get-tuple-element.17), channel_id=1, source_target_pairs={{0,24},{8,0},{16,8},{24,16},{1,25},{9,1},{17,9},{25,17},{2,26},{10... | collective-permute-start | bytes 245768 | tf_op jit(solution)/shard_map/ppermute | solution.py:20
  37.7 1.5 %collective-permute-start.7 = (f32[2,5,16,128]{3,2,1,0:T(8,128)}, f32[2,5,16,128]{3,2,1,0:T(8,128)S(1)}, u32[]{:S(2)}, u32[]{:S(2)}) collective-permute-start(f32[2,5,16,128]{3,2,1,0:T(8,128)} %get-tuple-element.21), channel_id=1, source_target_pairs={{0,1},{1,0},{2,3},{3,2},{4,5},{5,4},{6,7},{7,6},{8,9},{9,8},{10,11... | collective-permute-start | bytes 245768 | tf_op jit(solution)/shard_map/ppermute | solution.py:20
  39.9 0.2 collective-permute-done.3.axl_ref
  40.1 0.0 copy-start.3
  40.1 2.3 %collective-permute-done.7.az_ref = f32[2,5,16,128]{3,2,1,0:T(8,128)S(1)} collective-permute-done((f32[2,5,16,128]{3,2,1,0:T(8,128)}, f32[2,5,16,128]{3,2,1,0:T(8,128)S(1)}, u32[]{:S(2)}, u32[]{:S(2)}) %collective-permute-start.7) | collective-permute-done | bytes 81952 | tf_op jit(solution)/shard_map/ppermute | solution.py:20
  42.4 0.0 copy-start.4
  42.4 0.0 collective-permute-done.4.axr_ref
  42.4 0.0 copy-start.2
  42.4 2.3 %collective-permute-done.5.ayl_ref = f32[5,8,8,128]{3,2,1,0:T(8,128)S(1)} collective-permute-done((f32[5,8,8,128]{3,2,1,0:T(8,128)}, f32[5,8,8,128]{3,2,1,0:T(8,128)S(1)}, u32[]{:S(2)}, u32[]{:S(2)}) %collective-permute-start.5) | collective-permute-done | bytes 163872 | tf_op jit(solution)/shard_map/ppermute | solution.py:20
  44.7 0.0 copy-start.1
  44.7 0.0 collective-permute-done.6.ayr_ref
  44.7 0.0 copy-start
  44.7 0.0 copy-done.3
  44.7 0.0 copy-done.4
  44.7 0.0 copy-done.2
  44.7 0.6 %copy-done.1 = f32[5,8,8,128]{3,2,1,0:T(8,128)} copy-done((f32[5,8,8,128]{3,2,1,0:T(8,128)}, f32[5,8,8,128]{3,2,1,0:T(8,128)S(1)}, u32[]{:S(2)}) %copy-start.1) | copy-done | bytes 163864
  45.4 0.1 copy-done
  45.5 3.4 %shard_map.106 = (f32[5,32,16,128]{3,2,1,0:T(8,128)}, f32[16,128]{1,0:T(8,128)}) custom-call(s32[16]{0:T(128)} %row_ref.1, s32[1]{0:T(128)S(6)} %copy.38.cnt_ref, f32[5,32,16,128]{3,2,1,0:T(8,128)} %get-tuple-element.16.sec_ref, f32[5,2,16,128]{3,2,1,0:T(8,128)} %copy-done.3, f32[5,3,16,128]{3,2,1,0:T(8,128)} %copy-done.2, ...), custom_call_target="tpu_custom_call", output_to_operand_aliasing={{0}: (2, {})} | custom-call | tf_op jit(solution)/shard_map/pallas_call | solution.py:257
  48.9 1.0 %fusion.6 = f32[32,32,1]{1,0,2:T(8,128)S(1)} fusion(s32[16,128]{1,0:T(8,128)S(1)} %get-tuple-element.26, f32[16,128]{1,0:T(8,128)} %get-tuple-element.23, s32[16,128]{1,0:T(8,128)S(1)} %get-tuple-element.27), kind=kOutput, calls=%fused_computation.12 | convolution fusion | flops 25362432 | bytes 28672 | tf_op jit(solution)/shard_map/rzo,rzk->ok/dot_general | solution.py:290
  49.9 10.7 %all_to_all.9 = f32[32,1,32]{2,1,0:T(1,128)S(1)} all-to-all(f32[32,1,32]{2,1,0:T(1,128)S(1)} %bitcast.20), channel_id=1, replica_groups=mesh['gx'=4,'gy'=4,'gz'=2] {'gx','gy','gz'}, dimensions={0} | all-to-all | bytes 8192 | tf_op jit(solution)/shard_map/all_to_all | solution.py:291
  60.5 0.6 reduce_sum.49
  (2 shorter events, 0.0 us)
Async XLA Ops:
  0.6 9.6 %copy-start.11 = (s32[1024]{0:T(1024)S(1)}, s32[1024]{0:T(1024)}, u32[]{:S(2)}) copy-start(s32[1024]{0:T(1024)} %param.17) | copy-start | bytes 12292
  0.6 10.3 %copy-start.10 = (s32[16,128]{1,0:T(8,128)S(1)}, s32[16,128]{1,0:T(8,128)}, u32[]{:S(2)}) copy-start(s32[16,128]{1,0:T(8,128)} %param.14) | copy-start | bytes 24580
  0.7 10.7 %copy-start.8 = (f32[3,5,5]{2,0,1:T(4,128)S(1)}, f32[3,5,5]{2,0,1:T(4,128)}, u32[]{:S(2)}) copy-start(f32[3,5,5]{2,0,1:T(4,128)} %param.11) | copy-start | bytes 904
  0.7 11.3 %copy-start.9 = (f32[3,5,5]{2,0,1:T(4,128)S(1)}, f32[3,5,5]{2,0,1:T(4,128)}, u32[]{:S(2)}) copy-start(f32[3,5,5]{2,0,1:T(4,128)} %param.12) | copy-start | bytes 904
  3.0 9.9 %collective-permute-start.1 = (f32[5,32,128]{2,1,0:T(8,128)}, f32[5,32,128]{2,1,0:T(8,128)S(1)}, u32[]{:S(2)}, u32[]{:S(2)}) collective-permute-start(f32[5,32,128]{2,1,0:T(8,128)} %get-tuple-element.14), channel_id=1, source_target_pairs={{0,6},{2,0},{4,2},{6,4},{1,7},{3,1},{5,3},{7,5},{8,14},{10,8},{12,... | collective-permute-start | bytes 245768 | tf_op jit(solution)/shard_map/ppermute | solution.py:20
  8.1 4.5 %collective-permute-start = (f32[5,16,128]{2,1,0:T(8,128)}, f32[5,16,128]{2,1,0:T(8,128)S(1)}, u32[]{:S(2)}, u32[]{:S(2)}) collective-permute-start(f32[5,16,128]{2,1,0:T(8,128)} %get-tuple-element.13), channel_id=1, source_target_pairs={{0,24},{8,0},{16,8},{24,16},{1,25},{9,1},{17,9},{25,17},{2,26},{10... | collective-permute-start | bytes 122888 | tf_op jit(solution)/shard_map/ppermute | solution.py:20
  8.7 4.2 %collective-permute-start.2 = (f32[5,16,128]{2,1,0:T(8,128)}, f32[5,16,128]{2,1,0:T(8,128)S(1)}, u32[]{:S(2)}, u32[]{:S(2)}) collective-permute-start(f32[5,16,128]{2,1,0:T(8,128)} %get-tuple-element.15), channel_id=1, source_target_pairs={{0,1},{1,0},{2,3},{3,2},{4,5},{5,4},{6,7},{7,6},{8,9},{9,8},{10,11... | collective-permute-start | bytes 122888 | tf_op jit(solution)/shard_map/ppermute | solution.py:20
  12.5 0.6 %copy-start.6 = (f32[5,16,128]{2,1,0:T(8,128)}, f32[5,16,128]{2,1,0:T(8,128)S(1)}, u32[]{:S(2)}) copy-start(f32[5,16,128]{2,1,0:T(8,128)S(1)} %collective-permute-done.xf_ref) | copy-start | bytes 122884
  12.9 0.6 copy-start.7
  13.5 0.7 %copy-start.5 = (f32[5,32,128]{2,1,0:T(8,128)}, f32[5,32,128]{2,1,0:T(8,128)S(1)}, u32[]{:S(2)}) copy-start(f32[5,32,128]{2,1,0:T(8,128)S(1)} %collective-permute-done.1.yf_ref) | copy-start | bytes 245764
  31.7 13.0 %collective-permute-start.6 = (f32[5,16,8,128]{3,2,1,0:T(8,128)}, f32[5,16,8,128]{3,2,1,0:T(8,128)S(1)}, u32[]{:S(2)}, u32[]{:S(2)}) collective-permute-start(f32[5,16,8,128]{3,2,1,0:T(8,128)} %get-tuple-element.20), channel_id=1, source_target_pairs={{0,2},{2,4},{4,6},{6,0},{1,3},{3,5},{5,7},{7,1},{8,10},{10,12},{12... | collective-permute-start | bytes 983048 | tf_op jit(solution)/shard_map/ppermute | solution.py:20
  32.1 12.6 %collective-permute-start.5 = (f32[5,8,8,128]{3,2,1,0:T(8,128)}, f32[5,8,8,128]{3,2,1,0:T(8,128)S(1)}, u32[]{:S(2)}, u32[]{:S(2)}) collective-permute-start(f32[5,8,8,128]{3,2,1,0:T(8,128)} %get-tuple-element.19), channel_id=1, source_target_pairs={{0,6},{2,0},{4,2},{6,4},{1,7},{3,1},{5,3},{7,5},{8,14},{10,8},{12,... | collective-permute-start | bytes 491528 | tf_op jit(solution)/shard_map/ppermute | solution.py:20
  36.0 6.4 %collective-permute-start.4 = (f32[5,3,16,128]{3,2,1,0:T(8,128)}, f32[5,3,16,128]{3,2,1,0:T(8,128)S(1)}, u32[]{:S(2)}, u32[]{:S(2)}) collective-permute-start(f32[5,3,16,128]{3,2,1,0:T(8,128)} %get-tuple-element.18), channel_id=1, source_target_pairs={{0,8},{8,16},{16,24},{24,0},{1,9},{9,17},{17,25},{25,1},{2,10},{10... | collective-permute-start | bytes 368648 | tf_op jit(solution)/shard_map/ppermute | solution.py:20
  36.0 4.1 %collective-permute-start.3 = (f32[5,2,16,128]{3,2,1,0:T(8,128)}, f32[5,2,16,128]{3,2,1,0:T(8,128)S(1)}, u32[]{:S(2)}, u32[]{:S(2)}) collective-permute-start(f32[5,2,16,128]{3,2,1,0:T(8,128)} %get-tuple-element.17), channel_id=1, source_target_pairs={{0,24},{8,0},{16,8},{24,16},{1,25},{9,1},{17,9},{25,17},{2,26},{10... | collective-permute-start | bytes 245768 | tf_op jit(solution)/shard_map/ppermute | solution.py:20
  37.7 4.7 %collective-permute-start.7 = (f32[2,5,16,128]{3,2,1,0:T(8,128)}, f32[2,5,16,128]{3,2,1,0:T(8,128)S(1)}, u32[]{:S(2)}, u32[]{:S(2)}) collective-permute-start(f32[2,5,16,128]{3,2,1,0:T(8,128)} %get-tuple-element.21), channel_id=1, source_target_pairs={{0,1},{1,0},{2,3},{3,2},{4,5},{5,4},{6,7},{7,6},{8,9},{9,8},{10,11... | collective-permute-start | bytes 245768 | tf_op jit(solution)/shard_map/ppermute | solution.py:20
  40.1 4.6 %copy-start.3 = (f32[5,2,16,128]{3,2,1,0:T(8,128)}, f32[5,2,16,128]{3,2,1,0:T(8,128)S(1)}, u32[]{:S(2)}) copy-start(f32[5,2,16,128]{3,2,1,0:T(8,128)S(1)} %collective-permute-done.3.axl_ref) | copy-start | bytes 245764
  42.4 2.4 %copy-start.4 = (f32[2,5,16,128]{3,2,1,0:T(8,128)}, f32[2,5,16,128]{3,2,1,0:T(8,128)S(1)}, u32[]{:S(2)}) copy-start(f32[2,5,16,128]{3,2,1,0:T(8,128)S(1)} %collective-permute-done.7.az_ref) | copy-start | bytes 245764
  42.4 2.4 %copy-start.2 = (f32[5,3,16,128]{3,2,1,0:T(8,128)}, f32[5,3,16,128]{3,2,1,0:T(8,128)S(1)}, u32[]{:S(2)}) copy-start(f32[5,3,16,128]{3,2,1,0:T(8,128)S(1)} %collective-permute-done.4.axr_ref) | copy-start | bytes 368644
  44.7 0.7 %copy-start.1 = (f32[5,8,8,128]{3,2,1,0:T(8,128)}, f32[5,8,8,128]{3,2,1,0:T(8,128)S(1)}, u32[]{:S(2)}) copy-start(f32[5,8,8,128]{3,2,1,0:T(8,128)S(1)} %collective-permute-done.5.ayl_ref) | copy-start | bytes 491524
  44.7 0.8 %copy-start = (f32[5,16,8,128]{3,2,1,0:T(8,128)}, f32[5,16,8,128]{3,2,1,0:T(8,128)S(1)}, u32[]{:S(2)}) copy-start(f32[5,16,8,128]{3,2,1,0:T(8,128)S(1)} %collective-permute-done.6.ayr_ref) | copy-start | bytes 983044

commit v10 on v5

--- a/solution.py
+++ b/solution.py
@@ -28,16 +28,15 @@
 
 
 def fronts_kernel(adj_ref, xf_ref, yf_ref, zf_ref):
-    nf, nx, ny, nz = adj_ref.shape
+    _, nx, ny, nz = adj_ref.shape
     row, lane = iotas(ny, nz)
-    for f in range(nf):
-        xf_ref[f] = adj_ref[f, 0]
-        zacc = jnp.zeros((ny, nz), F32)
-        for x in range(nx):
-            s = adj_ref[f, x]
-            yf_ref[f, pl.ds(x, 1), :] = s[0:1, :]
-            zacc = zacc + pltpu.roll(jnp.where(lane == 0, s, 0.0), x, 1)
-        zf_ref[f] = zacc
+    xf_ref[0] = adj_ref[0, 0]
+    zacc = jnp.zeros((ny, nz), F32)
+    for x in range(nx):
+        s = adj_ref[0, x]
+        yf_ref[0, pl.ds(x, 1), :] = s[0:1, :]
+        zacc = zacc + pltpu.roll(jnp.where(lane == 0, s, 0.0), x, 1)
+    zf_ref[0] = zacc
 
 
 def offset_terms(plus, minus, w):
@@ -197,13 +196,19 @@
     assert nx % XC == 0 and XC % 4 == 0 and ny == 16 and nx * 4 <= nz
     xf, yf, zf = pl.pallas_call(
         fronts_kernel,
+        grid=(nf,),
         out_shape=(
             jax.ShapeDtypeStruct((nf, ny, nz), F32),
             jax.ShapeDtypeStruct((nf, nx, nz), F32),
             jax.ShapeDtypeStruct((nf, ny, nz), F32),
         ),
-        in_specs=[VMEM],
-        out_specs=(VMEM, VMEM, VMEM),
+        in_specs=[pl.BlockSpec((1, nx, ny, nz), lambda f: (f, 0, 0, 0))],
+        out_specs=(
+            pl.BlockSpec((1, ny, nz), lambda f: (f, 0, 0)),
+            pl.BlockSpec((1, nx, nz), lambda f: (f, 0, 0)),
+            pl.BlockSpec((1, ny, nz), lambda f: (f, 0, 0)),
+        ),
+        compiler_params=pltpu.CompilerParams(dimension_semantics=("arbitrary",)),
     )(adjoint)
     xf = shift_from(xf, "gx", -1)
     yf = shift_from(yf, "gy", -1)

time: 61.6 us -> 63.2 us (1.026)
  Pallas kernels: 23.2 us -> 24.8 us
    pallas_call x1, Pallas kernels: 2.35 us -> 3.92 us  [on_device(): pl.pallas_call(fronts_kernel, grid=(nf,), out_shape=(jax.ShapeDtypeStruct...]
where the time goes in v10:
time: 63.2 us; the launch traced here: 62.7 us
  Pallas kernels  24.8 us (39%)
  starting transfers between devices  14.4 us (23%)
  blocking collectives  10.7 us (17%)
  waiting for transfers between devices  5.2 us (8%)
  local copies, waits for them, and re-layouts  3.31 us (5%)
  matrix products  2.07 us (3%)
  between operations  1.43 us (2%)
  other arithmetic  0.79 us (1%)
    pallas_call x1, Pallas kernels, on_device(): pl.pallas_call(stencil_kernel, grid=(nx // XC,), out_shape=(jax.ShapeDtyp...  17.5 us
    ppermute x8, starting transfers between devices, shift_from(): return lax.ppermute(x, axis, [(i, (i + by) % n) for i in range(n)])  14.4 us
    all_to_all x1, blocking collectives, on_device(): got = lax.all_to_all(t, AXES, 0, 0, tiled=True)  10.7 us
    ppermute x8, waiting for transfers between devices, shift_from(): return lax.ppermute(x, axis, [(i, (i + by) % n) for i in range(n)])  5.2 us
    pallas_call x1, Pallas kernels, on_device(): pl.pallas_call(fronts_kernel, grid=(nf,), out_shape=(jax.ShapeDtypeStruct...  3.92 us
    pallas_call x1, Pallas kernels, on_device(): pl.pallas_call(fix_kernel, out_shape=(jax.ShapeDtypeStruct((nf, nx, ny, n...  3.37 us
    unnamed x26, local copies, waits for them, and re-layouts  3.24 us
  transfers between devices with their start and end apart: 8, of which 4 were waited for; matrix products, arithmetic and copies ran while one was open for 4% of the time, Pallas kernels for 0%

profile of v10, /device:TPU:0, one launch (start us, length us, event | category | flops | bytes accessed | tf_op | source)
XLA Modules:
  0.0 62.7 jit_solution(2688664269735225851)
XLA Ops:
  0.6 0.0 copy-start.11
  0.6 0.0 copy-start.10
  0.7 0.0 copy-start.8
  0.7 0.0 copy-start.9
  0.7 3.9 %shard_map.104 = (f32[5,16,128]{2,1,0:T(8,128)}, f32[5,32,128]{2,1,0:T(8,128)}, f32[5,16,128]{2,1,0:T(8,128)}) custom-call(f32[5,32,16,128]{3,2,1,0:T(8,128)} %adj_ref.3), custom_call_target="tpu_custom_call" | custom-call | tf_op jit(solution)/shard_map/pallas_call | solution.py:197
  4.6 5.0 %collective-permute-start.1 = (f32[5,32,128]{2,1,0:T(8,128)}, f32[5,32,128]{2,1,0:T(8,128)S(1)}, u32[]{:S(2)}, u32[]{:S(2)}) collective-permute-start(f32[5,32,128]{2,1,0:T(8,128)} %get-tuple-element.14), channel_id=1, source_target_pairs={{0,6},{2,0},{4,2},{6,4},{1,7},{3,1},{5,3},{7,5},{8,14},{10,8},{12,... | collective-permute-start | bytes 245768 | tf_op jit(solution)/shard_map/ppermute | solution.py:20
  9.6 0.7 %collective-permute-start = (f32[5,16,128]{2,1,0:T(8,128)}, f32[5,16,128]{2,1,0:T(8,128)S(1)}, u32[]{:S(2)}, u32[]{:S(2)}) collective-permute-start(f32[5,16,128]{2,1,0:T(8,128)} %get-tuple-element.13), channel_id=1, source_target_pairs={{0,24},{8,0},{16,8},{24,16},{1,25},{9,1},{17,9},{25,17},{2,26},{10... | collective-permute-start | bytes 122888 | tf_op jit(solution)/shard_map/ppermute | solution.py:20
  10.3 1.5 %collective-permute-start.2 = (f32[5,16,128]{2,1,0:T(8,128)}, f32[5,16,128]{2,1,0:T(8,128)S(1)}, u32[]{:S(2)}, u32[]{:S(2)}) collective-permute-start(f32[5,16,128]{2,1,0:T(8,128)} %get-tuple-element.15), channel_id=1, source_target_pairs={{0,1},{1,0},{2,3},{3,2},{4,5},{5,4},{6,7},{7,6},{8,9},{9,8},{10,11... | collective-permute-start | bytes 122888 | tf_op jit(solution)/shard_map/ppermute | solution.py:20
  11.8 0.0 copy-done.11
  11.8 0.1 reshape.62
  11.9 0.2 convert_reduce_fusion
  12.1 0.1 fusion.16
  12.2 0.3 fusion.2
  12.5 0.0 copy-done.10
  12.6 0.3 fusion.3
  12.9 0.0 copy-done.8
  12.9 0.6 copy.24.fp_ref
  13.5 0.0 copy-done.9
  13.5 0.6 copy.25.fm_ref
  14.1 0.0 collective-permute-done.xf_ref
  14.1 0.0 copy-start.6
  14.1 0.4 collective-permute-done.2.zf_ref
  14.5 0.0 copy-start.7
  14.5 0.0 collective-permute-done.1.yf_ref
  14.5 0.2 copy-done.6
  14.7 0.4 copy-done.7
  15.1 0.0 copy-start.3
  15.1 0.6 %copy-done.3 = f32[5,32,128]{2,1,0:T(8,128)} copy-done((f32[5,32,128]{2,1,0:T(8,128)}, f32[5,32,128]{2,1,0:T(8,128)S(1)}, u32[]{:S(2)}) %copy-start.3) | copy-done | bytes 81944
  15.8 17.5 %shard_map.105 = (f32[5,32,16,128]{3,2,1,0:T(8,128)}, f32[5,2,16,128]{3,2,1,0:T(8,128)}, f32[5,3,16,128]{3,2,1,0:T(8,128)}, f32[5,8,8,128]{3,2,1,0:T(8,128)}, f3...) custom-call(f32[3,5,5]{2,1,0:T(8,128)} %copy.24.fp_ref, f32[3,5,5]{2,1,0:T(8,128)} %copy.25.fm_ref, ...), custom_call_target="tpu_custom_call" | custom-call | tf_op jit(solution)/shard_map/pallas_call | solution.py:218
  33.3 0.1 collective-permute-start.6
  33.4 0.3 fusion.4
  33.7 3.9 %collective-permute-start.5 = (f32[5,8,8,128]{3,2,1,0:T(8,128)}, f32[5,8,8,128]{3,2,1,0:T(8,128)S(1)}, u32[]{:S(2)}, u32[]{:S(2)}) collective-permute-start(f32[5,8,8,128]{3,2,1,0:T(8,128)} %get-tuple-element.19), channel_id=1, source_target_pairs={{0,6},{2,0},{4,2},{6,4},{1,7},{3,1},{5,3},{7,5},{8,14},{10,8},{12,... | collective-permute-start | bytes 491528 | tf_op jit(solution)/shard_map/ppermute | solution.py:20
  37.6 0.0 collective-permute-start.4
  37.6 1.7 %collective-permute-start.3 = (f32[5,2,16,128]{3,2,1,0:T(8,128)}, f32[5,2,16,128]{3,2,1,0:T(8,128)S(1)}, u32[]{:S(2)}, u32[]{:S(2)}) collective-permute-start(f32[5,2,16,128]{3,2,1,0:T(8,128)} %get-tuple-element.17), channel_id=1, source_target_pairs={{0,24},{8,0},{16,8},{24,16},{1,25},{9,1},{17,9},{25,17},{2,26},{10... | collective-permute-start | bytes 245768 | tf_op jit(solution)/shard_map/ppermute | solution.py:20
  39.3 1.5 %collective-permute-start.7 = (f32[2,5,16,128]{3,2,1,0:T(8,128)}, f32[2,5,16,128]{3,2,1,0:T(8,128)S(1)}, u32[]{:S(2)}, u32[]{:S(2)}) collective-permute-start(f32[2,5,16,128]{3,2,1,0:T(8,128)} %get-tuple-element.21), channel_id=1, source_target_pairs={{0,1},{1,0},{2,3},{3,2},{4,5},{5,4},{6,7},{7,6},{8,9},{9,8},{10,11... | collective-permute-start | bytes 245768 | tf_op jit(solution)/shard_map/ppermute | solution.py:20
  41.5 0.2 collective-permute-done.3.axl_ref
  41.7 0.0 copy-start.4
  41.7 2.3 %collective-permute-done.7.az_ref = f32[2,5,16,128]{3,2,1,0:T(8,128)S(1)} collective-permute-done((f32[2,5,16,128]{3,2,1,0:T(8,128)}, f32[2,5,16,128]{3,2,1,0:T(8,128)S(1)}, u32[]{:S(2)}, u32[]{:S(2)}) %collective-permute-start.7) | collective-permute-done | bytes 81952 | tf_op jit(solution)/shard_map/ppermute | solution.py:20
  44.0 0.0 copy-start.5
  44.0 0.0 collective-permute-done.4.axr_ref
  44.0 0.0 copy-start.2
  44.0 2.3 %collective-permute-done.5.ayl_ref = f32[5,8,8,128]{3,2,1,0:T(8,128)S(1)} collective-permute-done((f32[5,8,8,128]{3,2,1,0:T(8,128)}, f32[5,8,8,128]{3,2,1,0:T(8,128)S(1)}, u32[]{:S(2)}, u32[]{:S(2)}) %collective-permute-start.5) | collective-permute-done | bytes 163872 | tf_op jit(solution)/shard_map/ppermute | solution.py:20
  46.3 0.0 copy-start.1
  46.3 0.0 collective-permute-done.6.ayr_ref
  46.3 0.0 copy-start
  46.3 0.0 copy-done.4
  46.3 0.0 copy-done.5
  46.3 0.0 copy-done.2
  46.3 0.6 %copy-done.1 = f32[5,8,8,128]{3,2,1,0:T(8,128)} copy-done((f32[5,8,8,128]{3,2,1,0:T(8,128)}, f32[5,8,8,128]{3,2,1,0:T(8,128)S(1)}, u32[]{:S(2)}) %copy-start.1) | copy-done | bytes 163864
  47.0 0.1 copy-done
  47.1 3.4 %shard_map.106 = (f32[5,32,16,128]{3,2,1,0:T(8,128)}, f32[16,128]{1,0:T(8,128)}) custom-call(s32[16]{0:T(128)} %row_ref.1, s32[1]{0:T(128)S(6)} %copy.38.cnt_ref, f32[5,32,16,128]{3,2,1,0:T(8,128)} %get-tuple-element.16.sec_ref, f32[5,2,16,128]{3,2,1,0:T(8,128)} %copy-done.4, f32[5,3,16,128]{3,2,1,0:T(8,128)} %copy-done.2, ...), custom_call_target="tpu_custom_call", output_to_operand_aliasing={{0}: (2, {})} | custom-call | tf_op jit(solution)/shard_map/pallas_call | solution.py:258
  50.5 1.0 %fusion.6 = f32[32,32,1]{1,0,2:T(8,128)S(1)} fusion(s32[16,128]{1,0:T(8,128)S(1)} %get-tuple-element.26, f32[16,128]{1,0:T(8,128)} %get-tuple-element.23, s32[16,128]{1,0:T(8,128)S(1)} %get-tuple-element.27), kind=kOutput, calls=%fused_computation.12 | convolution fusion | flops 25362432 | bytes 28672 | tf_op jit(solution)/shard_map/rzo,rzk->ok/dot_general | solution.py:291
  51.5 10.7 %all_to_all.9 = f32[32,1,32]{2,1,0:T(1,128)S(1)} all-to-all(f32[32,1,32]{2,1,0:T(1,128)S(1)} %bitcast.20), channel_id=1, replica_groups=mesh['gx'=4,'gy'=4,'gz'=2] {'gx','gy','gz'}, dimensions={0} | all-to-all | bytes 8192 | tf_op jit(solution)/shard_map/all_to_all | solution.py:292
  62.1 0.6 reduce_sum.49
  (2 shorter events, 0.0 us)
Async XLA Ops:
  0.6 11.2 %copy-start.11 = (s32[1024]{0:T(1024)S(1)}, s32[1024]{0:T(1024)}, u32[]{:S(2)}) copy-start(s32[1024]{0:T(1024)} %param.17) | copy-start | bytes 12292
  0.6 11.9 %copy-start.10 = (s32[16,128]{1,0:T(8,128)S(1)}, s32[16,128]{1,0:T(8,128)}, u32[]{:S(2)}) copy-start(s32[16,128]{1,0:T(8,128)} %param.14) | copy-start | bytes 24580
  0.7 12.3 %copy-start.8 = (f32[3,5,5]{2,0,1:T(4,128)S(1)}, f32[3,5,5]{2,0,1:T(4,128)}, u32[]{:S(2)}) copy-start(f32[3,5,5]{2,0,1:T(4,128)} %param.11) | copy-start | bytes 904
  0.7 12.9 %copy-start.9 = (f32[3,5,5]{2,0,1:T(4,128)S(1)}, f32[3,5,5]{2,0,1:T(4,128)}, u32[]{:S(2)}) copy-start(f32[3,5,5]{2,0,1:T(4,128)} %param.12) | copy-start | bytes 904
  4.6 9.9 %collective-permute-start.1 = (f32[5,32,128]{2,1,0:T(8,128)}, f32[5,32,128]{2,1,0:T(8,128)S(1)}, u32[]{:S(2)}, u32[]{:S(2)}) collective-permute-start(f32[5,32,128]{2,1,0:T(8,128)} %get-tuple-element.14), channel_id=1, source_target_pairs={{0,6},{2,0},{4,2},{6,4},{1,7},{3,1},{5,3},{7,5},{8,14},{10,8},{12,... | collective-permute-start | bytes 245768 | tf_op jit(solution)/shard_map/ppermute | solution.py:20
  9.6 4.5 %collective-permute-start = (f32[5,16,128]{2,1,0:T(8,128)}, f32[5,16,128]{2,1,0:T(8,128)S(1)}, u32[]{:S(2)}, u32[]{:S(2)}) collective-permute-start(f32[5,16,128]{2,1,0:T(8,128)} %get-tuple-element.13), channel_id=1, source_target_pairs={{0,24},{8,0},{16,8},{24,16},{1,25},{9,1},{17,9},{25,17},{2,26},{10... | collective-permute-start | bytes 122888 | tf_op jit(solution)/shard_map/ppermute | solution.py:20
  10.3 4.2 %collective-permute-start.2 = (f32[5,16,128]{2,1,0:T(8,128)}, f32[5,16,128]{2,1,0:T(8,128)S(1)}, u32[]{:S(2)}, u32[]{:S(2)}) collective-permute-start(f32[5,16,128]{2,1,0:T(8,128)} %get-tuple-element.15), channel_id=1, source_target_pairs={{0,1},{1,0},{2,3},{3,2},{4,5},{5,4},{6,7},{7,6},{8,9},{9,8},{10,11... | collective-permute-start | bytes 122888 | tf_op jit(solution)/shard_map/ppermute | solution.py:20
  14.1 0.6 copy-start.6
  14.5 0.6 copy-start.7
  15.1 0.7 %copy-start.3 = (f32[5,32,128]{2,1,0:T(8,128)}, f32[5,32,128]{2,1,0:T(8,128)S(1)}, u32[]{:S(2)}) copy-start(f32[5,32,128]{2,1,0:T(8,128)S(1)} %collective-permute-done.1.yf_ref) | copy-start | bytes 245764
  33.3 13.0 %collective-permute-start.6 = (f32[5,16,8,128]{3,2,1,0:T(8,128)}, f32[5,16,8,128]{3,2,1,0:T(8,128)S(1)}, u32[]{:S(2)}, u32[]{:S(2)}) collective-permute-start(f32[5,16,8,128]{3,2,1,0:T(8,128)} %get-tuple-element.20), channel_id=1, source_target_pairs={{0,2},{2,4},{4,6},{6,0},{1,3},{3,5},{5,7},{7,1},{8,10},{10,12},{12... | collective-permute-start | bytes 983048 | tf_op jit(solution)/shard_map/ppermute | solution.py:20
  33.7 12.6 %collective-permute-start.5 = (f32[5,8,8,128]{3,2,1,0:T(8,128)}, f32[5,8,8,128]{3,2,1,0:T(8,128)S(1)}, u32[]{:S(2)}, u32[]{:S(2)}) collective-permute-start(f32[5,8,8,128]{3,2,1,0:T(8,128)} %get-tuple-element.19), channel_id=1, source_target_pairs={{0,6},{2,0},{4,2},{6,4},{1,7},{3,1},{5,3},{7,5},{8,14},{10,8},{12,... | collective-permute-start | bytes 491528 | tf_op jit(solution)/shard_map/ppermute | solution.py:20
  37.6 6.4 %collective-permute-start.4 = (f32[5,3,16,128]{3,2,1,0:T(8,128)}, f32[5,3,16,128]{3,2,1,0:T(8,128)S(1)}, u32[]{:S(2)}, u32[]{:S(2)}) collective-permute-start(f32[5,3,16,128]{3,2,1,0:T(8,128)} %get-tuple-element.18), channel_id=1, source_target_pairs={{0,8},{8,16},{16,24},{24,0},{1,9},{9,17},{17,25},{25,1},{2,10},{10... | collective-permute-start | bytes 368648 | tf_op jit(solution)/shard_map/ppermute | solution.py:20
  37.6 4.1 %collective-permute-start.3 = (f32[5,2,16,128]{3,2,1,0:T(8,128)}, f32[5,2,16,128]{3,2,1,0:T(8,128)S(1)}, u32[]{:S(2)}, u32[]{:S(2)}) collective-permute-start(f32[5,2,16,128]{3,2,1,0:T(8,128)} %get-tuple-element.17), channel_id=1, source_target_pairs={{0,24},{8,0},{16,8},{24,16},{1,25},{9,1},{17,9},{25,17},{2,26},{10... | collective-permute-start | bytes 245768 | tf_op jit(solution)/shard_map/ppermute | solution.py:20
  39.3 4.7 %collective-permute-start.7 = (f32[2,5,16,128]{3,2,1,0:T(8,128)}, f32[2,5,16,128]{3,2,1,0:T(8,128)S(1)}, u32[]{:S(2)}, u32[]{:S(2)}) collective-permute-start(f32[2,5,16,128]{3,2,1,0:T(8,128)} %get-tuple-element.21), channel_id=1, source_target_pairs={{0,1},{1,0},{2,3},{3,2},{4,5},{5,4},{6,7},{7,6},{8,9},{9,8},{10,11... | collective-permute-start | bytes 245768 | tf_op jit(solution)/shard_map/ppermute | solution.py:20
  41.7 4.6 %copy-start.4 = (f32[5,2,16,128]{3,2,1,0:T(8,128)}, f32[5,2,16,128]{3,2,1,0:T(8,128)S(1)}, u32[]{:S(2)}) copy-start(f32[5,2,16,128]{3,2,1,0:T(8,128)S(1)} %collective-permute-done.3.axl_ref) | copy-start | bytes 245764
  44.0 2.4 %copy-start.5 = (f32[2,5,16,128]{3,2,1,0:T(8,128)}, f32[2,5,16,128]{3,2,1,0:T(8,128)S(1)}, u32[]{:S(2)}) copy-start(f32[2,5,16,128]{3,2,1,0:T(8,128)S(1)} %collective-permute-done.7.az_ref) | copy-start | bytes 245764
  44.0 2.4 %copy-start.2 = (f32[5,3,16,128]{3,2,1,0:T(8,128)}, f32[5,3,16,128]{3,2,1,0:T(8,128)S(1)}, u32[]{:S(2)}) copy-start(f32[5,3,16,128]{3,2,1,0:T(8,128)S(1)} %collective-permute-done.4.axr_ref) | copy-start | bytes 368644
  46.3 0.7 %copy-start.1 = (f32[5,8,8,128]{3,2,1,0:T(8,128)}, f32[5,8,8,128]{3,2,1,0:T(8,128)S(1)}, u32[]{:S(2)}) copy-start(f32[5,8,8,128]{3,2,1,0:T(8,128)S(1)} %collective-permute-done.5.ayl_ref) | copy-start | bytes 491524
  46.3 0.8 %copy-start = (f32[5,16,8,128]{3,2,1,0:T(8,128)}, f32[5,16,8,128]{3,2,1,0:T(8,128)S(1)}, u32[]{:S(2)}) copy-start(f32[5,16,8,128]{3,2,1,0:T(8,128)S(1)} %collective-permute-done.6.ayr_ref) | copy-start | bytes 983044

commit v11 on v5

--- a/solution.py
+++ b/solution.py
@@ -27,10 +27,14 @@
     )
 
 
-def fronts_kernel(adj_ref, xf_ref, yf_ref, zf_ref):
+def fronts_kernel(adj_hbm, xf_ref, yf_ref, zf_ref, adj_ref, sems):
     nf, nx, ny, nz = adj_ref.shape
     row, lane = iotas(ny, nz)
+    copies = [pltpu.make_async_copy(adj_hbm.at[f], adj_ref.at[f], sems.at[f]) for f in range(nf)]
+    for c in copies:
+        c.start()
     for f in range(nf):
+        copies[f].wait()
         xf_ref[f] = adj_ref[f, 0]
         zacc = jnp.zeros((ny, nz), F32)
         for x in range(nx):
@@ -202,8 +206,9 @@
             jax.ShapeDtypeStruct((nf, nx, nz), F32),
             jax.ShapeDtypeStruct((nf, ny, nz), F32),
         ),
-        in_specs=[VMEM],
+        in_specs=[pl.BlockSpec(memory_space=pl.ANY)],
         out_specs=(VMEM, VMEM, VMEM),
+        scratch_shapes=[pltpu.VMEM((nf, nx, ny, nz), F32), pltpu.SemaphoreType.DMA((nf,))],
     )(adjoint)
     xf = shift_from(xf, "gx", -1)
     yf = shift_from(yf, "gy", -1)

time: 61.6 us -> 61.6 us (level)
  no operation moved by 1% of the time
where the time goes in v11:
time: 61.6 us; the launch traced here: 61.1 us
  Pallas kernels  23.2 us (38%)
  starting transfers between devices  14.4 us (23%)
  blocking collectives  10.7 us (17%)
  waiting for transfers between devices  5.21 us (8%)
  local copies, waits for them, and re-layouts  3.31 us (5%)
  matrix products  2.08 us (3%)
  between operations  1.43 us (2%)
  other arithmetic  0.79 us (1%)
    pallas_call x1, Pallas kernels, on_device(): pl.pallas_call(stencil_kernel, grid=(nx // XC,), out_shape=(jax.ShapeDtyp...  17.5 us
    ppermute x8, starting transfers between devices, shift_from(): return lax.ppermute(x, axis, [(i, (i + by) % n) for i in range(n)])  14.4 us
    all_to_all x1, blocking collectives, on_device(): got = lax.all_to_all(t, AXES, 0, 0, tiled=True)  10.7 us
    ppermute x8, waiting for transfers between devices, shift_from(): return lax.ppermute(x, axis, [(i, (i + by) % n) for i in range(n)])  5.21 us
    pallas_call x1, Pallas kernels, on_device(): pl.pallas_call(fix_kernel, out_shape=(jax.ShapeDtypeStruct((nf, nx, ny, n...  3.37 us
    unnamed x26, local copies, waits for them, and re-layouts  3.24 us
    pallas_call x1, Pallas kernels, on_device(): pl.pallas_call(fronts_kernel, out_shape=(jax.ShapeDtypeStruct((nf, ny, nz...  2.31 us
  transfers between devices with their start and end apart: 8, of which 4 were waited for; matrix products, arithmetic and copies ran while one was open for 4% of the time, Pallas kernels for 0%

profile of v11, /device:TPU:0, one launch (start us, length us, event | category | flops | bytes accessed | tf_op | source)
XLA Modules:
  0.0 61.1 jit_solution(18438140990270269370)
XLA Ops:
  0.6 0.0 copy-start.11
  0.6 0.0 copy-start.10
  0.7 0.0 copy-start.8
  0.7 0.0 copy-start.9
  0.7 2.3 %shard_map.104 = (f32[5,16,128]{2,1,0:T(8,128)}, f32[5,32,128]{2,1,0:T(8,128)}, f32[5,16,128]{2,1,0:T(8,128)}) custom-call(f32[5,32,16,128]{3,2,1,0:T(8,128)} %adj_ref.1), custom_call_target="tpu_custom_call" | custom-call | tf_op jit(solution)/shard_map/pallas_call | solution.py:202
  3.0 5.1 %collective-permute-start.1 = (f32[5,32,128]{2,1,0:T(8,128)}, f32[5,32,128]{2,1,0:T(8,128)S(1)}, u32[]{:S(2)}, u32[]{:S(2)}) collective-permute-start(f32[5,32,128]{2,1,0:T(8,128)} %get-tuple-element.14), channel_id=1, source_target_pairs={{0,6},{2,0},{4,2},{6,4},{1,7},{3,1},{5,3},{7,5},{8,14},{10,8},{12,... | collective-permute-start | bytes 245768 | tf_op jit(solution)/shard_map/ppermute | solution.py:20
  8.1 0.7 %collective-permute-start = (f32[5,16,128]{2,1,0:T(8,128)}, f32[5,16,128]{2,1,0:T(8,128)S(1)}, u32[]{:S(2)}, u32[]{:S(2)}) collective-permute-start(f32[5,16,128]{2,1,0:T(8,128)} %get-tuple-element.13), channel_id=1, source_target_pairs={{0,24},{8,0},{16,8},{24,16},{1,25},{9,1},{17,9},{25,17},{2,26},{10... | collective-permute-start | bytes 122888 | tf_op jit(solution)/shard_map/ppermute | solution.py:20
  8.7 1.5 %collective-permute-start.2 = (f32[5,16,128]{2,1,0:T(8,128)}, f32[5,16,128]{2,1,0:T(8,128)S(1)}, u32[]{:S(2)}, u32[]{:S(2)}) collective-permute-start(f32[5,16,128]{2,1,0:T(8,128)} %get-tuple-element.15), channel_id=1, source_target_pairs={{0,1},{1,0},{2,3},{3,2},{4,5},{5,4},{6,7},{7,6},{8,9},{9,8},{10,11... | collective-permute-start | bytes 122888 | tf_op jit(solution)/shard_map/ppermute | solution.py:20
  10.3 0.0 copy-done.11
  10.3 0.1 reshape.62
  10.3 0.2 convert_reduce_fusion
  10.6 0.1 fusion.16
  10.7 0.3 fusion.2
  11.0 0.0 copy-done.10
  11.0 0.3 fusion.3
  11.4 0.0 copy-done.8
  11.4 0.6 copy.24.fp_ref
  12.0 0.0 copy-done.9
  12.0 0.6 copy.25.fm_ref
  12.6 0.0 collective-permute-done.xf_ref
  12.6 0.0 copy-start.6
  12.6 0.4 collective-permute-done.2.zf_ref
  12.9 0.0 copy-start.7
  13.0 0.0 collective-permute-done.1.yf_ref
  13.0 0.2 copy-done.6
  13.2 0.4 copy-done.7
  13.6 0.0 copy-start.3
  13.6 0.6 %copy-done.3 = f32[5,32,128]{2,1,0:T(8,128)} copy-done((f32[5,32,128]{2,1,0:T(8,128)}, f32[5,32,128]{2,1,0:T(8,128)S(1)}, u32[]{:S(2)}) %copy-start.3) | copy-done | bytes 81944
  14.2 17.5 %shard_map.105 = (f32[5,32,16,128]{3,2,1,0:T(8,128)}, f32[5,2,16,128]{3,2,1,0:T(8,128)}, f32[5,3,16,128]{3,2,1,0:T(8,128)}, f32[5,8,8,128]{3,2,1,0:T(8,128)}, f3...) custom-call(f32[3,5,5]{2,1,0:T(8,128)} %copy.24.fp_ref, f32[3,5,5]{2,1,0:T(8,128)} %copy.25.fm_ref, ...), custom_call_target="tpu_custom_call" | custom-call | tf_op jit(solution)/shard_map/pallas_call | solution.py:218
  31.7 0.1 collective-permute-start.6
  31.8 0.3 fusion.4
  32.1 3.9 %collective-permute-start.5 = (f32[5,8,8,128]{3,2,1,0:T(8,128)}, f32[5,8,8,128]{3,2,1,0:T(8,128)S(1)}, u32[]{:S(2)}, u32[]{:S(2)}) collective-permute-start(f32[5,8,8,128]{3,2,1,0:T(8,128)} %get-tuple-element.19), channel_id=1, source_target_pairs={{0,6},{2,0},{4,2},{6,4},{1,7},{3,1},{5,3},{7,5},{8,14},{10,8},{12,... | collective-permute-start | bytes 491528 | tf_op jit(solution)/shard_map/ppermute | solution.py:20
  36.0 0.0 collective-permute-start.4
  36.0 1.7 %collective-permute-start.3 = (f32[5,2,16,128]{3,2,1,0:T(8,128)}, f32[5,2,16,128]{3,2,1,0:T(8,128)S(1)}, u32[]{:S(2)}, u32[]{:S(2)}) collective-permute-start(f32[5,2,16,128]{3,2,1,0:T(8,128)} %get-tuple-element.17), channel_id=1, source_target_pairs={{0,24},{8,0},{16,8},{24,16},{1,25},{9,1},{17,9},{25,17},{2,26},{10... | collective-permute-start | bytes 245768 | tf_op jit(solution)/shard_map/ppermute | solution.py:20
  37.7 1.5 %collective-permute-start.7 = (f32[2,5,16,128]{3,2,1,0:T(8,128)}, f32[2,5,16,128]{3,2,1,0:T(8,128)S(1)}, u32[]{:S(2)}, u32[]{:S(2)}) collective-permute-start(f32[2,5,16,128]{3,2,1,0:T(8,128)} %get-tuple-element.21), channel_id=1, source_target_pairs={{0,1},{1,0},{2,3},{3,2},{4,5},{5,4},{6,7},{7,6},{8,9},{9,8},{10,11... | collective-permute-start | bytes 245768 | tf_op jit(solution)/shard_map/ppermute | solution.py:20
  39.9 0.2 collective-permute-done.3.axl_ref
  40.1 0.0 copy-start.4
  40.1 2.3 %collective-permute-done.7.az_ref = f32[2,5,16,128]{3,2,1,0:T(8,128)S(1)} collective-permute-done((f32[2,5,16,128]{3,2,1,0:T(8,128)}, f32[2,5,16,128]{3,2,1,0:T(8,128)S(1)}, u32[]{:S(2)}, u32[]{:S(2)}) %collective-permute-start.7) | collective-permute-done | bytes 81952 | tf_op jit(solution)/shard_map/ppermute | solution.py:20
  42.4 0.0 copy-start.5
  42.4 0.0 collective-permute-done.4.axr_ref
  42.4 0.0 copy-start.2
  42.4 2.3 %collective-permute-done.5.ayl_ref = f32[5,8,8,128]{3,2,1,0:T(8,128)S(1)} collective-permute-done((f32[5,8,8,128]{3,2,1,0:T(8,128)}, f32[5,8,8,128]{3,2,1,0:T(8,128)S(1)}, u32[]{:S(2)}, u32[]{:S(2)}) %collective-permute-start.5) | collective-permute-done | bytes 163872 | tf_op jit(solution)/shard_map/ppermute | solution.py:20
  44.7 0.0 copy-start.1
  44.7 0.0 collective-permute-done.6.ayr_ref
  44.7 0.0 copy-start
  44.8 0.0 copy-done.4
  44.8 0.0 copy-done.5
  44.8 0.0 copy-done.2
  44.8 0.6 %copy-done.1 = f32[5,8,8,128]{3,2,1,0:T(8,128)} copy-done((f32[5,8,8,128]{3,2,1,0:T(8,128)}, f32[5,8,8,128]{3,2,1,0:T(8,128)S(1)}, u32[]{:S(2)}) %copy-start.1) | copy-done | bytes 163864
  45.4 0.1 copy-done
  45.5 3.4 %shard_map.106 = (f32[5,32,16,128]{3,2,1,0:T(8,128)}, f32[16,128]{1,0:T(8,128)}) custom-call(s32[16]{0:T(128)} %row_ref.1, s32[1]{0:T(128)S(6)} %copy.38.cnt_ref, f32[5,32,16,128]{3,2,1,0:T(8,128)} %get-tuple-element.16.sec_ref, f32[5,2,16,128]{3,2,1,0:T(8,128)} %copy-done.4, f32[5,3,16,128]{3,2,1,0:T(8,128)} %copy-done.2, ...), custom_call_target="tpu_custom_call", output_to_operand_aliasing={{0}: (2, {})} | custom-call | tf_op jit(solution)/shard_map/pallas_call | solution.py:258
  48.9 1.0 %fusion.6 = f32[32,32,1]{1,0,2:T(8,128)S(1)} fusion(s32[16,128]{1,0:T(8,128)S(1)} %get-tuple-element.26, f32[16,128]{1,0:T(8,128)} %get-tuple-element.23, s32[16,128]{1,0:T(8,128)S(1)} %get-tuple-element.27), kind=kOutput, calls=%fused_computation.12 | convolution fusion | flops 25362432 | bytes 28672 | tf_op jit(solution)/shard_map/rzo,rzk->ok/dot_general | solution.py:291
  49.9 10.7 %all_to_all.9 = f32[32,1,32]{2,1,0:T(1,128)S(1)} all-to-all(f32[32,1,32]{2,1,0:T(1,128)S(1)} %bitcast.20), channel_id=1, replica_groups=mesh['gx'=4,'gy'=4,'gz'=2] {'gx','gy','gz'}, dimensions={0} | all-to-all | bytes 8192 | tf_op jit(solution)/shard_map/all_to_all | solution.py:292
  60.6 0.6 reduce_sum.49
  (2 shorter events, 0.0 us)
Async XLA Ops:
  0.6 9.6 %copy-start.11 = (s32[1024]{0:T(1024)S(1)}, s32[1024]{0:T(1024)}, u32[]{:S(2)}) copy-start(s32[1024]{0:T(1024)} %param.17) | copy-start | bytes 12292
  0.6 10.3 %copy-start.10 = (s32[16,128]{1,0:T(8,128)S(1)}, s32[16,128]{1,0:T(8,128)}, u32[]{:S(2)}) copy-start(s32[16,128]{1,0:T(8,128)} %param.14) | copy-start | bytes 24580
  0.7 10.7 %copy-start.8 = (f32[3,5,5]{2,0,1:T(4,128)S(1)}, f32[3,5,5]{2,0,1:T(4,128)}, u32[]{:S(2)}) copy-start(f32[3,5,5]{2,0,1:T(4,128)} %param.11) | copy-start | bytes 904
  0.7 11.3 %copy-start.9 = (f32[3,5,5]{2,0,1:T(4,128)S(1)}, f32[3,5,5]{2,0,1:T(4,128)}, u32[]{:S(2)}) copy-start(f32[3,5,5]{2,0,1:T(4,128)} %param.12) | copy-start | bytes 904
  3.0 10.0 %collective-permute-start.1 = (f32[5,32,128]{2,1,0:T(8,128)}, f32[5,32,128]{2,1,0:T(8,128)S(1)}, u32[]{:S(2)}, u32[]{:S(2)}) collective-permute-start(f32[5,32,128]{2,1,0:T(8,128)} %get-tuple-element.14), channel_id=1, source_target_pairs={{0,6},{2,0},{4,2},{6,4},{1,7},{3,1},{5,3},{7,5},{8,14},{10,8},{12,... | collective-permute-start | bytes 245768 | tf_op jit(solution)/shard_map/ppermute | solution.py:20
  8.1 4.5 %collective-permute-start = (f32[5,16,128]{2,1,0:T(8,128)}, f32[5,16,128]{2,1,0:T(8,128)S(1)}, u32[]{:S(2)}, u32[]{:S(2)}) collective-permute-start(f32[5,16,128]{2,1,0:T(8,128)} %get-tuple-element.13), channel_id=1, source_target_pairs={{0,24},{8,0},{16,8},{24,16},{1,25},{9,1},{17,9},{25,17},{2,26},{10... | collective-permute-start | bytes 122888 | tf_op jit(solution)/shard_map/ppermute | solution.py:20
  8.7 4.2 %collective-permute-start.2 = (f32[5,16,128]{2,1,0:T(8,128)}, f32[5,16,128]{2,1,0:T(8,128)S(1)}, u32[]{:S(2)}, u32[]{:S(2)}) collective-permute-start(f32[5,16,128]{2,1,0:T(8,128)} %get-tuple-element.15), channel_id=1, source_target_pairs={{0,1},{1,0},{2,3},{3,2},{4,5},{5,4},{6,7},{7,6},{8,9},{9,8},{10,11... | collective-permute-start | bytes 122888 | tf_op jit(solution)/shard_map/ppermute | solution.py:20
  12.6 0.6 %copy-start.6 = (f32[5,16,128]{2,1,0:T(8,128)}, f32[5,16,128]{2,1,0:T(8,128)S(1)}, u32[]{:S(2)}) copy-start(f32[5,16,128]{2,1,0:T(8,128)S(1)} %collective-permute-done.xf_ref) | copy-start | bytes 122884
  12.9 0.6 copy-start.7
  13.6 0.7 %copy-start.3 = (f32[5,32,128]{2,1,0:T(8,128)}, f32[5,32,128]{2,1,0:T(8,128)S(1)}, u32[]{:S(2)}) copy-start(f32[5,32,128]{2,1,0:T(8,128)S(1)} %collective-permute-done.1.yf_ref) | copy-start | bytes 245764
  31.7 13.0 %collective-permute-start.6 = (f32[5,16,8,128]{3,2,1,0:T(8,128)}, f32[5,16,8,128]{3,2,1,0:T(8,128)S(1)}, u32[]{:S(2)}, u32[]{:S(2)}) collective-permute-start(f32[5,16,8,128]{3,2,1,0:T(8,128)} %get-tuple-element.20), channel_id=1, source_target_pairs={{0,2},{2,4},{4,6},{6,0},{1,3},{3,5},{5,7},{7,1},{8,10},{10,12},{12... | collective-permute-start | bytes 983048 | tf_op jit(solution)/shard_map/ppermute | solution.py:20
  32.1 12.6 %collective-permute-start.5 = (f32[5,8,8,128]{3,2,1,0:T(8,128)}, f32[5,8,8,128]{3,2,1,0:T(8,128)S(1)}, u32[]{:S(2)}, u32[]{:S(2)}) collective-permute-start(f32[5,8,8,128]{3,2,1,0:T(8,128)} %get-tuple-element.19), channel_id=1, source_target_pairs={{0,6},{2,0},{4,2},{6,4},{1,7},{3,1},{5,3},{7,5},{8,14},{10,8},{12,... | collective-permute-start | bytes 491528 | tf_op jit(solution)/shard_map/ppermute | solution.py:20
  36.0 6.4 %collective-permute-start.4 = (f32[5,3,16,128]{3,2,1,0:T(8,128)}, f32[5,3,16,128]{3,2,1,0:T(8,128)S(1)}, u32[]{:S(2)}, u32[]{:S(2)}) collective-permute-start(f32[5,3,16,128]{3,2,1,0:T(8,128)} %get-tuple-element.18), channel_id=1, source_target_pairs={{0,8},{8,16},{16,24},{24,0},{1,9},{9,17},{17,25},{25,1},{2,10},{10... | collective-permute-start | bytes 368648 | tf_op jit(solution)/shard_map/ppermute | solution.py:20
  36.0 4.1 %collective-permute-start.3 = (f32[5,2,16,128]{3,2,1,0:T(8,128)}, f32[5,2,16,128]{3,2,1,0:T(8,128)S(1)}, u32[]{:S(2)}, u32[]{:S(2)}) collective-permute-start(f32[5,2,16,128]{3,2,1,0:T(8,128)} %get-tuple-element.17), channel_id=1, source_target_pairs={{0,24},{8,0},{16,8},{24,16},{1,25},{9,1},{17,9},{25,17},{2,26},{10... | collective-permute-start | bytes 245768 | tf_op jit(solution)/shard_map/ppermute | solution.py:20
  37.7 4.7 %collective-permute-start.7 = (f32[2,5,16,128]{3,2,1,0:T(8,128)}, f32[2,5,16,128]{3,2,1,0:T(8,128)S(1)}, u32[]{:S(2)}, u32[]{:S(2)}) collective-permute-start(f32[2,5,16,128]{3,2,1,0:T(8,128)} %get-tuple-element.21), channel_id=1, source_target_pairs={{0,1},{1,0},{2,3},{3,2},{4,5},{5,4},{6,7},{7,6},{8,9},{9,8},{10,11... | collective-permute-start | bytes 245768 | tf_op jit(solution)/shard_map/ppermute | solution.py:20
  40.1 4.6 %copy-start.4 = (f32[5,2,16,128]{3,2,1,0:T(8,128)}, f32[5,2,16,128]{3,2,1,0:T(8,128)S(1)}, u32[]{:S(2)}) copy-start(f32[5,2,16,128]{3,2,1,0:T(8,128)S(1)} %collective-permute-done.3.axl_ref) | copy-start | bytes 245764
  42.4 2.4 %copy-start.5 = (f32[2,5,16,128]{3,2,1,0:T(8,128)}, f32[2,5,16,128]{3,2,1,0:T(8,128)S(1)}, u32[]{:S(2)}) copy-start(f32[2,5,16,128]{3,2,1,0:T(8,128)S(1)} %collective-permute-done.7.az_ref) | copy-start | bytes 245764
  42.4 2.4 %copy-start.2 = (f32[5,3,16,128]{3,2,1,0:T(8,128)}, f32[5,3,16,128]{3,2,1,0:T(8,128)S(1)}, u32[]{:S(2)}) copy-start(f32[5,3,16,128]{3,2,1,0:T(8,128)S(1)} %collective-permute-done.4.axr_ref) | copy-start | bytes 368644
  44.7 0.7 %copy-start.1 = (f32[5,8,8,128]{3,2,1,0:T(8,128)}, f32[5,8,8,128]{3,2,1,0:T(8,128)S(1)}, u32[]{:S(2)}) copy-start(f32[5,8,8,128]{3,2,1,0:T(8,128)S(1)} %collective-permute-done.5.ayl_ref) | copy-start | bytes 491524
  44.7 0.8 %copy-start = (f32[5,16,8,128]{3,2,1,0:T(8,128)}, f32[5,16,8,128]{3,2,1,0:T(8,128)S(1)}, u32[]{:S(2)}) copy-start(f32[5,16,8,128]{3,2,1,0:T(8,128)S(1)} %collective-permute-done.6.ayr_ref) | copy-start | bytes 983044

commit v12 on v5

--- a/solution.py
+++ b/solution.py
@@ -13,6 +13,7 @@
 HI = lax.Precision.HIGHEST
 VMEM = pl.BlockSpec(memory_space=pltpu.VMEM)
 SMEM = pl.BlockSpec(memory_space=pltpu.SMEM)
+HBM = pl.BlockSpec(memory_space=pltpu.HBM)
 
 
 def shift_from(x, axis, by):
@@ -161,24 +162,33 @@
             xr_ref[f] = acc_ref[f, nx + 2:nx + 5]
 
 
-def fix_kernel(row_ref, cnt_ref, sec_ref, axl_ref, axr_ref, ayl_ref, ayr_ref, az_ref,
-               coef_ref, out_ref, wt_ref):
-    nf, nx, ny, nz = sec_ref.shape
+def fix_kernel(row_ref, cnt_ref, sec_hbm, axl_ref, axr_ref, ayl_ref, ayr_ref, az_ref,
+               coef_ref, out_hbm, wt_ref, buf, in_sems, out_sems):
+    nf, nx, ny, nz = buf.shape
+    nch = nx // XC
+    chunk = lambda ref, c: ref.at[:, pl.ds(c * XC, XC)]
+    loads = [pltpu.make_async_copy(chunk(sec_hbm, c), chunk(buf, c), in_sems.at[c]) for c in range(nch)]
+    stores = [pltpu.make_async_copy(chunk(buf, c), chunk(out_hbm, c), out_sems.at[c]) for c in range(nch)]
+    for cp in loads:
+        cp.start()
     row, lane = iotas(ny, nz)
     pad = jnp.zeros((ny - 8, nz), F32)
-    for x in range(nx):
-        for f in range(nf):
-            ty = jnp.concatenate([ayr_ref[f, x // 2], pad], 0)
-            add = jnp.where(row < 3, pltpu.roll(ty, (ny - 4 * (x % 2)) % ny, 0), 0.0)
-            ty = jnp.concatenate([ayl_ref[f, x // 4], pad], 0)
-            add = add + jnp.where(row >= ny - 2, pltpu.roll(ty, (ny - 2 - 2 * (x % 4)) % ny, 0), 0.0)
-            add = add + jnp.where(lane < 3, pltpu.roll(az_ref[1, f], (nz - 4 * x) % nz, 1), 0.0)
-            add = add + jnp.where(lane >= nz - 2, pltpu.roll(az_ref[0, f], (nz - 2 - 4 * x) % nz, 1), 0.0)
-            if x < 3:
-                add = add + axr_ref[f, x]
-            if x >= nx - 2:
-                add = add + axl_ref[f, x - (nx - 2)]
-            out_ref[f, x] = sec_ref[f, x] + SECTION * add
+    for c in range(nch):
+        loads[c].wait()
+        for x in range(c * XC, (c + 1) * XC):
+            for f in range(nf):
+                ty = jnp.concatenate([ayr_ref[f, x // 2], pad], 0)
+                add = jnp.where(row < 3, pltpu.roll(ty, (ny - 4 * (x % 2)) % ny, 0), 0.0)
+                ty = jnp.concatenate([ayl_ref[f, x // 4], pad], 0)
+                add = add + jnp.where(row >= ny - 2, pltpu.roll(ty, (ny - 2 - 2 * (x % 4)) % ny, 0), 0.0)
+                add = add + jnp.where(lane < 3, pltpu.roll(az_ref[1, f], (nz - 4 * x) % nz, 1), 0.0)
+                add = add + jnp.where(lane >= nz - 2, pltpu.roll(az_ref[0, f], (nz - 2 - 4 * x) % nz, 1), 0.0)
+                if x < 3:
+                    add = add + axr_ref[f, x]
+                if x >= nx - 2:
+                    add = add + axl_ref[f, x - (nx - 2)]
+                buf[f, x] = buf[f, x] + SECTION * add
+        stores[c].start()
     live_n = cnt_ref[0]
     for r in range(wt_ref.shape[0]):
         idx = row_ref[r]
@@ -186,9 +196,11 @@
         ly = idx % ny
         val = None
         for f in range(nf):
-            v = out_ref[f, lx, pl.ds(ly, 1), :] * coef_ref[f, pl.ds(r, 1), :]
+            v = buf[f, lx, pl.ds(ly, 1), :] * coef_ref[f, pl.ds(r, 1), :]
             val = v if val is None else val + v
         wt_ref[pl.ds(r, 1), :] = val * jnp.where(r < live_n, 1.0, 0.0).astype(F32)
+    for cp in stores:
+        cp.wait()
 
 
 def on_device(ndev, adjoint, stencil_weights, flux_plus, flux_minus, wall_row, wall_panel, wall_coef,
@@ -256,8 +268,13 @@
             jax.ShapeDtypeStruct((nf, nx, ny, nz), F32),
             jax.ShapeDtypeStruct((nr, nz), F32),
         ),
-        in_specs=[SMEM, SMEM] + [VMEM] * 7,
-        out_specs=(VMEM, VMEM),
+        in_specs=[SMEM, SMEM, HBM] + [VMEM] * 6,
+        out_specs=(HBM, VMEM),
+        scratch_shapes=[
+            pltpu.VMEM((nf, nx, ny, nz), F32),
+            pltpu.SemaphoreType.DMA((nx // XC,)),
+            pltpu.SemaphoreType.DMA((nx // XC,)),
+        ],
         input_output_aliases={2: 0},
     )(wall_row, wall_count, sec, axl, axr, ayl, ayr, az, wall_coef)
 

time: 61.6 us -> 63 us (1.023)
  Pallas kernels: 23.2 us -> 24.6 us
    pallas_call x1, Pallas kernels: 3.37 us -> 4.7 us  [on_device(): pl.pallas_call(fix_kernel, out_shape=(jax.ShapeDtypeStruct((nf, nx, ny, n...]
where the time goes in v12:
time: 63 us; the launch traced here: 62.5 us
  Pallas kernels  24.6 us (39%)
  starting transfers between devices  14.4 us (23%)
  blocking collectives  10.7 us (17%)
  waiting for transfers between devices  5.2 us (8%)
  local copies, waits for them, and re-layouts  3.31 us (5%)
  matrix products  2.08 us (3%)
  between operations  1.43 us (2%)
  other arithmetic  0.79 us (1%)
    pallas_call x1, Pallas kernels, on_device(): pl.pallas_call(stencil_kernel, grid=(nx // XC,), out_shape=(jax.ShapeDtyp...  17.5 us
    ppermute x8, starting transfers between devices, shift_from(): return lax.ppermute(x, axis, [(i, (i + by) % n) for i in range(n)])  14.4 us
    all_to_all x1, blocking collectives, on_device(): got = lax.all_to_all(t, AXES, 0, 0, tiled=True)  10.7 us
    ppermute x8, waiting for transfers between devices, shift_from(): return lax.ppermute(x, axis, [(i, (i + by) % n) for i in range(n)])  5.2 us
    pallas_call x1, Pallas kernels, on_device(): pl.pallas_call(fix_kernel, out_shape=(jax.ShapeDtypeStruct((nf, nx, ny, n...  4.7 us
    unnamed x26, local copies, waits for them, and re-layouts  3.24 us
    pallas_call x1, Pallas kernels, on_device(): pl.pallas_call(fronts_kernel, out_shape=(jax.ShapeDtypeStruct((nf, ny, nz...  2.35 us
  transfers between devices with their start and end apart: 8, of which 4 were waited for; matrix products, arithmetic and copies ran while one was open for 4% of the time, Pallas kernels for 0%

profile of v12, /device:TPU:0, one launch (start us, length us, event | category | flops | bytes accessed | tf_op | source)
XLA Modules:
  0.0 62.5 jit_solution(9296040287932521562)
XLA Ops:
  0.6 0.0 copy-start.11
  0.6 0.0 copy-start.10
  0.7 0.0 copy-start.8
  0.7 0.0 copy-start.9
  0.7 2.4 %shard_map.104 = (f32[5,16,128]{2,1,0:T(8,128)}, f32[5,32,128]{2,1,0:T(8,128)}, f32[5,16,128]{2,1,0:T(8,128)}) custom-call(f32[5,32,16,128]{3,2,1,0:T(8,128)} %adj_ref.3), custom_call_target="tpu_custom_call" | custom-call | tf_op jit(solution)/shard_map/pallas_call | solution.py:210
  3.0 5.0 %collective-permute-start.1 = (f32[5,32,128]{2,1,0:T(8,128)}, f32[5,32,128]{2,1,0:T(8,128)S(1)}, u32[]{:S(2)}, u32[]{:S(2)}) collective-permute-start(f32[5,32,128]{2,1,0:T(8,128)} %get-tuple-element.14), channel_id=1, source_target_pairs={{0,6},{2,0},{4,2},{6,4},{1,7},{3,1},{5,3},{7,5},{8,14},{10,8},{12,... | collective-permute-start | bytes 245768 | tf_op jit(solution)/shard_map/ppermute | solution.py:21
  8.1 0.7 %collective-permute-start = (f32[5,16,128]{2,1,0:T(8,128)}, f32[5,16,128]{2,1,0:T(8,128)S(1)}, u32[]{:S(2)}, u32[]{:S(2)}) collective-permute-start(f32[5,16,128]{2,1,0:T(8,128)} %get-tuple-element.13), channel_id=1, source_target_pairs={{0,24},{8,0},{16,8},{24,16},{1,25},{9,1},{17,9},{25,17},{2,26},{10... | collective-permute-start | bytes 122888 | tf_op jit(solution)/shard_map/ppermute | solution.py:21
  8.7 1.5 %collective-permute-start.2 = (f32[5,16,128]{2,1,0:T(8,128)}, f32[5,16,128]{2,1,0:T(8,128)S(1)}, u32[]{:S(2)}, u32[]{:S(2)}) collective-permute-start(f32[5,16,128]{2,1,0:T(8,128)} %get-tuple-element.15), channel_id=1, source_target_pairs={{0,1},{1,0},{2,3},{3,2},{4,5},{5,4},{6,7},{7,6},{8,9},{9,8},{10,11... | collective-permute-start | bytes 122888 | tf_op jit(solution)/shard_map/ppermute | solution.py:21
  10.2 0.0 copy-done.11
  10.2 0.1 reshape.62
  10.3 0.2 convert_reduce_fusion
  10.5 0.1 fusion.16
  10.7 0.3 fusion.2
  11.0 0.0 copy-done.10
  11.0 0.3 fusion.3
  11.3 0.0 copy-done.8
  11.3 0.6 copy.24.fp_ref
  11.9 0.0 copy-done.9
  11.9 0.6 copy.25.fm_ref
  12.5 0.0 collective-permute-done.xf_ref
  12.5 0.0 copy-start.6
  12.5 0.4 collective-permute-done.2.zf_ref
  12.9 0.0 copy-start.7
  12.9 0.0 collective-permute-done.1.yf_ref
  12.9 0.2 copy-done.6
  13.2 0.4 copy-done.7
  13.5 0.0 copy-start.3
  13.5 0.6 %copy-done.3 = f32[5,32,128]{2,1,0:T(8,128)} copy-done((f32[5,32,128]{2,1,0:T(8,128)}, f32[5,32,128]{2,1,0:T(8,128)S(1)}, u32[]{:S(2)}) %copy-start.3) | copy-done | bytes 81944
  14.2 17.5 %shard_map.105 = (f32[5,32,16,128]{3,2,1,0:T(8,128)}, f32[5,2,16,128]{3,2,1,0:T(8,128)}, f32[5,3,16,128]{3,2,1,0:T(8,128)}, f32[5,8,8,128]{3,2,1,0:T(8,128)}, f3...) custom-call(f32[3,5,5]{2,1,0:T(8,128)} %copy.24.fp_ref, f32[3,5,5]{2,1,0:T(8,128)} %copy.25.fm_ref, ...), custom_call_target="tpu_custom_call" | custom-call | tf_op jit(solution)/shard_map/pallas_call | solution.py:225
  31.7 0.1 collective-permute-start.6
  31.8 0.3 fusion.4
  32.1 3.9 %collective-permute-start.5 = (f32[5,8,8,128]{3,2,1,0:T(8,128)}, f32[5,8,8,128]{3,2,1,0:T(8,128)S(1)}, u32[]{:S(2)}, u32[]{:S(2)}) collective-permute-start(f32[5,8,8,128]{3,2,1,0:T(8,128)} %get-tuple-element.19), channel_id=1, source_target_pairs={{0,6},{2,0},{4,2},{6,4},{1,7},{3,1},{5,3},{7,5},{8,14},{10,8},{12,... | collective-permute-start | bytes 491528 | tf_op jit(solution)/shard_map/ppermute | solution.py:21
  36.0 0.0 collective-permute-start.4
  36.0 1.7 %collective-permute-start.3 = (f32[5,2,16,128]{3,2,1,0:T(8,128)}, f32[5,2,16,128]{3,2,1,0:T(8,128)S(1)}, u32[]{:S(2)}, u32[]{:S(2)}) collective-permute-start(f32[5,2,16,128]{3,2,1,0:T(8,128)} %get-tuple-element.17), channel_id=1, source_target_pairs={{0,24},{8,0},{16,8},{24,16},{1,25},{9,1},{17,9},{25,17},{2,26},{10... | collective-permute-start | bytes 245768 | tf_op jit(solution)/shard_map/ppermute | solution.py:21
  37.7 1.5 %collective-permute-start.7 = (f32[2,5,16,128]{3,2,1,0:T(8,128)}, f32[2,5,16,128]{3,2,1,0:T(8,128)S(1)}, u32[]{:S(2)}, u32[]{:S(2)}) collective-permute-start(f32[2,5,16,128]{3,2,1,0:T(8,128)} %get-tuple-element.21), channel_id=1, source_target_pairs={{0,1},{1,0},{2,3},{3,2},{4,5},{5,4},{6,7},{7,6},{8,9},{9,8},{10,11... | collective-permute-start | bytes 245768 | tf_op jit(solution)/shard_map/ppermute | solution.py:21
  39.9 0.2 collective-permute-done.3.axl_ref
  40.1 0.0 copy-start.4
  40.1 2.3 %collective-permute-done.7.az_ref = f32[2,5,16,128]{3,2,1,0:T(8,128)S(1)} collective-permute-done((f32[2,5,16,128]{3,2,1,0:T(8,128)}, f32[2,5,16,128]{3,2,1,0:T(8,128)S(1)}, u32[]{:S(2)}, u32[]{:S(2)}) %collective-permute-start.7) | collective-permute-done | bytes 81952 | tf_op jit(solution)/shard_map/ppermute | solution.py:21
  42.4 0.0 copy-start.5
  42.4 0.0 collective-permute-done.4.axr_ref
  42.4 0.0 copy-start.2
  42.4 2.3 %collective-permute-done.5.ayl_ref = f32[5,8,8,128]{3,2,1,0:T(8,128)S(1)} collective-permute-done((f32[5,8,8,128]{3,2,1,0:T(8,128)}, f32[5,8,8,128]{3,2,1,0:T(8,128)S(1)}, u32[]{:S(2)}, u32[]{:S(2)}) %collective-permute-start.5) | collective-permute-done | bytes 163872 | tf_op jit(solution)/shard_map/ppermute | solution.py:21
  44.7 0.0 copy-start.1
  44.7 0.0 collective-permute-done.6.ayr_ref
  44.7 0.0 copy-start
  44.7 0.0 copy-done.4
  44.7 0.0 copy-done.5
  44.8 0.0 copy-done.2
  44.8 0.6 %copy-done.1 = f32[5,8,8,128]{3,2,1,0:T(8,128)} copy-done((f32[5,8,8,128]{3,2,1,0:T(8,128)}, f32[5,8,8,128]{3,2,1,0:T(8,128)S(1)}, u32[]{:S(2)}) %copy-start.1) | copy-done | bytes 163864
  45.4 0.1 copy-done
  45.5 4.7 %shard_map.106 = (f32[5,32,16,128]{3,2,1,0:T(8,128)}, f32[16,128]{1,0:T(8,128)}) custom-call(s32[16]{0:T(128)} %row_ref.1, s32[1]{0:T(128)S(6)} %copy.38.cnt_ref, f32[5,32,16,128]{3,2,1,0:T(8,128)} %get-tuple-element.16.sec_hbm, f32[5,2,16,128]{3,2,1,0:T(8,128)} %copy-done.4, f32[5,3,16,128]{3,2,1,0:T(8,128)} %copy-done.2, ...), custom_call_target="tpu_custom_call", output_to_operand_aliasing={{0}: (2, {})} | custom-call | tf_op jit(solution)/shard_map/pallas_call | solution.py:265
  50.2 1.0 %fusion.6 = f32[32,32,1]{1,0,2:T(8,128)S(1)} fusion(s32[16,128]{1,0:T(8,128)S(1)} %get-tuple-element.26, f32[16,128]{1,0:T(8,128)} %get-tuple-element.23, s32[16,128]{1,0:T(8,128)S(1)} %get-tuple-element.27), kind=kOutput, calls=%fused_computation.12 | convolution fusion | flops 25362432 | bytes 28672 | tf_op jit(solution)/shard_map/rzo,rzk->ok/dot_general | solution.py:303
  51.2 10.7 %all_to_all.9 = f32[32,1,32]{2,1,0:T(1,128)S(1)} all-to-all(f32[32,1,32]{2,1,0:T(1,128)S(1)} %bitcast.20), channel_id=1, replica_groups=mesh['gx'=4,'gy'=4,'gz'=2] {'gx','gy','gz'}, dimensions={0} | all-to-all | bytes 8192 | tf_op jit(solution)/shard_map/all_to_all | solution.py:304
  61.9 0.6 reduce_sum.49
  (2 shorter events, 0.0 us)
Async XLA Ops:
  0.6 9.6 %copy-start.11 = (s32[1024]{0:T(1024)S(1)}, s32[1024]{0:T(1024)}, u32[]{:S(2)}) copy-start(s32[1024]{0:T(1024)} %param.17) | copy-start | bytes 12292
  0.6 10.3 %copy-start.10 = (s32[16,128]{1,0:T(8,128)S(1)}, s32[16,128]{1,0:T(8,128)}, u32[]{:S(2)}) copy-start(s32[16,128]{1,0:T(8,128)} %param.14) | copy-start | bytes 24580
  0.7 10.7 %copy-start.8 = (f32[3,5,5]{2,0,1:T(4,128)S(1)}, f32[3,5,5]{2,0,1:T(4,128)}, u32[]{:S(2)}) copy-start(f32[3,5,5]{2,0,1:T(4,128)} %param.11) | copy-start | bytes 904
  0.7 11.3 %copy-start.9 = (f32[3,5,5]{2,0,1:T(4,128)S(1)}, f32[3,5,5]{2,0,1:T(4,128)}, u32[]{:S(2)}) copy-start(f32[3,5,5]{2,0,1:T(4,128)} %param.12) | copy-start | bytes 904
  3.0 9.9 %collective-permute-start.1 = (f32[5,32,128]{2,1,0:T(8,128)}, f32[5,32,128]{2,1,0:T(8,128)S(1)}, u32[]{:S(2)}, u32[]{:S(2)}) collective-permute-start(f32[5,32,128]{2,1,0:T(8,128)} %get-tuple-element.14), channel_id=1, source_target_pairs={{0,6},{2,0},{4,2},{6,4},{1,7},{3,1},{5,3},{7,5},{8,14},{10,8},{12,... | collective-permute-start | bytes 245768 | tf_op jit(solution)/shard_map/ppermute | solution.py:21
  8.1 4.5 %collective-permute-start = (f32[5,16,128]{2,1,0:T(8,128)}, f32[5,16,128]{2,1,0:T(8,128)S(1)}, u32[]{:S(2)}, u32[]{:S(2)}) collective-permute-start(f32[5,16,128]{2,1,0:T(8,128)} %get-tuple-element.13), channel_id=1, source_target_pairs={{0,24},{8,0},{16,8},{24,16},{1,25},{9,1},{17,9},{25,17},{2,26},{10... | collective-permute-start | bytes 122888 | tf_op jit(solution)/shard_map/ppermute | solution.py:21
  8.7 4.2 %collective-permute-start.2 = (f32[5,16,128]{2,1,0:T(8,128)}, f32[5,16,128]{2,1,0:T(8,128)S(1)}, u32[]{:S(2)}, u32[]{:S(2)}) collective-permute-start(f32[5,16,128]{2,1,0:T(8,128)} %get-tuple-element.15), channel_id=1, source_target_pairs={{0,1},{1,0},{2,3},{3,2},{4,5},{5,4},{6,7},{7,6},{8,9},{9,8},{10,11... | collective-permute-start | bytes 122888 | tf_op jit(solution)/shard_map/ppermute | solution.py:21
  12.5 0.6 copy-start.6
  12.9 0.6 copy-start.7
  13.5 0.7 %copy-start.3 = (f32[5,32,128]{2,1,0:T(8,128)}, f32[5,32,128]{2,1,0:T(8,128)S(1)}, u32[]{:S(2)}) copy-start(f32[5,32,128]{2,1,0:T(8,128)S(1)} %collective-permute-done.1.yf_ref) | copy-start | bytes 245764
  31.7 13.0 %collective-permute-start.6 = (f32[5,16,8,128]{3,2,1,0:T(8,128)}, f32[5,16,8,128]{3,2,1,0:T(8,128)S(1)}, u32[]{:S(2)}, u32[]{:S(2)}) collective-permute-start(f32[5,16,8,128]{3,2,1,0:T(8,128)} %get-tuple-element.20), channel_id=1, source_target_pairs={{0,2},{2,4},{4,6},{6,0},{1,3},{3,5},{5,7},{7,1},{8,10},{10,12},{12... | collective-permute-start | bytes 983048 | tf_op jit(solution)/shard_map/ppermute | solution.py:21
  32.1 12.6 %collective-permute-start.5 = (f32[5,8,8,128]{3,2,1,0:T(8,128)}, f32[5,8,8,128]{3,2,1,0:T(8,128)S(1)}, u32[]{:S(2)}, u32[]{:S(2)}) collective-permute-start(f32[5,8,8,128]{3,2,1,0:T(8,128)} %get-tuple-element.19), channel_id=1, source_target_pairs={{0,6},{2,0},{4,2},{6,4},{1,7},{3,1},{5,3},{7,5},{8,14},{10,8},{12,... | collective-permute-start | bytes 491528 | tf_op jit(solution)/shard_map/ppermute | solution.py:21
  36.0 6.4 %collective-permute-start.4 = (f32[5,3,16,128]{3,2,1,0:T(8,128)}, f32[5,3,16,128]{3,2,1,0:T(8,128)S(1)}, u32[]{:S(2)}, u32[]{:S(2)}) collective-permute-start(f32[5,3,16,128]{3,2,1,0:T(8,128)} %get-tuple-element.18), channel_id=1, source_target_pairs={{0,8},{8,16},{16,24},{24,0},{1,9},{9,17},{17,25},{25,1},{2,10},{10... | collective-permute-start | bytes 368648 | tf_op jit(solution)/shard_map/ppermute | solution.py:21
  36.0 4.1 %collective-permute-start.3 = (f32[5,2,16,128]{3,2,1,0:T(8,128)}, f32[5,2,16,128]{3,2,1,0:T(8,128)S(1)}, u32[]{:S(2)}, u32[]{:S(2)}) collective-permute-start(f32[5,2,16,128]{3,2,1,0:T(8,128)} %get-tuple-element.17), channel_id=1, source_target_pairs={{0,24},{8,0},{16,8},{24,16},{1,25},{9,1},{17,9},{25,17},{2,26},{10... | collective-permute-start | bytes 245768 | tf_op jit(solution)/shard_map/ppermute | solution.py:21
  37.7 4.7 %collective-permute-start.7 = (f32[2,5,16,128]{3,2,1,0:T(8,128)}, f32[2,5,16,128]{3,2,1,0:T(8,128)S(1)}, u32[]{:S(2)}, u32[]{:S(2)}) collective-permute-start(f32[2,5,16,128]{3,2,1,0:T(8,128)} %get-tuple-element.21), channel_id=1, source_target_pairs={{0,1},{1,0},{2,3},{3,2},{4,5},{5,4},{6,7},{7,6},{8,9},{9,8},{10,11... | collective-permute-start | bytes 245768 | tf_op jit(solution)/shard_map/ppermute | solution.py:21
  40.1 4.6 %copy-start.4 = (f32[5,2,16,128]{3,2,1,0:T(8,128)}, f32[5,2,16,128]{3,2,1,0:T(8,128)S(1)}, u32[]{:S(2)}) copy-start(f32[5,2,16,128]{3,2,1,0:T(8,128)S(1)} %collective-permute-done.3.axl_ref) | copy-start | bytes 245764
  42.4 2.4 %copy-start.5 = (f32[2,5,16,128]{3,2,1,0:T(8,128)}, f32[2,5,16,128]{3,2,1,0:T(8,128)S(1)}, u32[]{:S(2)}) copy-start(f32[2,5,16,128]{3,2,1,0:T(8,128)S(1)} %collective-permute-done.7.az_ref) | copy-start | bytes 245764
  42.4 2.4 %copy-start.2 = (f32[5,3,16,128]{3,2,1,0:T(8,128)}, f32[5,3,16,128]{3,2,1,0:T(8,128)S(1)}, u32[]{:S(2)}) copy-start(f32[5,3,16,128]{3,2,1,0:T(8,128)S(1)} %collective-permute-done.4.axr_ref) | copy-start | bytes 368644
  44.7 0.7 %copy-start.1 = (f32[5,8,8,128]{3,2,1,0:T(8,128)}, f32[5,8,8,128]{3,2,1,0:T(8,128)S(1)}, u32[]{:S(2)}) copy-start(f32[5,8,8,128]{3,2,1,0:T(8,128)S(1)} %collective-permute-done.5.ayl_ref) | copy-start | bytes 491524
  44.7 0.8 %copy-start = (f32[5,16,8,128]{3,2,1,0:T(8,128)}, f32[5,16,8,128]{3,2,1,0:T(8,128)S(1)}, u32[]{:S(2)}) copy-start(f32[5,16,8,128]{3,2,1,0:T(8,128)S(1)} %collective-permute-done.6.ayr_ref) | copy-start | bytes 983044

commit v13 on v5

--- a/solution.py
+++ b/solution.py
@@ -162,7 +162,7 @@
 
 
 def fix_kernel(row_ref, cnt_ref, sec_ref, axl_ref, axr_ref, ayl_ref, ayr_ref, az_ref,
-               coef_ref, out_ref, wt_ref):
+               coef_ref, own_ref, rank_ref, out_ref, t_ref):
     nf, nx, ny, nz = sec_ref.shape
     row, lane = iotas(ny, nz)
     pad = jnp.zeros((ny - 8, nz), F32)
@@ -180,7 +180,11 @@
                 add = add + axl_ref[f, x - (nx - 2)]
             out_ref[f, x] = sec_ref[f, x] + SECTION * add
     live_n = cnt_ref[0]
-    for r in range(wt_ref.shape[0]):
+    ndev, per = t_ref.shape
+    own_ids = lax.broadcasted_iota(jnp.int32, (ndev, nz), 0)
+    rank_ids = lax.broadcasted_iota(jnp.int32, (per, nz), 0)
+    total = jnp.zeros((ndev, per), F32)
+    for r in range(coef_ref.shape[1]):
         idx = row_ref[r]
         lx = idx // ny
         ly = idx % ny
@@ -188,7 +192,12 @@
         for f in range(nf):
             v = out_ref[f, lx, pl.ds(ly, 1), :] * coef_ref[f, pl.ds(r, 1), :]
             val = v if val is None else val + v
-        wt_ref[pl.ds(r, 1), :] = val * jnp.where(r < live_n, 1.0, 0.0).astype(F32)
+        val = val * jnp.where(r < live_n, 1.0, 0.0).astype(F32)
+        a = jnp.where(own_ref[pl.ds(r, 1), :] == own_ids, val, 0.0)
+        b = jnp.where(rank_ref[pl.ds(r, 1), :] == rank_ids, 1.0, 0.0)
+        total = total + lax.dot_general(a, b, (((1,), (1,)), ((), ())), precision=HI,
+                                        preferred_element_type=F32)
+    t_ref[...] = total
 
 
 def on_device(ndev, adjoint, stencil_weights, flux_plus, flux_minus, wall_row, wall_panel, wall_coef,
@@ -249,18 +258,6 @@
         az = shift_from(zz, "gz", 1)
     else:
         az = jnp.stack([shift_from(zz[0], "gz", -1), shift_from(zz[1], "gz", 1)])
-    nr = wall_row.shape[0]
-    section, wt = pl.pallas_call(
-        fix_kernel,
-        out_shape=(
-            jax.ShapeDtypeStruct((nf, nx, ny, nz), F32),
-            jax.ShapeDtypeStruct((nr, nz), F32),
-        ),
-        in_specs=[SMEM, SMEM] + [VMEM] * 7,
-        out_specs=(VMEM, VMEM),
-        input_output_aliases={2: 0},
-    )(wall_row, wall_count, sec, axl, axr, ayl, ayr, az, wall_coef)
-
     npan = panel_owner.shape[0]
     per = npan // ndev
     nb = 32
@@ -281,9 +278,18 @@
 
     cell_own = lookup(panel_owner.reshape(na, nb).astype(F32))
     cell_rank = lookup(rank)
-    oh_o = (cell_own[..., None] == jnp.arange(ndev, dtype=jnp.int32)).astype(F32)
-    oh_k = (cell_rank[..., None] == jnp.arange(per, dtype=jnp.int32)).astype(F32)
-    t = jnp.einsum("rzo,rzk->ok", oh_o * wt[..., None], oh_k, precision=HI)
+    nr = wall_row.shape[0]
+    section, t = pl.pallas_call(
+        fix_kernel,
+        out_shape=(
+            jax.ShapeDtypeStruct((nf, nx, ny, nz), F32),
+            jax.ShapeDtypeStruct((ndev, per), F32),
+        ),
+        in_specs=[SMEM, SMEM] + [VMEM] * 9,
+        out_specs=(VMEM, VMEM),
+        input_output_aliases={2: 0},
+    )(wall_row, wall_count, sec, axl, axr, ayl, ayr, az, wall_coef, cell_own, cell_rank)
+
     got = lax.all_to_all(t, AXES, 0, 0, tiled=True)
     return section, jnp.sum(got, axis=0)
 

time: 61.6 us -> 61 us (level)
  waiting for transfers between devices: 5.2 us -> 7.95 us
  starting transfers between devices: 14.4 us -> 12.2 us
  blocking collectives: 10.7 us -> 9.65 us
  matrix products: 2.08 us -> 1.09 us
    ppermute x8, waiting for transfers between devices: 5.2 us -> 7.95 us  [shift_from(): return lax.ppermute(x, axis, [(i, (i + by) % n) for i in range(n)])]
    ppermute x8, starting transfers between devices: 14.4 us -> 12.2 us  [shift_from(): return lax.ppermute(x, axis, [(i, (i + by) % n) for i in range(n)])]
    all_to_all x1, blocking collectives: 10.7 us -> 9.65 us  [on_device(): got = lax.all_to_all(t, AXES, 0, 0, tiled=True)]
    dot_general x1 -> x0, matrix products: 0.99 us -> none  [on_device(): t = jnp.einsum('rzo,rzk->ok', oh_o * wt[..., None], oh_k, precision=HI)]
  transfers between devices with their start and end apart: 8 -> 8, of which waited for: 4 -> 2; matrix products, arithmetic and copies ran while one was open for 4% -> 5% of each run, Pallas kernels for 0% -> 0%
where the time goes in v13:
time: 61 us; the launch traced here: 60.5 us
  Pallas kernels  23.5 us (39%)
  starting transfers between devices  12.2 us (20%)
  blocking collectives  9.65 us (16%)
  waiting for transfers between devices  7.95 us (13%)
  local copies, waits for them, and re-layouts  3.28 us (5%)
  between operations  1.47 us (2%)
  other arithmetic  1.38 us (2%)
  matrix products  1.09 us (2%)
    pallas_call x1, Pallas kernels, on_device(): pl.pallas_call(stencil_kernel, grid=(nx // XC,), out_shape=(jax.ShapeDtyp...  17.5 us
    ppermute x8, starting transfers between devices, shift_from(): return lax.ppermute(x, axis, [(i, (i + by) % n) for i in range(n)])  12.2 us
    all_to_all x1, blocking collectives, on_device(): got = lax.all_to_all(t, AXES, 0, 0, tiled=True)  9.65 us
    ppermute x8, waiting for transfers between devices, shift_from(): return lax.ppermute(x, axis, [(i, (i + by) % n) for i in range(n)])  7.95 us
    pallas_call x1, Pallas kernels, on_device(): pl.pallas_call(fix_kernel, out_shape=(jax.ShapeDtypeStruct((nf, nx, ny, n...  3.64 us
    unnamed x26, local copies, waits for them, and re-layouts  3.21 us
    pallas_call x1, Pallas kernels, on_device(): pl.pallas_call(fronts_kernel, out_shape=(jax.ShapeDtypeStruct((nf, ny, nz...  2.35 us
  transfers between devices with their start and end apart: 8, of which 2 were waited for; matrix products, arithmetic and copies ran while one was open for 5% of the time, Pallas kernels for 0%

profile of v13, /device:TPU:0, one launch (start us, length us, event | category | flops | bytes accessed | tf_op | source)
XLA Modules:
  0.0 60.5 jit_solution(5960973057372214499)
XLA Ops:
  0.6 0.0 copy-start.11
  0.6 0.0 copy-start.10
  0.7 0.0 copy-start.8
  0.7 0.0 copy-start.9
  0.7 2.4 %shard_map.104 = (f32[5,16,128]{2,1,0:T(8,128)}, f32[5,32,128]{2,1,0:T(8,128)}, f32[5,16,128]{2,1,0:T(8,128)}) custom-call(f32[5,32,16,128]{3,2,1,0:T(8,128)} %adj_ref.3), custom_call_target="tpu_custom_call" | custom-call | tf_op jit(solution)/shard_map/pallas_call | solution.py:207
  3.0 2.4 %collective-permute-start = (f32[5,16,128]{2,1,0:T(8,128)}, f32[5,16,128]{2,1,0:T(8,128)S(1)}, u32[]{:S(2)}, u32[]{:S(2)}) collective-permute-start(f32[5,16,128]{2,1,0:T(8,128)} %get-tuple-element.13), channel_id=1, source_target_pairs={{0,24},{8,0},{16,8},{24,16},{1,25},{9,1},{17,9},{25,17},{2,26},{10... | collective-permute-start | bytes 122888 | tf_op jit(solution)/shard_map/ppermute | solution.py:20
  5.4 1.5 %collective-permute-start.2 = (f32[5,16,128]{2,1,0:T(8,128)}, f32[5,16,128]{2,1,0:T(8,128)S(1)}, u32[]{:S(2)}, u32[]{:S(2)}) collective-permute-start(f32[5,16,128]{2,1,0:T(8,128)} %get-tuple-element.15), channel_id=1, source_target_pairs={{0,1},{1,0},{2,3},{3,2},{4,5},{5,4},{6,7},{7,6},{8,9},{9,8},{10,11... | collective-permute-start | bytes 122888 | tf_op jit(solution)/shard_map/ppermute | solution.py:20
  6.9 3.6 %collective-permute-start.1 = (f32[5,32,128]{2,1,0:T(8,128)}, f32[5,32,128]{2,1,0:T(8,128)S(1)}, u32[]{:S(2)}, u32[]{:S(2)}) collective-permute-start(f32[5,32,128]{2,1,0:T(8,128)} %get-tuple-element.14), channel_id=1, source_target_pairs={{0,6},{2,0},{4,2},{6,4},{1,7},{3,1},{5,3},{7,5},{8,14},{10,8},{12,... | collective-permute-start | bytes 245768 | tf_op jit(solution)/shard_map/ppermute | solution.py:20
  10.5 0.0 copy-done.11
  10.5 0.1 reshape.53
  10.6 0.2 convert_reduce_fusion
  10.8 0.1 fusion.10
  10.9 0.3 fusion.2
  11.2 0.0 copy-done.10
  11.3 0.3 fusion.3
  11.6 0.0 copy-done.8
  11.6 0.6 copy.22.fp_ref
  12.2 0.0 copy-done.9
  12.2 0.6 copy.23.fm_ref
  12.8 0.0 collective-permute-done.xf_ref
  12.8 0.0 copy-start.6
  12.8 0.0 collective-permute-done.2.zf_ref
  12.8 0.0 copy-start.7
  12.8 0.1 collective-permute-done.1.yf_ref
  12.9 0.6 copy-done.6
  13.5 0.0 copy-done.7
  13.5 0.0 copy-start.3
  13.5 0.6 %copy-done.3 = f32[5,32,128]{2,1,0:T(8,128)} copy-done((f32[5,32,128]{2,1,0:T(8,128)}, f32[5,32,128]{2,1,0:T(8,128)S(1)}, u32[]{:S(2)}) %copy-start.3) | copy-done | bytes 81944
  14.1 17.5 %shard_map.105 = (f32[5,32,16,128]{3,2,1,0:T(8,128)}, f32[5,2,16,128]{3,2,1,0:T(8,128)}, f32[5,3,16,128]{3,2,1,0:T(8,128)}, f32[5,8,8,128]{3,2,1,0:T(8,128)}, f3...) custom-call(f32[3,5,5]{2,1,0:T(8,128)} %copy.22.fp_ref, f32[3,5,5]{2,1,0:T(8,128)} %copy.23.fm_ref, ...), custom_call_target="tpu_custom_call" | custom-call | tf_op jit(solution)/shard_map/pallas_call | solution.py:222
  31.6 0.1 collective-permute-start.6
  31.7 0.3 fusion.4
  32.1 0.2 collective-permute-start.3
  32.2 0.5 collective-permute-start.7
  32.7 0.1 collective-permute-start.4
  32.9 3.8 %collective-permute-start.5 = (f32[5,8,8,128]{3,2,1,0:T(8,128)}, f32[5,8,8,128]{3,2,1,0:T(8,128)S(1)}, u32[]{:S(2)}, u32[]{:S(2)}) collective-permute-start(f32[5,8,8,128]{3,2,1,0:T(8,128)} %get-tuple-element.19), channel_id=1, source_target_pairs={{0,6},{2,0},{4,2},{6,4},{1,7},{3,1},{5,3},{7,5},{8,14},{10,8},{12,... | collective-permute-start | bytes 491528 | tf_op jit(solution)/shard_map/ppermute | solution.py:20
  36.7 0.6 round-nearest-even_convert_fusion
  37.9 0.0 collective-permute-done.3.axl_ref
  37.9 0.0 copy-start.4
  37.9 0.0 collective-permute-done.7.az_ref
  37.9 0.0 copy-start.5
  38.0 0.0 collective-permute-done.4.axr_ref
  38.0 0.0 copy-start.2
  38.0 7.9 %collective-permute-done.5.ayl_ref = f32[5,8,8,128]{3,2,1,0:T(8,128)S(1)} collective-permute-done((f32[5,8,8,128]{3,2,1,0:T(8,128)}, f32[5,8,8,128]{3,2,1,0:T(8,128)S(1)}, u32[]{:S(2)}, u32[]{:S(2)}) %collective-permute-start.5) | collective-permute-done | bytes 163872 | tf_op jit(solution)/shard_map/ppermute | solution.py:20
  45.9 0.0 copy-start.1
  45.9 0.0 collective-permute-done.6.ayr_ref
  45.9 0.0 copy-start
  45.9 0.0 copy-done.4
  45.9 0.0 copy-done.5
  45.9 0.0 copy-done.2
  45.9 0.6 %copy-done.1 = f32[5,8,8,128]{3,2,1,0:T(8,128)} copy-done((f32[5,8,8,128]{3,2,1,0:T(8,128)}, f32[5,8,8,128]{3,2,1,0:T(8,128)S(1)}, u32[]{:S(2)}) %copy-start.1) | copy-done | bytes 163864
  46.5 0.1 copy-done
  46.6 3.6 %shard_map.106 = (f32[5,32,16,128]{3,2,1,0:T(8,128)}, f32[32,32]{1,0:T(8,128)}) custom-call(s32[16]{0:T(128)} %row_ref.1, s32[1]{0:T(128)S(6)} %copy.32.cnt_ref, f32[5,32,16,128]{3,2,1,0:T(8,128)} %get-tuple-element.16.sec_ref, f32[5,2,16,128]{3,2,1,0:T(8,128)} %copy-done.4, f32[5,3,16,128]{3,2,1,0:T(8,128)} %copy-done.2, ...), custom_call_target="tpu_custom_call", output_to_operand_aliasing={{0}: (2, {})} | custom-call | tf_op jit(solution)/shard_map/pallas_call | solution.py:282
  50.3 9.7 %all_to_all.9 = f32[32,1,32]{2,1,0:T(1,128)S(1)} all-to-all(f32[32,1,32]{2,1,0:T(1,128)} %bitcast.19), channel_id=1, replica_groups=mesh['gx'=4,'gy'=4,'gz'=2] {'gx','gy','gz'}, dimensions={0} | all-to-all | bytes 8192 | tf_op jit(solution)/shard_map/all_to_all | solution.py:293
  59.9 0.6 reduce_sum.49
  (1 shorter events, 0.0 us)
Async XLA Ops:
  0.6 9.9 %copy-start.11 = (s32[1024]{0:T(1024)S(1)}, s32[1024]{0:T(1024)}, u32[]{:S(2)}) copy-start(s32[1024]{0:T(1024)} %param.17) | copy-start | bytes 12292
  0.6 10.6 %copy-start.10 = (s32[16,128]{1,0:T(8,128)S(1)}, s32[16,128]{1,0:T(8,128)}, u32[]{:S(2)}) copy-start(s32[16,128]{1,0:T(8,128)} %param.14) | copy-start | bytes 24580
  0.7 11.0 %copy-start.8 = (f32[3,5,5]{2,0,1:T(4,128)S(1)}, f32[3,5,5]{2,0,1:T(4,128)}, u32[]{:S(2)}) copy-start(f32[3,5,5]{2,0,1:T(4,128)} %param.11) | copy-start | bytes 904
  0.7 11.6 %copy-start.9 = (f32[3,5,5]{2,0,1:T(4,128)S(1)}, f32[3,5,5]{2,0,1:T(4,128)}, u32[]{:S(2)}) copy-start(f32[3,5,5]{2,0,1:T(4,128)} %param.12) | copy-start | bytes 904
  3.0 9.8 %collective-permute-start = (f32[5,16,128]{2,1,0:T(8,128)}, f32[5,16,128]{2,1,0:T(8,128)S(1)}, u32[]{:S(2)}, u32[]{:S(2)}) collective-permute-start(f32[5,16,128]{2,1,0:T(8,128)} %get-tuple-element.13), channel_id=1, source_target_pairs={{0,24},{8,0},{16,8},{24,16},{1,25},{9,1},{17,9},{25,17},{2,26},{10... | collective-permute-start | bytes 122888 | tf_op jit(solution)/shard_map/ppermute | solution.py:20
  5.4 7.4 %collective-permute-start.2 = (f32[5,16,128]{2,1,0:T(8,128)}, f32[5,16,128]{2,1,0:T(8,128)S(1)}, u32[]{:S(2)}, u32[]{:S(2)}) collective-permute-start(f32[5,16,128]{2,1,0:T(8,128)} %get-tuple-element.15), channel_id=1, source_target_pairs={{0,1},{1,0},{2,3},{3,2},{4,5},{5,4},{6,7},{7,6},{8,9},{9,8},{10,11... | collective-permute-start | bytes 122888 | tf_op jit(solution)/shard_map/ppermute | solution.py:20
  6.9 6.0 %collective-permute-start.1 = (f32[5,32,128]{2,1,0:T(8,128)}, f32[5,32,128]{2,1,0:T(8,128)S(1)}, u32[]{:S(2)}, u32[]{:S(2)}) collective-permute-start(f32[5,32,128]{2,1,0:T(8,128)} %get-tuple-element.14), channel_id=1, source_target_pairs={{0,6},{2,0},{4,2},{6,4},{1,7},{3,1},{5,3},{7,5},{8,14},{10,8},{12,... | collective-permute-start | bytes 245768 | tf_op jit(solution)/shard_map/ppermute | solution.py:20
  12.8 0.6 %copy-start.6 = (f32[5,16,128]{2,1,0:T(8,128)}, f32[5,16,128]{2,1,0:T(8,128)S(1)}, u32[]{:S(2)}) copy-start(f32[5,16,128]{2,1,0:T(8,128)S(1)} %collective-permute-done.xf_ref) | copy-start | bytes 122884
  12.8 0.6 %copy-start.7 = (f32[5,16,128]{2,1,0:T(8,128)}, f32[5,16,128]{2,1,0:T(8,128)S(1)}, u32[]{:S(2)}) copy-start(f32[5,16,128]{2,1,0:T(8,128)S(1)} %collective-permute-done.2.zf_ref) | copy-start | bytes 122884
  13.5 0.6 %copy-start.3 = (f32[5,32,128]{2,1,0:T(8,128)}, f32[5,32,128]{2,1,0:T(8,128)S(1)}, u32[]{:S(2)}) copy-start(f32[5,32,128]{2,1,0:T(8,128)S(1)} %collective-permute-done.1.yf_ref) | copy-start | bytes 245764
  31.6 14.2 %collective-permute-start.6 = (f32[5,16,8,128]{3,2,1,0:T(8,128)}, f32[5,16,8,128]{3,2,1,0:T(8,128)S(1)}, u32[]{:S(2)}, u32[]{:S(2)}) collective-permute-start(f32[5,16,8,128]{3,2,1,0:T(8,128)} %get-tuple-element.20), channel_id=1, source_target_pairs={{0,2},{2,4},{4,6},{6,0},{1,3},{3,5},{5,7},{7,1},{8,10},{10,12},{12... | collective-permute-start | bytes 983048 | tf_op jit(solution)/shard_map/ppermute | solution.py:20
  32.1 5.9 %collective-permute-start.3 = (f32[5,2,16,128]{3,2,1,0:T(8,128)}, f32[5,2,16,128]{3,2,1,0:T(8,128)S(1)}, u32[]{:S(2)}, u32[]{:S(2)}) collective-permute-start(f32[5,2,16,128]{3,2,1,0:T(8,128)} %get-tuple-element.17), channel_id=1, source_target_pairs={{0,24},{8,0},{16,8},{24,16},{1,25},{9,1},{17,9},{25,17},{2,26},{10... | collective-permute-start | bytes 245768 | tf_op jit(solution)/shard_map/ppermute | solution.py:20
  32.2 5.7 %collective-permute-start.7 = (f32[2,5,16,128]{3,2,1,0:T(8,128)}, f32[2,5,16,128]{3,2,1,0:T(8,128)S(1)}, u32[]{:S(2)}, u32[]{:S(2)}) collective-permute-start(f32[2,5,16,128]{3,2,1,0:T(8,128)} %get-tuple-element.21), channel_id=1, source_target_pairs={{0,1},{1,0},{2,3},{3,2},{4,5},{5,4},{6,7},{7,6},{8,9},{9,8},{10,11... | collective-permute-start | bytes 245768 | tf_op jit(solution)/shard_map/ppermute | solution.py:20
  32.7 5.2 %collective-permute-start.4 = (f32[5,3,16,128]{3,2,1,0:T(8,128)}, f32[5,3,16,128]{3,2,1,0:T(8,128)S(1)}, u32[]{:S(2)}, u32[]{:S(2)}) collective-permute-start(f32[5,3,16,128]{3,2,1,0:T(8,128)} %get-tuple-element.18), channel_id=1, source_target_pairs={{0,8},{8,16},{16,24},{24,0},{1,9},{9,17},{17,25},{25,1},{2,10},{10... | collective-permute-start | bytes 368648 | tf_op jit(solution)/shard_map/ppermute | solution.py:20
  32.9 13.0 %collective-permute-start.5 = (f32[5,8,8,128]{3,2,1,0:T(8,128)}, f32[5,8,8,128]{3,2,1,0:T(8,128)S(1)}, u32[]{:S(2)}, u32[]{:S(2)}) collective-permute-start(f32[5,8,8,128]{3,2,1,0:T(8,128)} %get-tuple-element.19), channel_id=1, source_target_pairs={{0,6},{2,0},{4,2},{6,4},{1,7},{3,1},{5,3},{7,5},{8,14},{10,8},{12,... | collective-permute-start | bytes 491528 | tf_op jit(solution)/shard_map/ppermute | solution.py:20
  37.9 7.9 %copy-start.4 = (f32[5,2,16,128]{3,2,1,0:T(8,128)}, f32[5,2,16,128]{3,2,1,0:T(8,128)S(1)}, u32[]{:S(2)}) copy-start(f32[5,2,16,128]{3,2,1,0:T(8,128)S(1)} %collective-permute-done.3.axl_ref) | copy-start | bytes 245764
  37.9 7.9 %copy-start.5 = (f32[2,5,16,128]{3,2,1,0:T(8,128)}, f32[2,5,16,128]{3,2,1,0:T(8,128)S(1)}, u32[]{:S(2)}) copy-start(f32[2,5,16,128]{3,2,1,0:T(8,128)S(1)} %collective-permute-done.7.az_ref) | copy-start | bytes 245764
  38.0 7.9 %copy-start.2 = (f32[5,3,16,128]{3,2,1,0:T(8,128)}, f32[5,3,16,128]{3,2,1,0:T(8,128)S(1)}, u32[]{:S(2)}) copy-start(f32[5,3,16,128]{3,2,1,0:T(8,128)S(1)} %collective-permute-done.4.axr_ref) | copy-start | bytes 368644
  45.9 0.7 %copy-start.1 = (f32[5,8,8,128]{3,2,1,0:T(8,128)}, f32[5,8,8,128]{3,2,1,0:T(8,128)S(1)}, u32[]{:S(2)}) copy-start(f32[5,8,8,128]{3,2,1,0:T(8,128)S(1)} %collective-permute-done.5.ayl_ref) | copy-start | bytes 491524
  45.9 0.8 %copy-start = (f32[5,16,8,128]{3,2,1,0:T(8,128)}, f32[5,16,8,128]{3,2,1,0:T(8,128)S(1)}, u32[]{:S(2)}) copy-start(f32[5,16,8,128]{3,2,1,0:T(8,128)S(1)} %collective-permute-done.6.ayr_ref) | copy-start | bytes 983044

commit v14 on v13

--- a/solution.py
+++ b/solution.py
@@ -258,6 +258,7 @@
         az = shift_from(zz, "gz", 1)
     else:
         az = jnp.stack([shift_from(zz[0], "gz", -1), shift_from(zz[1], "gz", 1)])
+    az, wall_panel, panel_owner = lax.optimization_barrier((az, wall_panel, panel_owner))
     npan = panel_owner.shape[0]
     per = npan // ndev
     nb = 32

time: 61 us -> 63.4 us (1.039)
  waiting for transfers between devices: 7.95 us -> 11.3 us
  starting transfers between devices: 12.2 us -> 11.4 us
    ppermute x8, waiting for transfers between devices: 7.95 us -> 11.3 us  [shift_from(): return lax.ppermute(x, axis, [(i, (i + by) % n) for i in range(n)])]
    ppermute x8, starting transfers between devices: 12.2 us -> 11.4 us  [shift_from(): return lax.ppermute(x, axis, [(i, (i + by) % n) for i in range(n)])]
  transfers between devices with their start and end apart: 8 -> 8, of which waited for: 2 -> 3; matrix products, arithmetic and copies ran while one was open for 5% -> 5% of each run, Pallas kernels for 0% -> 0%
where the time goes in v14:
time: 63.4 us; the launch traced here: 62.9 us
  Pallas kernels  23.5 us (37%)
  starting transfers between devices  11.4 us (18%)
  waiting for transfers between devices  11.3 us (18%)
  blocking collectives  9.58 us (15%)
  local copies, waits for them, and re-layouts  3.3 us (5%)
  between operations  1.4 us (2%)
  other arithmetic  1.39 us (2%)
  matrix products  1.09 us (2%)
    pallas_call x1, Pallas kernels, on_device(): pl.pallas_call(stencil_kernel, grid=(nx // XC,), out_shape=(jax.ShapeDtyp...  17.5 us
    ppermute x8, starting transfers between devices, shift_from(): return lax.ppermute(x, axis, [(i, (i + by) % n) for i in range(n)])  11.4 us
    ppermute x8, waiting for transfers between devices, shift_from(): return lax.ppermute(x, axis, [(i, (i + by) % n) for i in range(n)])  11.3 us
    all_to_all x1, blocking collectives, on_device(): got = lax.all_to_all(t, AXES, 0, 0, tiled=True)  9.58 us
    pallas_call x1, Pallas kernels, on_device(): pl.pallas_call(fix_kernel, out_shape=(jax.ShapeDtypeStruct((nf, nx, ny, n...  3.64 us
    unnamed x26, local copies, waits for them, and re-layouts  3.23 us
    pallas_call x1, Pallas kernels, on_device(): pl.pallas_call(fronts_kernel, out_shape=(jax.ShapeDtypeStruct((nf, ny, nz...  2.34 us
  transfers between devices with their start and end apart: 8, of which 3 were waited for; matrix products, arithmetic and copies ran while one was open for 5% of the time, Pallas kernels for 0%

profile of v14, /device:TPU:0, one launch (start us, length us, event | category | flops | bytes accessed | tf_op | source)
XLA Modules:
  0.0 62.9 jit_solution(17305500199721638450)
XLA Ops:
  0.6 0.0 copy-start.8
  0.6 0.0 copy-start.9
  0.6 2.3 %shard_map.104 = (f32[5,16,128]{2,1,0:T(8,128)}, f32[5,32,128]{2,1,0:T(8,128)}, f32[5,16,128]{2,1,0:T(8,128)}) custom-call(f32[5,32,16,128]{3,2,1,0:T(8,128)} %adj_ref.3), custom_call_target="tpu_custom_call" | custom-call | tf_op jit(solution)/shard_map/pallas_call | solution.py:207
  3.0 5.0 %collective-permute-start.1 = (f32[5,32,128]{2,1,0:T(8,128)}, f32[5,32,128]{2,1,0:T(8,128)S(1)}, u32[]{:S(2)}, u32[]{:S(2)}) collective-permute-start(f32[5,32,128]{2,1,0:T(8,128)} %get-tuple-element.17), channel_id=1, source_target_pairs={{0,6},{2,0},{4,2},{6,4},{1,7},{3,1},{5,3},{7,5},{8,14},{10,8},{12,... | collective-permute-start | bytes 245768 | tf_op jit(solution)/shard_map/ppermute | solution.py:20
  8.0 0.7 %collective-permute-start = (f32[5,16,128]{2,1,0:T(8,128)}, f32[5,16,128]{2,1,0:T(8,128)S(1)}, u32[]{:S(2)}, u32[]{:S(2)}) collective-permute-start(f32[5,16,128]{2,1,0:T(8,128)} %get-tuple-element.16), channel_id=1, source_target_pairs={{0,24},{8,0},{16,8},{24,16},{1,25},{9,1},{17,9},{25,17},{2,26},{10... | collective-permute-start | bytes 122888 | tf_op jit(solution)/shard_map/ppermute | solution.py:20
  8.7 1.5 %collective-permute-start.2 = (f32[5,16,128]{2,1,0:T(8,128)}, f32[5,16,128]{2,1,0:T(8,128)S(1)}, u32[]{:S(2)}, u32[]{:S(2)}) collective-permute-start(f32[5,16,128]{2,1,0:T(8,128)} %get-tuple-element.18), channel_id=1, source_target_pairs={{0,1},{1,0},{2,3},{3,2},{4,5},{5,4},{6,7},{7,6},{8,9},{9,8},{10,11... | collective-permute-start | bytes 122888 | tf_op jit(solution)/shard_map/ppermute | solution.py:20
  10.2 0.0 copy-done.8
  10.2 0.6 copy.22.fp_ref
  10.8 0.0 copy-done.9
  10.8 0.6 copy.23.fm_ref
  11.4 0.0 copy-start.11
  11.4 0.0 copy-start.10
  11.4 0.0 collective-permute-done.xf_ref
  11.4 0.0 copy-start.6
  11.4 1.5 %collective-permute-done.2.zf_ref = f32[5,16,128]{2,1,0:T(8,128)S(1)} collective-permute-done((f32[5,16,128]{2,1,0:T(8,128)}, f32[5,16,128]{2,1,0:T(8,128)S(1)}, u32[]{:S(2)}, u32[]{:S(2)}) %collective-permute-start.2) | collective-permute-done | bytes 40992 | tf_op jit(solution)/shard_map/ppermute | solution.py:20
  12.9 0.0 copy-start.7
  12.9 0.0 collective-permute-done.1.yf_ref
  12.9 0.0 copy-done.6
  12.9 0.6 copy-done.7
  13.5 0.0 copy-start.3
  13.5 0.6 %copy-done.3 = f32[5,32,128]{2,1,0:T(8,128)} copy-done((f32[5,32,128]{2,1,0:T(8,128)}, f32[5,32,128]{2,1,0:T(8,128)S(1)}, u32[]{:S(2)}) %copy-start.3) | copy-done | bytes 81944
  14.2 17.5 %shard_map.105 = (f32[5,32,16,128]{3,2,1,0:T(8,128)}, f32[5,2,16,128]{3,2,1,0:T(8,128)}, f32[5,3,16,128]{3,2,1,0:T(8,128)}, f32[5,8,8,128]{3,2,1,0:T(8,128)}, f3...) custom-call(f32[3,5,5]{2,1,0:T(8,128)} %copy.22.fp_ref, f32[3,5,5]{2,1,0:T(8,128)} %copy.23.fm_ref, ...), custom_call_target="tpu_custom_call" | custom-call | tf_op jit(solution)/shard_map/pallas_call | solution.py:222
  31.7 1.6 %collective-permute-start.7 = (f32[2,5,16,128]{3,2,1,0:T(8,128)}, f32[2,5,16,128]{3,2,1,0:T(8,128)S(1)}, u32[]{:S(2)}, u32[]{:S(2)}) collective-permute-start(f32[2,5,16,128]{3,2,1,0:T(8,128)} %get-tuple-element.24), channel_id=1, source_target_pairs={{0,1},{1,0},{2,3},{3,2},{4,5},{5,4},{6,7},{7,6},{8,9},{9,8},{10,11... | collective-permute-start | bytes 245768 | tf_op jit(solution)/shard_map/ppermute | solution.py:20
  33.9 0.1 collective-permute-start.3
  34.0 0.5 collective-permute-start.4
  34.5 1.0 %collective-permute-start.5 = (f32[5,8,8,128]{3,2,1,0:T(8,128)}, f32[5,8,8,128]{3,2,1,0:T(8,128)S(1)}, u32[]{:S(2)}, u32[]{:S(2)}) collective-permute-start(f32[5,8,8,128]{3,2,1,0:T(8,128)} %get-tuple-element.22), channel_id=1, source_target_pairs={{0,6},{2,0},{4,2},{6,4},{1,7},{3,1},{5,3},{7,5},{8,14},{10,8},{12,... | collective-permute-start | bytes 491528 | tf_op jit(solution)/shard_map/ppermute | solution.py:20
  35.5 1.0 %collective-permute-start.6 = (f32[5,16,8,128]{3,2,1,0:T(8,128)}, f32[5,16,8,128]{3,2,1,0:T(8,128)S(1)}, u32[]{:S(2)}, u32[]{:S(2)}) collective-permute-start(f32[5,16,8,128]{3,2,1,0:T(8,128)} %get-tuple-element.23), channel_id=1, source_target_pairs={{0,2},{2,4},{4,6},{6,0},{1,3},{3,5},{5,7},{7,1},{8,10},{10,12},{12... | collective-permute-start | bytes 983048 | tf_op jit(solution)/shard_map/ppermute | solution.py:20
  36.5 0.0 collective-permute-done.7.az_ref
  36.5 0.0 copy-done.11
  36.5 0.0 copy-start.4
  36.5 0.1 reshape.53
  36.6 0.2 convert_reduce_fusion
  36.8 0.1 fusion.10
  37.0 0.3 fusion.2
  37.3 0.0 copy-done.10
  37.3 0.3 fusion.3
  37.6 0.3 fusion.4
  38.0 0.6 round-nearest-even_convert_fusion
  38.6 0.0 collective-permute-done.3.axl_ref
  38.6 0.0 copy-start.5
  38.6 0.2 collective-permute-done.4.axr_ref
  38.8 0.0 copy-start.2
  38.8 9.6 %collective-permute-done.5.ayl_ref = f32[5,8,8,128]{3,2,1,0:T(8,128)S(1)} collective-permute-done((f32[5,8,8,128]{3,2,1,0:T(8,128)}, f32[5,8,8,128]{3,2,1,0:T(8,128)S(1)}, u32[]{:S(2)}, u32[]{:S(2)}) %collective-permute-start.5) | collective-permute-done | bytes 163872 | tf_op jit(solution)/shard_map/ppermute | solution.py:20
  48.3 0.0 copy-start.1
  48.4 0.0 collective-permute-done.6.ayr_ref
  48.4 0.0 copy-start
  48.4 0.0 copy-done.4
  48.4 0.0 copy-done.5
  48.4 0.0 copy-done.2
  48.4 0.6 %copy-done.1 = f32[5,8,8,128]{3,2,1,0:T(8,128)} copy-done((f32[5,8,8,128]{3,2,1,0:T(8,128)}, f32[5,8,8,128]{3,2,1,0:T(8,128)S(1)}, u32[]{:S(2)}) %copy-start.1) | copy-done | bytes 163864
  49.0 0.1 copy-done
  49.1 3.6 %shard_map.106 = (f32[5,32,16,128]{3,2,1,0:T(8,128)}, f32[32,32]{1,0:T(8,128)}) custom-call(s32[16]{0:T(128)} %row_ref.1, s32[1]{0:T(128)S(6)} %copy.32.cnt_ref, f32[5,32,16,128]{3,2,1,0:T(8,128)} %get-tuple-element.19.sec_ref, f32[5,2,16,128]{3,2,1,0:T(8,128)} %copy-done.5, f32[5,3,16,128]{3,2,1,0:T(8,128)} %copy-done.2, ...), custom_call_target="tpu_custom_call", output_to_operand_aliasing={{0}: (2, {})} | custom-call | tf_op jit(solution)/shard_map/pallas_call | solution.py:283
  52.8 9.6 %all_to_all.9 = f32[32,1,32]{2,1,0:T(1,128)S(1)} all-to-all(f32[32,1,32]{2,1,0:T(1,128)} %bitcast.19), channel_id=1, replica_groups=mesh['gx'=4,'gy'=4,'gz'=2] {'gx','gy','gz'}, dimensions={0} | all-to-all | bytes 8192 | tf_op jit(solution)/shard_map/all_to_all | solution.py:294
  62.4 0.6 reduce_sum.49
  (1 shorter events, 0.0 us)
Async XLA Ops:
  0.6 9.6 %copy-start.8 = (f32[3,5,5]{2,0,1:T(4,128)S(1)}, f32[3,5,5]{2,0,1:T(4,128)}, u32[]{:S(2)}) copy-start(f32[3,5,5]{2,0,1:T(4,128)} %param.11) | copy-start | bytes 904
  0.6 10.2 %copy-start.9 = (f32[3,5,5]{2,0,1:T(4,128)S(1)}, f32[3,5,5]{2,0,1:T(4,128)}, u32[]{:S(2)}) copy-start(f32[3,5,5]{2,0,1:T(4,128)} %param.12) | copy-start | bytes 904
  3.0 9.9 %collective-permute-start.1 = (f32[5,32,128]{2,1,0:T(8,128)}, f32[5,32,128]{2,1,0:T(8,128)S(1)}, u32[]{:S(2)}, u32[]{:S(2)}) collective-permute-start(f32[5,32,128]{2,1,0:T(8,128)} %get-tuple-element.17), channel_id=1, source_target_pairs={{0,6},{2,0},{4,2},{6,4},{1,7},{3,1},{5,3},{7,5},{8,14},{10,8},{12,... | collective-permute-start | bytes 245768 | tf_op jit(solution)/shard_map/ppermute | solution.py:20
  8.0 3.4 %collective-permute-start = (f32[5,16,128]{2,1,0:T(8,128)}, f32[5,16,128]{2,1,0:T(8,128)S(1)}, u32[]{:S(2)}, u32[]{:S(2)}) collective-permute-start(f32[5,16,128]{2,1,0:T(8,128)} %get-tuple-element.16), channel_id=1, source_target_pairs={{0,24},{8,0},{16,8},{24,16},{1,25},{9,1},{17,9},{25,17},{2,26},{10... | collective-permute-start | bytes 122888 | tf_op jit(solution)/shard_map/ppermute | solution.py:20
  8.7 4.2 %collective-permute-start.2 = (f32[5,16,128]{2,1,0:T(8,128)}, f32[5,16,128]{2,1,0:T(8,128)S(1)}, u32[]{:S(2)}, u32[]{:S(2)}) collective-permute-start(f32[5,16,128]{2,1,0:T(8,128)} %get-tuple-element.18), channel_id=1, source_target_pairs={{0,1},{1,0},{2,3},{3,2},{4,5},{5,4},{6,7},{7,6},{8,9},{9,8},{10,11... | collective-permute-start | bytes 122888 | tf_op jit(solution)/shard_map/ppermute | solution.py:20
  11.4 25.1 %copy-start.11 = (s32[1024]{0:T(1024)S(1)}, s32[1024]{0:T(1024)}, u32[]{:S(2)}) copy-start(s32[1024]{0:T(1024)} %param.17) | copy-start | bytes 12292
  11.4 25.8 %copy-start.10 = (s32[16,128]{1,0:T(8,128)S(1)}, s32[16,128]{1,0:T(8,128)}, u32[]{:S(2)}) copy-start(s32[16,128]{1,0:T(8,128)} %param.14) | copy-start | bytes 24580
  11.4 1.5 %copy-start.6 = (f32[5,16,128]{2,1,0:T(8,128)}, f32[5,16,128]{2,1,0:T(8,128)S(1)}, u32[]{:S(2)}) copy-start(f32[5,16,128]{2,1,0:T(8,128)S(1)} %collective-permute-done.xf_ref) | copy-start | bytes 122884
  12.9 0.6 copy-start.7
  13.5 0.7 %copy-start.3 = (f32[5,32,128]{2,1,0:T(8,128)}, f32[5,32,128]{2,1,0:T(8,128)S(1)}, u32[]{:S(2)}) copy-start(f32[5,32,128]{2,1,0:T(8,128)S(1)} %collective-permute-done.1.yf_ref) | copy-start | bytes 245764
  31.7 4.8 %collective-permute-start.7 = (f32[2,5,16,128]{3,2,1,0:T(8,128)}, f32[2,5,16,128]{3,2,1,0:T(8,128)S(1)}, u32[]{:S(2)}, u32[]{:S(2)}) collective-permute-start(f32[2,5,16,128]{3,2,1,0:T(8,128)} %get-tuple-element.24), channel_id=1, source_target_pairs={{0,1},{1,0},{2,3},{3,2},{4,5},{5,4},{6,7},{7,6},{8,9},{9,8},{10,11... | collective-permute-start | bytes 245768 | tf_op jit(solution)/shard_map/ppermute | solution.py:20
  33.9 4.6 %collective-permute-start.3 = (f32[5,2,16,128]{3,2,1,0:T(8,128)}, f32[5,2,16,128]{3,2,1,0:T(8,128)S(1)}, u32[]{:S(2)}, u32[]{:S(2)}) collective-permute-start(f32[5,2,16,128]{3,2,1,0:T(8,128)} %get-tuple-element.20), channel_id=1, source_target_pairs={{0,24},{8,0},{16,8},{24,16},{1,25},{9,1},{17,9},{25,17},{2,26},{10... | collective-permute-start | bytes 245768 | tf_op jit(solution)/shard_map/ppermute | solution.py:20
  34.0 4.8 %collective-permute-start.4 = (f32[5,3,16,128]{3,2,1,0:T(8,128)}, f32[5,3,16,128]{3,2,1,0:T(8,128)S(1)}, u32[]{:S(2)}, u32[]{:S(2)}) collective-permute-start(f32[5,3,16,128]{3,2,1,0:T(8,128)} %get-tuple-element.21), channel_id=1, source_target_pairs={{0,8},{8,16},{16,24},{24,0},{1,9},{9,17},{17,25},{25,1},{2,10},{10... | collective-permute-start | bytes 368648 | tf_op jit(solution)/shard_map/ppermute | solution.py:20
  34.5 13.8 %collective-permute-start.5 = (f32[5,8,8,128]{3,2,1,0:T(8,128)}, f32[5,8,8,128]{3,2,1,0:T(8,128)S(1)}, u32[]{:S(2)}, u32[]{:S(2)}) collective-permute-start(f32[5,8,8,128]{3,2,1,0:T(8,128)} %get-tuple-element.22), channel_id=1, source_target_pairs={{0,6},{2,0},{4,2},{6,4},{1,7},{3,1},{5,3},{7,5},{8,14},{10,8},{12,... | collective-permute-start | bytes 491528 | tf_op jit(solution)/shard_map/ppermute | solution.py:20
  35.5 12.9 %collective-permute-start.6 = (f32[5,16,8,128]{3,2,1,0:T(8,128)}, f32[5,16,8,128]{3,2,1,0:T(8,128)S(1)}, u32[]{:S(2)}, u32[]{:S(2)}) collective-permute-start(f32[5,16,8,128]{3,2,1,0:T(8,128)} %get-tuple-element.23), channel_id=1, source_target_pairs={{0,2},{2,4},{4,6},{6,0},{1,3},{3,5},{5,7},{7,1},{8,10},{10,12},{12... | collective-permute-start | bytes 983048 | tf_op jit(solution)/shard_map/ppermute | solution.py:20
  36.5 11.8 %copy-start.4 = (f32[2,5,16,128]{3,2,1,0:T(8,128)}, f32[2,5,16,128]{3,2,1,0:T(8,128)S(1)}, u32[]{:S(2)}) copy-start(f32[2,5,16,128]{3,2,1,0:T(8,128)S(1)} %collective-permute-done.7.az_ref) | copy-start | bytes 245764
  38.6 9.8 %copy-start.5 = (f32[5,2,16,128]{3,2,1,0:T(8,128)}, f32[5,2,16,128]{3,2,1,0:T(8,128)S(1)}, u32[]{:S(2)}) copy-start(f32[5,2,16,128]{3,2,1,0:T(8,128)S(1)} %collective-permute-done.3.axl_ref) | copy-start | bytes 245764
  38.8 9.6 %copy-start.2 = (f32[5,3,16,128]{3,2,1,0:T(8,128)}, f32[5,3,16,128]{3,2,1,0:T(8,128)S(1)}, u32[]{:S(2)}) copy-start(f32[5,3,16,128]{3,2,1,0:T(8,128)S(1)} %collective-permute-done.4.axr_ref) | copy-start | bytes 368644
  48.3 0.7 %copy-start.1 = (f32[5,8,8,128]{3,2,1,0:T(8,128)}, f32[5,8,8,128]{3,2,1,0:T(8,128)S(1)}, u32[]{:S(2)}) copy-start(f32[5,8,8,128]{3,2,1,0:T(8,128)S(1)} %collective-permute-done.5.ayl_ref) | copy-start | bytes 491524
  48.4 0.8 %copy-start = (f32[5,16,8,128]{3,2,1,0:T(8,128)}, f32[5,16,8,128]{3,2,1,0:T(8,128)S(1)}, u32[]{:S(2)}) copy-start(f32[5,16,8,128]{3,2,1,0:T(8,128)S(1)} %collective-permute-done.6.ayr_ref) | copy-start | bytes 983044

commit v15 on v13

--- a/solution.py
+++ b/solution.py
@@ -104,58 +104,63 @@
             minus.append(m)
         return plus, minus
 
-    yr_parts = {}
-    yl_parts = {}
-    for xl in range(XC):
-        x = i * XC + xl
-        last = x == nx - 1
-        nxt = jnp.minimum(x + 1, nx - 1)
-        a = [adj_ref[f, x] for f in range(nf)]
-        plus, minus = flux(0, [jnp.where(last, xf_ref[g], adj_ref[g, nxt]) - a[g] for g in range(nf)])
-        for f in range(nf):
-            sx = offset_terms(plus[f], minus[f], lambda s, k: w_ref[0, s, k, f, xl])
-            for o in range(6):
-                acc_ref[f, x + o] = acc_ref[f, x + o] + sx[o]
-        a = [adj_ref[f, x] for f in range(nf)]
-        plus, minus = flux(1, [
-            jnp.where(row == ny - 1, yf_ref[g, pl.ds(x, 1), :], pltpu.roll(a[g], ny - 1, 0)) - a[g]
-            for g in range(nf)
-        ])
-        for f in range(nf):
-            sy = offset_terms(plus[f], minus[f], lambda s, k: w_ref[1, s, k, f, xl])
-            iy, wyr, wyl = split_rows(sy, row8, ny)
-            acc_ref[f, x + 2] = acc_ref[f, x + 2] + iy
-            rear = pltpu.roll(wyr, 4 * (xl % 2), 0)
-            lead = pltpu.roll(wyl, (2 + 2 * (xl % 4)) % 8, 0)
-            kr = (f, xl // 2)
-            kl = (f, xl // 4)
-            yr_parts[kr] = rear if kr not in yr_parts else yr_parts[kr] + rear
-            yl_parts[kl] = lead if kl not in yl_parts else yl_parts[kl] + lead
-        a = [adj_ref[f, x] for f in range(nf)]
-        zshift = nz - 1 - x
-        plus, minus = flux(2, [
-            jnp.where(lane == nz - 1, pltpu.roll(zf_ref[g], zshift, 1), pltpu.roll(a[g], nz - 1, 1)) - a[g]
-            for g in range(nf)
-        ])
-        for f in range(nf):
-            sz = offset_terms(plus[f], minus[f], lambda s, k: w_ref[2, s, k, f, xl])
-            iz, wzr, wzl = split_lanes(sz, lane, nz)
-            acc_ref[f, x + 2] = acc_ref[f, x + 2] + iz
-            zz_ref[0, f] = zz_ref[0, f] + pltpu.roll(wzl, 2 + 4 * x, 1)
-            zz_ref[1, f] = zz_ref[1, f] + pltpu.roll(wzr, 4 * x, 1)
-    for (f, t), v in yr_parts.items():
-        yr_ref[f, t] = v
-    for (f, t), v in yl_parts.items():
-        yl_ref[f, t] = v
-
-    @pl.when(i == pl.num_programs(0) - 1)
+    n = pl.num_programs(0) - 1
+
+    @pl.when(i < n)
     def _():
-        def body(x, c):
+        yr_parts = {}
+        yl_parts = {}
+        for xl in range(XC):
+            x = i * XC + xl
+            last = x == nx - 1
+            nxt = jnp.minimum(x + 1, nx - 1)
+            a = [adj_ref[f, x] for f in range(nf)]
+            plus, minus = flux(0, [jnp.where(last, xf_ref[g], adj_ref[g, nxt]) - a[g] for g in range(nf)])
             for f in range(nf):
-                sec_ref[f, x] = SECTION * (adj_ref[f, x] + acc_ref[f, x + 2])
-            return c
-
-        lax.fori_loop(0, nx, body, 0)
+                sx = offset_terms(plus[f], minus[f], lambda s, k: w_ref[0, s, k, f, xl])
+                for o in range(6):
+                    acc_ref[f, x + o] = acc_ref[f, x + o] + sx[o]
+            a = [adj_ref[f, x] for f in range(nf)]
+            plus, minus = flux(1, [
+                jnp.where(row == ny - 1, yf_ref[g, pl.ds(x, 1), :], pltpu.roll(a[g], ny - 1, 0)) - a[g]
+                for g in range(nf)
+            ])
+            for f in range(nf):
+                sy = offset_terms(plus[f], minus[f], lambda s, k: w_ref[1, s, k, f, xl])
+                iy, wyr, wyl = split_rows(sy, row8, ny)
+                acc_ref[f, x + 2] = acc_ref[f, x + 2] + iy
+                rear = pltpu.roll(wyr, 4 * (xl % 2), 0)
+                lead = pltpu.roll(wyl, (2 + 2 * (xl % 4)) % 8, 0)
+                kr = (f, xl // 2)
+                kl = (f, xl // 4)
+                yr_parts[kr] = rear if kr not in yr_parts else yr_parts[kr] + rear
+                yl_parts[kl] = lead if kl not in yl_parts else yl_parts[kl] + lead
+            a = [adj_ref[f, x] for f in range(nf)]
+            zshift = nz - 1 - x
+            plus, minus = flux(2, [
+                jnp.where(lane == nz - 1, pltpu.roll(zf_ref[g], zshift, 1), pltpu.roll(a[g], nz - 1, 1)) - a[g]
+                for g in range(nf)
+            ])
+            for f in range(nf):
+                sz = offset_terms(plus[f], minus[f], lambda s, k: w_ref[2, s, k, f, xl])
+                iz, wzr, wzl = split_lanes(sz, lane, nz)
+                acc_ref[f, x + 2] = acc_ref[f, x + 2] + iz
+                zz_ref[0, f] = zz_ref[0, f] + pltpu.roll(wzl, 2 + 4 * x, 1)
+                zz_ref[1, f] = zz_ref[1, f] + pltpu.roll(wzr, 4 * x, 1)
+        for (f, t), v in yr_parts.items():
+            yr_ref[f, t] = v
+        for (f, t), v in yl_parts.items():
+            yl_ref[f, t] = v
+
+    @pl.when(i >= 1)
+    def _():
+        for xl in range(XC):
+            x = (i - 1) * XC + xl
+            for f in range(nf):
+                sec_ref[f, xl] = SECTION * (adj_ref[f, x] + acc_ref[f, x + 2])
+
+    @pl.when(i == n)
+    def _():
         for f in range(nf):
             xl_ref[f] = acc_ref[f, 0:2]
             xr_ref[f] = acc_ref[f, nx + 2:nx + 5]
@@ -218,10 +223,11 @@
     yf = shift_from(yf, "gy", -1)
     zf = shift_from(zf, "gz", -1)
     const4 = lambda i: (0, 0, 0, 0)
+    last = nx // XC - 1
     const3 = lambda i: (0, 0, 0)
     sec, xl, xr, yl, yr, zz = pl.pallas_call(
         stencil_kernel,
-        grid=(nx // XC,),
+        grid=(nx // XC + 1,),
         out_shape=(
             jax.ShapeDtypeStruct((nf, nx, ny, nz), F32),
             jax.ShapeDtypeStruct((nf, 2, ny, nz), F32),
@@ -237,14 +243,14 @@
             pl.BlockSpec((nf, ny, nz), const3),
             pl.BlockSpec((nf, nx, nz), const3),
             pl.BlockSpec((nf, ny, nz), const3),
-            pl.BlockSpec((3, 2, 3, nf, XC, ny, nz), lambda i: (0, 0, 0, 0, i, 0, 0)),
+            pl.BlockSpec((3, 2, 3, nf, XC, ny, nz), lambda i: (0, 0, 0, 0, jnp.minimum(i, last), 0, 0)),
         ],
         out_specs=(
-            pl.BlockSpec((nf, nx, ny, nz), const4),
+            pl.BlockSpec((nf, XC, ny, nz), lambda i: (0, jnp.maximum(i - 1, 0), 0, 0)),
             pl.BlockSpec((nf, 2, ny, nz), const4),
             pl.BlockSpec((nf, 3, ny, nz), const4),
-            pl.BlockSpec((nf, XC // 4, 8, nz), lambda i: (0, i, 0, 0)),
-            pl.BlockSpec((nf, XC // 2, 8, nz), lambda i: (0, i, 0, 0)),
+            pl.BlockSpec((nf, XC // 4, 8, nz), lambda i: (0, jnp.minimum(i, last), 0, 0)),
+            pl.BlockSpec((nf, XC // 2, 8, nz), lambda i: (0, jnp.minimum(i, last), 0, 0)),
             pl.BlockSpec((2, nf, ny, nz), const4),
         ),
         scratch_shapes=[pltpu.VMEM((nf, nx + 5, ny, nz), F32)],

time: 61 us -> 60.8 us (level)
  no operation moved by 1% of the time
where the time goes in v15:
time: 60.8 us; the launch traced here: 60.3 us
  Pallas kernels  23.4 us (38%)
  starting transfers between devices  12.2 us (20%)
  blocking collectives  9.65 us (16%)
  waiting for transfers between devices  7.94 us (13%)
  local copies, waits for them, and re-layouts  3.28 us (5%)
  between operations  1.47 us (2%)
  other arithmetic  1.38 us (2%)
  matrix products  1.09 us (2%)
    pallas_call x1, Pallas kernels, on_device(): pl.pallas_call(stencil_kernel, grid=(nx // XC + 1,), out_shape=(jax.Shape...  17.4 us
    ppermute x8, starting transfers between devices, shift_from(): return lax.ppermute(x, axis, [(i, (i + by) % n) for i in range(n)])  12.2 us
    all_to_all x1, blocking collectives, on_device(): got = lax.all_to_all(t, AXES, 0, 0, tiled=True)  9.65 us
    ppermute x8, waiting for transfers between devices, shift_from(): return lax.ppermute(x, axis, [(i, (i + by) % n) for i in range(n)])  7.94 us
    pallas_call x1, Pallas kernels, on_device(): pl.pallas_call(fix_kernel, out_shape=(jax.ShapeDtypeStruct((nf, nx, ny, n...  3.64 us
    unnamed x26, local copies, waits for them, and re-layouts  3.21 us
    pallas_call x1, Pallas kernels, on_device(): pl.pallas_call(fronts_kernel, out_shape=(jax.ShapeDtypeStruct((nf, ny, nz...  2.35 us
  transfers between devices with their start and end apart: 8, of which 2 were waited for; matrix products, arithmetic and copies ran while one was open for 5% of the time, Pallas kernels for 0%

profile of v15, /device:TPU:0, one launch (start us, length us, event | category | flops | bytes accessed | tf_op | source)
XLA Modules:
  0.0 60.3 jit_solution(2437168053836053576)
XLA Ops:
  0.6 0.0 copy-start.11
  0.6 0.0 copy-start.10
  0.7 0.0 copy-start.8
  0.7 0.0 copy-start.9
  0.7 2.4 %shard_map.104 = (f32[5,16,128]{2,1,0:T(8,128)}, f32[5,32,128]{2,1,0:T(8,128)}, f32[5,16,128]{2,1,0:T(8,128)}) custom-call(f32[5,32,16,128]{3,2,1,0:T(8,128)} %adj_ref.3), custom_call_target="tpu_custom_call" | custom-call | tf_op jit(solution)/shard_map/pallas_call | solution.py:212
  3.0 2.4 %collective-permute-start = (f32[5,16,128]{2,1,0:T(8,128)}, f32[5,16,128]{2,1,0:T(8,128)S(1)}, u32[]{:S(2)}, u32[]{:S(2)}) collective-permute-start(f32[5,16,128]{2,1,0:T(8,128)} %get-tuple-element.13), channel_id=1, source_target_pairs={{0,24},{8,0},{16,8},{24,16},{1,25},{9,1},{17,9},{25,17},{2,26},{10... | collective-permute-start | bytes 122888 | tf_op jit(solution)/shard_map/ppermute | solution.py:20
  5.4 1.5 %collective-permute-start.2 = (f32[5,16,128]{2,1,0:T(8,128)}, f32[5,16,128]{2,1,0:T(8,128)S(1)}, u32[]{:S(2)}, u32[]{:S(2)}) collective-permute-start(f32[5,16,128]{2,1,0:T(8,128)} %get-tuple-element.15), channel_id=1, source_target_pairs={{0,1},{1,0},{2,3},{3,2},{4,5},{5,4},{6,7},{7,6},{8,9},{9,8},{10,11... | collective-permute-start | bytes 122888 | tf_op jit(solution)/shard_map/ppermute | solution.py:20
  6.9 3.6 %collective-permute-start.1 = (f32[5,32,128]{2,1,0:T(8,128)}, f32[5,32,128]{2,1,0:T(8,128)S(1)}, u32[]{:S(2)}, u32[]{:S(2)}) collective-permute-start(f32[5,32,128]{2,1,0:T(8,128)} %get-tuple-element.14), channel_id=1, source_target_pairs={{0,6},{2,0},{4,2},{6,4},{1,7},{3,1},{5,3},{7,5},{8,14},{10,8},{12,... | collective-permute-start | bytes 245768 | tf_op jit(solution)/shard_map/ppermute | solution.py:20
  10.5 0.0 copy-done.11
  10.5 0.1 reshape.53
  10.6 0.2 convert_reduce_fusion
  10.8 0.1 fusion.10
  10.9 0.3 fusion.2
  11.2 0.0 copy-done.10
  11.3 0.3 fusion.3
  11.6 0.0 copy-done.8
  11.6 0.6 copy.22.fp_ref
  12.2 0.0 copy-done.9
  12.2 0.6 copy.23.fm_ref
  12.8 0.0 collective-permute-done.xf_ref
  12.8 0.0 copy-start.6
  12.8 0.0 collective-permute-done.2.zf_ref
  12.8 0.0 copy-start.7
  12.8 0.1 collective-permute-done.1.yf_ref
  12.9 0.6 copy-done.6
  13.5 0.0 copy-done.7
  13.5 0.0 copy-start.3
  13.5 0.6 %copy-done.3 = f32[5,32,128]{2,1,0:T(8,128)} copy-done((f32[5,32,128]{2,1,0:T(8,128)}, f32[5,32,128]{2,1,0:T(8,128)S(1)}, u32[]{:S(2)}) %copy-start.3) | copy-done | bytes 81944
  14.1 17.4 %shard_map.105 = (f32[5,32,16,128]{3,2,1,0:T(8,128)}, f32[5,2,16,128]{3,2,1,0:T(8,128)}, f32[5,3,16,128]{3,2,1,0:T(8,128)}, f32[5,8,8,128]{3,2,1,0:T(8,128)}, f3...) custom-call(f32[3,5,5]{2,1,0:T(8,128)} %copy.22.fp_ref, f32[3,5,5]{2,1,0:T(8,128)} %copy.23.fm_ref, ...), custom_call_target="tpu_custom_call" | custom-call | tf_op jit(solution)/shard_map/pallas_call | solution.py:228
  31.5 0.1 collective-permute-start.6
  31.6 0.3 fusion.4
  31.9 0.2 collective-permute-start.3
  32.1 0.5 collective-permute-start.7
  32.6 0.1 collective-permute-start.4
  32.7 3.8 %collective-permute-start.5 = (f32[5,8,8,128]{3,2,1,0:T(8,128)}, f32[5,8,8,128]{3,2,1,0:T(8,128)S(1)}, u32[]{:S(2)}, u32[]{:S(2)}) collective-permute-start(f32[5,8,8,128]{3,2,1,0:T(8,128)} %get-tuple-element.19), channel_id=1, source_target_pairs={{0,6},{2,0},{4,2},{6,4},{1,7},{3,1},{5,3},{7,5},{8,14},{10,8},{12,... | collective-permute-start | bytes 491528 | tf_op jit(solution)/shard_map/ppermute | solution.py:20
  36.5 0.6 round-nearest-even_convert_fusion
  37.8 0.0 collective-permute-done.3.axl_ref
  37.8 0.0 copy-start.4
  37.8 0.0 collective-permute-done.7.az_ref
  37.8 0.0 copy-start.5
  37.8 0.0 collective-permute-done.4.axr_ref
  37.8 0.0 copy-start.2
  37.8 7.9 %collective-permute-done.5.ayl_ref = f32[5,8,8,128]{3,2,1,0:T(8,128)S(1)} collective-permute-done((f32[5,8,8,128]{3,2,1,0:T(8,128)}, f32[5,8,8,128]{3,2,1,0:T(8,128)S(1)}, u32[]{:S(2)}, u32[]{:S(2)}) %collective-permute-start.5) | collective-permute-done | bytes 163872 | tf_op jit(solution)/shard_map/ppermute | solution.py:20
  45.7 0.0 copy-start.1
  45.7 0.0 collective-permute-done.6.ayr_ref
  45.7 0.0 copy-start
  45.7 0.0 copy-done.4
  45.7 0.0 copy-done.5
  45.7 0.0 copy-done.2
  45.7 0.6 %copy-done.1 = f32[5,8,8,128]{3,2,1,0:T(8,128)} copy-done((f32[5,8,8,128]{3,2,1,0:T(8,128)}, f32[5,8,8,128]{3,2,1,0:T(8,128)S(1)}, u32[]{:S(2)}) %copy-start.1) | copy-done | bytes 163864
  46.4 0.1 copy-done
  46.5 3.6 %shard_map.106 = (f32[5,32,16,128]{3,2,1,0:T(8,128)}, f32[32,32]{1,0:T(8,128)}) custom-call(s32[16]{0:T(128)} %row_ref.1, s32[1]{0:T(128)S(6)} %copy.32.cnt_ref, f32[5,32,16,128]{3,2,1,0:T(8,128)} %get-tuple-element.16.sec_ref, f32[5,2,16,128]{3,2,1,0:T(8,128)} %copy-done.4, f32[5,3,16,128]{3,2,1,0:T(8,128)} %copy-done.2, ...), custom_call_target="tpu_custom_call", output_to_operand_aliasing={{0}: (2, {})} | custom-call | tf_op jit(solution)/shard_map/pallas_call | solution.py:288
  50.1 9.7 %all_to_all.9 = f32[32,1,32]{2,1,0:T(1,128)S(1)} all-to-all(f32[32,1,32]{2,1,0:T(1,128)} %bitcast.19), channel_id=1, replica_groups=mesh['gx'=4,'gy'=4,'gz'=2] {'gx','gy','gz'}, dimensions={0} | all-to-all | bytes 8192 | tf_op jit(solution)/shard_map/all_to_all | solution.py:299
  59.8 0.6 reduce_sum.49
  (1 shorter events, 0.0 us)
Async XLA Ops:
  0.6 9.9 %copy-start.11 = (s32[1024]{0:T(1024)S(1)}, s32[1024]{0:T(1024)}, u32[]{:S(2)}) copy-start(s32[1024]{0:T(1024)} %param.17) | copy-start | bytes 12292
  0.6 10.6 %copy-start.10 = (s32[16,128]{1,0:T(8,128)S(1)}, s32[16,128]{1,0:T(8,128)}, u32[]{:S(2)}) copy-start(s32[16,128]{1,0:T(8,128)} %param.14) | copy-start | bytes 24580
  0.7 11.0 %copy-start.8 = (f32[3,5,5]{2,0,1:T(4,128)S(1)}, f32[3,5,5]{2,0,1:T(4,128)}, u32[]{:S(2)}) copy-start(f32[3,5,5]{2,0,1:T(4,128)} %param.11) | copy-start | bytes 904
  0.7 11.6 %copy-start.9 = (f32[3,5,5]{2,0,1:T(4,128)S(1)}, f32[3,5,5]{2,0,1:T(4,128)}, u32[]{:S(2)}) copy-start(f32[3,5,5]{2,0,1:T(4,128)} %param.12) | copy-start | bytes 904
  3.0 9.8 %collective-permute-start = (f32[5,16,128]{2,1,0:T(8,128)}, f32[5,16,128]{2,1,0:T(8,128)S(1)}, u32[]{:S(2)}, u32[]{:S(2)}) collective-permute-start(f32[5,16,128]{2,1,0:T(8,128)} %get-tuple-element.13), channel_id=1, source_target_pairs={{0,24},{8,0},{16,8},{24,16},{1,25},{9,1},{17,9},{25,17},{2,26},{10... | collective-permute-start | bytes 122888 | tf_op jit(solution)/shard_map/ppermute | solution.py:20
  5.4 7.4 %collective-permute-start.2 = (f32[5,16,128]{2,1,0:T(8,128)}, f32[5,16,128]{2,1,0:T(8,128)S(1)}, u32[]{:S(2)}, u32[]{:S(2)}) collective-permute-start(f32[5,16,128]{2,1,0:T(8,128)} %get-tuple-element.15), channel_id=1, source_target_pairs={{0,1},{1,0},{2,3},{3,2},{4,5},{5,4},{6,7},{7,6},{8,9},{9,8},{10,11... | collective-permute-start | bytes 122888 | tf_op jit(solution)/shard_map/ppermute | solution.py:20
  6.9 6.0 %collective-permute-start.1 = (f32[5,32,128]{2,1,0:T(8,128)}, f32[5,32,128]{2,1,0:T(8,128)S(1)}, u32[]{:S(2)}, u32[]{:S(2)}) collective-permute-start(f32[5,32,128]{2,1,0:T(8,128)} %get-tuple-element.14), channel_id=1, source_target_pairs={{0,6},{2,0},{4,2},{6,4},{1,7},{3,1},{5,3},{7,5},{8,14},{10,8},{12,... | collective-permute-start | bytes 245768 | tf_op jit(solution)/shard_map/ppermute | solution.py:20
  12.8 0.6 %copy-start.6 = (f32[5,16,128]{2,1,0:T(8,128)}, f32[5,16,128]{2,1,0:T(8,128)S(1)}, u32[]{:S(2)}) copy-start(f32[5,16,128]{2,1,0:T(8,128)S(1)} %collective-permute-done.xf_ref) | copy-start | bytes 122884
  12.8 0.6 %copy-start.7 = (f32[5,16,128]{2,1,0:T(8,128)}, f32[5,16,128]{2,1,0:T(8,128)S(1)}, u32[]{:S(2)}) copy-start(f32[5,16,128]{2,1,0:T(8,128)S(1)} %collective-permute-done.2.zf_ref) | copy-start | bytes 122884
  13.5 0.6 %copy-start.3 = (f32[5,32,128]{2,1,0:T(8,128)}, f32[5,32,128]{2,1,0:T(8,128)S(1)}, u32[]{:S(2)}) copy-start(f32[5,32,128]{2,1,0:T(8,128)S(1)} %collective-permute-done.1.yf_ref) | copy-start | bytes 245764
  31.5 14.2 %collective-permute-start.6 = (f32[5,16,8,128]{3,2,1,0:T(8,128)}, f32[5,16,8,128]{3,2,1,0:T(8,128)S(1)}, u32[]{:S(2)}, u32[]{:S(2)}) collective-permute-start(f32[5,16,8,128]{3,2,1,0:T(8,128)} %get-tuple-element.20), channel_id=1, source_target_pairs={{0,2},{2,4},{4,6},{6,0},{1,3},{3,5},{5,7},{7,1},{8,10},{10,12},{12... | collective-permute-start | bytes 983048 | tf_op jit(solution)/shard_map/ppermute | solution.py:20
  31.9 5.9 %collective-permute-start.3 = (f32[5,2,16,128]{3,2,1,0:T(8,128)}, f32[5,2,16,128]{3,2,1,0:T(8,128)S(1)}, u32[]{:S(2)}, u32[]{:S(2)}) collective-permute-start(f32[5,2,16,128]{3,2,1,0:T(8,128)} %get-tuple-element.17), channel_id=1, source_target_pairs={{0,24},{8,0},{16,8},{24,16},{1,25},{9,1},{17,9},{25,17},{2,26},{10... | collective-permute-start | bytes 245768 | tf_op jit(solution)/shard_map/ppermute | solution.py:20
  32.1 5.7 %collective-permute-start.7 = (f32[2,5,16,128]{3,2,1,0:T(8,128)}, f32[2,5,16,128]{3,2,1,0:T(8,128)S(1)}, u32[]{:S(2)}, u32[]{:S(2)}) collective-permute-start(f32[2,5,16,128]{3,2,1,0:T(8,128)} %get-tuple-element.21), channel_id=1, source_target_pairs={{0,1},{1,0},{2,3},{3,2},{4,5},{5,4},{6,7},{7,6},{8,9},{9,8},{10,11... | collective-permute-start | bytes 245768 | tf_op jit(solution)/shard_map/ppermute | solution.py:20
  32.6 5.2 %collective-permute-start.4 = (f32[5,3,16,128]{3,2,1,0:T(8,128)}, f32[5,3,16,128]{3,2,1,0:T(8,128)S(1)}, u32[]{:S(2)}, u32[]{:S(2)}) collective-permute-start(f32[5,3,16,128]{3,2,1,0:T(8,128)} %get-tuple-element.18), channel_id=1, source_target_pairs={{0,8},{8,16},{16,24},{24,0},{1,9},{9,17},{17,25},{25,1},{2,10},{10... | collective-permute-start | bytes 368648 | tf_op jit(solution)/shard_map/ppermute | solution.py:20
  32.7 13.0 %collective-permute-start.5 = (f32[5,8,8,128]{3,2,1,0:T(8,128)}, f32[5,8,8,128]{3,2,1,0:T(8,128)S(1)}, u32[]{:S(2)}, u32[]{:S(2)}) collective-permute-start(f32[5,8,8,128]{3,2,1,0:T(8,128)} %get-tuple-element.19), channel_id=1, source_target_pairs={{0,6},{2,0},{4,2},{6,4},{1,7},{3,1},{5,3},{7,5},{8,14},{10,8},{12,... | collective-permute-start | bytes 491528 | tf_op jit(solution)/shard_map/ppermute | solution.py:20
  37.8 7.9 %copy-start.4 = (f32[5,2,16,128]{3,2,1,0:T(8,128)}, f32[5,2,16,128]{3,2,1,0:T(8,128)S(1)}, u32[]{:S(2)}) copy-start(f32[5,2,16,128]{3,2,1,0:T(8,128)S(1)} %collective-permute-done.3.axl_ref) | copy-start | bytes 245764
  37.8 7.9 %copy-start.5 = (f32[2,5,16,128]{3,2,1,0:T(8,128)}, f32[2,5,16,128]{3,2,1,0:T(8,128)S(1)}, u32[]{:S(2)}) copy-start(f32[2,5,16,128]{3,2,1,0:T(8,128)S(1)} %collective-permute-done.7.az_ref) | copy-start | bytes 245764
  37.8 7.9 %copy-start.2 = (f32[5,3,16,128]{3,2,1,0:T(8,128)}, f32[5,3,16,128]{3,2,1,0:T(8,128)S(1)}, u32[]{:S(2)}) copy-start(f32[5,3,16,128]{3,2,1,0:T(8,128)S(1)} %collective-permute-done.4.axr_ref) | copy-start | bytes 368644
  45.7 0.7 %copy-start.1 = (f32[5,8,8,128]{3,2,1,0:T(8,128)}, f32[5,8,8,128]{3,2,1,0:T(8,128)S(1)}, u32[]{:S(2)}) copy-start(f32[5,8,8,128]{3,2,1,0:T(8,128)S(1)} %collective-permute-done.5.ayl_ref) | copy-start | bytes 491524
  45.7 0.8 %copy-start = (f32[5,16,8,128]{3,2,1,0:T(8,128)}, f32[5,16,8,128]{3,2,1,0:T(8,128)S(1)}, u32[]{:S(2)}) copy-start(f32[5,16,8,128]{3,2,1,0:T(8,128)S(1)} %collective-permute-done.6.ayr_ref) | copy-start | bytes 983044

commit v16 on v15

--- a/solution.py
+++ b/solution.py
@@ -294,6 +294,7 @@
         in_specs=[SMEM, SMEM] + [VMEM] * 9,
         out_specs=(VMEM, VMEM),
         input_output_aliases={2: 0},
+        compiler_params=pltpu.CompilerParams(vmem_limit_bytes=16 * 1024 * 1024),
     )(wall_row, wall_count, sec, axl, axr, ayl, ayr, az, wall_coef, cell_own, cell_rank)
 
     got = lax.all_to_all(t, AXES, 0, 0, tiled=True)

time: 60.8 us -> 59.7 us (0.982)
  local copies, waits for them, and re-layouts: 3.28 us -> 2.51 us
  waiting for transfers between devices: 7.94 us -> 8.55 us
    unnamed x26 -> x20, local copies, waits for them, and re-layouts: 3.21 us -> 2.44 us
    ppermute x8, waiting for transfers between devices: 7.94 us -> 8.55 us  [shift_from(): return lax.ppermute(x, axis, [(i, (i + by) % n) for i in range(n)])]
  transfers between devices with their start and end apart: 8 -> 8, of which waited for: 2 -> 1; matrix products, arithmetic and copies ran while one was open for 5% -> 4% of each run, Pallas kernels for 0% -> 0%
where the time goes in v16:
time: 59.7 us; the launch traced here: 59.3 us
  Pallas kernels  23.2 us (39%)
  starting transfers between devices  12.2 us (20%)
  blocking collectives  9.49 us (16%)
  waiting for transfers between devices  8.55 us (14%)
  local copies, waits for them, and re-layouts  2.51 us (4%)
  between operations  1.44 us (2%)
  matrix products  1.09 us (2%)
  other arithmetic  0.79 us (1%)
    pallas_call x1, Pallas kernels, on_device(): pl.pallas_call(stencil_kernel, grid=(nx // XC + 1,), out_shape=(jax.Shape...  17.4 us
    ppermute x8, starting transfers between devices, shift_from(): return lax.ppermute(x, axis, [(i, (i + by) % n) for i in range(n)])  12.2 us
    all_to_all x1, blocking collectives, on_device(): got = lax.all_to_all(t, AXES, 0, 0, tiled=True)  9.49 us
    ppermute x8, waiting for transfers between devices, shift_from(): return lax.ppermute(x, axis, [(i, (i + by) % n) for i in range(n)])  8.55 us
    pallas_call x1, Pallas kernels, on_device(): pl.pallas_call(fix_kernel, out_shape=(jax.ShapeDtypeStruct((nf, nx, ny, n...  3.51 us
    unnamed x20, local copies, waits for them, and re-layouts  2.44 us
    pallas_call x1, Pallas kernels, on_device(): pl.pallas_call(fronts_kernel, out_shape=(jax.ShapeDtypeStruct((nf, ny, nz...  2.35 us
  transfers between devices with their start and end apart: 8, of which 1 were waited for; matrix products, arithmetic and copies ran while one was open for 4% of the time, Pallas kernels for 0%

profile of v16, /device:TPU:0, one launch (start us, length us, event | category | flops | bytes accessed | tf_op | source)
XLA Modules:
  0.0 59.3 jit_solution(6958703414058129334)
XLA Ops:
  0.6 0.0 copy-start.8
  0.6 0.0 copy-start.7
  0.7 0.0 copy-start.5
  0.7 0.0 copy-start.6
  0.7 2.3 %shard_map.104 = (f32[5,16,128]{2,1,0:T(8,128)}, f32[5,32,128]{2,1,0:T(8,128)}, f32[5,16,128]{2,1,0:T(8,128)}) custom-call(f32[5,32,16,128]{3,2,1,0:T(8,128)} %adj_ref.3), custom_call_target="tpu_custom_call" | custom-call | tf_op jit(solution)/shard_map/pallas_call | solution.py:212
  3.0 2.4 %collective-permute-start = (f32[5,16,128]{2,1,0:T(8,128)}, f32[5,16,128]{2,1,0:T(8,128)S(1)}, u32[]{:S(2)}, u32[]{:S(2)}) collective-permute-start(f32[5,16,128]{2,1,0:T(8,128)} %get-tuple-element.13), channel_id=1, source_target_pairs={{0,24},{8,0},{16,8},{24,16},{1,25},{9,1},{17,9},{25,17},{2,26},{10... | collective-permute-start | bytes 122888 | tf_op jit(solution)/shard_map/ppermute | solution.py:20
  5.4 1.5 %collective-permute-start.2 = (f32[5,16,128]{2,1,0:T(8,128)}, f32[5,16,128]{2,1,0:T(8,128)S(1)}, u32[]{:S(2)}, u32[]{:S(2)}) collective-permute-start(f32[5,16,128]{2,1,0:T(8,128)} %get-tuple-element.15), channel_id=1, source_target_pairs={{0,1},{1,0},{2,3},{3,2},{4,5},{5,4},{6,7},{7,6},{8,9},{9,8},{10,11... | collective-permute-start | bytes 122888 | tf_op jit(solution)/shard_map/ppermute | solution.py:20
  6.9 3.6 %collective-permute-start.1 = (f32[5,32,128]{2,1,0:T(8,128)}, f32[5,32,128]{2,1,0:T(8,128)S(1)}, u32[]{:S(2)}, u32[]{:S(2)}) collective-permute-start(f32[5,32,128]{2,1,0:T(8,128)} %get-tuple-element.14), channel_id=1, source_target_pairs={{0,6},{2,0},{4,2},{6,4},{1,7},{3,1},{5,3},{7,5},{8,14},{10,8},{12,... | collective-permute-start | bytes 245768 | tf_op jit(solution)/shard_map/ppermute | solution.py:20
  10.5 0.0 copy-done.8
  10.5 0.1 reshape.53
  10.6 0.2 convert_reduce_fusion
  10.8 0.1 fusion.10
  10.9 0.3 fusion.2
  11.2 0.0 copy-done.7
  11.3 0.3 fusion.3
  11.6 0.0 copy-done.5
  11.6 0.6 %copy.22.fp_ref = f32[3,5,5]{2,1,0:T(8,128)} copy(f32[3,5,5]{2,0,1:T(4,128)S(1)} %copy-done.5) | data formatting | bytes 600 | tf_op args[2]
  12.2 0.0 copy-done.6
  12.2 0.6 %copy.23.fm_ref = f32[3,5,5]{2,1,0:T(8,128)} copy(f32[3,5,5]{2,0,1:T(4,128)S(1)} %copy-done.6) | data formatting | bytes 600 | tf_op args[3]
  12.8 0.0 copy-start
  12.8 0.0 copy-start.1
  12.8 0.0 collective-permute-done.xf_ref
  12.8 0.0 copy-start.3
  12.8 0.0 collective-permute-done.2.zf_ref
  12.8 0.0 copy-start.4
  12.9 0.0 collective-permute-done.1.yf_ref
  12.9 0.5 copy-done.3
  13.4 0.0 copy-done.4
  13.5 0.0 copy-start.2
  13.5 0.6 %copy-done.2 = f32[5,32,128]{2,1,0:T(8,128)} copy-done((f32[5,32,128]{2,1,0:T(8,128)}, f32[5,32,128]{2,1,0:T(8,128)S(1)}, u32[]{:S(2)}) %copy-start.2) | copy-done | bytes 81944
  14.1 17.4 %shard_map.105 = (f32[5,32,16,128]{3,2,1,0:T(8,128)}, f32[5,2,16,128]{3,2,1,0:T(8,128)}, f32[5,3,16,128]{3,2,1,0:T(8,128)}, f32[5,8,8,128]{3,2,1,0:T(8,128)}, f3...) custom-call(f32[3,5,5]{2,1,0:T(8,128)} %copy.22.fp_ref, f32[3,5,5]{2,1,0:T(8,128)} %copy.23.fm_ref, ...), custom_call_target="tpu_custom_call" | custom-call | tf_op jit(solution)/shard_map/pallas_call | solution.py:228
  31.5 0.1 collective-permute-start.6
  31.5 0.3 fusion.4
  31.9 0.2 collective-permute-start.3
  32.1 0.5 collective-permute-start.7
  32.6 0.1 collective-permute-start.4
  32.7 3.8 %collective-permute-start.5 = (f32[5,8,8,128]{3,2,1,0:T(8,128)}, f32[5,8,8,128]{3,2,1,0:T(8,128)S(1)}, u32[]{:S(2)}, u32[]{:S(2)}) collective-permute-start(f32[5,8,8,128]{3,2,1,0:T(8,128)} %get-tuple-element.19), channel_id=1, source_target_pairs={{0,6},{2,0},{4,2},{6,4},{1,7},{3,1},{5,3},{7,5},{8,14},{10,8},{12,... | collective-permute-start | bytes 491528 | tf_op jit(solution)/shard_map/ppermute | solution.py:20
  37.2 0.0 collective-permute-done.3.axl_ref
  37.2 0.0 collective-permute-done.7.az_ref
  37.2 0.0 collective-permute-done.4.axr_ref
  37.2 8.5 %collective-permute-done.5.ayl_ref = f32[5,8,8,128]{3,2,1,0:T(8,128)S(1)} collective-permute-done((f32[5,8,8,128]{3,2,1,0:T(8,128)}, f32[5,8,8,128]{3,2,1,0:T(8,128)S(1)}, u32[]{:S(2)}, u32[]{:S(2)}) %collective-permute-start.5) | collective-permute-done | bytes 163872 | tf_op jit(solution)/shard_map/ppermute | solution.py:20
  45.7 0.0 collective-permute-done.6.ayr_ref
  45.7 0.0 copy-done
  45.7 0.0 copy-done.1
  45.7 3.5 %shard_map.106 = (f32[5,32,16,128]{3,2,1,0:T(8,128)}, f32[32,32]{1,0:T(8,128)S(1)}) custom-call(s32[16]{0:T(128)S(1)} %copy-done.1, s32[1]{0:T(128)S(6)} %copy.32.cnt_ref, f32[5,32,16,128]{3,2,1,0:T(8,128)} %get-tuple-element.16.sec_ref, f32[5,2,16,128]{3,2,1,0:T(8,128)S(1)} %collective-permute-done.3.axl_ref, ...), custom_call_target="tpu_custom_call", output_to_operand_aliasing={{0}: (2, {})} | custom-call | tf_op jit(solution)/shard_map/pallas_call | solution.py:288
  49.2 9.5 %all_to_all.9 = f32[32,1,32]{2,1,0:T(1,128)S(1)} all-to-all(f32[32,1,32]{2,1,0:T(1,128)S(1)} %bitcast.19), channel_id=1, replica_groups=mesh['gx'=4,'gy'=4,'gz'=2] {'gx','gy','gz'}, dimensions={0} | all-to-all | bytes 8192 | tf_op jit(solution)/shard_map/all_to_all | solution.py:300
  58.7 0.6 reduce_sum.49
  (2 shorter events, 0.0 us)
Async XLA Ops:
  0.6 9.9 %copy-start.8 = (s32[1024]{0:T(1024)S(1)}, s32[1024]{0:T(1024)}, u32[]{:S(2)}) copy-start(s32[1024]{0:T(1024)} %param.17) | copy-start | bytes 12292
  0.6 10.6 %copy-start.7 = (s32[16,128]{1,0:T(8,128)S(1)}, s32[16,128]{1,0:T(8,128)}, u32[]{:S(2)}) copy-start(s32[16,128]{1,0:T(8,128)} %param.14) | copy-start | bytes 24580
  0.7 11.0 %copy-start.5 = (f32[3,5,5]{2,0,1:T(4,128)S(1)}, f32[3,5,5]{2,0,1:T(4,128)}, u32[]{:S(2)}) copy-start(f32[3,5,5]{2,0,1:T(4,128)} %param.11) | copy-start | bytes 904
  0.7 11.6 %copy-start.6 = (f32[3,5,5]{2,0,1:T(4,128)S(1)}, f32[3,5,5]{2,0,1:T(4,128)}, u32[]{:S(2)}) copy-start(f32[3,5,5]{2,0,1:T(4,128)} %param.12) | copy-start | bytes 904
  3.0 9.8 %collective-permute-start = (f32[5,16,128]{2,1,0:T(8,128)}, f32[5,16,128]{2,1,0:T(8,128)S(1)}, u32[]{:S(2)}, u32[]{:S(2)}) collective-permute-start(f32[5,16,128]{2,1,0:T(8,128)} %get-tuple-element.13), channel_id=1, source_target_pairs={{0,24},{8,0},{16,8},{24,16},{1,25},{9,1},{17,9},{25,17},{2,26},{10... | collective-permute-start | bytes 122888 | tf_op jit(solution)/shard_map/ppermute | solution.py:20
  5.4 7.4 %collective-permute-start.2 = (f32[5,16,128]{2,1,0:T(8,128)}, f32[5,16,128]{2,1,0:T(8,128)S(1)}, u32[]{:S(2)}, u32[]{:S(2)}) collective-permute-start(f32[5,16,128]{2,1,0:T(8,128)} %get-tuple-element.15), channel_id=1, source_target_pairs={{0,1},{1,0},{2,3},{3,2},{4,5},{5,4},{6,7},{7,6},{8,9},{9,8},{10,11... | collective-permute-start | bytes 122888 | tf_op jit(solution)/shard_map/ppermute | solution.py:20
  6.9 6.0 %collective-permute-start.1 = (f32[5,32,128]{2,1,0:T(8,128)}, f32[5,32,128]{2,1,0:T(8,128)S(1)}, u32[]{:S(2)}, u32[]{:S(2)}) collective-permute-start(f32[5,32,128]{2,1,0:T(8,128)} %get-tuple-element.14), channel_id=1, source_target_pairs={{0,6},{2,0},{4,2},{6,4},{1,7},{3,1},{5,3},{7,5},{8,14},{10,8},{12,... | collective-permute-start | bytes 245768 | tf_op jit(solution)/shard_map/ppermute | solution.py:20
  12.8 32.9 %copy-start = (f32[5,16,128]{2,1,0:T(8,128)S(1)}, f32[5,16,128]{2,1,0:T(8,128)}, u32[]{:S(2)}) copy-start(f32[5,16,128]{2,1,0:T(8,128)} %coef_ref.1) | copy-start | bytes 122884
  12.8 32.9 %copy-start.1 = (s32[16]{0:T(128)S(1)}, s32[16]{0:T(128)}, u32[]{:S(2)}) copy-start(s32[16]{0:T(128)} %row_ref.1) | copy-start | bytes 196
  12.8 0.6 %copy-start.3 = (f32[5,16,128]{2,1,0:T(8,128)}, f32[5,16,128]{2,1,0:T(8,128)S(1)}, u32[]{:S(2)}) copy-start(f32[5,16,128]{2,1,0:T(8,128)S(1)} %collective-permute-done.xf_ref) | copy-start | bytes 122884
  12.8 0.6 %copy-start.4 = (f32[5,16,128]{2,1,0:T(8,128)}, f32[5,16,128]{2,1,0:T(8,128)S(1)}, u32[]{:S(2)}) copy-start(f32[5,16,128]{2,1,0:T(8,128)S(1)} %collective-permute-done.2.zf_ref) | copy-start | bytes 122884
  13.5 0.6 %copy-start.2 = (f32[5,32,128]{2,1,0:T(8,128)}, f32[5,32,128]{2,1,0:T(8,128)S(1)}, u32[]{:S(2)}) copy-start(f32[5,32,128]{2,1,0:T(8,128)S(1)} %collective-permute-done.1.yf_ref) | copy-start | bytes 245764
  31.5 14.2 %collective-permute-start.6 = (f32[5,16,8,128]{3,2,1,0:T(8,128)}, f32[5,16,8,128]{3,2,1,0:T(8,128)S(1)}, u32[]{:S(2)}, u32[]{:S(2)}) collective-permute-start(f32[5,16,8,128]{3,2,1,0:T(8,128)} %get-tuple-element.20), channel_id=1, source_target_pairs={{0,2},{2,4},{4,6},{6,0},{1,3},{3,5},{5,7},{7,1},{8,10},{10,12},{12... | collective-permute-start | bytes 983048 | tf_op jit(solution)/shard_map/ppermute | solution.py:20
  31.9 5.3 %collective-permute-start.3 = (f32[5,2,16,128]{3,2,1,0:T(8,128)}, f32[5,2,16,128]{3,2,1,0:T(8,128)S(1)}, u32[]{:S(2)}, u32[]{:S(2)}) collective-permute-start(f32[5,2,16,128]{3,2,1,0:T(8,128)} %get-tuple-element.17), channel_id=1, source_target_pairs={{0,24},{8,0},{16,8},{24,16},{1,25},{9,1},{17,9},{25,17},{2,26},{10... | collective-permute-start | bytes 245768 | tf_op jit(solution)/shard_map/ppermute | solution.py:20
  32.1 5.1 %collective-permute-start.7 = (f32[2,5,16,128]{3,2,1,0:T(8,128)}, f32[2,5,16,128]{3,2,1,0:T(8,128)S(1)}, u32[]{:S(2)}, u32[]{:S(2)}) collective-permute-start(f32[2,5,16,128]{3,2,1,0:T(8,128)} %get-tuple-element.21), channel_id=1, source_target_pairs={{0,1},{1,0},{2,3},{3,2},{4,5},{5,4},{6,7},{7,6},{8,9},{9,8},{10,11... | collective-permute-start | bytes 245768 | tf_op jit(solution)/shard_map/ppermute | solution.py:20
  32.6 4.6 %collective-permute-start.4 = (f32[5,3,16,128]{3,2,1,0:T(8,128)}, f32[5,3,16,128]{3,2,1,0:T(8,128)S(1)}, u32[]{:S(2)}, u32[]{:S(2)}) collective-permute-start(f32[5,3,16,128]{3,2,1,0:T(8,128)} %get-tuple-element.18), channel_id=1, source_target_pairs={{0,8},{8,16},{16,24},{24,0},{1,9},{9,17},{17,25},{25,1},{2,10},{10... | collective-permute-start | bytes 368648 | tf_op jit(solution)/shard_map/ppermute | solution.py:20
  32.7 13.0 %collective-permute-start.5 = (f32[5,8,8,128]{3,2,1,0:T(8,128)}, f32[5,8,8,128]{3,2,1,0:T(8,128)S(1)}, u32[]{:S(2)}, u32[]{:S(2)}) collective-permute-start(f32[5,8,8,128]{3,2,1,0:T(8,128)} %get-tuple-element.19), channel_id=1, source_target_pairs={{0,6},{2,0},{4,2},{6,4},{1,7},{3,1},{5,3},{7,5},{8,14},{10,8},{12,... | collective-permute-start | bytes 491528 | tf_op jit(solution)/shard_map/ppermute | solution.py:20

commit v17 on v16

--- a/solution.py
+++ b/solution.py
@@ -254,7 +254,9 @@
             pl.BlockSpec((2, nf, ny, nz), const4),
         ),
         scratch_shapes=[pltpu.VMEM((nf, nx + 5, ny, nz), F32)],
-        compiler_params=pltpu.CompilerParams(dimension_semantics=("arbitrary",)),
+        compiler_params=pltpu.CompilerParams(
+            dimension_semantics=("arbitrary",), vmem_limit_bytes=48 * 1024 * 1024
+        ),
     )(flux_plus, flux_minus, adjoint, xf, yf, zf, stencil_weights)
     axl = shift_from(xl, "gx", -1)
     axr = shift_from(xr, "gx", 1)

time: 59.7 us -> 58.3 us (0.977)
  local copies, waits for them, and re-layouts: 2.51 us -> 0.11 us
  blocking collectives: 9.49 us -> 10.4 us
    unnamed x20 -> x16, local copies, waits for them, and re-layouts: 2.44 us -> 0.04 us
    all_to_all x1, blocking collectives: 9.49 us -> 10.4 us  [on_device(): got = lax.all_to_all(t, AXES, 0, 0, tiled=True)]
    pallas_call x1, Pallas kernels: 17.4 us -> 16.7 us  [on_device(): pl.pallas_call(stencil_kernel, grid=(nx // XC + 1,), out_shape=(jax.Shape...]
  transfers between devices with their start and end apart: 8 -> 8, of which waited for: 1 -> 2; matrix products, arithmetic and copies ran while one was open for 4% -> 2% of each run, Pallas kernels for 0% -> 0%
where the time goes in v17:
time: 58.3 us; the launch traced here: 57.8 us
  Pallas kernels  22.7 us (39%)
  starting transfers between devices  12.4 us (21%)
  blocking collectives  10.4 us (18%)
  waiting for transfers between devices  8.91 us (15%)
  between operations  1.48 us (3%)
  matrix products  1.08 us (2%)
  other arithmetic  0.79 us (1%)
    pallas_call x1, Pallas kernels, on_device(): pl.pallas_call(stencil_kernel, grid=(nx // XC + 1,), out_shape=(jax.Shape...  16.7 us
    ppermute x8, starting transfers between devices, shift_from(): return lax.ppermute(x, axis, [(i, (i + by) % n) for i in range(n)])  12.4 us
    all_to_all x1, blocking collectives, on_device(): got = lax.all_to_all(t, AXES, 0, 0, tiled=True)  10.4 us
    ppermute x8, waiting for transfers between devices, shift_from(): return lax.ppermute(x, axis, [(i, (i + by) % n) for i in range(n)])  8.91 us
    pallas_call x1, Pallas kernels, on_device(): pl.pallas_call(fix_kernel, out_shape=(jax.ShapeDtypeStruct((nf, nx, ny, n...  3.51 us
    pallas_call x1, Pallas kernels, on_device(): pl.pallas_call(fronts_kernel, out_shape=(jax.ShapeDtypeStruct((nf, ny, nz...  2.41 us
  transfers between devices with their start and end apart: 8, of which 2 were waited for; matrix products, arithmetic and copies ran while one was open for 2% of the time, Pallas kernels for 0%

profile of v17, /device:TPU:0, one launch (start us, length us, event | category | flops | bytes accessed | tf_op | source)
XLA Modules:
  0.0 57.8 jit_solution(12236720372282832040)
XLA Ops:
  0.6 0.0 copy-start
  0.6 0.0 copy-start.6
  0.7 0.0 copy-start.5
  0.7 0.0 copy-start.3
  0.7 0.0 copy-start.4
  0.7 2.4 %shard_map.104 = (f32[5,16,128]{2,1,0:T(8,128)}, f32[5,32,128]{2,1,0:T(8,128)}, f32[5,16,128]{2,1,0:T(8,128)}) custom-call(f32[5,32,16,128]{3,2,1,0:T(8,128)} %adj_ref.3), custom_call_target="tpu_custom_call" | custom-call | tf_op jit(solution)/shard_map/pallas_call | solution.py:212
  3.1 2.4 %collective-permute-start = (f32[5,16,128]{2,1,0:T(8,128)}, f32[5,16,128]{2,1,0:T(8,128)S(1)}, u32[]{:S(2)}, u32[]{:S(2)}) collective-permute-start(f32[5,16,128]{2,1,0:T(8,128)} %get-tuple-element.13), channel_id=1, source_target_pairs={{0,24},{8,0},{16,8},{24,16},{1,25},{9,1},{17,9},{25,17},{2,26},{10... | collective-permute-start | bytes 122888 | tf_op jit(solution)/shard_map/ppermute | solution.py:20
  5.5 1.5 %collective-permute-start.2 = (f32[5,16,128]{2,1,0:T(8,128)}, f32[5,16,128]{2,1,0:T(8,128)S(1)}, u32[]{:S(2)}, u32[]{:S(2)}) collective-permute-start(f32[5,16,128]{2,1,0:T(8,128)} %get-tuple-element.15), channel_id=1, source_target_pairs={{0,1},{1,0},{2,3},{3,2},{4,5},{5,4},{6,7},{7,6},{8,9},{9,8},{10,11... | collective-permute-start | bytes 122888 | tf_op jit(solution)/shard_map/ppermute | solution.py:20
  7.0 3.6 %collective-permute-start.1 = (f32[5,32,128]{2,1,0:T(8,128)}, f32[5,32,128]{2,1,0:T(8,128)S(1)}, u32[]{:S(2)}, u32[]{:S(2)}) collective-permute-start(f32[5,32,128]{2,1,0:T(8,128)} %get-tuple-element.14), channel_id=1, source_target_pairs={{0,6},{2,0},{4,2},{6,4},{1,7},{3,1},{5,3},{7,5},{8,14},{10,8},{12,... | collective-permute-start | bytes 245768 | tf_op jit(solution)/shard_map/ppermute | solution.py:20
  10.6 0.0 copy-done.6
  10.6 0.1 reshape.53
  10.7 0.2 convert_reduce_fusion
  10.9 0.1 fusion.10
  11.0 0.3 fusion.2
  11.3 0.0 copy-done.5
  11.3 0.3 fusion.3
  11.7 0.0 copy-done.3
  11.7 0.0 copy-done.4
  11.7 0.0 copy-start.1
  11.7 0.0 copy-start.2
  11.8 0.0 collective-permute-done.xf_ref
  11.8 0.0 collective-permute-done.2.zf_ref
  11.8 1.2 %collective-permute-done.1.yf_ref = f32[5,32,128]{2,1,0:T(8,128)S(1)} collective-permute-done((f32[5,32,128]{2,1,0:T(8,128)}, f32[5,32,128]{2,1,0:T(8,128)S(1)}, u32[]{:S(2)}, u32[]{:S(2)}) %collective-permute-start.1) | collective-permute-done | bytes 81952 | tf_op jit(solution)/shard_map/ppermute | solution.py:20
  13.0 0.0 copy-done
  13.0 16.7 %shard_map.105 = (f32[5,32,16,128]{3,2,1,0:T(8,128)}, f32[5,2,16,128]{3,2,1,0:T(8,128)S(1)}, f32[5,3,16,128]{3,2,1,0:T(8,128)S(1)}, f32[5,8,8,128]{3,2,1,0:T(8,1...) custom-call(f32[3,5,5]{2,1,0:T(8,128)S(1)} %copy.22.fp_ref, f32[3,5,5]{2,1,0:T(8,128)S(1)} %copy.23.fm_ref, ...), custom_call_target="tpu_custom_call" | custom-call | tf_op jit(solution)/shard_map/pallas_call | solution.py:228
  29.7 0.3 collective-permute-start.6
  30.0 0.3 fusion.4
  30.3 0.1 collective-permute-start.3
  30.4 0.6 collective-permute-start.7
  30.9 0.2 collective-permute-start.4
  31.1 3.8 %collective-permute-start.5 = (f32[5,8,8,128]{3,2,1,0:T(8,128)S(1)}, f32[5,8,8,128]{3,2,1,0:T(8,128)S(1)}, u32[]{:S(2)}, u32[]{:S(2)}) collective-permute-start(f32[5,8,8,128]{3,2,1,0:T(8,128)S(1)} %get-tuple-element.19), channel_id=1, source_target_pairs={{0,6},{2,0},{4,2},{6,4},{1,7},{3,1},{5,3},{7,5},{8,14},{10,8},{12,... | collective-permute-start | bytes 491528 | tf_op jit(solution)/shard_map/ppermute | solution.py:20
  35.6 0.0 collective-permute-done.3.axl_ref
  35.6 0.0 collective-permute-done.7.az_ref
  35.6 0.0 collective-permute-done.4.axr_ref
  35.6 7.7 %collective-permute-done.5.ayl_ref = f32[5,8,8,128]{3,2,1,0:T(8,128)S(1)} collective-permute-done((f32[5,8,8,128]{3,2,1,0:T(8,128)S(1)}, f32[5,8,8,128]{3,2,1,0:T(8,128)S(1)}, u32[]{:S(2)}, u32[]{:S(2)}) %collective-permute-start.5) | collective-permute-done | bytes 163872 | tf_op jit(solution)/shard_map/ppermute | solution.py:20
  43.3 0.0 collective-permute-done.6.ayr_ref
  43.3 0.0 copy-done.1
  43.3 0.0 copy-done.2
  43.3 3.5 %shard_map.106 = (f32[5,32,16,128]{3,2,1,0:T(8,128)}, f32[32,32]{1,0:T(8,128)S(1)}) custom-call(s32[16]{0:T(128)S(1)} %copy-done.2, s32[1]{0:T(128)S(6)} %copy.32.cnt_ref, f32[5,32,16,128]{3,2,1,0:T(8,128)} %get-tuple-element.16.sec_ref, f32[5,2,16,128]{3,2,1,0:T(8,128)S(1)} %collective-permute-done.3.axl_ref, ...), custom_call_target="tpu_custom_call", output_to_operand_aliasing={{0}: (2, {})} | custom-call | tf_op jit(solution)/shard_map/pallas_call | solution.py:290
  46.8 10.4 %all_to_all.9 = f32[32,1,32]{2,1,0:T(1,128)S(1)} all-to-all(f32[32,1,32]{2,1,0:T(1,128)S(1)} %bitcast.19), channel_id=1, replica_groups=mesh['gx'=4,'gy'=4,'gz'=2] {'gx','gy','gz'}, dimensions={0} | all-to-all | bytes 8192 | tf_op jit(solution)/shard_map/all_to_all | solution.py:302
  57.2 0.6 reduce_sum.49
  (4 shorter events, 0.0 us)
Async XLA Ops:
  0.6 12.3 %copy-start = (f32[5,32,16,128]{3,2,1,0:T(8,128)S(1)}, f32[5,32,16,128]{3,2,1,0:T(8,128)}, u32[]{:S(2)}) copy-start(f32[5,32,16,128]{3,2,1,0:T(8,128)} %adj_ref.3) | copy-start | bytes 3932164
  0.6 10.0 %copy-start.6 = (s32[1024]{0:T(1024)S(1)}, s32[1024]{0:T(1024)}, u32[]{:S(2)}) copy-start(s32[1024]{0:T(1024)} %param.17) | copy-start | bytes 12292
  0.7 10.7 %copy-start.5 = (s32[16,128]{1,0:T(8,128)S(1)}, s32[16,128]{1,0:T(8,128)}, u32[]{:S(2)}) copy-start(s32[16,128]{1,0:T(8,128)} %param.14) | copy-start | bytes 24580
  0.7 11.0 %copy-start.3 = (f32[3,5,5]{2,0,1:T(4,128)S(1)}, f32[3,5,5]{2,0,1:T(4,128)}, u32[]{:S(2)}) copy-start(f32[3,5,5]{2,0,1:T(4,128)} %param.11) | copy-start | bytes 904
  0.7 11.0 %copy-start.4 = (f32[3,5,5]{2,0,1:T(4,128)S(1)}, f32[3,5,5]{2,0,1:T(4,128)}, u32[]{:S(2)}) copy-start(f32[3,5,5]{2,0,1:T(4,128)} %param.12) | copy-start | bytes 904
  3.1 8.7 %collective-permute-start = (f32[5,16,128]{2,1,0:T(8,128)}, f32[5,16,128]{2,1,0:T(8,128)S(1)}, u32[]{:S(2)}, u32[]{:S(2)}) collective-permute-start(f32[5,16,128]{2,1,0:T(8,128)} %get-tuple-element.13), channel_id=1, source_target_pairs={{0,24},{8,0},{16,8},{24,16},{1,25},{9,1},{17,9},{25,17},{2,26},{10... | collective-permute-start | bytes 122888 | tf_op jit(solution)/shard_map/ppermute | solution.py:20
  5.5 6.3 %collective-permute-start.2 = (f32[5,16,128]{2,1,0:T(8,128)}, f32[5,16,128]{2,1,0:T(8,128)S(1)}, u32[]{:S(2)}, u32[]{:S(2)}) collective-permute-start(f32[5,16,128]{2,1,0:T(8,128)} %get-tuple-element.15), channel_id=1, source_target_pairs={{0,1},{1,0},{2,3},{3,2},{4,5},{5,4},{6,7},{7,6},{8,9},{9,8},{10,11... | collective-permute-start | bytes 122888 | tf_op jit(solution)/shard_map/ppermute | solution.py:20
  7.0 6.0 %collective-permute-start.1 = (f32[5,32,128]{2,1,0:T(8,128)}, f32[5,32,128]{2,1,0:T(8,128)S(1)}, u32[]{:S(2)}, u32[]{:S(2)}) collective-permute-start(f32[5,32,128]{2,1,0:T(8,128)} %get-tuple-element.14), channel_id=1, source_target_pairs={{0,6},{2,0},{4,2},{6,4},{1,7},{3,1},{5,3},{7,5},{8,14},{10,8},{12,... | collective-permute-start | bytes 245768 | tf_op jit(solution)/shard_map/ppermute | solution.py:20
  11.7 31.6 %copy-start.1 = (f32[5,16,128]{2,1,0:T(8,128)S(1)}, f32[5,16,128]{2,1,0:T(8,128)}, u32[]{:S(2)}) copy-start(f32[5,16,128]{2,1,0:T(8,128)} %coef_ref.1) | copy-start | bytes 122884
  11.7 31.6 %copy-start.2 = (s32[16]{0:T(128)S(1)}, s32[16]{0:T(128)}, u32[]{:S(2)}) copy-start(s32[16]{0:T(128)} %row_ref.1) | copy-start | bytes 196
  29.7 13.6 %collective-permute-start.6 = (f32[5,16,8,128]{3,2,1,0:T(8,128)S(1)}, f32[5,16,8,128]{3,2,1,0:T(8,128)S(1)}, u32[]{:S(2)}, u32[]{:S(2)}) collective-permute-start(f32[5,16,8,128]{3,2,1,0:T(8,128)S(1)} %get-tuple-element.20), channel_id=1, source_target_pairs={{0,2},{2,4},{4,6},{6,0},{1,3},{3,5},{5,7},{7,1},{8,10},{10,12},{12... | collective-permute-start | bytes 983048 | tf_op jit(solution)/shard_map/ppermute | solution.py:20
  30.3 5.3 %collective-permute-start.3 = (f32[5,2,16,128]{3,2,1,0:T(8,128)S(1)}, f32[5,2,16,128]{3,2,1,0:T(8,128)S(1)}, u32[]{:S(2)}, u32[]{:S(2)}) collective-permute-start(f32[5,2,16,128]{3,2,1,0:T(8,128)S(1)} %get-tuple-element.17), channel_id=1, source_target_pairs={{0,24},{8,0},{16,8},{24,16},{1,25},{9,1},{17,9},{25,17},{2,26},{10... | collective-permute-start | bytes 245768 | tf_op jit(solution)/shard_map/ppermute | solution.py:20
  30.4 5.2 %collective-permute-start.7 = (f32[2,5,16,128]{3,2,1,0:T(8,128)S(1)}, f32[2,5,16,128]{3,2,1,0:T(8,128)S(1)}, u32[]{:S(2)}, u32[]{:S(2)}) collective-permute-start(f32[2,5,16,128]{3,2,1,0:T(8,128)S(1)} %get-tuple-element.21), channel_id=1, source_target_pairs={{0,1},{1,0},{2,3},{3,2},{4,5},{5,4},{6,7},{7,6},{8,9},{9,8},{10,11... | collective-permute-start | bytes 245768 | tf_op jit(solution)/shard_map/ppermute | solution.py:20
  30.9 4.7 %collective-permute-start.4 = (f32[5,3,16,128]{3,2,1,0:T(8,128)S(1)}, f32[5,3,16,128]{3,2,1,0:T(8,128)S(1)}, u32[]{:S(2)}, u32[]{:S(2)}) collective-permute-start(f32[5,3,16,128]{3,2,1,0:T(8,128)S(1)} %get-tuple-element.18), channel_id=1, source_target_pairs={{0,8},{8,16},{16,24},{24,0},{1,9},{9,17},{17,25},{25,1},{2,10},{10... | collective-permute-start | bytes 368648 | tf_op jit(solution)/shard_map/ppermute | solution.py:20
  31.1 12.2 %collective-permute-start.5 = (f32[5,8,8,128]{3,2,1,0:T(8,128)S(1)}, f32[5,8,8,128]{3,2,1,0:T(8,128)S(1)}, u32[]{:S(2)}, u32[]{:S(2)}) collective-permute-start(f32[5,8,8,128]{3,2,1,0:T(8,128)S(1)} %get-tuple-element.19), channel_id=1, source_target_pairs={{0,6},{2,0},{4,2},{6,4},{1,7},{3,1},{5,3},{7,5},{8,14},{10,8},{12,... | collective-permute-start | bytes 491528 | tf_op jit(solution)/shard_map/ppermute | solution.py:20
